TPU v7x, 32 devices: a whole 2x2x4 slice. The times are simulated.
32 devices in a mesh: grp: 2 (over y), seq: 4 (over z), head: 4 (over x, core).
Axes of the slice: x: 2, y: 2, z: 4, core: 2. Of those that a mesh axis runs over, the one named last changes fastest.
Arguments:
- inner_input: bfloat16 [8192, 4096], P(('grp', 'seq'), 'head'), parts along dimension 0, may hold values from -6 to 6
- state_input: bfloat16 [2, 8192, 512], P(None, ('grp', 'seq'), 'head'), parts along dimension 1, may hold values from -6 to 6
- conv_inner: bfloat16 [4, 4096], P(None, 'head'), may hold values from -3 to 3
- bias_inner: float32 [4096], P('head'), may hold values from -3 to 3
- conv_state: bfloat16 [2, 4, 512], P(None, None, 'head'), may hold values from -3 to 3
- bias_state: float32 [2, 512], P(None, 'head'), may hold values from -3 to 3
- step_size: float32 [64, 8192], P('head', ('grp', 'seq')), parts along dimension 1, may hold values from 0.005 to 0.045
- decay_rate: float32 [64], P('head'), may hold values from 0.0048828125 to 2.5
- skip_gain: float32 [64], P('head'), may hold values from -4 to 5
- lengths: int32 [6], P('grp'), parts along dimension 0, may hold values from 1 to 2048, 4096 in all
Outputs:
- mixed: bfloat16 [8192, 4096], P(('grp', 'seq'), 'head'), parts along dimension 0
There are 2 independent parts, one for each index of `grp`. A program takes and returns all parts, laid end to end along the dimension named above; an argument that names none is the same for every part. Nothing has to cross between parts.
All inputs are finite; a program needn't handle non-finite values.
Results may differ from a plain program's by a relative error of at most 0.0034.
Values may be sent and summed in bfloat16 or wider, within the bound.
No kernel may reach another device: no remote copies, remote signals or barrier semaphores. Data moves between devices by JAX's collectives and lax.ppermute only.
A program may use at most 64 MiB of HBM per device.

v0:
```python
import jax
import jax.numpy as jnp
from jax import lax
from jax.sharding import PartitionSpec as P

BLOCK = 128


def shifted(value, axis, steps):
    count = lax.axis_size(axis)
    initial, last = (max(0, -steps), min(count, count - steps))
    return lax.ppermute(value, axis, [(source, source + steps) for source in range(initial, last)])


def from_partner(block, axis, stride):
    count = lax.axis_size(axis)
    route = []
    for low in range(count):
        high = low | 1 << stride
        if high != low and high < count:
            route += [(low, high), (high, low)]
    return lax.ppermute(block, axis, route)


def segment_of(lengths, positions):
    starts = jnp.cumsum(lengths, dtype=jnp.int32) - lengths
    covered = (starts[None, :] <= positions[:, None]).astype(jnp.int32)
    return jnp.sum(covered, axis=1, dtype=jnp.int32) - 1


def convolve(extended, weight, bias_row, seg_ext, row_count):
    own_seg = seg_ext[3:]
    summed = (
        jnp.zeros(extended.shape[:-2] + (row_count, extended.shape[-1]), jnp.float32) + bias_row
    )
    for offset in range(4):
        kept_mask = (seg_ext[offset : offset + row_count] == own_seg).astype(jnp.float32)[:, None]
        window = extended[..., offset : offset + row_count, :].astype(jnp.float32)
        summed = summed + weight[offset].astype(jnp.float32) * window * kept_mask
    return jax.nn.silu(summed).astype(jnp.bfloat16)


def body(
    inner_input,
    state_input,
    conv_inner,
    bias_inner,
    conv_state,
    bias_state,
    step_size,
    decay_rate,
    skip_gain,
    lengths,
):
    precise = lax.Precision.HIGHEST
    own_rows = inner_input.shape[0]
    head_count = decay_rate.shape[0]
    head_width = inner_input.shape[1] // head_count
    group_half = state_input.shape[2]
    block_count = own_rows // BLOCK
    positions = lax.axis_index("seq") * own_rows + jnp.arange(own_rows + 3, dtype=jnp.int32) - 3
    seg_ext = segment_of(lengths, positions)
    inner_tail, state_tail = shifted((inner_input[-3:], state_input[:, -3:]), "seq", 1)
    weight_state = jnp.swapaxes(conv_state, 0, 1)[:, :, None, :]
    state_half = convolve(
        jnp.concatenate([state_tail, state_input], 1),
        weight_state,
        bias_state[:, None, :],
        seg_ext,
        own_rows,
    )
    partner = from_partner(state_half, "head", 0)
    inner_conv = convolve(
        jnp.concatenate([inner_tail, inner_input], 0), conv_inner, bias_inner, seg_ext, own_rows
    )
    lower_half = lax.axis_index("head") % 2 == 0
    state_full = jnp.where(
        lower_half,
        jnp.concatenate([state_half, partner], 2),
        jnp.concatenate([partner, state_half], 2),
    )
    b_blocks = state_full[0].reshape(block_count, BLOCK, 2 * group_half)
    c_blocks = state_full[1].reshape(block_count, BLOCK, 2 * group_half)
    steps_dt = step_size.reshape(head_count, block_count, BLOCK)
    log_decay = jnp.cumsum(-steps_dt * decay_rate[:, None, None], axis=2)
    seg_own = seg_ext[3:].reshape(block_count, BLOCK)
    seg_prev = seg_ext[2 : 2 + own_rows].reshape(block_count, BLOCK)[:, 0]
    scores = jnp.einsum("btn,bsn->bts", c_blocks, b_blocks, preferred_element_type=jnp.float32)
    block_pos = jnp.arange(BLOCK, dtype=jnp.int32)
    allowed = (block_pos[:, None] >= block_pos[None, :])[None] & (
        seg_own[:, :, None] == seg_own[:, None, :]
    )
    decay_grid = (
        jnp.exp(log_decay[:, :, :, None] - log_decay[:, :, None, :]) * steps_dt[:, :, None, :]
    )
    weights = jnp.where(allowed[None], decay_grid * scores[None], 0.0).astype(jnp.bfloat16)
    inner_blocks = inner_conv.reshape(block_count, BLOCK, head_count, head_width)
    intra_out = jnp.einsum(
        "hbts,bshp->bthp", weights, inner_blocks, preferred_element_type=jnp.float32
    )
    ending = (
        jnp.exp(log_decay[:, :, -1:] - log_decay)
        * steps_dt
        * (seg_own == seg_own[:, -1:]).astype(jnp.float32)[None]
    )
    weighted = (
        inner_blocks.astype(jnp.float32) * jnp.transpose(ending, (1, 2, 0))[:, :, :, None]
    ).astype(jnp.bfloat16)
    block_states = jnp.einsum(
        "bshp,bsn->bhpn", weighted, b_blocks, preferred_element_type=jnp.float32
    )
    block_decay = jnp.transpose(
        jnp.exp(log_decay[:, :, -1]) * (seg_own[:, -1] == seg_prev).astype(jnp.float32)[None]
    )

    def local_step(carry_pair, block_item):
        entering, prefix = carry_pair
        decay_block, state_block = block_item
        return (
            (decay_block[:, None, None] * entering + state_block, prefix * decay_block),
            (entering, prefix),
        )

    start_state = jnp.zeros((head_count, head_width, 2 * group_half), jnp.float32)
    start_prefix = jnp.ones((head_count,), jnp.float32)
    (local_end, total_decay), (entering, prefixes) = lax.scan(
        local_step, (start_state, start_prefix), (block_decay, block_states)
    )
    c_float = c_blocks.astype(jnp.float32)

    def relay(step_num, incoming):
        return shifted(
            (total_decay[:, None, None] * incoming + local_end).astype(jnp.bfloat16), "seq", 1
        ).astype(jnp.float32)

    incoming = lax.fori_loop(0, lax.axis_size("seq") - 1, relay, jnp.zeros_like(local_end))
    full_states = entering + prefixes[:, :, None, None] * incoming[None]
    inter_out = jnp.einsum("btn,bhpn->bthp", c_float, full_states, precision=precise)
    entry_coef = jnp.exp(log_decay) * (seg_own == seg_prev[:, None]).astype(jnp.float32)[None]
    inter_out = inter_out * jnp.transpose(entry_coef, (1, 2, 0))[:, :, :, None]
    mixed_out = (
        intra_out + inter_out + skip_gain[None, None, :, None] * inner_blocks.astype(jnp.float32)
    )
    return mixed_out.astype(jnp.bfloat16).reshape(own_rows, head_count * head_width)


def solution(mesh):
    return jax.shard_map(
        body,
        mesh=mesh,
        in_specs=(
            P(("grp", "seq"), "head"),
            P(None, ("grp", "seq"), "head"),
            P(None, "head"),
            P("head"),
            P(None, None, "head"),
            P(None, "head"),
            P("head", ("grp", "seq")),
            P("head"),
            P("head"),
            P("grp"),
        ),
        out_specs=P(("grp", "seq"), "head"),
        check_vma=False,
    )
```

profile of v0, /device:TPU:0, one launch (start us, length us, event | category | flops | bytes accessed | tf_op | source)
XLA Modules:
  0.0 150.1 jit_solution(6673128358136536196)
XLA Ops:
  0.0 1.3 slice.90
  1.3 5.5 %collective-permute-start.1 = (bf16[3,1024]{1,0:T(4,128)(2,1)}, bf16[3,1024]{1,0:T(4,128)(2,1)}, u32[]{:S(2)}, u32[]{:S(2)}) collective-permute-start(bf16[3,1024]{1,0:T(4,128)(2,1)} %slice.90), channel_id=1, source_target_pairs={{0,4},{4,8},{8,12},{1,5},{5,9},{9,13},{2,6},{6,10},{10,14},{3,7},{... | collective-permute-start | bytes 18440 | tf_op jit(solution)/shard_map/ppermute | solution.py:12
  6.8 0.7 slice.102
  7.5 2.9 %collective-permute-start.2 = (bf16[2,3,128]{2,1,0:T(4,128)(2,1)S(1)}, bf16[2,3,128]{2,1,0:T(4,128)(2,1)S(1)}, u32[]{:S(2)}, u32[]{:S(2)}) collective-permute-start(bf16[2,3,128]{2,1,0:T(4,128)(2,1)S(1)} %slice.102), channel_id=1, source_target_pairs={{0,4},{4,8},{8,12},{1,5},{5,9},{9,13},{2,6},{6,10},{10,14},{3,7},{... | collective-permute-start | bytes 4616 | tf_op jit(solution)/shard_map/ppermute | solution.py:12
  10.4 0.8 reduce-window.9
  12.4 0.9 copy.66
  13.3 0.7 fusion.27
  14.0 4.5 %reduce_window_sum.18 = f32[16,8,128]{2,1,0:T(8,128)S(1)} reduce-window(f32[16,8,128]{2,1,0:T(8,128)S(1)} %fusion.27, f32[]{:T(128)} %constant.63.clone.1), window={size=1x1x128 pad=0_0x0_0x127_0}, to_apply=%region_2.3 | reduce-window | flops 2080768 | bytes 131076 | tf_op jit(solution)/shard_map/jit(cumsum)/reduce_window_sum | solution.py:85
  18.9 0.9 copy_bitcast_fusion
  19.8 1.5 slice_convert_fusion.3
  22.2 0.8 slice_convert_fusion.7
  23.2 2.5 %multiply_convert_fusion.1 = bf16[2,1024,128]{2,1,0:T(8,128)(2,1)S(1)} fusion(bf16[2,1024,128]{2,1,0:T(8,128)(2,1)} %param.15, bf16[2,3,128]{2,1,0:T(4,128)(2,1)S(1)} %collective-permute-done.2, f32[2,128]{1,0:T(2,128)S(1)} %bitcast.92, f32[1024]{0:T(1024)S(1)} %get-tuple-element.149, f32[2,128]{1,0:T(2,128)S(1)} %bitcast.93, ...), kind=kLoop, calls=%fused_computation.38 | loop fusion | flops 7602176 | bytes 1067520 | tf_op jit(solution)/shard_map/convert_element_type | solution.py:40
  25.8 9.1 %multiply_convert_fusion = bf16[1024,1024]{1,0:T(8,128)(2,1)} fusion(bf16[1024,1024]{1,0:T(8,128)(2,1)} %param.14, bf16[3,1024]{1,0:T(4,128)(2,1)} %collective-permute-done.1, f32[1024]{0:T(1024)} %bitcast.88, f32[1024]{0:T(1024)S(1)} %get-tuple-element.149, f32[1024]{0:T(1024)} %bitcast.89, f32[1024]{0:T(1024)S(1)} %get-tuple-element.150, ...), kind=kLoop, calls=%fused_computation.28 | loop fusion | flops 30408704 | bytes 4233216 | tf_op jit(solution)/shard_map/convert_element_type | solution.py:40
  34.9 6.4 %reshape.191 = bf16[8,128,16,64]{3,2,1,0:T(8,128)(2,1)} reshape(bf16[1024,1024]{1,0:T(8,128)(2,1)} %multiply_convert_fusion) | data formatting | bytes 4194304 | tf_op jit(solution)/shard_map/reshape | solution.py:97
  41.3 5.8 %copy.50 = bf16[8,128,16,64]{1,3,2,0:T(8,128)(2,1)} copy(bf16[8,128,16,64]{3,2,1,0:T(8,128)(2,1)} %reshape.191) | data formatting | bytes 4194304 | tf_op jit(solution)/shard_map/reshape | solution.py:97
  47.5 1.3 copy-done
  48.9 4.5 %fusion.22 = f32[8,16,64,256]{3,2,1,0:T(8,128)} fusion(bf16[8,128,256,1]{2,1,3,0:T(8,128)(2,1)S(1)} %bitcast.81, bf16[8,128,16,64]{1,3,2,0:T(8,128)(2,1)S(1)} %copy-done, f32[8,128,16]{1,2,0:T(8,128)S(1)} %copy.54), kind=kOutput, calls=%fused_computation.34 | convolution fusion | flops 540016640 | bytes 11075584 | tf_op jit(solution)/shard_map/bshp,bsn->bhpn/dot_general | solution.py:109
  53.3 26.1 %while.28 = (s32[]{:T(128)}, f32[16,64,256]{2,1,0:T(8,128)S(1)}, f32[16]{0:T(128)S(1)}, f32[8,16,64,256]{3,2,1,0:T(8,128)}, f32[8,16]{1,0:T(8,128)S(1)}, /*index...) while((s32[]{:T(128)}, f32[16,64,256]{2,1,0:T(8,128)S(1)}, ...), condition=%wide.region_4.5_spmd.clone, body=%wide.region_3.4_spmd.clone.sunk | while | flops 1048611 | bytes 5243521 | solution.py:126
  53.3 1.2 bitcast_dynamic-update-slice_fusion.2
  54.5 0.7 fusion.45
  55.2 1.4 bitcast_add_fusion.3
  56.6 1.1 bitcast_dynamic-update-slice_fusion.2
  58.4 1.4 bitcast_add_fusion.3
  59.9 1.1 bitcast_dynamic-update-slice_fusion.2
  60.9 0.7 fusion.45
  61.6 1.4 bitcast_add_fusion.3
  63.1 1.1 bitcast_dynamic-update-slice_fusion.2
  64.9 1.4 bitcast_add_fusion.3
  66.4 1.1 bitcast_dynamic-update-slice_fusion.2
  68.2 1.4 bitcast_add_fusion.3
  69.7 1.1 bitcast_dynamic-update-slice_fusion.2
  71.4 1.4 bitcast_add_fusion.3
  72.9 1.1 bitcast_dynamic-update-slice_fusion.2
  74.7 1.4 bitcast_add_fusion.3
  76.2 1.1 bitcast_dynamic-update-slice_fusion.2
  77.9 1.4 bitcast_add_fusion.3
  79.4 1.1 fusion.36
  80.5 46.1 %while.29 = (s32[]{:T(128)}, f32[16,64,256]{2,1,0:T(8,128)S(1)}, f32[16]{0:T(128)S(1)}, f32[16,64,256]{2,1,0:T(8,128)S(1)}, s32[]{:T(128)}, /*index=5*/s32[]{:T(128)}) while((s32[]{:T(128)}, f32[16,64,256]{2,1,0:T(8,128)S(1)}, f32[16]{0:T(128)S(1)}, f32[16,64,256]{2,1,0:T(8,128)S(1)}, s32[]{:T(128)}, /*index=5*/s32[]{:T(128)}) %tuple.59), condition=%wide.region_6.7_spmd.clone, body=%wide.region_5.6_spmd.clone.sunk | while | flops 1310723 | bytes 6291639 | solution.py:136
  80.7 3.5 %collective-permute-start = (bf16[16,64,256]{2,1,0:T(8,128)(2,1)S(1)}, bf16[16,64,256]{2,1,0:T(8,128)(2,1)S(1)}, u32[]{:S(2)}, u32[]{:S(2)}) collective-permute-start(bf16[16,64,256]{2,1,0:T(8,128)(2,1)S(1)} %fusion.46), channel_id=1, source_target_pairs={{0,4},{4,8},{8,12},{1,5},{5,9},{9,13},{2,6},{6,10},{10,14},{3,7},{... | collective-permute-start | bytes 1572872 | tf_op jit(solution)/shard_map/while/body/eval_jaxpr/ppermute | solution.py:12
  84.2 11.8 %collective-permute-done = bf16[16,64,256]{2,1,0:T(8,128)(2,1)S(1)} collective-permute-done((bf16[16,64,256]{2,1,0:T(8,128)(2,1)S(1)}, bf16[16,64,256]{2,1,0:T(8,128)(2,1)S(1)}, u32[]{:S(2)}, u32[]{:S(2)}) %collective-permute-start) | collective-permute-done | bytes 524320 | tf_op jit(solution)/shard_map/while/body/eval_jaxpr/ppermute | solution.py:12
  96.3 4.4 %collective-permute-start = (bf16[16,64,256]{2,1,0:T(8,128)(2,1)S(1)}, bf16[16,64,256]{2,1,0:T(8,128)(2,1)S(1)}, u32[]{:S(2)}, u32[]{:S(2)}) collective-permute-start(bf16[16,64,256]{2,1,0:T(8,128)(2,1)S(1)} %fusion.46), channel_id=1, source_target_pairs={{0,4},{4,8},{8,12},{1,5},{5,9},{9,13},{2,6},{6,10},{10,14},{3,7},{... | collective-permute-start | bytes 1572872 | tf_op jit(solution)/shard_map/while/body/eval_jaxpr/ppermute | solution.py:12
  100.7 11.0 %collective-permute-done = bf16[16,64,256]{2,1,0:T(8,128)(2,1)S(1)} collective-permute-done((bf16[16,64,256]{2,1,0:T(8,128)(2,1)S(1)}, bf16[16,64,256]{2,1,0:T(8,128)(2,1)S(1)}, u32[]{:S(2)}, u32[]{:S(2)}) %collective-permute-start) | collective-permute-done | bytes 524320 | tf_op jit(solution)/shard_map/while/body/eval_jaxpr/ppermute | solution.py:12
  112.0 4.4 %collective-permute-start = (bf16[16,64,256]{2,1,0:T(8,128)(2,1)S(1)}, bf16[16,64,256]{2,1,0:T(8,128)(2,1)S(1)}, u32[]{:S(2)}, u32[]{:S(2)}) collective-permute-start(bf16[16,64,256]{2,1,0:T(8,128)(2,1)S(1)} %fusion.46), channel_id=1, source_target_pairs={{0,4},{4,8},{8,12},{1,5},{5,9},{9,13},{2,6},{6,10},{10,14},{3,7},{... | collective-permute-start | bytes 1572872 | tf_op jit(solution)/shard_map/while/body/eval_jaxpr/ppermute | solution.py:12
  116.4 10.1 %collective-permute-done = bf16[16,64,256]{2,1,0:T(8,128)(2,1)S(1)} collective-permute-done((bf16[16,64,256]{2,1,0:T(8,128)(2,1)S(1)}, bf16[16,64,256]{2,1,0:T(8,128)(2,1)S(1)}, u32[]{:S(2)}, u32[]{:S(2)}) %collective-permute-start) | collective-permute-done | bytes 524320 | tf_op jit(solution)/shard_map/while/body/eval_jaxpr/ppermute | solution.py:12
  126.7 7.8 %fusion.5 = f32[8,128,16,64]{1,3,2,0:T(8,128)S(1)} fusion(bf16[8,128,256,1]{2,1,3,0:T(8,128)(2,1)} %bitcast.80, f32[8,16,64,256]{3,2,1,0:T(8,128)} %get-tuple-element.67, f32[16,64,256]{2,1,0:T(8,128)S(1)} %get-tuple-element.71, f32[8,16]{1,0:T(8,128)S(1)} %get-tuple-element.68), kind=kOutput, calls=%fused_computation.10 | convolution fusion | flops 3225419776 | bytes 14156288 | tf_op jit(solution)/shard_map/btn,bhpn->bthp/dot_general | solution.py:138
  134.6 4.8 %fusion.11 = bf16[8,128,16,64]{1,3,2,0:T(8,128)(2,1)S(1)} fusion(bf16[8,128,16,64]{1,3,2,0:T(8,128)(2,1)S(1)} %copy-done.1, f32[8,128,16,64]{1,3,2,0:T(8,128)S(1)} %fusion.5, f32[16]{0:T(128)S(1)} %copy-done.5, f32[8,128,16]{1,2,0:T(8,128)S(1)} %copy.55, f32[8,128,128]{2,1,0:T(8,128)S(1)} %copy-done.3, f32[16,8,128]{2,0,1:T(8,128)S(1)} %copy_bitcast_fusion, ...), kind=kOutput, calls=%fused_computation.19 | convolution fusion | flops 285212672 | bytes 9240640 | tf_op jit(solution)/shard_map/hbts,bshp->bthp/dot_general | solution.py:98
  139.3 4.3 %copy.61 = bf16[8,128,16,64]{3,2,1,0:T(8,128)(2,1)} copy(bf16[8,128,16,64]{1,3,2,0:T(8,128)(2,1)S(1)} %fusion.11) | data formatting | bytes 4194304 | tf_op jit(solution)/shard_map/reshape | solution.py:144
  143.6 6.5 %reshape.190 = bf16[1024,1024]{1,0:T(8,128)(2,1)} reshape(bf16[8,128,16,64]{3,2,1,0:T(8,128)(2,1)} %copy.61) | data formatting | bytes 4194304 | tf_op jit(solution)/shard_map/reshape | solution.py:144
  (61 shorter events, 8.3 us)
Async XLA Ops:
  1.3 24.5 %collective-permute-start.1 = (bf16[3,1024]{1,0:T(4,128)(2,1)}, bf16[3,1024]{1,0:T(4,128)(2,1)}, u32[]{:S(2)}, u32[]{:S(2)}) collective-permute-start(bf16[3,1024]{1,0:T(4,128)(2,1)} %slice.90), channel_id=1, source_target_pairs={{0,4},{4,8},{8,12},{1,5},{5,9},{9,13},{2,6},{6,10},{10,14},{3,7},{... | collective-permute-start | bytes 18440 | tf_op jit(solution)/shard_map/ppermute | solution.py:12
  7.5 15.7 %collective-permute-start.2 = (bf16[2,3,128]{2,1,0:T(4,128)(2,1)S(1)}, bf16[2,3,128]{2,1,0:T(4,128)(2,1)S(1)}, u32[]{:S(2)}, u32[]{:S(2)}) collective-permute-start(bf16[2,3,128]{2,1,0:T(4,128)(2,1)S(1)} %slice.102), channel_id=1, source_target_pairs={{0,4},{4,8},{8,12},{1,5},{5,9},{9,13},{2,6},{6,10},{10,14},{3,7},{... | collective-permute-start | bytes 4616 | tf_op jit(solution)/shard_map/ppermute | solution.py:12
  25.7 21.3 %collective-permute-start.3 = (bf16[2,1024,128]{2,1,0:T(8,128)(2,1)S(1)}, bf16[2,1024,128]{2,1,0:T(8,128)(2,1)S(1)}, u32[]{:S(2)}, u32[]{:S(2)}) collective-permute-start(bf16[2,1024,128]{2,1,0:T(8,128)(2,1)S(1)} %multiply_convert_fusion.1), channel_id=1, source_target_pairs={{0,1},{1,0},{2,3},{3,2},{4,5},{5,4},{6,7},{7,6},{8,9},{9,8},{10,11... | collective-permute-start | bytes 1572872 | tf_op jit(solution)/shard_map/ppermute | solution.py:22
  47.1 1.8 %copy-start = (bf16[8,128,16,64]{1,3,2,0:T(8,128)(2,1)S(1)}, bf16[8,128,16,64]{1,3,2,0:T(8,128)(2,1)}, u32[]{:S(2)}) copy-start(bf16[8,128,16,64]{1,3,2,0:T(8,128)(2,1)} %copy.50) | copy-start | bytes 6291460
  47.5 31.9 %copy-start.2 = (bf16[1,1024,256]{2,1,0:T(8,128)(2,1)}, bf16[1,1024,256]{2,1,0:T(8,128)(2,1)S(1)}, u32[]{:S(2)}) copy-start(bf16[1,1024,256]{2,1,0:T(8,128)(2,1)S(1)} %get-tuple-element.137) | copy-start | bytes 1572868
  48.9 4.5 %copy-start.4 = (f32[8,16]{1,0:T(8,128)S(1)}, f32[8,16]{1,0:T(8,128)}, u32[]{:S(2)}) copy-start(f32[8,16]{1,0:T(8,128)} %custom-call.4) | copy-start | bytes 1540
  80.7 15.3 %collective-permute-start = (bf16[16,64,256]{2,1,0:T(8,128)(2,1)S(1)}, bf16[16,64,256]{2,1,0:T(8,128)(2,1)S(1)}, u32[]{:S(2)}, u32[]{:S(2)}) collective-permute-start(bf16[16,64,256]{2,1,0:T(8,128)(2,1)S(1)} %fusion.46), channel_id=1, source_target_pairs={{0,4},{4,8},{8,12},{1,5},{5,9},{9,13},{2,6},{6,10},{10,14},{3,7},{... | collective-permute-start | bytes 1572872 | tf_op jit(solution)/shard_map/while/body/eval_jaxpr/ppermute | solution.py:12
  96.3 15.4 %collective-permute-start = (bf16[16,64,256]{2,1,0:T(8,128)(2,1)S(1)}, bf16[16,64,256]{2,1,0:T(8,128)(2,1)S(1)}, u32[]{:S(2)}, u32[]{:S(2)}) collective-permute-start(bf16[16,64,256]{2,1,0:T(8,128)(2,1)S(1)} %fusion.46), channel_id=1, source_target_pairs={{0,4},{4,8},{8,12},{1,5},{5,9},{9,13},{2,6},{6,10},{10,14},{3,7},{... | collective-permute-start | bytes 1572872 | tf_op jit(solution)/shard_map/while/body/eval_jaxpr/ppermute | solution.py:12
  112.0 14.5 %collective-permute-start = (bf16[16,64,256]{2,1,0:T(8,128)(2,1)S(1)}, bf16[16,64,256]{2,1,0:T(8,128)(2,1)S(1)}, u32[]{:S(2)}, u32[]{:S(2)}) collective-permute-start(bf16[16,64,256]{2,1,0:T(8,128)(2,1)S(1)} %fusion.46), channel_id=1, source_target_pairs={{0,4},{4,8},{8,12},{1,5},{5,9},{9,13},{2,6},{6,10},{10,14},{3,7},{... | collective-permute-start | bytes 1572872 | tf_op jit(solution)/shard_map/while/body/eval_jaxpr/ppermute | solution.py:12
  126.6 7.9 %copy-start.1 = (bf16[8,128,16,64]{1,3,2,0:T(8,128)(2,1)S(1)}, bf16[8,128,16,64]{1,3,2,0:T(8,128)(2,1)}, u32[]{:S(2)}) copy-start(bf16[8,128,16,64]{1,3,2,0:T(8,128)(2,1)} %copy.50) | copy-start | bytes 6291460
  126.7 7.9 %copy-start.3 = (f32[8,128,128]{2,1,0:T(8,128)S(1)}, f32[8,128,128]{2,1,0:T(8,128)}, u32[]{:S(2)}) copy-start(f32[8,128,128]{2,1,0:T(8,128)} %fusion.36) | copy-start | bytes 1572868
  126.7 7.9 %copy-start.5 = (f32[16]{0:T(128)S(1)}, f32[16]{0:T(128)}, u32[]{:S(2)}) copy-start(f32[16]{0:T(128)} %param.22) | copy-start | bytes 196
where the time goes:
time: 152 us; the launch traced here: 150 us
  other arithmetic  48.7 us (32%)
  waiting for transfers between devices  32.9 us (22%)
  local copies, waits for them, and re-layouts  29 us (19%)
  starting transfers between devices  20.8 us (14%)
  matrix products  18.2 us (12%)
    ppermute x5, waiting for transfers between devices, shifted(): lax.ppermute(value, axis, [(source, source + steps) for source in range(i...  32.9 us
    ppermute x5, starting transfers between devices, shifted(): lax.ppermute(value, axis, [(source, source + steps) for source in range(i...  20.7 us
    reshape x2, local copies, waits for them, and re-layouts, body(): inner_conv.reshape(block_count, BLOCK, head_count, head_width)  12.1 us
    convert_element_type x2, other arithmetic, convolve(): return jax.nn.silu(summed).astype(jnp.bfloat16)  11.6 us
    add x8, other arithmetic, local_step(): decay_block[:, None, None] * entering + state_block  11.3 us
    reshape x2, local copies, waits for them, and re-layouts, body(): mixed_out.astype(jnp.bfloat16).reshape(own_rows, head_count * head_width)  10.8 us
    dynamic_update_slice x8, other arithmetic, body(): lax.scan(local_step, (start_state, start_prefix), (block_decay, block_sta...  8.84 us
    dot_general x1, matrix products, body(): jnp.einsum('btn,bhpn->bthp', c_float, full_states, precision=precise)  7.85 us
  transfers between devices with their start and end apart: 6, of which 3 were waited for; matrix products, arithmetic and copies ran while one was open for 25% of the time, Pallas kernels for 0%

commit v1 on v0

v1 whole, which is shorter than its diff:
```python
import functools

import jax
import jax.numpy as jnp
from jax import lax
from jax.experimental import pallas as pl
from jax.experimental.pallas import tpu as pltpu
from jax.sharding import PartitionSpec as P

BLOCK = 128


def shifted(value, axis, steps):
    count = lax.axis_size(axis)
    initial, last = (max(0, -steps), min(count, count - steps))
    return lax.ppermute(value, axis, [(source, source + steps) for source in range(initial, last)])


def from_partner(block, axis, stride):
    count = lax.axis_size(axis)
    route = []
    for low in range(count):
        high = low | 1 << stride
        if high != low and high < count:
            route += [(low, high), (high, low)]
    return lax.ppermute(block, axis, route)


def segment_of(lengths, positions):
    starts = jnp.cumsum(lengths, dtype=jnp.int32) - lengths
    covered = (starts[None, :] <= positions[:, None]).astype(jnp.int32)
    return jnp.sum(covered, axis=1, dtype=jnp.int32) - 1


def convolve(extended, weight, bias_row, seg_ext, row_count):
    own_seg = seg_ext[3:]
    summed = (
        jnp.zeros(extended.shape[:-2] + (row_count, extended.shape[-1]), jnp.float32) + bias_row
    )
    for offset in range(4):
        kept_mask = (seg_ext[offset : offset + row_count] == own_seg).astype(jnp.float32)[:, None]
        window = extended[..., offset : offset + row_count, :].astype(jnp.float32)
        summed = summed + weight[offset].astype(jnp.float32) * window * kept_mask
    return jax.nn.silu(summed).astype(jnp.bfloat16)


def split_dot_nt(lhs, value):
    high = value.astype(jnp.bfloat16)
    low = (value - high.astype(jnp.float32)).astype(jnp.bfloat16)
    dims = (((1,), (1,)), ((), ()))
    return lax.dot_general(lhs, high, dims, preferred_element_type=jnp.float32) + lax.dot_general(
        lhs, low, dims, preferred_element_type=jnp.float32
    )


def block_kernel(with_y, head_count, head_width, *refs):
    if with_y:
        (decay_ref, skip_ref, x_ref, b_ref, c_ref, l_ref, lt_ref, dt_ref, dtt_ref, segr_ref,
         segc_ref, entry_ref, ein_ref, out_ref, state_ref) = refs
    else:
        (decay_ref, x_ref, b_ref, l_ref, lt_ref, dtt_ref, segc_ref, state_ref) = refs
    blk = pl.program_id(0)

    @pl.when(blk == 0)
    def _():
        if with_y:
            state_ref[...] = ein_ref[...]
        else:
            state_ref[...] = jnp.zeros(state_ref.shape, jnp.float32)

    b_mat = b_ref[...]
    seg_col = segc_ref[...]
    end_col = (seg_col == seg_col[BLOCK - 1 : BLOCK, :]).astype(jnp.float32)
    if with_y:
        c_mat = c_ref[...]
        seg_row = segr_ref[...]
        scores = lax.dot_general(
            c_mat, b_mat, (((1,), (1,)), ((), ())), preferred_element_type=jnp.float32
        )
        rows = lax.broadcasted_iota(jnp.int32, (BLOCK, BLOCK), 0)
        cols = lax.broadcasted_iota(jnp.int32, (BLOCK, BLOCK), 1)
        allowed = (rows >= cols) & (seg_col == seg_row)
        entry_col = entry_ref[...]
    for h in range(head_count):
        lanes = slice(h * head_width, (h + 1) * head_width)
        l_col = lt_ref[:, h : h + 1]
        dt_col = dtt_ref[:, h : h + 1]
        x_h = x_ref[:, lanes]
        state_h = state_ref[h]
        if with_y:
            l_row = l_ref[h : h + 1, :]
            dt_row = dt_ref[h : h + 1, :]
            weights = jnp.where(allowed, jnp.exp(l_col - l_row) * dt_row * scores, 0.0)
            intra = jnp.dot(weights.astype(jnp.bfloat16), x_h, preferred_element_type=jnp.float32)
            inter = split_dot_nt(c_mat, state_h) * (jnp.exp(l_col) * entry_col)
            mixed = intra + inter + skip_ref[h] * x_h.astype(jnp.float32)
            out_ref[:, lanes] = mixed.astype(jnp.bfloat16)
        ending = jnp.exp(l_col[BLOCK - 1 : BLOCK, :] - l_col) * dt_col * end_col
        weighted = (x_h.astype(jnp.float32) * ending).astype(jnp.bfloat16)
        block_state = lax.dot_general(
            weighted, b_mat, (((0,), (0,)), ((), ())), preferred_element_type=jnp.float32
        )
        state_ref[h] = decay_ref[blk * head_count + h] * state_h + block_state


def run_blocks(with_y, decay_flat, skip_gain, x, b_full, c_full, l, lt, dt, dtt, seg_row, seg_col,
               entry_col, entering):
    rows, width = x.shape
    head_count = l.shape[0]
    head_width = width // head_count
    n_size = b_full.shape[1]
    block_count = rows // BLOCK
    smem = pl.BlockSpec(memory_space=pltpu.SMEM)
    row_block = lambda cols: pl.BlockSpec((BLOCK, cols), lambda b: (b, 0))
    head_block = pl.BlockSpec((head_count, BLOCK), lambda b: (0, b))
    state_spec = pl.BlockSpec((head_count, head_width, n_size), lambda b: (0, 0, 0))
    state_shape = (head_count, head_width, n_size)
    kernel = functools.partial(block_kernel, with_y, head_count, head_width)
    params = pltpu.CompilerParams(dimension_semantics=("arbitrary",))
    if with_y:
        return pl.pallas_call(
            kernel,
            grid=(block_count,),
            in_specs=[smem, smem, row_block(width), row_block(n_size), row_block(n_size), head_block,
                      row_block(head_count), head_block, row_block(head_count),
                      pl.BlockSpec((1, BLOCK), lambda b: (0, b)), row_block(1), row_block(1),
                      state_spec],
            out_specs=row_block(width),
            out_shape=jax.ShapeDtypeStruct((rows, width), jnp.bfloat16),
            scratch_shapes=[pltpu.VMEM(state_shape, jnp.float32)],
            compiler_params=params,
        )(decay_flat, skip_gain, x, b_full, c_full, l, lt, dt, dtt, seg_row, seg_col, entry_col,
          entering)
    return pl.pallas_call(
        kernel,
        grid=(block_count,),
        in_specs=[smem, row_block(width), row_block(n_size), head_block, row_block(head_count),
                  row_block(head_count), row_block(1)],
        out_specs=state_spec,
        out_shape=jax.ShapeDtypeStruct(state_shape, jnp.float32),
        compiler_params=params,
    )(decay_flat, x, b_full, l, lt, dtt, seg_col)


def body(
    inner_input,
    state_input,
    conv_inner,
    bias_inner,
    conv_state,
    bias_state,
    step_size,
    decay_rate,
    skip_gain,
    lengths,
):
    precise = lax.Precision.HIGHEST
    own_rows = inner_input.shape[0]
    head_count = decay_rate.shape[0]
    group_half = state_input.shape[2]
    block_count = own_rows // BLOCK
    positions = lax.axis_index("seq") * own_rows + jnp.arange(own_rows + 3, dtype=jnp.int32) - 3
    seg_ext = segment_of(lengths, positions)
    inner_tail, state_tail = shifted((inner_input[-3:], state_input[:, -3:]), "seq", 1)
    weight_state = jnp.swapaxes(conv_state, 0, 1)[:, :, None, :]
    state_half = convolve(
        jnp.concatenate([state_tail, state_input], 1),
        weight_state,
        bias_state[:, None, :],
        seg_ext,
        own_rows,
    )
    partner = from_partner(state_half, "head", 0)
    inner_conv = convolve(
        jnp.concatenate([inner_tail, inner_input], 0), conv_inner, bias_inner, seg_ext, own_rows
    )
    lower_half = lax.axis_index("head") % 2 == 0
    state_full = jnp.where(
        lower_half,
        jnp.concatenate([state_half, partner], 2),
        jnp.concatenate([partner, state_half], 2),
    )
    b_full = state_full[0]
    c_full = state_full[1]
    steps_dt = step_size.reshape(head_count, block_count, BLOCK)
    upper = (
        lax.broadcasted_iota(jnp.int32, (BLOCK, BLOCK), 0)
        <= lax.broadcasted_iota(jnp.int32, (BLOCK, BLOCK), 1)
    ).astype(jnp.float32)
    log_decay = jnp.einsum(
        "hbs,st->hbt", -steps_dt * decay_rate[:, None, None], upper, precision=precise
    )
    seg_own = seg_ext[3:].reshape(block_count, BLOCK)
    seg_prev = seg_ext[2 : 2 + own_rows].reshape(block_count, BLOCK)[:, 0]
    block_decay = jnp.exp(log_decay[:, :, -1]) * (seg_own[:, -1] == seg_prev).astype(jnp.float32)[
        None
    ]
    decay_flat = jnp.transpose(block_decay).reshape(-1)
    l_flat = log_decay.reshape(head_count, own_rows)
    l_t = jnp.transpose(l_flat)
    dt_t = jnp.transpose(step_size)
    seg_row = seg_ext[3:].reshape(1, own_rows)
    seg_col = seg_ext[3:].reshape(own_rows, 1)
    entry_col = (seg_own == seg_prev[:, None]).astype(jnp.float32).reshape(own_rows, 1)

    local_end = run_blocks(
        False, decay_flat, None, inner_conv, b_full, None, l_flat, l_t, None, dt_t, None, seg_col,
        None, None
    )
    total_decay = jnp.prod(block_decay, axis=1)

    def relay(step_num, incoming):
        return shifted(
            (total_decay[:, None, None] * incoming + local_end).astype(jnp.bfloat16), "seq", 1
        ).astype(jnp.float32)

    incoming = lax.fori_loop(0, lax.axis_size("seq") - 1, relay, jnp.zeros_like(local_end))
    return run_blocks(
        True, decay_flat, skip_gain, inner_conv, b_full, c_full, l_flat, l_t, step_size, dt_t,
        seg_row, seg_col, entry_col, incoming
    )


def solution(mesh):
    return jax.shard_map(
        body,
        mesh=mesh,
        in_specs=(
            P(("grp", "seq"), "head"),
            P(None, ("grp", "seq"), "head"),
            P(None, "head"),
            P("head"),
            P(None, None, "head"),
            P(None, "head"),
            P("head", ("grp", "seq")),
            P("head"),
            P("head"),
            P("grp"),
        ),
        out_specs=P(("grp", "seq"), "head"),
        check_vma=False,
    )
```

time: 152 us -> 145 us (0.954)
  Pallas kernels: 0 us -> 64.8 us
  other arithmetic: 48.7 us -> 16.4 us
  local copies, waits for them, and re-layouts: 29 us -> 8.61 us
  matrix products: 18.2 us -> 0.18 us
    pallas_call x0 -> x2, Pallas kernels: none -> 64.8 us  [the longest x1 47.9 us: run_blocks(): pl.pallas_call(kernel, grid=(block_count,), in_specs=[smem, smem, row_blo...]
    reshape x6 -> x3, local copies, waits for them, and re-layouts: 23.9 us -> 2.41 us  [the longest x1 1.02 us: body(): seg_col = seg_ext[3:].reshape(own_rows, 1)]
    dot_general x4 -> x1, matrix products: 18.2 us -> 0.18 us  [body(): jnp.einsum('hbs,st->hbt', -steps_dt * decay_rate[:, None, None], upper, p...]
    add x8 -> x0, other arithmetic: 11.3 us -> none  [local_step(): decay_block[:, None, None] * entering + state_block]
    dynamic_update_slice x8 -> x0, other arithmetic: 8.84 us -> none  [body(): lax.scan(local_step, (start_state, start_prefix), (block_decay, block_sta...]
    mul x10 -> x1, other arithmetic: 6.29 us -> 0.73 us  [body(): -steps_dt * decay_rate[:, None, None]]
    another operation x2 -> x1, other arithmetic: 5.35 us -> 0.83 us  [the longest x1 4.52 us: body(): log_decay = jnp.cumsum(-steps_dt * decay_rate[:, None, None], axis=2)]
  transfers between devices with their start and end apart: 6 -> 6, of which waited for: 3 -> 3; matrix products, arithmetic and copies ran while one was open for 25% -> 15% of each run, Pallas kernels for 0% -> 0%
where the time goes in v1:
time: 145 us; the launch traced here: 144 us
  Pallas kernels  64.8 us (45%)
  waiting for transfers between devices  32.8 us (23%)
  starting transfers between devices  20.8 us (14%)
  other arithmetic  16.4 us (11%)
  local copies, waits for them, and re-layouts  8.61 us (6%)
    pallas_call x1, Pallas kernels, run_blocks(): pl.pallas_call(kernel, grid=(block_count,), in_specs=[smem, smem, row_blo...  47.9 us
    ppermute x5, waiting for transfers between devices, shifted(): lax.ppermute(value, axis, [(source, source + steps) for source in range(i...  32.8 us
    ppermute x5, starting transfers between devices, shifted(): lax.ppermute(value, axis, [(source, source + steps) for source in range(i...  20.7 us
    pallas_call x1, Pallas kernels, run_blocks(): pl.pallas_call(kernel, grid=(block_count,), in_specs=[smem, row_block(wid...  16.9 us
    convert_element_type x2, other arithmetic, convolve(): return jax.nn.silu(summed).astype(jnp.bfloat16)  10.1 us
  transfers between devices with their start and end apart: 6, of which 3 were waited for; matrix products, arithmetic and copies ran while one was open for 15% of the time, Pallas kernels for 0%

profile of v1, /device:TPU:0, one launch (start us, length us, event | category | flops | bytes accessed | tf_op | source)
XLA Modules:
  0.0 143.9 jit_solution(16857354338877825058)
XLA Ops:
  0.0 0.8 slice.105
  0.8 4.9 %collective-permute-start.2 = (bf16[2,3,128]{2,1,0:T(4,128)(2,1)S(1)}, bf16[2,3,128]{2,1,0:T(4,128)(2,1)S(1)}, u32[]{:S(2)}, u32[]{:S(2)}) collective-permute-start(bf16[2,3,128]{2,1,0:T(4,128)(2,1)S(1)} %slice.105), channel_id=1, source_target_pairs={{0,4},{4,8},{8,12},{1,5},{5,9},{9,13},{2,6},{6,10},{10,14},{3,7},{... | collective-permute-start | bytes 4616 | tf_op jit(solution)/shard_map/ppermute | solution.py:16
  5.7 0.7 slice.95
  6.4 3.5 %collective-permute-start.1 = (bf16[3,1024]{1,0:T(4,128)(2,1)S(1)}, bf16[3,1024]{1,0:T(4,128)(2,1)S(1)}, u32[]{:S(2)}, u32[]{:S(2)}) collective-permute-start(bf16[3,1024]{1,0:T(4,128)(2,1)S(1)} %slice.95), channel_id=1, source_target_pairs={{0,4},{4,8},{8,12},{1,5},{5,9},{9,13},{2,6},{6,10},{10,14},{3,7},{... | collective-permute-start | bytes 18440 | tf_op jit(solution)/shard_map/ppermute | solution.py:16
  9.9 0.8 reduce-window.9
  10.7 0.7 bitcast_subtract_fusion
  11.4 0.1 convert_reduce_fusion
  11.5 0.1 fusion.14
  11.6 0.2 slice_reduce_fusion
  11.8 0.1 fusion.9
  11.8 0.9 slice_convert_fusion.3
  12.7 0.8 negate_bitcast_fusion
  13.6 0.7 bitcast_multiply_fusion
  14.3 0.2 fusion.7
  14.5 0.0 copy-start.3
  14.5 0.1 slice.114
  14.6 0.1 copy.48
  14.7 0.1 fusion.12
  14.8 0.8 slice_convert_fusion.7
  15.7 0.2 copy.41
  15.9 1.9 %copy.42 = f32[16,1024]{0,1:T(8,128)} copy(f32[16,1024]{1,0:T(8,128)} %refs_7_.1) | data formatting | bytes 131072 | tf_op args[6]
  17.8 0.6 reshape.130.refs_0_
  18.4 1.0 copy.46.refs_6_.refs_10_
  19.4 0.8 copy.45.refs_3_.refs_5_
  20.2 1.1 copy.47.refs_11_
  21.2 0.0 collective-permute-done.2
  21.3 1.2 multiply_convert_fusion.1
  22.5 0.1 collective-permute-start.3
  22.6 0.0 collective-permute-done.1
  22.6 8.9 %multiply_convert_fusion.refs_1_.refs_2_ = bf16[1024,1024]{1,0:T(8,128)(2,1)} fusion(bf16[1024,1024]{1,0:T(8,128)(2,1)} %param.12, bf16[3,1024]{1,0:T(4,128)(2,1)S(1)} %collective-permute-done.1, f32[1024]{0:T(1024)S(1)} %bitcast.57, f32[1024]{0:T(1024)S(1)} %get-tuple-element.54, f32[1024]{0:T(1024)S(1)} %bitcast.58, f32[1024]{0:T(1024)S(1)} %get-tuple-element.55, ...), kind=kLoop, calls=%fused_computation.3 | loop fusion | flops 30408704 | bytes 4233216 | tf_op jit(solution)/shard_map/convert_element_type | solution.py:44
  31.5 0.0 collective-permute-done.3
  31.5 0.4 maximum_select_fusion
  31.9 1.1 slice_bitcast_fusion
  33.0 16.9 %shard_map.100 = f32[16,64,256]{2,1,0:T(8,128)S(1)} custom-call(f32[128]{0:T(128)} %reshape.130.refs_0_, bf16[1024,1024]{1,0:T(8,128)(2,1)} %multiply_convert_fusion.refs_1_.refs_2_, bf16[1024,256]{1,0:T(8,128)(2,1)} %get-tuple-element.52.refs_2_.refs_3_, f32[16,1024]{1,0:T(8,128)} %copy.45.refs_3_.refs_5_, f32[1024,16]{1,0:T(8,128)} %bitcast.48, ...), custom_call_target="tpu_custom_call" | custom-call | tf_op jit(solution)/shard_map/pallas_call | solution.py:134
  49.9 46.1 %while.11 = (s32[]{:T(128)}, f32[16,64,256]{2,1,0:T(8,128)S(1)}, f32[16]{0:T(128)S(1)}, f32[16,64,256]{2,1,0:T(8,128)S(1)}, s32[]{:T(128)}, /*index=5*/s32[]{:T(128)}) while((s32[]{:T(128)}, f32[16,64,256]{2,1,0:T(8,128)S(1)}, f32[16]{0:T(128)S(1)}, f32[16,64,256]{2,1,0:T(8,128)S(1)}, s32[]{:T(128)}, /*index=5*/s32[]{:T(128)}) %tuple.36), condition=%wide.region_4.5_spmd.clone, body=%wide.region_3.4_spmd.clone.sunk | while | flops 1310723 | bytes 6291639 | solution.py:217
  49.9 0.2 fusion.17
  50.1 3.5 %collective-permute-start = (bf16[16,64,256]{2,1,0:T(8,128)(2,1)S(1)}, bf16[16,64,256]{2,1,0:T(8,128)(2,1)S(1)}, u32[]{:S(2)}, u32[]{:S(2)}) collective-permute-start(bf16[16,64,256]{2,1,0:T(8,128)(2,1)S(1)} %fusion.17), channel_id=1, source_target_pairs={{0,4},{4,8},{8,12},{1,5},{5,9},{9,13},{2,6},{6,10},{10,14},{3,7},{... | collective-permute-start | bytes 1572872 | tf_op jit(solution)/shard_map/while/body/eval_jaxpr/ppermute | solution.py:16
  53.6 11.8 %collective-permute-done = bf16[16,64,256]{2,1,0:T(8,128)(2,1)S(1)} collective-permute-done((bf16[16,64,256]{2,1,0:T(8,128)(2,1)S(1)}, bf16[16,64,256]{2,1,0:T(8,128)(2,1)S(1)}, u32[]{:S(2)}, u32[]{:S(2)}) %collective-permute-start) | collective-permute-done | bytes 524320 | tf_op jit(solution)/shard_map/while/body/eval_jaxpr/ppermute | solution.py:16
  65.4 0.1 convert_element_type.180
  65.5 0.2 fusion.17
  65.7 4.4 %collective-permute-start = (bf16[16,64,256]{2,1,0:T(8,128)(2,1)S(1)}, bf16[16,64,256]{2,1,0:T(8,128)(2,1)S(1)}, u32[]{:S(2)}, u32[]{:S(2)}) collective-permute-start(bf16[16,64,256]{2,1,0:T(8,128)(2,1)S(1)} %fusion.17), channel_id=1, source_target_pairs={{0,4},{4,8},{8,12},{1,5},{5,9},{9,13},{2,6},{6,10},{10,14},{3,7},{... | collective-permute-start | bytes 1572872 | tf_op jit(solution)/shard_map/while/body/eval_jaxpr/ppermute | solution.py:16
  70.1 11.0 %collective-permute-done = bf16[16,64,256]{2,1,0:T(8,128)(2,1)S(1)} collective-permute-done((bf16[16,64,256]{2,1,0:T(8,128)(2,1)S(1)}, bf16[16,64,256]{2,1,0:T(8,128)(2,1)S(1)}, u32[]{:S(2)}, u32[]{:S(2)}) %collective-permute-start) | collective-permute-done | bytes 524320 | tf_op jit(solution)/shard_map/while/body/eval_jaxpr/ppermute | solution.py:16
  81.1 0.1 convert_element_type.180
  81.2 0.2 fusion.17
  81.4 4.4 %collective-permute-start = (bf16[16,64,256]{2,1,0:T(8,128)(2,1)S(1)}, bf16[16,64,256]{2,1,0:T(8,128)(2,1)S(1)}, u32[]{:S(2)}, u32[]{:S(2)}) collective-permute-start(bf16[16,64,256]{2,1,0:T(8,128)(2,1)S(1)} %fusion.17), channel_id=1, source_target_pairs={{0,4},{4,8},{8,12},{1,5},{5,9},{9,13},{2,6},{6,10},{10,14},{3,7},{... | collective-permute-start | bytes 1572872 | tf_op jit(solution)/shard_map/while/body/eval_jaxpr/ppermute | solution.py:16
  85.8 10.1 %collective-permute-done = bf16[16,64,256]{2,1,0:T(8,128)(2,1)S(1)} collective-permute-done((bf16[16,64,256]{2,1,0:T(8,128)(2,1)S(1)}, bf16[16,64,256]{2,1,0:T(8,128)(2,1)S(1)}, u32[]{:S(2)}, u32[]{:S(2)}) %collective-permute-start) | collective-permute-done | bytes 524320 | tf_op jit(solution)/shard_map/while/body/eval_jaxpr/ppermute | solution.py:16
  95.9 0.1 convert_element_type.180
  96.0 47.9 %shard_map.101 = bf16[1024,1024]{1,0:T(8,128)(2,1)} custom-call(f32[128]{0:T(128)} %reshape.130.refs_0_, f32[16]{0:T(128)} %refs_1_.1, bf16[1024,1024]{1,0:T(8,128)(2,1)} %multiply_convert_fusion.refs_1_.refs_2_, bf16[1024,256]{1,0:T(8,128)(2,1)} %get-tuple-element.52.refs_2_.refs_3_, bf16[1024,256]{1,0:T(8,128)(2,1)} %get-tuple-element.51.refs_4_, ...), custom_call_target="tpu_custom_call" | custom-call | tf_op jit(solution)/shard_map/pallas_call | solution.py:121
  (14 shorter events, 0.1 us)
Async XLA Ops:
  0.0 21.2 %copy-start.1 = (bf16[2,1024,128]{2,1,0:T(8,128)(2,1)S(1)}, bf16[2,1024,128]{2,1,0:T(8,128)(2,1)}, u32[]{:S(2)}) copy-start(bf16[2,1024,128]{2,1,0:T(8,128)(2,1)} %param.13) | copy-start | bytes 1572868
  0.0 21.2 %copy-start.4 = (f32[2,128]{1,0:T(2,128)S(1)}, f32[2,128]{1,0:T(2,128)}, u32[]{:S(2)}) copy-start(f32[2,128]{1,0:T(2,128)} %param.17) | copy-start | bytes 3076
  0.8 20.5 %collective-permute-start.2 = (bf16[2,3,128]{2,1,0:T(4,128)(2,1)S(1)}, bf16[2,3,128]{2,1,0:T(4,128)(2,1)S(1)}, u32[]{:S(2)}, u32[]{:S(2)}) collective-permute-start(bf16[2,3,128]{2,1,0:T(4,128)(2,1)S(1)} %slice.105), channel_id=1, source_target_pairs={{0,4},{4,8},{8,12},{1,5},{5,9},{9,13},{2,6},{6,10},{10,14},{3,7},{... | collective-permute-start | bytes 4616 | tf_op jit(solution)/shard_map/ppermute | solution.py:16
  6.4 16.1 %collective-permute-start.1 = (bf16[3,1024]{1,0:T(4,128)(2,1)S(1)}, bf16[3,1024]{1,0:T(4,128)(2,1)S(1)}, u32[]{:S(2)}, u32[]{:S(2)}) collective-permute-start(bf16[3,1024]{1,0:T(4,128)(2,1)S(1)} %slice.95), channel_id=1, source_target_pairs={{0,4},{4,8},{8,12},{1,5},{5,9},{9,13},{2,6},{6,10},{10,14},{3,7},{... | collective-permute-start | bytes 18440 | tf_op jit(solution)/shard_map/ppermute | solution.py:16
  11.6 10.9 %copy-start.2 = (s32[1024]{0:T(1024)}, s32[1024]{0:T(1024)S(1)}, u32[]{:S(2)}) copy-start(s32[1024]{0:T(1024)S(1)} %get-tuple-element.57) | copy-start | bytes 12292
  14.5 8.1 %copy-start.3 = (f32[1024]{0:T(1024)S(1)}, f32[1024]{0:T(1024)}, u32[]{:S(2)}) copy-start(f32[1024]{0:T(1024)} %param.15) | copy-start | bytes 12292
  15.9 15.6 %copy-start = (f32[16,8,128]{0,2,1:T(8,128)}, f32[16,8,128]{0,2,1:T(8,128)S(1)}, u32[]{:S(2)}) copy-start(f32[16,8,128]{0,2,1:T(8,128)S(1)} %copy.41) | copy-start | bytes 196612
  22.5 9.0 %collective-permute-start.3 = (bf16[2,1024,128]{2,1,0:T(8,128)(2,1)S(1)}, bf16[2,1024,128]{2,1,0:T(8,128)(2,1)S(1)}, u32[]{:S(2)}, u32[]{:S(2)}) collective-permute-start(bf16[2,1024,128]{2,1,0:T(8,128)(2,1)S(1)} %multiply_convert_fusion.1), channel_id=1, source_target_pairs={{0,1},{1,0},{2,3},{3,2},{4,5},{5,4},{6,7},{7,6},{8,9},{9,8},{10,11... | collective-permute-start | bytes 1572872 | tf_op jit(solution)/shard_map/ppermute | solution.py:26
  50.1 15.3 %collective-permute-start = (bf16[16,64,256]{2,1,0:T(8,128)(2,1)S(1)}, bf16[16,64,256]{2,1,0:T(8,128)(2,1)S(1)}, u32[]{:S(2)}, u32[]{:S(2)}) collective-permute-start(bf16[16,64,256]{2,1,0:T(8,128)(2,1)S(1)} %fusion.17), channel_id=1, source_target_pairs={{0,4},{4,8},{8,12},{1,5},{5,9},{9,13},{2,6},{6,10},{10,14},{3,7},{... | collective-permute-start | bytes 1572872 | tf_op jit(solution)/shard_map/while/body/eval_jaxpr/ppermute | solution.py:16
  65.7 15.4 %collective-permute-start = (bf16[16,64,256]{2,1,0:T(8,128)(2,1)S(1)}, bf16[16,64,256]{2,1,0:T(8,128)(2,1)S(1)}, u32[]{:S(2)}, u32[]{:S(2)}) collective-permute-start(bf16[16,64,256]{2,1,0:T(8,128)(2,1)S(1)} %fusion.17), channel_id=1, source_target_pairs={{0,4},{4,8},{8,12},{1,5},{5,9},{9,13},{2,6},{6,10},{10,14},{3,7},{... | collective-permute-start | bytes 1572872 | tf_op jit(solution)/shard_map/while/body/eval_jaxpr/ppermute | solution.py:16
  81.4 14.5 %collective-permute-start = (bf16[16,64,256]{2,1,0:T(8,128)(2,1)S(1)}, bf16[16,64,256]{2,1,0:T(8,128)(2,1)S(1)}, u32[]{:S(2)}, u32[]{:S(2)}) collective-permute-start(bf16[16,64,256]{2,1,0:T(8,128)(2,1)S(1)} %fusion.17), channel_id=1, source_target_pairs={{0,4},{4,8},{8,12},{1,5},{5,9},{9,13},{2,6},{6,10},{10,14},{3,7},{... | collective-permute-start | bytes 1572872 | tf_op jit(solution)/shard_map/while/body/eval_jaxpr/ppermute | solution.py:16

commit v2 on v1

v2 whole, which is shorter than its diff:
```python
import functools

import jax
import jax.numpy as jnp
from jax import lax
from jax.experimental import pallas as pl
from jax.experimental.pallas import tpu as pltpu
from jax.sharding import PartitionSpec as P

BLOCK = 128


def shifted(value, axis, steps):
    count = lax.axis_size(axis)
    initial, last = (max(0, -steps), min(count, count - steps))
    return lax.ppermute(value, axis, [(source, source + steps) for source in range(initial, last)])


def from_partner(block, axis, stride):
    count = lax.axis_size(axis)
    route = []
    for low in range(count):
        high = low | 1 << stride
        if high != low and high < count:
            route += [(low, high), (high, low)]
    return lax.ppermute(block, axis, route)


def segment_of(lengths, positions):
    starts = jnp.cumsum(lengths, dtype=jnp.int32) - lengths
    covered = (starts[None, :] <= positions[:, None]).astype(jnp.int32)
    return jnp.sum(covered, axis=1, dtype=jnp.int32) - 1


def convolve(extended, weight, bias_row, seg_ext, row_count):
    own_seg = seg_ext[3:]
    summed = (
        jnp.zeros(extended.shape[:-2] + (row_count, extended.shape[-1]), jnp.float32) + bias_row
    )
    for offset in range(4):
        kept_mask = (seg_ext[offset : offset + row_count] == own_seg).astype(jnp.float32)[:, None]
        window = extended[..., offset : offset + row_count, :].astype(jnp.float32)
        summed = summed + weight[offset].astype(jnp.float32) * window * kept_mask
    return jax.nn.silu(summed).astype(jnp.bfloat16)


def split_dot(lhs, value):
    high = value.astype(jnp.bfloat16)
    low = (value - high.astype(jnp.float32)).astype(jnp.bfloat16)
    return jnp.dot(lhs, high, preferred_element_type=jnp.float32) + jnp.dot(
        lhs, low, preferred_element_type=jnp.float32
    )


def expand_heads(small, head_width):
    rows, heads = small.shape
    per_tile = 128 // head_width
    lane = lax.broadcasted_iota(jnp.int32, (rows, 128), 1) // head_width
    tiles = []
    for tile in range(heads // per_tile):
        picked = jnp.broadcast_to(small[:, tile * per_tile : tile * per_tile + 1], (rows, 128))
        for k in range(1, per_tile):
            column = small[:, tile * per_tile + k : tile * per_tile + k + 1]
            picked = jnp.where(lane == k, jnp.broadcast_to(column, (rows, 128)), picked)
        tiles.append(picked)
    return jnp.concatenate(tiles, axis=1)


def block_kernel(with_y, head_width, *refs):
    if with_y:
        (x_ref, bt_ref, b_ref, c_ref, l_ref, dt_ref, segr_ref, segc_ref, entry_ref, decay_ref,
         skip_ref, ein_ref, out_ref, state_ref) = refs
    else:
        (x_ref, bt_ref, l_ref, dt_ref, segc_ref, decay_ref, state_ref) = refs
    blk = pl.program_id(0)

    @pl.when(blk == 0)
    def _():
        if with_y:
            state_ref[...] = ein_ref[...]
        else:
            state_ref[...] = jnp.zeros(state_ref.shape, jnp.float32)

    seg_col = segc_ref[...]
    end_col = (seg_col == seg_col[BLOCK - 1 : BLOCK, :]).astype(jnp.float32)
    l_small = l_ref[...]
    dt_small = dt_ref[...]
    x = x_ref[...].astype(jnp.float32)
    state = state_ref[...]
    if with_y:
        c_mat = c_ref[...]
        seg_row = segr_ref[...]
        scores = lax.dot_general(
            c_mat, b_ref[...], (((1,), (1,)), ((), ())), preferred_element_type=jnp.float32
        )
        rows = lax.broadcasted_iota(jnp.int32, (BLOCK, BLOCK), 0)
        cols = lax.broadcasted_iota(jnp.int32, (BLOCK, BLOCK), 1)
        allowed = (rows >= cols) & (seg_col == seg_row)
        masked = jnp.where(allowed, scores, 0.0).astype(jnp.bfloat16)
        rising = expand_heads(jnp.exp(l_small), head_width)
        falling = expand_heads(jnp.exp(-l_small) * dt_small, head_width)
        intra = split_dot(masked, x * falling) * rising
        inter = split_dot(c_mat, state) * (rising * entry_ref[...])
        out_ref[...] = (intra + inter + skip_ref[...] * x).astype(jnp.bfloat16)
    ending = expand_heads(
        jnp.exp(l_small[BLOCK - 1 : BLOCK, :] - l_small) * dt_small * end_col, head_width
    )
    weighted = (x * ending).astype(jnp.bfloat16)
    state_ref[...] = decay_ref[0] * state + jnp.dot(
        bt_ref[...], weighted, preferred_element_type=jnp.float32
    )


def run_blocks(with_y, x, b_t, b_full, c_full, l_t, dt_t, seg_row, seg_col, entry_col, decay_x,
               skip_x, entering):
    rows, width = x.shape
    head_count = l_t.shape[1]
    head_width = width // head_count
    n_size = b_t.shape[0]
    block_count = rows // BLOCK
    row_block = lambda cols: pl.BlockSpec((BLOCK, cols), lambda b: (b, 0))
    bt_spec = pl.BlockSpec((n_size, BLOCK), lambda b: (0, b))
    decay_spec = pl.BlockSpec((1, 1, width), lambda b: (b, 0, 0))
    state_spec = pl.BlockSpec((n_size, width), lambda b: (0, 0))
    state_shape = jax.ShapeDtypeStruct((n_size, width), jnp.float32)
    kernel = functools.partial(block_kernel, with_y, head_width)
    params = pltpu.CompilerParams(dimension_semantics=("arbitrary",))
    if with_y:
        return pl.pallas_call(
            kernel,
            grid=(block_count,),
            in_specs=[row_block(width), bt_spec, row_block(n_size), row_block(n_size),
                      row_block(head_count), row_block(head_count),
                      pl.BlockSpec((1, BLOCK), lambda b: (0, b)), row_block(1), row_block(1),
                      decay_spec, pl.BlockSpec((1, width), lambda b: (0, 0)), state_spec],
            out_specs=row_block(width),
            out_shape=jax.ShapeDtypeStruct((rows, width), jnp.bfloat16),
            scratch_shapes=[pltpu.VMEM((n_size, width), jnp.float32)],
            compiler_params=params,
        )(x, b_t, b_full, c_full, l_t, dt_t, seg_row, seg_col, entry_col, decay_x, skip_x,
          entering)
    return pl.pallas_call(
        kernel,
        grid=(block_count,),
        in_specs=[row_block(width), bt_spec, row_block(head_count), row_block(head_count),
                  row_block(1), decay_spec],
        out_specs=state_spec,
        out_shape=state_shape,
        compiler_params=params,
    )(x, b_t, l_t, dt_t, seg_col, decay_x)


def body(
    inner_input,
    state_input,
    conv_inner,
    bias_inner,
    conv_state,
    bias_state,
    step_size,
    decay_rate,
    skip_gain,
    lengths,
):
    precise = lax.Precision.HIGHEST
    own_rows = inner_input.shape[0]
    head_count = decay_rate.shape[0]
    group_half = state_input.shape[2]
    block_count = own_rows // BLOCK
    positions = lax.axis_index("seq") * own_rows + jnp.arange(own_rows + 3, dtype=jnp.int32) - 3
    seg_ext = segment_of(lengths, positions)
    inner_tail, state_tail = shifted((inner_input[-3:], state_input[:, -3:]), "seq", 1)
    weight_state = jnp.swapaxes(conv_state, 0, 1)[:, :, None, :]
    state_half = convolve(
        jnp.concatenate([state_tail, state_input], 1),
        weight_state,
        bias_state[:, None, :],
        seg_ext,
        own_rows,
    )
    partner = from_partner(state_half, "head", 0)
    inner_conv = convolve(
        jnp.concatenate([inner_tail, inner_input], 0), conv_inner, bias_inner, seg_ext, own_rows
    )
    lower_half = lax.axis_index("head") % 2 == 0
    state_full = jnp.where(
        lower_half,
        jnp.concatenate([state_half, partner], 2),
        jnp.concatenate([partner, state_half], 2),
    )
    b_full = state_full[0]
    c_full = state_full[1]
    steps_dt = step_size.reshape(head_count, block_count, BLOCK)
    upper = (
        lax.broadcasted_iota(jnp.int32, (BLOCK, BLOCK), 0)
        <= lax.broadcasted_iota(jnp.int32, (BLOCK, BLOCK), 1)
    ).astype(jnp.float32)
    log_decay = jnp.einsum(
        "hbs,st->hbt", -steps_dt * decay_rate[:, None, None], upper, precision=precise
    )
    seg_own = seg_ext[3:].reshape(block_count, BLOCK)
    seg_prev = seg_ext[2 : 2 + own_rows].reshape(block_count, BLOCK)[:, 0]
    block_decay = jnp.exp(log_decay[:, :, -1]) * (seg_own[:, -1] == seg_prev).astype(jnp.float32)[
        None
    ]
    head_width = inner_input.shape[1] // head_count
    spread = lambda v: jnp.repeat(v, head_width, axis=-1)
    decay_x = spread(jnp.transpose(block_decay)).reshape(block_count, 1, -1)
    skip_x = spread(skip_gain).reshape(1, -1)
    l_t = jnp.transpose(log_decay.reshape(head_count, own_rows))
    dt_t = jnp.transpose(step_size)
    seg_row = seg_ext[3:].reshape(1, own_rows)
    seg_col = seg_ext[3:].reshape(own_rows, 1)
    entry_col = (seg_own == seg_prev[:, None]).astype(jnp.float32).reshape(own_rows, 1)
    b_t = jnp.transpose(b_full)

    local_end = run_blocks(
        False, inner_conv, b_t, None, None, l_t, dt_t, None, seg_col, None, decay_x, None, None
    )
    total_decay = spread(jnp.prod(block_decay, axis=1))[None, :]

    def relay(step_num, incoming):
        return shifted((total_decay * incoming + local_end).astype(jnp.bfloat16), "seq", 1).astype(
            jnp.float32
        )

    incoming = lax.fori_loop(0, lax.axis_size("seq") - 1, relay, jnp.zeros_like(local_end))
    return run_blocks(
        True, inner_conv, b_t, b_full, c_full, l_t, dt_t, seg_row, seg_col, entry_col, decay_x,
        skip_x, incoming
    )


def solution(mesh):
    return jax.shard_map(
        body,
        mesh=mesh,
        in_specs=(
            P(("grp", "seq"), "head"),
            P(None, ("grp", "seq"), "head"),
            P(None, "head"),
            P("head"),
            P(None, None, "head"),
            P(None, "head"),
            P("head", ("grp", "seq")),
            P("head"),
            P("head"),
            P("grp"),
        ),
        out_specs=P(("grp", "seq"), "head"),
        check_vma=False,
    )
```

time: 145 us -> 102 us (0.70)
  Pallas kernels: 64.8 us -> 21.8 us
  local copies, waits for them, and re-layouts: 8.61 us -> 11 us
  other arithmetic: 16.4 us -> 14.7 us
    pallas_call x2, Pallas kernels: 64.8 us -> 21.8 us  [run_blocks(): pl.pallas_call(kernel, grid=(block_count,), in_specs=[row_block(width), b...]
    convert_element_type x2, other arithmetic: 10.1 us -> 8.16 us  [convolve(): return jax.nn.silu(summed).astype(jnp.bfloat16)]
  transfers between devices with their start and end apart: 6 -> 6, of which waited for: 3 -> 3; matrix products, arithmetic and copies ran while one was open for 15% -> 21% of each run, Pallas kernels for 0% -> 0%
where the time goes in v2:
time: 102 us
  waiting for transfers between devices  32.9 us (32%)
  Pallas kernels  21.8 us (21%)
  starting transfers between devices  20.8 us (20%)
  other arithmetic  14.7 us (14%)
  local copies, waits for them, and re-layouts  11 us (11%)
    ppermute x5, waiting for transfers between devices, shifted(): lax.ppermute(value, axis, [(source, source + steps) for source in range(i...  32.9 us
    pallas_call x2, Pallas kernels, run_blocks(): pl.pallas_call(kernel, grid=(block_count,), in_specs=[row_block(width), b...  21.8 us
    ppermute x5, starting transfers between devices, shifted(): lax.ppermute(value, axis, [(source, source + steps) for source in range(i...  20.7 us
    convert_element_type x2, other arithmetic, convolve(): return jax.nn.silu(summed).astype(jnp.bfloat16)  8.16 us
  transfers between devices with their start and end apart: 6, of which 3 were waited for; matrix products, arithmetic and copies ran while one was open for 21% of the time, Pallas kernels for 0%

profile of v2, /device:TPU:0, one launch (start us, length us, event | category | flops | bytes accessed | tf_op | source)
XLA Modules:
  0.0 101.6 jit_solution(13104155196010540732)
XLA Ops:
  0.0 0.7 slice.102
  0.7 4.9 %collective-permute-start.2 = (bf16[2,3,128]{2,1,0:T(4,128)(2,1)S(1)}, bf16[2,3,128]{2,1,0:T(4,128)(2,1)S(1)}, u32[]{:S(2)}, u32[]{:S(2)}) collective-permute-start(bf16[2,3,128]{2,1,0:T(4,128)(2,1)S(1)} %slice.102), channel_id=1, source_target_pairs={{0,4},{4,8},{8,12},{1,5},{5,9},{9,13},{2,6},{6,10},{10,14},{3,7},{... | collective-permute-start | bytes 4616 | tf_op jit(solution)/shard_map/ppermute | solution.py:16
  5.6 0.7 slice.90
  6.4 3.5 %collective-permute-start.1 = (bf16[3,1024]{1,0:T(4,128)(2,1)S(1)}, bf16[3,1024]{1,0:T(4,128)(2,1)S(1)}, u32[]{:S(2)}, u32[]{:S(2)}) collective-permute-start(bf16[3,1024]{1,0:T(4,128)(2,1)S(1)} %slice.90), channel_id=1, source_target_pairs={{0,4},{4,8},{8,12},{1,5},{5,9},{9,13},{2,6},{6,10},{10,14},{3,7},{... | collective-permute-start | bytes 18440 | tf_op jit(solution)/shard_map/ppermute | solution.py:16
  9.9 0.8 reduce-window.9
  10.7 0.7 bitcast_subtract_fusion
  11.4 0.1 convert_reduce_fusion
  11.5 0.1 slice_bitcast_fusion.4
  11.5 0.2 slice_reduce_fusion
  11.7 0.1 fusion.11
  11.8 0.8 slice_convert_fusion.7
  12.6 0.9 slice_convert_fusion.3
  13.5 0.8 negate_bitcast_fusion
  14.4 0.9 bitcast_multiply_fusion
  15.3 0.2 fusion.9
  15.5 0.1 slice.132
  15.5 0.1 copy.48
  15.7 0.1 fusion.14
  15.8 1.0 %copy.40 = f32[16,8,128]{0,2,1:T(8,128)} copy(f32[16,8,128]{2,1,0:T(8,128)S(1)} %fusion.9) | data formatting | bytes 131072 | tf_op jit(solution)/shard_map/hbs,st->hbt/dot_general | solution.py:198
  16.8 1.8 %copy.41 = f32[16,1024]{0,1:T(8,128)} copy(f32[16,1024]{1,0:T(8,128)} %param.18) | data formatting | bytes 131072 | tf_op args[6]
  18.6 0.1 broadcast_in_dim.8
  18.7 0.7 reshape_reshape.6.refs_5_.refs_9_
  19.4 1.1 %copy.46.refs_4_.refs_7_ = s32[1024,1]{1,0:T(8,128)} copy(s32[1024,1]{0,1:T(1,128)S(1)} %bitcast.54) | data formatting | bytes 8192 | tf_op jit(solution)/shard_map/reshape | solution.py:213
  20.5 1.1 %copy.47.refs_8_ = f32[1024,1]{1,0:T(8,128)} copy(f32[1024,1]{0,1:T(1,128)S(1)} %bitcast.56) | data formatting | bytes 8192 | tf_op jit(solution)/shard_map/convert_element_type | solution.py:214
  21.6 0.7 reshape_reshape.7.refs_10_
  22.3 2.6 %multiply_convert_fusion.1 = bf16[2,1024,128]{2,1,0:T(8,128)(2,1)S(1)} fusion(bf16[2,1024,128]{2,1,0:T(8,128)(2,1)} %param.13, bf16[2,3,128]{2,1,0:T(4,128)(2,1)S(1)} %collective-permute-done.2, f32[2,128]{1,0:T(2,128)S(1)} %bitcast.63, f32[1024]{0:T(1024)S(1)} %get-tuple-element.61, f32[2,128]{1,0:T(2,128)S(1)} %bitcast.64, f32[1024]{0:T(1024)S(1)} %get-tuple-element.62, ...), kind=kLoop, calls=%fused_computation.11 | loop fusion | flops 7602176 | bytes 1067520 | tf_op jit(solution)/shard_map/convert_element_type | solution.py:44
  25.0 5.6 %multiply_convert_fusion.refs_0_ = bf16[1024,1024]{1,0:T(8,128)(2,1)} fusion(bf16[1024,1024]{1,0:T(8,128)(2,1)S(1)} %copy-done, bf16[3,1024]{1,0:T(4,128)(2,1)S(1)} %collective-permute-done.1, f32[1024]{0:T(1024)S(1)} %bitcast.59, f32[1024]{0:T(1024)S(1)} %get-tuple-element.61, f32[1024]{0:T(1024)S(1)} %bitcast.60, f32[1024]{0:T(1024)S(1)} %get-tuple-element.62, ...), kind=kLoop, calls=%fused_computation.4 | loop fusion | flops 30408704 | bytes 4233216 | tf_op jit(solution)/shard_map/convert_element_type | solution.py:44
  30.6 0.4 maximum_select_fusion
  30.9 1.1 %slice_bitcast_fusion = (bf16[1024,256]{1,0:T(8,128)(2,1)}, bf16[256,1024]{0,1:T(8,128)(2,1)S(1)}, bf16[1024,256]{1,0:T(8,128)(2,1)}) fusion(bf16[2,1024,256]{2,1,0:T(8,128)(2,1)S(1)} %maximum_select_fusion), kind=kLoop, calls=%fused_computation.16 | loop fusion | bytes 2621440 | tf_op jit(solution)/shard_map/squeeze | solution.py:192
  32.0 1.0 copy.45.refs_1_
  33.0 8.1 %shard_map.100 = f32[256,1024]{1,0:T(8,128)S(1)} custom-call(bf16[1024,1024]{1,0:T(8,128)(2,1)} %multiply_convert_fusion.refs_0_, bf16[256,1024]{1,0:T(8,128)(2,1)} %copy.45.refs_1_, f32[1024,16]{1,0:T(8,128)} %bitcast.50, f32[1024,16]{1,0:T(8,128)} %bitcast.52, s32[1024,1]{1,0:T(8,128)} %copy.46.refs_4_.refs_7_, f32[8,1,1024]{2,1,0:T(1,128)} %reshape_reshape.6.refs_5_.refs_9_), custom_call_target="tpu_custom_call" | custom-call | tf_op jit(solution)/shard_map/pallas_call | solution.py:142
  41.1 46.7 %while.11 = (s32[]{:T(128)}, f32[256,1024]{1,0:T(8,128)S(1)}, f32[256,1024]{1,0:T(8,128)S(1)}, f32[16]{0:T(128)S(1)}, s32[]{:T(128)}, /*index=5*/s32[]{:T(128)}) while((s32[]{:T(128)}, f32[256,1024]{1,0:T(8,128)S(1)}, f32[256,1024]{1,0:T(8,128)S(1)}, f32[16]{0:T(128)S(1)}, s32[]{:T(128)}, /*index=5*/s32[]{:T(128)}) %tuple.37), condition=%wide.region_4.5_spmd.clone, body=%wide.region_3.4_spmd.clone.sunk | while | flops 1310723 | bytes 6308023 | solution.py:227
  41.2 0.1 mul.289
  41.3 0.2 fusion.18
  41.5 3.5 %collective-permute-start = (bf16[256,1024]{1,0:T(8,128)(2,1)S(1)}, bf16[256,1024]{1,0:T(8,128)(2,1)S(1)}, u32[]{:S(2)}, u32[]{:S(2)}) collective-permute-start(bf16[256,1024]{1,0:T(8,128)(2,1)S(1)} %fusion.18), channel_id=1, source_target_pairs={{0,4},{4,8},{8,12},{1,5},{5,9},{9,13},{2,6},{6,10},{10,14},{3,7},{... | collective-permute-start | bytes 1572872 | tf_op jit(solution)/shard_map/while/body/eval_jaxpr/ppermute | solution.py:16
  45.0 11.8 %collective-permute-done = bf16[256,1024]{1,0:T(8,128)(2,1)S(1)} collective-permute-done((bf16[256,1024]{1,0:T(8,128)(2,1)S(1)}, bf16[256,1024]{1,0:T(8,128)(2,1)S(1)}, u32[]{:S(2)}, u32[]{:S(2)}) %collective-permute-start) | collective-permute-done | bytes 524320 | tf_op jit(solution)/shard_map/while/body/eval_jaxpr/ppermute | solution.py:16
  56.8 0.1 convert_element_type.180
  57.0 0.1 mul.289
  57.1 0.2 fusion.18
  57.3 4.4 %collective-permute-start = (bf16[256,1024]{1,0:T(8,128)(2,1)S(1)}, bf16[256,1024]{1,0:T(8,128)(2,1)S(1)}, u32[]{:S(2)}, u32[]{:S(2)}) collective-permute-start(bf16[256,1024]{1,0:T(8,128)(2,1)S(1)} %fusion.18), channel_id=1, source_target_pairs={{0,4},{4,8},{8,12},{1,5},{5,9},{9,13},{2,6},{6,10},{10,14},{3,7},{... | collective-permute-start | bytes 1572872 | tf_op jit(solution)/shard_map/while/body/eval_jaxpr/ppermute | solution.py:16
  61.7 11.0 %collective-permute-done = bf16[256,1024]{1,0:T(8,128)(2,1)S(1)} collective-permute-done((bf16[256,1024]{1,0:T(8,128)(2,1)S(1)}, bf16[256,1024]{1,0:T(8,128)(2,1)S(1)}, u32[]{:S(2)}, u32[]{:S(2)}) %collective-permute-start) | collective-permute-done | bytes 524320 | tf_op jit(solution)/shard_map/while/body/eval_jaxpr/ppermute | solution.py:16
  72.7 0.1 convert_element_type.180
  72.9 0.1 mul.289
  73.0 0.2 fusion.18
  73.2 4.4 %collective-permute-start = (bf16[256,1024]{1,0:T(8,128)(2,1)S(1)}, bf16[256,1024]{1,0:T(8,128)(2,1)S(1)}, u32[]{:S(2)}, u32[]{:S(2)}) collective-permute-start(bf16[256,1024]{1,0:T(8,128)(2,1)S(1)} %fusion.18), channel_id=1, source_target_pairs={{0,4},{4,8},{8,12},{1,5},{5,9},{9,13},{2,6},{6,10},{10,14},{3,7},{... | collective-permute-start | bytes 1572872 | tf_op jit(solution)/shard_map/while/body/eval_jaxpr/ppermute | solution.py:16
  77.6 10.1 %collective-permute-done = bf16[256,1024]{1,0:T(8,128)(2,1)S(1)} collective-permute-done((bf16[256,1024]{1,0:T(8,128)(2,1)S(1)}, bf16[256,1024]{1,0:T(8,128)(2,1)S(1)}, u32[]{:S(2)}, u32[]{:S(2)}) %collective-permute-start) | collective-permute-done | bytes 524320 | tf_op jit(solution)/shard_map/while/body/eval_jaxpr/ppermute | solution.py:16
  87.7 0.1 convert_element_type.180
  87.8 13.7 %shard_map.101 = bf16[1024,1024]{1,0:T(8,128)(2,1)} custom-call(bf16[1024,1024]{1,0:T(8,128)(2,1)} %multiply_convert_fusion.refs_0_, bf16[256,1024]{1,0:T(8,128)(2,1)} %copy.45.refs_1_, bf16[1024,256]{1,0:T(8,128)(2,1)} %get-tuple-element.56.refs_2_, bf16[1024,256]{1,0:T(8,128)(2,1)} %get-tuple-element.54.refs_3_, f32[1024,16]{1,0:T(8,128)} %bitcast.51, ...), custom_call_target="tpu_custom_call" | custom-call | tf_op jit(solution)/shard_map/pallas_call | solution.py:129
  (23 shorter events, 0.4 us)
Async XLA Ops:
  0.0 21.5 %copy-start.4 = (f32[16]{0:T(128)S(1)}, f32[16]{0:T(128)}, u32[]{:S(2)}) copy-start(f32[16]{0:T(128)} %param.20) | copy-start | bytes 196
  0.0 22.3 %copy-start.3 = (f32[2,128]{1,0:T(2,128)S(1)}, f32[2,128]{1,0:T(2,128)}, u32[]{:S(2)}) copy-start(f32[2,128]{1,0:T(2,128)} %param.17) | copy-start | bytes 3076
  0.7 21.5 %collective-permute-start.2 = (bf16[2,3,128]{2,1,0:T(4,128)(2,1)S(1)}, bf16[2,3,128]{2,1,0:T(4,128)(2,1)S(1)}, u32[]{:S(2)}, u32[]{:S(2)}) collective-permute-start(bf16[2,3,128]{2,1,0:T(4,128)(2,1)S(1)} %slice.102), channel_id=1, source_target_pairs={{0,4},{4,8},{8,12},{1,5},{5,9},{9,13},{2,6},{6,10},{10,14},{3,7},{... | collective-permute-start | bytes 4616 | tf_op jit(solution)/shard_map/ppermute | solution.py:16
  6.4 18.6 %collective-permute-start.1 = (bf16[3,1024]{1,0:T(4,128)(2,1)S(1)}, bf16[3,1024]{1,0:T(4,128)(2,1)S(1)}, u32[]{:S(2)}, u32[]{:S(2)}) collective-permute-start(bf16[3,1024]{1,0:T(4,128)(2,1)S(1)} %slice.90), channel_id=1, source_target_pairs={{0,4},{4,8},{8,12},{1,5},{5,9},{9,13},{2,6},{6,10},{10,14},{3,7},{... | collective-permute-start | bytes 18440 | tf_op jit(solution)/shard_map/ppermute | solution.py:16
  11.5 13.3 %copy-start.1 = (s32[1024]{0:T(1024)}, s32[1024]{0:T(1024)S(1)}, u32[]{:S(2)}) copy-start(s32[1024]{0:T(1024)S(1)} %get-tuple-element.59) | copy-start | bytes 12292
  14.4 10.6 %copy-start = (bf16[1024,1024]{1,0:T(8,128)(2,1)S(1)}, bf16[1024,1024]{1,0:T(8,128)(2,1)}, u32[]{:S(2)}) copy-start(bf16[1024,1024]{1,0:T(8,128)(2,1)} %param.12) | copy-start | bytes 6291460
  14.4 10.6 %copy-start.2 = (f32[1024]{0:T(1024)S(1)}, f32[1024]{0:T(1024)}, u32[]{:S(2)}) copy-start(f32[1024]{0:T(1024)} %param.15) | copy-start | bytes 12292
  24.9 5.7 %collective-permute-start.3 = (bf16[2,1024,128]{2,1,0:T(8,128)(2,1)S(1)}, bf16[2,1024,128]{2,1,0:T(8,128)(2,1)S(1)}, u32[]{:S(2)}, u32[]{:S(2)}) collective-permute-start(bf16[2,1024,128]{2,1,0:T(8,128)(2,1)S(1)} %multiply_convert_fusion.1), channel_id=1, source_target_pairs={{0,1},{1,0},{2,3},{3,2},{4,5},{5,4},{6,7},{7,6},{8,9},{9,8},{10,11... | collective-permute-start | bytes 1572872 | tf_op jit(solution)/shard_map/ppermute | solution.py:26
  41.5 15.3 %collective-permute-start = (bf16[256,1024]{1,0:T(8,128)(2,1)S(1)}, bf16[256,1024]{1,0:T(8,128)(2,1)S(1)}, u32[]{:S(2)}, u32[]{:S(2)}) collective-permute-start(bf16[256,1024]{1,0:T(8,128)(2,1)S(1)} %fusion.18), channel_id=1, source_target_pairs={{0,4},{4,8},{8,12},{1,5},{5,9},{9,13},{2,6},{6,10},{10,14},{3,7},{... | collective-permute-start | bytes 1572872 | tf_op jit(solution)/shard_map/while/body/eval_jaxpr/ppermute | solution.py:16
  57.3 15.4 %collective-permute-start = (bf16[256,1024]{1,0:T(8,128)(2,1)S(1)}, bf16[256,1024]{1,0:T(8,128)(2,1)S(1)}, u32[]{:S(2)}, u32[]{:S(2)}) collective-permute-start(bf16[256,1024]{1,0:T(8,128)(2,1)S(1)} %fusion.18), channel_id=1, source_target_pairs={{0,4},{4,8},{8,12},{1,5},{5,9},{9,13},{2,6},{6,10},{10,14},{3,7},{... | collective-permute-start | bytes 1572872 | tf_op jit(solution)/shard_map/while/body/eval_jaxpr/ppermute | solution.py:16
  73.2 14.5 %collective-permute-start = (bf16[256,1024]{1,0:T(8,128)(2,1)S(1)}, bf16[256,1024]{1,0:T(8,128)(2,1)S(1)}, u32[]{:S(2)}, u32[]{:S(2)}) collective-permute-start(bf16[256,1024]{1,0:T(8,128)(2,1)S(1)} %fusion.18), channel_id=1, source_target_pairs={{0,4},{4,8},{8,12},{1,5},{5,9},{9,13},{2,6},{6,10},{10,14},{3,7},{... | collective-permute-start | bytes 1572872 | tf_op jit(solution)/shard_map/while/body/eval_jaxpr/ppermute | solution.py:16

commit v3 on v2

--- a/solution.py
+++ b/solution.py
@@ -224,7 +224,11 @@
             jnp.float32
         )
 
-    incoming = lax.fori_loop(0, lax.axis_size("seq") - 1, relay, jnp.zeros_like(local_end))
+    part_rows = own_rows * lax.axis_size("seq")
+    hops = min(lax.axis_size("seq") - 1, -(-(part_rows // 2) // own_rows))
+    incoming = jnp.zeros_like(local_end)
+    for step_num in range(hops):
+        incoming = relay(step_num, incoming)
     return run_blocks(
         True, inner_conv, b_t, b_full, c_full, l_t, dt_t, seg_row, seg_col, entry_col, decay_x,
         skip_x, incoming

time: 102 us -> 87.2 us (0.85)
  waiting for transfers between devices: 32.9 us -> 21 us
  starting transfers between devices: 20.8 us -> 16.4 us
  Pallas kernels: 21.8 us -> 23.2 us
    ppermute x5 -> x4, waiting for transfers between devices: 32.9 us -> 21 us  [shifted(): lax.ppermute(value, axis, [(source, source + steps) for source in range(i...]
    ppermute x5 -> x4, starting transfers between devices: 20.7 us -> 16.3 us  [shifted(): lax.ppermute(value, axis, [(source, source + steps) for source in range(i...]
    convert_element_type x2, other arithmetic: 8.16 us -> 6.74 us  [convolve(): return jax.nn.silu(summed).astype(jnp.bfloat16)]
    pallas_call x2, Pallas kernels: 21.8 us -> 23.2 us  [run_blocks(): pl.pallas_call(kernel, grid=(block_count,), in_specs=[row_block(width), b...]
  transfers between devices with their start and end apart: 6 -> 5, of which waited for: 3 -> 2; matrix products, arithmetic and copies ran while one was open for 21% -> 23% of each run, Pallas kernels for 0% -> 0%
where the time goes in v3:
time: 87.2 us; the launch traced here: 86.5 us
  Pallas kernels  23.2 us (27%)
  waiting for transfers between devices  21 us (24%)
  starting transfers between devices  16.4 us (19%)
  other arithmetic  14.8 us (17%)
  local copies, waits for them, and re-layouts  10.8 us (12%)
    pallas_call x2, Pallas kernels, run_blocks(): pl.pallas_call(kernel, grid=(block_count,), in_specs=[row_block(width), b...  23.2 us
    ppermute x4, waiting for transfers between devices, shifted(): lax.ppermute(value, axis, [(source, source + steps) for source in range(i...  21 us
    ppermute x4, starting transfers between devices, shifted(): lax.ppermute(value, axis, [(source, source + steps) for source in range(i...  16.3 us
    convert_element_type x2, other arithmetic, convolve(): return jax.nn.silu(summed).astype(jnp.bfloat16)  6.74 us
    unnamed x17, local copies, waits for them, and re-layouts  2.03 us
  transfers between devices with their start and end apart: 5, of which 2 were waited for; matrix products, arithmetic and copies ran while one was open for 23% of the time, Pallas kernels for 0%

profile of v3, /device:TPU:0, one launch (start us, length us, event | category | flops | bytes accessed | tf_op | source)
XLA Modules:
  0.0 86.5 jit_solution(2404710915635238978)
XLA Ops:
  0.0 0.9 slice.102
  0.9 4.9 %collective-permute-start.1 = (bf16[2,3,128]{2,1,0:T(4,128)(2,1)S(1)}, bf16[2,3,128]{2,1,0:T(4,128)(2,1)S(1)}, u32[]{:S(2)}, u32[]{:S(2)}) collective-permute-start(bf16[2,3,128]{2,1,0:T(4,128)(2,1)S(1)} %slice.102), channel_id=1, source_target_pairs={{0,4},{4,8},{8,12},{1,5},{5,9},{9,13},{2,6},{6,10},{10,14},{3,7},{... | collective-permute-start | bytes 4616 | tf_op jit(solution)/shard_map/ppermute | solution.py:16
  5.8 0.7 slice.90
  6.5 3.5 %collective-permute-start = (bf16[3,1024]{1,0:T(4,128)(2,1)S(1)}, bf16[3,1024]{1,0:T(4,128)(2,1)S(1)}, u32[]{:S(2)}, u32[]{:S(2)}) collective-permute-start(bf16[3,1024]{1,0:T(4,128)(2,1)S(1)} %slice.90), channel_id=1, source_target_pairs={{0,4},{4,8},{8,12},{1,5},{5,9},{9,13},{2,6},{6,10},{10,14},{3,7},{... | collective-permute-start | bytes 18440 | tf_op jit(solution)/shard_map/ppermute | solution.py:16
  10.0 0.8 reduce-window.9
  10.8 0.7 bitcast_subtract_fusion
  11.5 0.1 convert_reduce_fusion
  11.6 0.1 slice_bitcast_fusion.4
  11.7 0.2 slice_reduce_fusion
  11.9 0.1 fusion.7
  11.9 0.9 slice_convert_fusion.3
  12.8 0.8 negate_bitcast_fusion
  13.7 0.7 bitcast_multiply_fusion
  14.4 0.2 fusion.5
  14.6 0.1 slice.132
  14.7 0.1 copy.48
  14.8 0.1 fusion.10
  14.9 0.1 broadcast_in_dim.10
  15.0 0.1 mul.235
  15.0 0.8 slice_convert_fusion.7
  15.9 1.0 %copy.40 = f32[16,8,128]{0,2,1:T(8,128)} copy(f32[16,8,128]{2,1,0:T(8,128)S(1)} %fusion.5) | data formatting | bytes 131072 | tf_op jit(solution)/shard_map/hbs,st->hbt/dot_general | solution.py:198
  16.9 1.9 %copy.41 = f32[16,1024]{0,1:T(8,128)} copy(f32[16,1024]{1,0:T(8,128)} %param.16) | data formatting | bytes 131072 | tf_op args[6]
  18.8 0.1 broadcast_in_dim.8
  18.8 0.7 reshape_reshape.6.refs_5_.refs_9_
  19.6 1.0 %copy.46.refs_4_.refs_7_ = s32[1024,1]{1,0:T(8,128)} copy(s32[1024,1]{0,1:T(1,128)S(1)} %bitcast.54) | data formatting | bytes 8192 | tf_op jit(solution)/shard_map/reshape | solution.py:213
  20.6 0.0 collective-permute-done.1
  20.6 0.0 copy-done.5
  20.6 1.2 %multiply_convert_fusion.1 = bf16[2,1024,128]{2,1,0:T(8,128)(2,1)S(1)} fusion(bf16[2,1024,128]{2,1,0:T(8,128)(2,1)S(1)} %copy-done.2, bf16[2,3,128]{2,1,0:T(4,128)(2,1)S(1)} %collective-permute-done.1, f32[2,128]{1,0:T(2,128)S(1)} %bitcast.63, f32[1024]{0:T(1024)S(1)} %get-tuple-element.12, f32[2,128]{1,0:T(2,128)S(1)} %bitcast.64, ...), kind=kLoop, calls=%fused_computation.9 | loop fusion | flops 7602176 | bytes 1067520 | tf_op jit(solution)/shard_map/convert_element_type | solution.py:44
  21.8 0.1 collective-permute-start.2
  21.9 0.0 collective-permute-done
  21.9 5.5 %multiply_convert_fusion.refs_0_ = bf16[1024,1024]{1,0:T(8,128)(2,1)} fusion(bf16[1024,1024]{1,0:T(8,128)(2,1)S(1)} %copy-done.1, bf16[3,1024]{1,0:T(4,128)(2,1)S(1)} %collective-permute-done, f32[1024]{0:T(1024)S(1)} %bitcast.59, f32[1024]{0:T(1024)S(1)} %get-tuple-element.12, f32[1024]{0:T(1024)S(1)} %bitcast.60, f32[1024]{0:T(1024)S(1)} %get-tuple-element.13, ...), kind=kLoop, calls=%fused_computation | loop fusion | flops 30408704 | bytes 4233216 | tf_op jit(solution)/shard_map/convert_element_type | solution.py:44
  27.5 0.0 copy-done.3
  27.5 0.0 collective-permute-done.2
  27.5 0.4 maximum_select_fusion
  27.9 1.1 %slice_bitcast_fusion = (bf16[1024,256]{1,0:T(8,128)(2,1)}, bf16[256,1024]{0,1:T(8,128)(2,1)S(1)}, bf16[1024,256]{1,0:T(8,128)(2,1)}) fusion(bf16[2,1024,256]{2,1,0:T(8,128)(2,1)S(1)} %maximum_select_fusion), kind=kLoop, calls=%fused_computation.14 | loop fusion | bytes 2621440 | tf_op jit(solution)/shard_map/squeeze | solution.py:192
  28.9 1.0 %copy.45.refs_1_ = bf16[256,1024]{1,0:T(8,128)(2,1)} copy(bf16[256,1024]{0,1:T(8,128)(2,1)S(1)} %get-tuple-element.6) | data formatting | bytes 1048576 | tf_op jit(solution)/shard_map/transpose | solution.py:215
  30.0 8.9 %shard_map.100 = f32[256,1024]{1,0:T(8,128)} custom-call(bf16[1024,1024]{1,0:T(8,128)(2,1)} %multiply_convert_fusion.refs_0_, bf16[256,1024]{1,0:T(8,128)(2,1)} %copy.45.refs_1_, f32[1024,16]{1,0:T(8,128)} %bitcast.50, f32[1024,16]{1,0:T(8,128)} %bitcast.52, s32[1024,1]{1,0:T(8,128)} %copy.46.refs_4_.refs_7_, f32[8,1,1024]{2,1,0:T(1,128)} %reshape_reshape.6.refs_5_.refs_9_), custom_call_target="tpu_custom_call" | custom-call | tf_op jit(solution)/shard_map/pallas_call | solution.py:142
  38.9 1.4 %add_convert_fusion.1 = bf16[256,1024]{1,0:T(8,128)(2,1)S(1)} fusion(f32[256,1024]{1,0:T(8,128)} %shard_map.100, f32[1024]{0:T(1024)S(1)} %broadcast_multiply_fusion), kind=kLoop, calls=%fused_computation.8 | loop fusion | flops 524288 | bytes 1576960 | tf_op jit(solution)/shard_map/convert_element_type | solution.py:223
  40.3 3.5 %collective-permute-start.3 = (bf16[256,1024]{1,0:T(8,128)(2,1)S(1)}, bf16[256,1024]{1,0:T(8,128)(2,1)S(1)}, u32[]{:S(2)}, u32[]{:S(2)}) collective-permute-start(bf16[256,1024]{1,0:T(8,128)(2,1)S(1)} %add_convert_fusion.1), channel_id=1, source_target_pairs={{0,4},{4,8},{8,12},{1,5},{5,9},{9,13},{2,6},{6,10},{10,14},{3,7},{... | collective-permute-start | bytes 1572872 | tf_op jit(solution)/shard_map/ppermute | solution.py:16
  43.9 11.8 %collective-permute-done.3 = bf16[256,1024]{1,0:T(8,128)(2,1)S(1)} collective-permute-done((bf16[256,1024]{1,0:T(8,128)(2,1)S(1)}, bf16[256,1024]{1,0:T(8,128)(2,1)S(1)}, u32[]{:S(2)}, u32[]{:S(2)}) %collective-permute-start.3) | collective-permute-done | bytes 524320 | tf_op jit(solution)/shard_map/ppermute | solution.py:16
  55.6 0.2 add_convert_fusion
  55.8 4.4 %collective-permute-start.4 = (bf16[256,1024]{1,0:T(8,128)(2,1)S(1)}, bf16[256,1024]{1,0:T(8,128)(2,1)S(1)}, u32[]{:S(2)}, u32[]{:S(2)}) collective-permute-start(bf16[256,1024]{1,0:T(8,128)(2,1)S(1)} %add_convert_fusion), channel_id=1, source_target_pairs={{0,4},{4,8},{8,12},{1,5},{5,9},{9,13},{2,6},{6,10},{10,14},{3,7},{... | collective-permute-start | bytes 1572872 | tf_op jit(solution)/shard_map/ppermute | solution.py:16
  60.2 0.1 broadcast_in_dim.9
  60.3 0.7 reshape_reshape.7.refs_10_
  61.0 1.0 %copy.47.refs_8_ = f32[1024,1]{1,0:T(8,128)} copy(f32[1024,1]{0,1:T(1,128)S(1)} %bitcast.56) | data formatting | bytes 8192 | tf_op jit(solution)/shard_map/convert_element_type | solution.py:214
  62.0 9.2 %collective-permute-done.4 = bf16[256,1024]{1,0:T(8,128)(2,1)S(1)} collective-permute-done((bf16[256,1024]{1,0:T(8,128)(2,1)S(1)}, bf16[256,1024]{1,0:T(8,128)(2,1)S(1)}, u32[]{:S(2)}, u32[]{:S(2)}) %collective-permute-start.4) | collective-permute-done | bytes 524320 | tf_op jit(solution)/shard_map/ppermute | solution.py:16
  71.2 1.1 %convert_element_type.158.refs_11_ = f32[256,1024]{1,0:T(8,128)} convert(bf16[256,1024]{1,0:T(8,128)(2,1)S(1)} %collective-permute-done.4) | non-fusion elementwise | flops 262144 | bytes 1572864 | tf_op jit(solution)/shard_map/convert_element_type | solution.py:223
  72.3 14.2 %shard_map.101 = bf16[1024,1024]{1,0:T(8,128)(2,1)} custom-call(bf16[1024,1024]{1,0:T(8,128)(2,1)} %multiply_convert_fusion.refs_0_, bf16[256,1024]{1,0:T(8,128)(2,1)} %copy.45.refs_1_, bf16[1024,256]{1,0:T(8,128)(2,1)} %get-tuple-element.7.refs_2_, bf16[1024,256]{1,0:T(8,128)(2,1)} %get-tuple-element.5.refs_3_, f32[1024,16]{1,0:T(8,128)} %bitcast.51, ...), custom_call_target="tpu_custom_call" | custom-call | tf_op jit(solution)/shard_map/pallas_call | solution.py:129
  (17 shorter events, 0.1 us)
Async XLA Ops:
  0.0 20.6 %copy-start.2 = (bf16[2,1024,128]{2,1,0:T(8,128)(2,1)S(1)}, bf16[2,1024,128]{2,1,0:T(8,128)(2,1)}, u32[]{:S(2)}) copy-start(bf16[2,1024,128]{2,1,0:T(8,128)(2,1)} %param.11) | copy-start | bytes 1572868
  0.0 21.9 %copy-start.1 = (bf16[1024,1024]{1,0:T(8,128)(2,1)S(1)}, bf16[1024,1024]{1,0:T(8,128)(2,1)}, u32[]{:S(2)}) copy-start(bf16[1024,1024]{1,0:T(8,128)(2,1)} %param.10) | copy-start | bytes 6291460
  0.0 20.6 %copy-start.5 = (f32[2,128]{1,0:T(2,128)S(1)}, f32[2,128]{1,0:T(2,128)}, u32[]{:S(2)}) copy-start(f32[2,128]{1,0:T(2,128)} %param.15) | copy-start | bytes 3076
  0.0 21.9 %copy-start.4 = (f32[1024]{0:T(1024)S(1)}, f32[1024]{0:T(1024)}, u32[]{:S(2)}) copy-start(f32[1024]{0:T(1024)} %param.13) | copy-start | bytes 12292
  0.9 19.7 %collective-permute-start.1 = (bf16[2,3,128]{2,1,0:T(4,128)(2,1)S(1)}, bf16[2,3,128]{2,1,0:T(4,128)(2,1)S(1)}, u32[]{:S(2)}, u32[]{:S(2)}) collective-permute-start(bf16[2,3,128]{2,1,0:T(4,128)(2,1)S(1)} %slice.102), channel_id=1, source_target_pairs={{0,4},{4,8},{8,12},{1,5},{5,9},{9,13},{2,6},{6,10},{10,14},{3,7},{... | collective-permute-start | bytes 4616 | tf_op jit(solution)/shard_map/ppermute | solution.py:16
  6.5 15.4 %collective-permute-start = (bf16[3,1024]{1,0:T(4,128)(2,1)S(1)}, bf16[3,1024]{1,0:T(4,128)(2,1)S(1)}, u32[]{:S(2)}, u32[]{:S(2)}) collective-permute-start(bf16[3,1024]{1,0:T(4,128)(2,1)S(1)} %slice.90), channel_id=1, source_target_pairs={{0,4},{4,8},{8,12},{1,5},{5,9},{9,13},{2,6},{6,10},{10,14},{3,7},{... | collective-permute-start | bytes 18440 | tf_op jit(solution)/shard_map/ppermute | solution.py:16
  11.7 15.8 %copy-start.3 = (s32[1024]{0:T(1024)}, s32[1024]{0:T(1024)S(1)}, u32[]{:S(2)}) copy-start(s32[1024]{0:T(1024)S(1)} %get-tuple-element.10) | copy-start | bytes 12292
  21.8 5.7 %collective-permute-start.2 = (bf16[2,1024,128]{2,1,0:T(8,128)(2,1)S(1)}, bf16[2,1024,128]{2,1,0:T(8,128)(2,1)S(1)}, u32[]{:S(2)}, u32[]{:S(2)}) collective-permute-start(bf16[2,1024,128]{2,1,0:T(8,128)(2,1)S(1)} %multiply_convert_fusion.1), channel_id=1, source_target_pairs={{0,1},{1,0},{2,3},{3,2},{4,5},{5,4},{6,7},{7,6},{8,9},{9,8},{10,11... | collective-permute-start | bytes 1572872 | tf_op jit(solution)/shard_map/ppermute | solution.py:26
  38.9 16.7 %copy-start = (f32[256,1024]{1,0:T(8,128)S(1)}, f32[256,1024]{1,0:T(8,128)}, u32[]{:S(2)}) copy-start(f32[256,1024]{1,0:T(8,128)} %shard_map.100) | copy-start | bytes 3145732
  38.9 21.3 %copy-start.6 = (f32[16]{0:T(128)S(1)}, f32[16]{0:T(128)}, u32[]{:S(2)}) copy-start(f32[16]{0:T(128)} %param.18) | copy-start | bytes 196
  40.3 15.3 %collective-permute-start.3 = (bf16[256,1024]{1,0:T(8,128)(2,1)S(1)}, bf16[256,1024]{1,0:T(8,128)(2,1)S(1)}, u32[]{:S(2)}, u32[]{:S(2)}) collective-permute-start(bf16[256,1024]{1,0:T(8,128)(2,1)S(1)} %add_convert_fusion.1), channel_id=1, source_target_pairs={{0,4},{4,8},{8,12},{1,5},{5,9},{9,13},{2,6},{6,10},{10,14},{3,7},{... | collective-permute-start | bytes 1572872 | tf_op jit(solution)/shard_map/ppermute | solution.py:16
  55.8 15.4 %collective-permute-start.4 = (bf16[256,1024]{1,0:T(8,128)(2,1)S(1)}, bf16[256,1024]{1,0:T(8,128)(2,1)S(1)}, u32[]{:S(2)}, u32[]{:S(2)}) collective-permute-start(bf16[256,1024]{1,0:T(8,128)(2,1)S(1)} %add_convert_fusion), channel_id=1, source_target_pairs={{0,4},{4,8},{8,12},{1,5},{5,9},{9,13},{2,6},{6,10},{10,14},{3,7},{... | collective-permute-start | bytes 1572872 | tf_op jit(solution)/shard_map/ppermute | solution.py:16

commit v4 on v3

--- a/solution.py
+++ b/solution.py
@@ -69,17 +69,14 @@
 def block_kernel(with_y, head_width, *refs):
     if with_y:
         (x_ref, bt_ref, b_ref, c_ref, l_ref, dt_ref, segr_ref, segc_ref, entry_ref, decay_ref,
-         skip_ref, ein_ref, out_ref, state_ref) = refs
+         skip_ref, out_ref, state_ref) = refs
     else:
         (x_ref, bt_ref, l_ref, dt_ref, segc_ref, decay_ref, state_ref) = refs
     blk = pl.program_id(0)
 
     @pl.when(blk == 0)
     def _():
-        if with_y:
-            state_ref[...] = ein_ref[...]
-        else:
-            state_ref[...] = jnp.zeros(state_ref.shape, jnp.float32)
+        state_ref[...] = jnp.zeros(state_ref.shape, jnp.float32)
 
     seg_col = segc_ref[...]
     end_col = (seg_col == seg_col[BLOCK - 1 : BLOCK, :]).astype(jnp.float32)
@@ -101,7 +98,7 @@
         falling = expand_heads(jnp.exp(-l_small) * dt_small, head_width)
         intra = split_dot(masked, x * falling) * rising
         inter = split_dot(c_mat, state) * (rising * entry_ref[...])
-        out_ref[...] = (intra + inter + skip_ref[...] * x).astype(jnp.bfloat16)
+        out_ref[...] = intra + inter + skip_ref[...] * x
     ending = expand_heads(
         jnp.exp(l_small[BLOCK - 1 : BLOCK, :] - l_small) * dt_small * end_col, head_width
     )
@@ -111,8 +108,33 @@
     )
 
 
+def correct_kernel(head_width, y_ref, c_ref, l_ref, entry_ref, prefix_ref, ein_ref, out_ref):
+    rising = expand_heads(jnp.exp(l_ref[...]), head_width)
+    carried = jnp.dot(c_ref[...], ein_ref[...], preferred_element_type=jnp.float32)
+    out_ref[...] = (y_ref[...] + carried * (rising * entry_ref[...] * prefix_ref[0])).astype(
+        jnp.bfloat16
+    )
+
+
+def run_correct(partial, c_full, l_t, entry_col, prefix_x, entering):
+    rows, width = partial.shape
+    head_count = l_t.shape[1]
+    n_size = c_full.shape[1]
+    row_block = lambda cols: pl.BlockSpec((BLOCK, cols), lambda b: (b, 0))
+    return pl.pallas_call(
+        functools.partial(correct_kernel, width // head_count),
+        grid=(rows // BLOCK,),
+        in_specs=[row_block(width), row_block(n_size), row_block(head_count), row_block(1),
+                  pl.BlockSpec((1, 1, width), lambda b: (b, 0, 0)),
+                  pl.BlockSpec((n_size, width), lambda b: (0, 0))],
+        out_specs=row_block(width),
+        out_shape=jax.ShapeDtypeStruct((rows, width), jnp.bfloat16),
+        compiler_params=pltpu.CompilerParams(dimension_semantics=("arbitrary",)),
+    )(partial, c_full, l_t, entry_col, prefix_x, entering)
+
+
 def run_blocks(with_y, x, b_t, b_full, c_full, l_t, dt_t, seg_row, seg_col, entry_col, decay_x,
-               skip_x, entering):
+               skip_x):
     rows, width = x.shape
     head_count = l_t.shape[1]
     head_width = width // head_count
@@ -132,13 +154,12 @@
             in_specs=[row_block(width), bt_spec, row_block(n_size), row_block(n_size),
                       row_block(head_count), row_block(head_count),
                       pl.BlockSpec((1, BLOCK), lambda b: (0, b)), row_block(1), row_block(1),
-                      decay_spec, pl.BlockSpec((1, width), lambda b: (0, 0)), state_spec],
+                      decay_spec, pl.BlockSpec((1, width), lambda b: (0, 0))],
             out_specs=row_block(width),
-            out_shape=jax.ShapeDtypeStruct((rows, width), jnp.bfloat16),
+            out_shape=jax.ShapeDtypeStruct((rows, width), jnp.float32),
             scratch_shapes=[pltpu.VMEM((n_size, width), jnp.float32)],
             compiler_params=params,
-        )(x, b_t, b_full, c_full, l_t, dt_t, seg_row, seg_col, entry_col, decay_x, skip_x,
-          entering)
+        )(x, b_t, b_full, c_full, l_t, dt_t, seg_row, seg_col, entry_col, decay_x, skip_x)
     return pl.pallas_call(
         kernel,
         grid=(block_count,),
@@ -215,24 +236,28 @@
     b_t = jnp.transpose(b_full)
 
     local_end = run_blocks(
-        False, inner_conv, b_t, None, None, l_t, dt_t, None, seg_col, None, decay_x, None, None
-    )
+        False, inner_conv, b_t, None, None, l_t, dt_t, None, seg_col, None, decay_x, None
+    )
+    partial = run_blocks(
+        True, inner_conv, b_t, b_full, c_full, l_t, dt_t, seg_row, seg_col, entry_col, decay_x,
+        skip_x
+    )
+    prefix = [jnp.ones((head_count,), jnp.float32)]
+    for blk in range(block_count - 1):
+        prefix.append(prefix[-1] * block_decay[:, blk])
+    prefix_x = spread(jnp.stack(prefix)).reshape(block_count, 1, -1)
     total_decay = spread(jnp.prod(block_decay, axis=1))[None, :]
 
     def relay(step_num, incoming):
-        return shifted((total_decay * incoming + local_end).astype(jnp.bfloat16), "seq", 1).astype(
-            jnp.float32
-        )
+        return shifted((total_decay * incoming.astype(jnp.float32) + local_end).astype(jnp.bfloat16),
+                       "seq", 1)
 
     part_rows = own_rows * lax.axis_size("seq")
     hops = min(lax.axis_size("seq") - 1, -(-(part_rows // 2) // own_rows))
-    incoming = jnp.zeros_like(local_end)
+    incoming = jnp.zeros(local_end.shape, jnp.bfloat16)
     for step_num in range(hops):
         incoming = relay(step_num, incoming)
-    return run_blocks(
-        True, inner_conv, b_t, b_full, c_full, l_t, dt_t, seg_row, seg_col, entry_col, decay_x,
-        skip_x, incoming
-    )
+    return run_correct(partial, c_full, l_t, entry_col, prefix_x, incoming)
 
 
 def solution(mesh):

time: 87.2 us -> 89.7 us (1.029)
  waiting for transfers between devices: 21 us -> 11.8 us
  Pallas kernels: 23.2 us -> 31.1 us
  other arithmetic: 14.8 us -> 16.7 us
  local copies, waits for them, and re-layouts: 10.8 us -> 12.4 us
    ppermute x4, waiting for transfers between devices: 21 us -> 11.7 us  [shifted(): lax.ppermute(value, axis, [(source, source + steps) for source in range(i...]
    pallas_call x0 -> x1, Pallas kernels: none -> 8.37 us  [run_correct(): pl.pallas_call(functools.partial(correct_kernel, width // head_count), gr...]
    convert_element_type x2, other arithmetic: 6.74 us -> 8.62 us  [convolve(): return jax.nn.silu(summed).astype(jnp.bfloat16)]
    unnamed x17 -> x11, local copies, waits for them, and re-layouts: 2.03 us -> 2.79 us
    convert_element_type x3 -> x2, other arithmetic: 2.67 us -> 2.69 us  [relay(): (total_decay * incoming.astype(jnp.float32) + local_end).astype(jnp.bfloa...]
  transfers between devices with their start and end apart: 5 -> 5, of which waited for: 2 -> 1; matrix products, arithmetic and copies ran while one was open for 23% -> 25% of each run, Pallas kernels for 0% -> 16%
where the time goes in v4:
time: 89.7 us; the launch traced here: 88.7 us
  Pallas kernels  31.1 us (35%)
  other arithmetic  16.7 us (19%)
  starting transfers between devices  16.4 us (18%)
  local copies, waits for them, and re-layouts  12.4 us (14%)
  waiting for transfers between devices  11.8 us (13%)
    pallas_call x2, Pallas kernels, run_blocks(): pl.pallas_call(kernel, grid=(block_count,), in_specs=[row_block(width), b...  22.8 us
    ppermute x4, starting transfers between devices, shifted(): lax.ppermute(value, axis, [(source, source + steps) for source in range(i...  16.3 us
    ppermute x4, waiting for transfers between devices, shifted(): lax.ppermute(value, axis, [(source, source + steps) for source in range(i...  11.7 us
    convert_element_type x2, other arithmetic, convolve(): return jax.nn.silu(summed).astype(jnp.bfloat16)  8.62 us
    pallas_call x1, Pallas kernels, run_correct(): pl.pallas_call(functools.partial(correct_kernel, width // head_count), gr...  8.37 us
    unnamed x11, local copies, waits for them, and re-layouts  2.79 us
    convert_element_type x2, other arithmetic, relay(): (total_decay * incoming.astype(jnp.float32) + local_end).astype(jnp.bfloa...  2.69 us
  transfers between devices with their start and end apart: 5, of which 1 were waited for; matrix products, arithmetic and copies ran while one was open for 25% of the time, Pallas kernels for 16%

profile of v4, /device:TPU:0, one launch (start us, length us, event | category | flops | bytes accessed | tf_op | source)
XLA Modules:
  0.0 88.7 jit_solution(7862558185196059421)
XLA Ops:
  0.0 0.8 slice.123
  0.8 4.9 %collective-permute-start.1 = (bf16[2,3,128]{2,1,0:T(4,128)(2,1)S(1)}, bf16[2,3,128]{2,1,0:T(4,128)(2,1)S(1)}, u32[]{:S(2)}, u32[]{:S(2)}) collective-permute-start(bf16[2,3,128]{2,1,0:T(4,128)(2,1)S(1)} %slice.123), channel_id=1, source_target_pairs={{0,4},{4,8},{8,12},{1,5},{5,9},{9,13},{2,6},{6,10},{10,14},{3,7},{... | collective-permute-start | bytes 4616 | tf_op jit(solution)/shard_map/ppermute | solution.py:16
  5.8 0.7 slice.111
  6.5 3.5 %collective-permute-start = (bf16[3,1024]{1,0:T(4,128)(2,1)S(1)}, bf16[3,1024]{1,0:T(4,128)(2,1)S(1)}, u32[]{:S(2)}, u32[]{:S(2)}) collective-permute-start(bf16[3,1024]{1,0:T(4,128)(2,1)S(1)} %slice.111), channel_id=1, source_target_pairs={{0,4},{4,8},{8,12},{1,5},{5,9},{9,13},{2,6},{6,10},{10,14},{3,7},{... | collective-permute-start | bytes 18440 | tf_op jit(solution)/shard_map/ppermute | solution.py:16
  10.0 0.8 reduce-window.9
  10.8 0.7 bitcast_subtract_fusion
  11.5 0.1 convert_reduce_fusion
  11.6 0.1 slice_bitcast_fusion.5
  11.7 0.2 slice_reduce_fusion
  11.8 0.1 fusion.7
  11.9 0.9 slice_convert_fusion.3
  12.8 0.8 negate_bitcast_fusion
  13.7 0.7 bitcast_multiply_fusion
  14.4 0.2 fusion.5
  14.6 0.1 slice.160
  14.7 0.1 copy.52
  14.8 0.1 fusion.10
  14.9 0.1 broadcast_in_dim.13
  15.0 0.1 mul.361
  15.0 0.8 slice_convert_fusion.7
  15.9 1.0 %copy.43 = f32[16,8,128]{0,2,1:T(8,128)} copy(f32[16,8,128]{2,1,0:T(8,128)S(1)} %fusion.5) | data formatting | bytes 131072 | tf_op jit(solution)/shard_map/hbs,st->hbt/dot_general | solution.py:219
  16.9 1.8 %copy.44 = f32[16,1024]{0,1:T(8,128)} copy(f32[16,1024]{1,0:T(8,128)} %param.16) | data formatting | bytes 131072 | tf_op args[6]
  18.7 0.1 broadcast_in_dim.10
  18.8 0.7 reshape_reshape.9.refs_9_.refs_5_
  19.5 1.0 %copy.47.refs_7_.refs_4_ = s32[1024,1]{1,0:T(8,128)} copy(s32[1024,1]{0,1:T(1,128)S(1)} %bitcast.73) | data formatting | bytes 8192 | tf_op jit(solution)/shard_map/reshape | solution.py:234
  20.6 2.6 %multiply_convert_fusion.1 = bf16[2,1024,128]{2,1,0:T(8,128)(2,1)S(1)} fusion(bf16[2,1024,128]{2,1,0:T(8,128)(2,1)} %param.11, bf16[2,3,128]{2,1,0:T(4,128)(2,1)S(1)} %collective-permute-done.1, f32[2,128]{1,0:T(2,128)S(1)} %bitcast.83, f32[1024]{0:T(1024)S(1)} %get-tuple-element.20, f32[2,128]{1,0:T(2,128)S(1)} %bitcast.84, f32[1024]{0:T(1024)S(1)} %get-tuple-element.21, ...), kind=kLoop, calls=%fused_computation.9 | loop fusion | flops 7602176 | bytes 1067520 | tf_op jit(solution)/shard_map/convert_element_type | solution.py:44
  23.1 0.1 collective-permute-start.2
  23.2 0.0 collective-permute-done
  23.2 6.1 %multiply_convert_fusion.refs_0_ = bf16[1024,1024]{1,0:T(8,128)(2,1)} fusion(bf16[1024,1024]{1,0:T(8,128)(2,1)S(1)} %copy-done, bf16[3,1024]{1,0:T(4,128)(2,1)S(1)} %collective-permute-done, f32[1024]{0:T(1024)S(1)} %bitcast.79, f32[1024]{0:T(1024)S(1)} %get-tuple-element.20, f32[1024]{0:T(1024)S(1)} %bitcast.80, f32[1024]{0:T(1024)S(1)} %get-tuple-element.21, ...), kind=kLoop, calls=%fused_computation | loop fusion | flops 30408704 | bytes 4233216 | tf_op jit(solution)/shard_map/convert_element_type | solution.py:44
  29.3 0.0 collective-permute-done.2
  29.3 0.4 maximum_select_fusion
  29.7 1.1 %slice_bitcast_fusion = (bf16[1024,256]{1,0:T(8,128)(2,1)}, bf16[256,1024]{0,1:T(8,128)(2,1)S(1)}, bf16[1024,256]{1,0:T(8,128)(2,1)}) fusion(bf16[2,1024,256]{2,1,0:T(8,128)(2,1)S(1)} %maximum_select_fusion), kind=kLoop, calls=%fused_computation.14 | loop fusion | bytes 2621440 | tf_op jit(solution)/shard_map/squeeze | solution.py:213
  30.7 1.0 %copy.46.refs_1_ = bf16[256,1024]{1,0:T(8,128)(2,1)} copy(bf16[256,1024]{0,1:T(8,128)(2,1)S(1)} %get-tuple-element.14) | data formatting | bytes 1048576 | tf_op jit(solution)/shard_map/transpose | solution.py:236
  31.7 9.0 %shard_map.101 = f32[256,1024]{1,0:T(8,128)} custom-call(bf16[1024,1024]{1,0:T(8,128)(2,1)} %multiply_convert_fusion.refs_0_, bf16[256,1024]{1,0:T(8,128)(2,1)} %copy.46.refs_1_, f32[1024,16]{1,0:T(8,128)} %bitcast.68, f32[1024,16]{1,0:T(8,128)} %bitcast.71, s32[1024,1]{1,0:T(8,128)} %copy.47.refs_7_.refs_4_, f32[8,1,1024]{2,1,0:T(1,128)} %reshape_reshape.9.refs_9_.refs_5_), custom_call_target="tpu_custom_call" | custom-call | tf_op jit(solution)/shard_map/pallas_call | solution.py:163
  40.7 1.3 %add_convert_fusion.1 = bf16[256,1024]{1,0:T(8,128)(2,1)S(1)} fusion(f32[256,1024]{1,0:T(8,128)} %shard_map.101, f32[1024]{0:T(1024)S(1)} %broadcast_multiply_fusion), kind=kLoop, calls=%fused_computation.8 | loop fusion | flops 524288 | bytes 1576960 | tf_op jit(solution)/shard_map/convert_element_type | solution.py:252
  42.0 3.5 %collective-permute-start.3 = (bf16[256,1024]{1,0:T(8,128)(2,1)S(1)}, bf16[256,1024]{1,0:T(8,128)(2,1)S(1)}, u32[]{:S(2)}, u32[]{:S(2)}) collective-permute-start(bf16[256,1024]{1,0:T(8,128)(2,1)S(1)} %add_convert_fusion.1), channel_id=1, source_target_pairs={{0,4},{4,8},{8,12},{1,5},{5,9},{9,13},{2,6},{6,10},{10,14},{3,7},{... | collective-permute-start | bytes 1572872 | tf_op jit(solution)/shard_map/ppermute | solution.py:16
  45.5 11.7 %collective-permute-done.3 = bf16[256,1024]{1,0:T(8,128)(2,1)S(1)} collective-permute-done((bf16[256,1024]{1,0:T(8,128)(2,1)S(1)}, bf16[256,1024]{1,0:T(8,128)(2,1)S(1)}, u32[]{:S(2)}, u32[]{:S(2)}) %collective-permute-start.3) | collective-permute-done | bytes 524320 | tf_op jit(solution)/shard_map/ppermute | solution.py:16
  57.3 1.4 %add_convert_fusion = bf16[256,1024]{1,0:T(8,128)(2,1)S(1)} fusion(f32[256,1024]{1,0:T(8,128)} %shard_map.101, bf16[256,1024]{1,0:T(8,128)(2,1)S(1)} %collective-permute-done.3, f32[1024]{0:T(1024)S(1)} %mul.361), kind=kLoop, calls=%fused_computation.7 | loop fusion | flops 1048576 | bytes 2101248 | tf_op jit(solution)/shard_map/convert_element_type | solution.py:252
  58.7 4.4 %collective-permute-start.4 = (bf16[256,1024]{1,0:T(8,128)(2,1)S(1)}, bf16[256,1024]{1,0:T(8,128)(2,1)S(1)}, u32[]{:S(2)}, u32[]{:S(2)}) collective-permute-start(bf16[256,1024]{1,0:T(8,128)(2,1)S(1)} %add_convert_fusion), channel_id=1, source_target_pairs={{0,4},{4,8},{8,12},{1,5},{5,9},{9,13},{2,6},{6,10},{10,14},{3,7},{... | collective-permute-start | bytes 1572872 | tf_op jit(solution)/shard_map/ppermute | solution.py:16
  63.1 1.1 %copy.48.refs_8_.entry_ref = f32[1024,1]{1,0:T(8,128)} copy(f32[1024,1]{0,1:T(1,128)S(1)} %bitcast.76) | data formatting | bytes 8192 | tf_op jit(solution)/shard_map/convert_element_type | solution.py:235
  64.2 0.1 broadcast_in_dim.11
  64.2 0.7 reshape_reshape.10.refs_10_
  65.0 0.1 broadcast_in_dim.12
  65.0 0.7 reshape_reshape.11.prefix_ref
  65.7 13.8 %shard_map.100.y_ref = f32[1024,1024]{1,0:T(8,128)} custom-call(bf16[1024,1024]{1,0:T(8,128)(2,1)} %multiply_convert_fusion.refs_0_, bf16[256,1024]{1,0:T(8,128)(2,1)} %copy.46.refs_1_, bf16[1024,256]{1,0:T(8,128)(2,1)} %get-tuple-element.15.refs_2_, bf16[1024,256]{1,0:T(8,128)(2,1)} %get-tuple-element.13.refs_3_.c_ref, f32[1024,16]{1,0:T(8,128)} %bitcast.69, ...), custom_call_target="tpu_custom_call" | custom-call | tf_op jit(solution)/shard_map/pallas_call | solution.py:151
  79.6 0.0 collective-permute-done.4.ein_ref
  79.6 0.8 copy-done.1
  80.4 8.4 %shard_map.102 = bf16[1024,1024]{1,0:T(8,128)(2,1)} custom-call(f32[1024,1024]{1,0:T(8,128)} %shard_map.100.y_ref, bf16[1024,256]{1,0:T(8,128)(2,1)} %get-tuple-element.13.refs_3_.c_ref, f32[1024,16]{1,0:T(8,128)} %bitcast.70, f32[1024,1]{1,0:T(8,128)} %copy.48.refs_8_.entry_ref, f32[8,1,1024]{2,1,0:T(1,128)} %reshape_reshape.11.prefix_ref, ...), custom_call_target="tpu_custom_call" | custom-call | tf_op jit(solution)/shard_map/pallas_call | solution.py:124
  (17 shorter events, 0.1 us)
Async XLA Ops:
  0.0 23.2 %copy-start = (bf16[1024,1024]{1,0:T(8,128)(2,1)S(1)}, bf16[1024,1024]{1,0:T(8,128)(2,1)}, u32[]{:S(2)}) copy-start(bf16[1024,1024]{1,0:T(8,128)(2,1)} %param.10) | copy-start | bytes 6291460
  0.8 19.7 %collective-permute-start.1 = (bf16[2,3,128]{2,1,0:T(4,128)(2,1)S(1)}, bf16[2,3,128]{2,1,0:T(4,128)(2,1)S(1)}, u32[]{:S(2)}, u32[]{:S(2)}) collective-permute-start(bf16[2,3,128]{2,1,0:T(4,128)(2,1)S(1)} %slice.123), channel_id=1, source_target_pairs={{0,4},{4,8},{8,12},{1,5},{5,9},{9,13},{2,6},{6,10},{10,14},{3,7},{... | collective-permute-start | bytes 4616 | tf_op jit(solution)/shard_map/ppermute | solution.py:16
  6.5 16.7 %collective-permute-start = (bf16[3,1024]{1,0:T(4,128)(2,1)S(1)}, bf16[3,1024]{1,0:T(4,128)(2,1)S(1)}, u32[]{:S(2)}, u32[]{:S(2)}) collective-permute-start(bf16[3,1024]{1,0:T(4,128)(2,1)S(1)} %slice.111), channel_id=1, source_target_pairs={{0,4},{4,8},{8,12},{1,5},{5,9},{9,13},{2,6},{6,10},{10,14},{3,7},{... | collective-permute-start | bytes 18440 | tf_op jit(solution)/shard_map/ppermute | solution.py:16
  11.7 18.0 %copy-start.2 = (s32[1024]{0:T(1024)}, s32[1024]{0:T(1024)S(1)}, u32[]{:S(2)}) copy-start(s32[1024]{0:T(1024)S(1)} %get-tuple-element.18) | copy-start | bytes 12292
  23.1 6.2 %collective-permute-start.2 = (bf16[2,1024,128]{2,1,0:T(8,128)(2,1)S(1)}, bf16[2,1024,128]{2,1,0:T(8,128)(2,1)S(1)}, u32[]{:S(2)}, u32[]{:S(2)}) collective-permute-start(bf16[2,1024,128]{2,1,0:T(8,128)(2,1)S(1)} %multiply_convert_fusion.1), channel_id=1, source_target_pairs={{0,1},{1,0},{2,3},{3,2},{4,5},{5,4},{6,7},{7,6},{8,9},{9,8},{10,11... | collective-permute-start | bytes 1572872 | tf_op jit(solution)/shard_map/ppermute | solution.py:26
  31.7 32.4 %copy-start.3 = (f32[16]{0:T(128)S(1)}, f32[16]{0:T(128)}, u32[]{:S(2)}) copy-start(f32[16]{0:T(128)} %param.18) | copy-start | bytes 196
  42.0 15.3 %collective-permute-start.3 = (bf16[256,1024]{1,0:T(8,128)(2,1)S(1)}, bf16[256,1024]{1,0:T(8,128)(2,1)S(1)}, u32[]{:S(2)}, u32[]{:S(2)}) collective-permute-start(bf16[256,1024]{1,0:T(8,128)(2,1)S(1)} %add_convert_fusion.1), channel_id=1, source_target_pairs={{0,4},{4,8},{8,12},{1,5},{5,9},{9,13},{2,6},{6,10},{10,14},{3,7},{... | collective-permute-start | bytes 1572872 | tf_op jit(solution)/shard_map/ppermute | solution.py:16
  58.7 20.9 %collective-permute-start.4 = (bf16[256,1024]{1,0:T(8,128)(2,1)S(1)}, bf16[256,1024]{1,0:T(8,128)(2,1)S(1)}, u32[]{:S(2)}, u32[]{:S(2)}) collective-permute-start(bf16[256,1024]{1,0:T(8,128)(2,1)S(1)} %add_convert_fusion), channel_id=1, source_target_pairs={{0,4},{4,8},{8,12},{1,5},{5,9},{9,13},{2,6},{6,10},{10,14},{3,7},{... | collective-permute-start | bytes 1572872 | tf_op jit(solution)/shard_map/ppermute | solution.py:16
  79.6 0.8 copy-start.1

commit v5 on v3

--- a/solution.py
+++ b/solution.py
@@ -68,10 +68,10 @@
 
 def block_kernel(with_y, head_width, *refs):
     if with_y:
-        (x_ref, bt_ref, b_ref, c_ref, l_ref, dt_ref, segr_ref, segc_ref, entry_ref, decay_ref,
+        (x_ref, b_ref, c_ref, l_ref, dt_ref, segr_ref, segc_ref, entry_ref, decay_ref,
          skip_ref, ein_ref, out_ref, state_ref) = refs
     else:
-        (x_ref, bt_ref, l_ref, dt_ref, segc_ref, decay_ref, state_ref) = refs
+        (x_ref, b_ref, l_ref, dt_ref, segc_ref, decay_ref, state_ref) = refs
     blk = pl.program_id(0)
 
     @pl.when(blk == 0)
@@ -106,17 +106,84 @@
         jnp.exp(l_small[BLOCK - 1 : BLOCK, :] - l_small) * dt_small * end_col, head_width
     )
     weighted = (x * ending).astype(jnp.bfloat16)
-    state_ref[...] = decay_ref[0] * state + jnp.dot(
-        bt_ref[...], weighted, preferred_element_type=jnp.float32
-    )
-
-
-def run_blocks(with_y, x, b_t, b_full, c_full, l_t, dt_t, seg_row, seg_col, entry_col, decay_x,
+    state_ref[...] = decay_ref[0] * state + lax.dot_general(
+        b_ref[...], weighted, (((0,), (0,)), ((), ())), preferred_element_type=jnp.float32
+    )
+
+
+def state_kernel(head_width, x_ref, b_ref, dt_ref, rate_ref, segc_ref, entry_ref, state_ref, l_ref,
+                 dtt_ref, decay_ref, total_ref):
+    blk = pl.program_id(0)
+
+    @pl.when(blk == 0)
+    def _():
+        state_ref[...] = jnp.zeros(state_ref.shape, jnp.float32)
+        total_ref[...] = jnp.ones(total_ref.shape, jnp.float32)
+
+    rows = lax.broadcasted_iota(jnp.int32, (2 * BLOCK, BLOCK), 0)
+    cols = lax.broadcasted_iota(jnp.int32, (2 * BLOCK, BLOCK), 1)
+    picker = jnp.where(
+        ((rows < BLOCK) & (rows >= cols)) | (rows - BLOCK == cols), 1.0, 0.0
+    ).astype(jnp.bfloat16)
+    rest = dt_ref[...]
+    summed = None
+    for _ in range(3):
+        piece = rest.astype(jnp.bfloat16)
+        part = lax.dot_general(
+            picker, piece, (((1,), (1,)), ((), ())), preferred_element_type=jnp.float32
+        )
+        summed = part if summed is None else summed + part
+        rest = rest - piece.astype(jnp.float32)
+    l_small = -summed[:BLOCK] * rate_ref[...]
+    dt_small = summed[BLOCK:]
+    l_ref[...] = l_small
+    dtt_ref[...] = dt_small
+    seg_col = segc_ref[...]
+    end_col = (seg_col == seg_col[BLOCK - 1 : BLOCK, :]).astype(jnp.float32)
+    decay_x = expand_heads(
+        jnp.exp(l_small[BLOCK - 1 : BLOCK, :]) * entry_ref[BLOCK - 1 : BLOCK, :], head_width
+    )
+    decay_ref[0] = decay_x
+    total_ref[...] = total_ref[...] * decay_x
+    ending = expand_heads(
+        jnp.exp(l_small[BLOCK - 1 : BLOCK, :] - l_small) * dt_small * end_col, head_width
+    )
+    weighted = (x_ref[...].astype(jnp.float32) * ending).astype(jnp.bfloat16)
+    state_ref[...] = decay_x * state_ref[...] + lax.dot_general(
+        b_ref[...], weighted, (((0,), (0,)), ((), ())), preferred_element_type=jnp.float32
+    )
+
+
+def run_state(x, b_full, step_size, rate_row, seg_col, entry_col):
+    rows, width = x.shape
+    head_count = step_size.shape[0]
+    n_size = b_full.shape[1]
+    block_count = rows // BLOCK
+    row_block = lambda cols: pl.BlockSpec((BLOCK, cols), lambda b: (b, 0))
+    whole = lambda shape: pl.BlockSpec(shape, lambda b: (0,) * len(shape))
+    return pl.pallas_call(
+        functools.partial(state_kernel, width // head_count),
+        grid=(block_count,),
+        in_specs=[row_block(width), row_block(n_size),
+                  pl.BlockSpec((head_count, BLOCK), lambda b: (0, b)), whole((1, head_count)),
+                  row_block(1), row_block(1)],
+        out_specs=[whole((n_size, width)), row_block(head_count), row_block(head_count),
+                   pl.BlockSpec((1, 1, width), lambda b: (b, 0, 0)), whole((1, width))],
+        out_shape=[jax.ShapeDtypeStruct((n_size, width), jnp.float32),
+                   jax.ShapeDtypeStruct((rows, head_count), jnp.float32),
+                   jax.ShapeDtypeStruct((rows, head_count), jnp.float32),
+                   jax.ShapeDtypeStruct((block_count, 1, width), jnp.float32),
+                   jax.ShapeDtypeStruct((1, width), jnp.float32)],
+        compiler_params=pltpu.CompilerParams(dimension_semantics=("arbitrary",)),
+    )(x, b_full, step_size, rate_row, seg_col, entry_col)
+
+
+def run_blocks(with_y, x, b_full, c_full, l_t, dt_t, seg_row, seg_col, entry_col, decay_x,
                skip_x, entering):
     rows, width = x.shape
     head_count = l_t.shape[1]
     head_width = width // head_count
-    n_size = b_t.shape[0]
+    n_size = b_full.shape[1]
     block_count = rows // BLOCK
     row_block = lambda cols: pl.BlockSpec((BLOCK, cols), lambda b: (b, 0))
     bt_spec = pl.BlockSpec((n_size, BLOCK), lambda b: (0, b))
@@ -129,7 +196,7 @@
         return pl.pallas_call(
             kernel,
             grid=(block_count,),
-            in_specs=[row_block(width), bt_spec, row_block(n_size), row_block(n_size),
+            in_specs=[row_block(width), row_block(n_size), row_block(n_size),
                       row_block(head_count), row_block(head_count),
                       pl.BlockSpec((1, BLOCK), lambda b: (0, b)), row_block(1), row_block(1),
                       decay_spec, pl.BlockSpec((1, width), lambda b: (0, 0)), state_spec],
@@ -137,7 +204,7 @@
             out_shape=jax.ShapeDtypeStruct((rows, width), jnp.bfloat16),
             scratch_shapes=[pltpu.VMEM((n_size, width), jnp.float32)],
             compiler_params=params,
-        )(x, b_t, b_full, c_full, l_t, dt_t, seg_row, seg_col, entry_col, decay_x, skip_x,
+        )(x, b_full, c_full, l_t, dt_t, seg_row, seg_col, entry_col, decay_x, skip_x,
           entering)
     return pl.pallas_call(
         kernel,
@@ -162,14 +229,19 @@
     skip_gain,
     lengths,
 ):
-    precise = lax.Precision.HIGHEST
     own_rows = inner_input.shape[0]
     head_count = decay_rate.shape[0]
     group_half = state_input.shape[2]
     block_count = own_rows // BLOCK
     positions = lax.axis_index("seq") * own_rows + jnp.arange(own_rows + 3, dtype=jnp.int32) - 3
     seg_ext = segment_of(lengths, positions)
-    inner_tail, state_tail = shifted((inner_input[-3:], state_input[:, -3:]), "seq", 1)
+    width = inner_input.shape[1]
+    tails = jnp.concatenate(
+        [inner_input[-3:], jnp.transpose(state_input[:, -3:], (1, 0, 2)).reshape(3, -1)], 1
+    )
+    tails = shifted(tails, "seq", 1)
+    inner_tail = tails[:, :width]
+    state_tail = jnp.transpose(tails[:, width:].reshape(3, 2, group_half), (1, 0, 2))
     weight_state = jnp.swapaxes(conv_state, 0, 1)[:, :, None, :]
     state_half = convolve(
         jnp.concatenate([state_tail, state_input], 1),
@@ -190,34 +262,18 @@
     )
     b_full = state_full[0]
     c_full = state_full[1]
-    steps_dt = step_size.reshape(head_count, block_count, BLOCK)
-    upper = (
-        lax.broadcasted_iota(jnp.int32, (BLOCK, BLOCK), 0)
-        <= lax.broadcasted_iota(jnp.int32, (BLOCK, BLOCK), 1)
-    ).astype(jnp.float32)
-    log_decay = jnp.einsum(
-        "hbs,st->hbt", -steps_dt * decay_rate[:, None, None], upper, precision=precise
-    )
+    head_width = inner_input.shape[1] // head_count
+    spread = lambda v: jnp.repeat(v, head_width, axis=-1)
+    skip_x = spread(skip_gain).reshape(1, -1)
     seg_own = seg_ext[3:].reshape(block_count, BLOCK)
     seg_prev = seg_ext[2 : 2 + own_rows].reshape(block_count, BLOCK)[:, 0]
-    block_decay = jnp.exp(log_decay[:, :, -1]) * (seg_own[:, -1] == seg_prev).astype(jnp.float32)[
-        None
-    ]
-    head_width = inner_input.shape[1] // head_count
-    spread = lambda v: jnp.repeat(v, head_width, axis=-1)
-    decay_x = spread(jnp.transpose(block_decay)).reshape(block_count, 1, -1)
-    skip_x = spread(skip_gain).reshape(1, -1)
-    l_t = jnp.transpose(log_decay.reshape(head_count, own_rows))
-    dt_t = jnp.transpose(step_size)
     seg_row = seg_ext[3:].reshape(1, own_rows)
     seg_col = seg_ext[3:].reshape(own_rows, 1)
     entry_col = (seg_own == seg_prev[:, None]).astype(jnp.float32).reshape(own_rows, 1)
-    b_t = jnp.transpose(b_full)
-
-    local_end = run_blocks(
-        False, inner_conv, b_t, None, None, l_t, dt_t, None, seg_col, None, decay_x, None, None
-    )
-    total_decay = spread(jnp.prod(block_decay, axis=1))[None, :]
+
+    local_end, l_t, dt_t, decay_x, total_decay = run_state(
+        inner_conv, b_full, step_size, decay_rate.reshape(1, -1), seg_col, entry_col
+    )
 
     def relay(step_num, incoming):
         return shifted((total_decay * incoming + local_end).astype(jnp.bfloat16), "seq", 1).astype(
@@ -230,7 +286,7 @@
     for step_num in range(hops):
         incoming = relay(step_num, incoming)
     return run_blocks(
-        True, inner_conv, b_t, b_full, c_full, l_t, dt_t, seg_row, seg_col, entry_col, decay_x,
+        True, inner_conv, b_full, c_full, l_t, dt_t, seg_row, seg_col, entry_col, decay_x,
         skip_x, incoming
     )
 

time: 87.2 us -> 81.4 us (0.933)
  local copies, waits for them, and re-layouts: 10.8 us -> 5.65 us
  starting transfers between devices: 16.4 us -> 12.9 us
  other arithmetic: 14.8 us -> 15.9 us
  waiting for transfers between devices: 21 us -> 22 us
  Pallas kernels: 23.2 us -> 24.1 us
    ppermute x4 -> x3, starting transfers between devices: 16.3 us -> 12.9 us  [shifted(): lax.ppermute(value, axis, [(source, source + steps) for source in range(i...]
    unnamed x17 -> x10, local copies, waits for them, and re-layouts: 2.03 us -> 0.02 us
    convert_element_type x2, other arithmetic: 6.74 us -> 8.17 us  [convolve(): return jax.nn.silu(summed).astype(jnp.bfloat16)]
    ppermute x4 -> x3, waiting for transfers between devices: 21 us -> 22 us  [shifted(): lax.ppermute(value, axis, [(source, source + steps) for source in range(i...]
    dot_general x1 -> x0, local copies, waits for them, and re-layouts: 1.02 us -> none  [body(): jnp.einsum('hbs,st->hbt', -steps_dt * decay_rate[:, None, None], upper, p...]
    transpose x1, local copies, waits for them, and re-layouts: 1.03 us -> 0.01 us  [body(): jnp.transpose(tails[:, width:].reshape(3, 2, group_half), (1, 0, 2))]
    slice x3 -> x2, local copies, waits for them, and re-layouts: 1.11 us -> 0.12 us  [the longest x1 0.11 us: body(): seg_prev = seg_ext[2:2 + own_rows].reshape(block_count, BLOCK)[:, 0]]
    pallas_call x2, Pallas kernels: 23.2 us -> 24.1 us  [the longest x1 14.3 us: run_blocks(): pl.pallas_call(kernel, grid=(block_count,), in_specs=[row_block(width), r...]
  transfers between devices with their start and end apart: 5 -> 4, of which waited for: 2 -> 2; matrix products, arithmetic and copies ran while one was open for 23% -> 15% of each run, Pallas kernels for 0% -> 0%
where the time goes in v5:
time: 81.4 us; the launch traced here: 80.8 us
  Pallas kernels  24.1 us (30%)
  waiting for transfers between devices  22 us (27%)
  other arithmetic  15.9 us (20%)
  starting transfers between devices  12.9 us (16%)
  local copies, waits for them, and re-layouts  5.65 us (7%)
    ppermute x3, waiting for transfers between devices, shifted(): lax.ppermute(value, axis, [(source, source + steps) for source in range(i...  22 us
    pallas_call x1, Pallas kernels, run_blocks(): pl.pallas_call(kernel, grid=(block_count,), in_specs=[row_block(width), r...  14.3 us
    ppermute x3, starting transfers between devices, shifted(): lax.ppermute(value, axis, [(source, source + steps) for source in range(i...  12.9 us
    pallas_call x1, Pallas kernels, run_state(): pl.pallas_call(functools.partial(state_kernel, width // head_count), grid...  9.86 us
    convert_element_type x2, other arithmetic, convolve(): return jax.nn.silu(summed).astype(jnp.bfloat16)  8.17 us
    convert_element_type x2, other arithmetic, relay(): (total_decay * incoming + local_end).astype(jnp.bfloat16)  2.13 us
  transfers between devices with their start and end apart: 4, of which 2 were waited for; matrix products, arithmetic and copies ran while one was open for 15% of the time, Pallas kernels for 0%

profile of v5, /device:TPU:0, one launch (start us, length us, event | category | flops | bytes accessed | tf_op | source)
XLA Modules:
  0.0 80.8 jit_solution(3105279683286821395)
XLA Ops:
  0.0 0.0 copy-start.1
  0.0 0.0 copy-start.3
  0.0 0.8 %slice_bitcast_fusion.4 = bf16[3,256]{1,0:T(4,128)(2,1)S(1)} fusion(bf16[2,1024,128]{2,1,0:T(8,128)(2,1)} %param.11), kind=kLoop, calls=%fused_computation.36 | loop fusion | bytes 3072 | tf_op jit(solution)/shard_map/reshape | solution.py:240
  0.8 0.7 slice.90
  1.6 4.9 %collective-permute-start = (bf16[3,1280]{1,0:T(4,128)(2,1)S(1)}, bf16[3,1280]{1,0:T(4,128)(2,1)S(1)}, u32[]{:S(2)}, u32[]{:S(2)}) collective-permute-start(bf16[3,1280]{1,0:T(4,128)(2,1)S(1)} %pad_maximum_fusion.2), channel_id=1, source_target_pairs={{0,4},{4,8},{8,12},{1,5},{5,9},{9,13},{2,6},{6,10},{10,14},{3,7},{... | collective-permute-start | bytes 23048 | tf_op jit(solution)/shard_map/ppermute | solution.py:16
  6.5 0.8 %reduce-window.9 = s32[3,1]{0,1:T(1,128)S(1)} reduce-window(s32[3,1]{0,1:T(1,128)} %bitcast.50, s32[]{:T(128)} %constant.32.clone.1), window={size=3x1 pad=2_0x0_0}, to_apply=%region_0.0 | reduce-window | flops 6 | bytes 28 | tf_op jit(solution)/shard_map/reduce-window.4
  7.4 0.7 bitcast_subtract_fusion
  8.0 0.1 convert_reduce_fusion
  8.1 0.1 slice_bitcast_fusion.2
  8.2 0.0 copy-start.2
  8.2 0.1 slice_reduce_fusion
  8.3 0.1 fusion.4
  8.4 0.9 %slice_convert_fusion.3 = (f32[1,1024]{1,0:T(1,128)S(1)}, f32[1,1024]{1,0:T(1,128)S(1)}, f32[1,1024]{1,0:T(1,128)S(1)}, f32[1,1024]{1,0:T(1,128)S(1)}) fusion(bf16[4,1024]{1,0:T(4,128)(2,1)} %param.12), kind=kLoop, calls=%fused_computation.28 | loop fusion | flops 4096 | bytes 24576 | tf_op jit(solution)/shard_map/mul | solution.py:43
  9.3 0.8 %slice_convert_fusion.7 = (f32[1,2,128]{2,0,1:T(1,128)S(1)}, f32[1,2,128]{2,0,1:T(1,128)S(1)}, f32[1,2,128]{2,0,1:T(1,128)S(1)}, f32[1,2,128]{2,0,1:T(1,128)S(1)}) fusion(bf16[4,2,128]{2,0,1:T(4,128)(2,1)} %bitcast.44), kind=kLoop, calls=%fused_computation.40 | loop fusion | flops 1024 | bytes 6144 | tf_op jit(solution)/shard_map/convert_element_type | solution.py:43
  10.1 1.0 %copy.20.entry_ref.refs_7_ = f32[1024,1]{1,0:T(8,128)} copy(f32[1024,1]{0,1:T(1,128)S(1)} %bitcast.39) | data formatting | bytes 8192 | tf_op jit(solution)/shard_map/convert_element_type | solution.py:272
  11.1 1.0 %copy.19.segc_ref.refs_6_ = s32[1024,1]{1,0:T(8,128)} copy(s32[1024,1]{0,1:T(1,128)S(1)} %bitcast.35) | data formatting | bytes 8192 | tf_op jit(solution)/shard_map/reshape | solution.py:271
  12.2 0.0 collective-permute-done
  12.2 2.6 %multiply_convert_fusion.1 = bf16[2,1024,128]{2,1,0:T(8,128)(2,1)S(1)} fusion(bf16[2,1024,128]{2,1,0:T(8,128)(2,1)} %param.11, bf16[2,3,128]{2,1,0:T(4,128)(2,1)S(1)} %slice_bitcast_fusion.3, f32[2,128]{1,0:T(2,128)S(1)} %bitcast.46, f32[1024]{0:T(1024)S(1)} %get-tuple-element.18, f32[2,128]{1,0:T(2,128)S(1)} %bitcast.47, f32[1024]{0:T(1024)S(1)} %get-tuple-element.19, ...), kind=kLoop, calls=%fused_computation.9 | loop fusion | flops 7602176 | bytes 1067520 | tf_op jit(solution)/shard_map/convert_element_type | solution.py:44
  14.8 0.1 collective-permute-start.1
  14.9 0.0 copy-done.1
  14.9 0.0 copy-done.3
  14.9 5.6 %multiply_convert_fusion.x_ref.refs_0_ = bf16[1024,1024]{1,0:T(8,128)(2,1)} fusion(bf16[1024,1024]{1,0:T(8,128)(2,1)S(1)} %copy-done.1, bf16[3,1024]{1,0:T(4,128)(2,1)S(1)} %slice.114, f32[1024]{0:T(1024)S(1)} %bitcast.42, f32[1024]{0:T(1024)S(1)} %get-tuple-element.18, f32[1024]{0:T(1024)S(1)} %bitcast.43, f32[1024]{0:T(1024)S(1)} %get-tuple-element.19, ...), kind=kLoop, calls=%fused_computation | loop fusion | flops 30408704 | bytes 4233216 | tf_op jit(solution)/shard_map/convert_element_type | solution.py:44
  20.5 0.0 copy-done.2
  20.5 0.0 collective-permute-done.1
  20.5 0.4 maximum_select_fusion
  20.8 1.1 %slice_bitcast_fusion = (bf16[1024,256]{1,0:T(8,128)(2,1)}, bf16[1024,256]{1,0:T(8,128)(2,1)}) fusion(bf16[2,1024,256]{2,1,0:T(8,128)(2,1)S(1)} %maximum_select_fusion), kind=kLoop, calls=%fused_computation.14 | loop fusion | bytes 2097152 | tf_op jit(solution)/shard_map/squeeze | solution.py:264
  21.9 9.9 %shard_map.100 = (f32[256,1024]{1,0:T(8,128)}, f32[1024,16]{1,0:T(8,128)}, f32[1024,16]{1,0:T(8,128)}, f32[8,1,1024]{2,1,0:T(1,128)}, f32[1,1024]{1,0:T(1,128)}) custom-call(bf16[1024,1024]{1,0:T(8,128)(2,1)} %multiply_convert_fusion.x_ref.refs_0_, bf16[1024,256]{1,0:T(8,128)(2,1)} %get-tuple-element.16.b_ref.refs_1_, f32[16,1024]{1,0:T(8,128)} %dt_ref.1, ...), custom_call_target="tpu_custom_call" | custom-call | tf_op jit(solution)/shard_map/pallas_call | solution.py:164
  31.8 0.0 copy-start
  31.8 0.0 copy-start.4
  31.8 0.8 broadcast_multiply_fusion
  32.5 1.3 %add_convert_fusion.1 = bf16[256,1024]{1,0:T(8,128)(2,1)S(1)} fusion(f32[256,1024]{1,0:T(8,128)} %get-tuple-element.14, f32[1024]{0:T(1024)S(1)} %broadcast_multiply_fusion), kind=kLoop, calls=%fused_computation.8 | loop fusion | flops 524288 | bytes 1576960 | tf_op jit(solution)/shard_map/convert_element_type | solution.py:279
  33.9 3.5 %collective-permute-start.2 = (bf16[256,1024]{1,0:T(8,128)(2,1)S(1)}, bf16[256,1024]{1,0:T(8,128)(2,1)S(1)}, u32[]{:S(2)}, u32[]{:S(2)}) collective-permute-start(bf16[256,1024]{1,0:T(8,128)(2,1)S(1)} %add_convert_fusion.1), channel_id=1, source_target_pairs={{0,4},{4,8},{8,12},{1,5},{5,9},{9,13},{2,6},{6,10},{10,14},{3,7},{... | collective-permute-start | bytes 1572872 | tf_op jit(solution)/shard_map/ppermute | solution.py:16
  37.4 11.8 %collective-permute-done.2 = bf16[256,1024]{1,0:T(8,128)(2,1)S(1)} collective-permute-done((bf16[256,1024]{1,0:T(8,128)(2,1)S(1)}, bf16[256,1024]{1,0:T(8,128)(2,1)S(1)}, u32[]{:S(2)}, u32[]{:S(2)}) %collective-permute-start.2) | collective-permute-done | bytes 524320 | tf_op jit(solution)/shard_map/ppermute | solution.py:16
  49.2 0.0 copy-done
  49.2 0.8 %add_convert_fusion = bf16[256,1024]{1,0:T(8,128)(2,1)S(1)} fusion(f32[256,1024]{1,0:T(8,128)S(1)} %copy-done, bf16[256,1024]{1,0:T(8,128)(2,1)S(1)} %collective-permute-done.2, f32[1024]{0:T(1024)} %bitcast.38), kind=kLoop, calls=%fused_computation.7 | loop fusion | flops 1048576 | bytes 2101248 | tf_op jit(solution)/shard_map/convert_element_type | solution.py:279
  50.0 4.4 %collective-permute-start.3 = (bf16[256,1024]{1,0:T(8,128)(2,1)S(1)}, bf16[256,1024]{1,0:T(8,128)(2,1)S(1)}, u32[]{:S(2)}, u32[]{:S(2)}) collective-permute-start(bf16[256,1024]{1,0:T(8,128)(2,1)S(1)} %add_convert_fusion), channel_id=1, source_target_pairs={{0,4},{4,8},{8,12},{1,5},{5,9},{9,13},{2,6},{6,10},{10,14},{3,7},{... | collective-permute-start | bytes 1572872 | tf_op jit(solution)/shard_map/ppermute | solution.py:16
  54.4 0.0 copy-done.4
  54.4 0.1 broadcast_in_dim.4
  54.5 0.7 reshape_reshape.3.refs_9_
  55.2 10.2 %collective-permute-done.3 = bf16[256,1024]{1,0:T(8,128)(2,1)S(1)} collective-permute-done((bf16[256,1024]{1,0:T(8,128)(2,1)S(1)}, bf16[256,1024]{1,0:T(8,128)(2,1)S(1)}, u32[]{:S(2)}, u32[]{:S(2)}) %collective-permute-start.3) | collective-permute-done | bytes 524320 | tf_op jit(solution)/shard_map/ppermute | solution.py:16
  65.4 1.1 %convert_element_type.149.refs_10_ = f32[256,1024]{1,0:T(8,128)} convert(bf16[256,1024]{1,0:T(8,128)(2,1)S(1)} %collective-permute-done.3) | non-fusion elementwise | flops 262144 | bytes 1572864 | tf_op jit(solution)/shard_map/convert_element_type | solution.py:279
  66.5 14.3 %shard_map.101 = bf16[1024,1024]{1,0:T(8,128)(2,1)} custom-call(bf16[1024,1024]{1,0:T(8,128)(2,1)} %multiply_convert_fusion.x_ref.refs_0_, bf16[1024,256]{1,0:T(8,128)(2,1)} %get-tuple-element.16.b_ref.refs_1_, bf16[1024,256]{1,0:T(8,128)(2,1)} %get-tuple-element.15.refs_2_, f32[1024,16]{1,0:T(8,128)} %get-tuple-element.10.refs_3_, ...), custom_call_target="tpu_custom_call" | custom-call | tf_op jit(solution)/shard_map/pallas_call | solution.py:196
  (5 shorter events, 0.0 us)
Async XLA Ops:
  0.0 14.9 %copy-start.1 = (bf16[1024,1024]{1,0:T(8,128)(2,1)S(1)}, bf16[1024,1024]{1,0:T(8,128)(2,1)}, u32[]{:S(2)}) copy-start(bf16[1024,1024]{1,0:T(8,128)(2,1)} %param.10) | copy-start | bytes 6291460
  0.0 14.9 %copy-start.3 = (f32[1024]{0:T(1024)S(1)}, f32[1024]{0:T(1024)}, u32[]{:S(2)}) copy-start(f32[1024]{0:T(1024)} %param.13) | copy-start | bytes 12292
  1.6 10.6 %collective-permute-start = (bf16[3,1280]{1,0:T(4,128)(2,1)S(1)}, bf16[3,1280]{1,0:T(4,128)(2,1)S(1)}, u32[]{:S(2)}, u32[]{:S(2)}) collective-permute-start(bf16[3,1280]{1,0:T(4,128)(2,1)S(1)} %pad_maximum_fusion.2), channel_id=1, source_target_pairs={{0,4},{4,8},{8,12},{1,5},{5,9},{9,13},{2,6},{6,10},{10,14},{3,7},{... | collective-permute-start | bytes 23048 | tf_op jit(solution)/shard_map/ppermute | solution.py:16
  8.2 12.3 %copy-start.2 = (s32[1024]{0:T(1024)}, s32[1024]{0:T(1024)S(1)}, u32[]{:S(2)}) copy-start(s32[1024]{0:T(1024)S(1)} %get-tuple-element.22) | copy-start | bytes 12292
  14.8 5.7 %collective-permute-start.1 = (bf16[2,1024,128]{2,1,0:T(8,128)(2,1)S(1)}, bf16[2,1024,128]{2,1,0:T(8,128)(2,1)S(1)}, u32[]{:S(2)}, u32[]{:S(2)}) collective-permute-start(bf16[2,1024,128]{2,1,0:T(8,128)(2,1)S(1)} %multiply_convert_fusion.1), channel_id=1, source_target_pairs={{0,1},{1,0},{2,3},{3,2},{4,5},{5,4},{6,7},{7,6},{8,9},{9,8},{10,11... | collective-permute-start | bytes 1572872 | tf_op jit(solution)/shard_map/ppermute | solution.py:26
  31.8 17.4 %copy-start = (f32[256,1024]{1,0:T(8,128)S(1)}, f32[256,1024]{1,0:T(8,128)}, u32[]{:S(2)}) copy-start(f32[256,1024]{1,0:T(8,128)} %get-tuple-element.14) | copy-start | bytes 3145732
  31.8 22.7 %copy-start.4 = (f32[16]{0:T(128)S(1)}, f32[16]{0:T(128)}, u32[]{:S(2)}) copy-start(f32[16]{0:T(128)} %param.18) | copy-start | bytes 196
  33.9 15.3 %collective-permute-start.2 = (bf16[256,1024]{1,0:T(8,128)(2,1)S(1)}, bf16[256,1024]{1,0:T(8,128)(2,1)S(1)}, u32[]{:S(2)}, u32[]{:S(2)}) collective-permute-start(bf16[256,1024]{1,0:T(8,128)(2,1)S(1)} %add_convert_fusion.1), channel_id=1, source_target_pairs={{0,4},{4,8},{8,12},{1,5},{5,9},{9,13},{2,6},{6,10},{10,14},{3,7},{... | collective-permute-start | bytes 1572872 | tf_op jit(solution)/shard_map/ppermute | solution.py:16
  50.0 15.4 %collective-permute-start.3 = (bf16[256,1024]{1,0:T(8,128)(2,1)S(1)}, bf16[256,1024]{1,0:T(8,128)(2,1)S(1)}, u32[]{:S(2)}, u32[]{:S(2)}) collective-permute-start(bf16[256,1024]{1,0:T(8,128)(2,1)S(1)} %add_convert_fusion), channel_id=1, source_target_pairs={{0,4},{4,8},{8,12},{1,5},{5,9},{9,13},{2,6},{6,10},{10,14},{3,7},{... | collective-permute-start | bytes 1572872 | tf_op jit(solution)/shard_map/ppermute | solution.py:16

commit v6 on v5

--- a/solution.py
+++ b/solution.py
@@ -69,17 +69,14 @@
 def block_kernel(with_y, head_width, *refs):
     if with_y:
         (x_ref, b_ref, c_ref, l_ref, dt_ref, segr_ref, segc_ref, entry_ref, decay_ref,
-         skip_ref, ein_ref, out_ref, state_ref) = refs
+         skip_ref, out_ref, state_ref) = refs
     else:
         (x_ref, b_ref, l_ref, dt_ref, segc_ref, decay_ref, state_ref) = refs
     blk = pl.program_id(0)
 
     @pl.when(blk == 0)
     def _():
-        if with_y:
-            state_ref[...] = ein_ref[...]
-        else:
-            state_ref[...] = jnp.zeros(state_ref.shape, jnp.float32)
+        state_ref[...] = jnp.zeros(state_ref.shape, jnp.float32)
 
     seg_col = segc_ref[...]
     end_col = (seg_col == seg_col[BLOCK - 1 : BLOCK, :]).astype(jnp.float32)
@@ -101,7 +98,7 @@
         falling = expand_heads(jnp.exp(-l_small) * dt_small, head_width)
         intra = split_dot(masked, x * falling) * rising
         inter = split_dot(c_mat, state) * (rising * entry_ref[...])
-        out_ref[...] = (intra + inter + skip_ref[...] * x).astype(jnp.bfloat16)
+        out_ref[...] = intra + inter + skip_ref[...] * x
     ending = expand_heads(
         jnp.exp(l_small[BLOCK - 1 : BLOCK, :] - l_small) * dt_small * end_col, head_width
     )
@@ -178,8 +175,42 @@
     )(x, b_full, step_size, rate_row, seg_col, entry_col)
 
 
+def correct_kernel(head_width, y_ref, c_ref, l_ref, entry_ref, prefix_ref, ein_ref, out_ref):
+    rows, cols = y_ref.shape
+    rising = expand_heads(jnp.exp(l_ref[0]), head_width)
+    blocks = prefix_ref.shape[0]
+    prefix = jnp.broadcast_to(prefix_ref[...], (blocks, BLOCK, cols)).reshape(rows, cols)
+    carried = jnp.dot(c_ref[...], ein_ref[...], preferred_element_type=jnp.float32)
+    out_ref[...] = (y_ref[...] + carried * (rising * entry_ref[...] * prefix)).astype(jnp.bfloat16)
+
+
+def run_correct(partial, c_full, l_t, entry_col, prefix_x, entering):
+    rows, width = partial.shape
+    head_count = l_t.shape[1]
+    head_width = width // head_count
+    n_size = c_full.shape[1]
+    tile = 256
+    tiles = width // tile
+    heads_per = tile // head_width
+    l_tiles = jnp.transpose(l_t.reshape(rows, tiles, heads_per), (1, 0, 2))
+    block_count = prefix_x.shape[0]
+    return pl.pallas_call(
+        functools.partial(correct_kernel, head_width),
+        grid=(tiles,),
+        in_specs=[pl.BlockSpec((rows, tile), lambda j: (0, j)),
+                  pl.BlockSpec((rows, n_size), lambda j: (0, 0)),
+                  pl.BlockSpec((1, rows, heads_per), lambda j: (j, 0, 0)),
+                  pl.BlockSpec((rows, 1), lambda j: (0, 0)),
+                  pl.BlockSpec((block_count, 1, tile), lambda j: (0, 0, j)),
+                  pl.BlockSpec((n_size, tile), lambda j: (0, j))],
+        out_specs=pl.BlockSpec((rows, tile), lambda j: (0, j)),
+        out_shape=jax.ShapeDtypeStruct((rows, width), jnp.bfloat16),
+        compiler_params=pltpu.CompilerParams(dimension_semantics=("arbitrary",)),
+    )(partial, c_full, l_tiles, entry_col, prefix_x, entering)
+
+
 def run_blocks(with_y, x, b_full, c_full, l_t, dt_t, seg_row, seg_col, entry_col, decay_x,
-               skip_x, entering):
+               skip_x):
     rows, width = x.shape
     head_count = l_t.shape[1]
     head_width = width // head_count
@@ -199,13 +230,12 @@
             in_specs=[row_block(width), row_block(n_size), row_block(n_size),
                       row_block(head_count), row_block(head_count),
                       pl.BlockSpec((1, BLOCK), lambda b: (0, b)), row_block(1), row_block(1),
-                      decay_spec, pl.BlockSpec((1, width), lambda b: (0, 0)), state_spec],
+                      decay_spec, pl.BlockSpec((1, width), lambda b: (0, 0))],
             out_specs=row_block(width),
-            out_shape=jax.ShapeDtypeStruct((rows, width), jnp.bfloat16),
+            out_shape=jax.ShapeDtypeStruct((rows, width), jnp.float32),
             scratch_shapes=[pltpu.VMEM((n_size, width), jnp.float32)],
             compiler_params=params,
-        )(x, b_full, c_full, l_t, dt_t, seg_row, seg_col, entry_col, decay_x, skip_x,
-          entering)
+        )(x, b_full, c_full, l_t, dt_t, seg_row, seg_col, entry_col, decay_x, skip_x)
     return pl.pallas_call(
         kernel,
         grid=(block_count,),
@@ -275,20 +305,26 @@
         inner_conv, b_full, step_size, decay_rate.reshape(1, -1), seg_col, entry_col
     )
 
+    partial = run_blocks(
+        True, inner_conv, b_full, c_full, l_t, dt_t, seg_row, seg_col, entry_col, decay_x, skip_x
+    )
+    prefix = [jnp.ones((1, 1, decay_x.shape[2]), jnp.float32)]
+    for blk in range(block_count - 1):
+        prefix.append(prefix[-1] * decay_x[blk : blk + 1])
+    prefix_x = jnp.concatenate(prefix, 0)
+
     def relay(step_num, incoming):
-        return shifted((total_decay * incoming + local_end).astype(jnp.bfloat16), "seq", 1).astype(
-            jnp.float32
-        )
+        return shifted((total_decay * incoming.astype(jnp.float32) + local_end).astype(jnp.bfloat16),
+                       "seq", 1)
 
     part_rows = own_rows * lax.axis_size("seq")
     hops = min(lax.axis_size("seq") - 1, -(-(part_rows // 2) // own_rows))
-    incoming = jnp.zeros_like(local_end)
+    incoming = jnp.zeros(local_end.shape, jnp.bfloat16)
     for step_num in range(hops):
         incoming = relay(step_num, incoming)
-    return run_blocks(
-        True, inner_conv, b_full, c_full, l_t, dt_t, seg_row, seg_col, entry_col, decay_x,
-        skip_x, incoming
-    )
+        if step_num == 0:
+            incoming, partial = lax.optimization_barrier((incoming, partial))
+    return run_correct(partial, c_full, l_t, entry_col, prefix_x, incoming)
 
 
 def solution(mesh):

time: 81.4 us -> 81.3 us (level)
  waiting for transfers between devices: 22 us -> 9.27 us
  Pallas kernels: 24.1 us -> 31 us
  local copies, waits for them, and re-layouts: 5.65 us -> 9.77 us
  other arithmetic: 15.9 us -> 18.1 us
  starting transfers between devices: 12.9 us -> 12 us
    ppermute x3, waiting for transfers between devices: 22 us -> 9.26 us  [shifted(): lax.ppermute(value, axis, [(source, source + steps) for source in range(i...]
    pallas_call x0 -> x1, Pallas kernels: none -> 7.36 us  [run_correct(): pl.pallas_call(functools.partial(correct_kernel, head_width), grid=(tiles...]
    convert_element_type x2, other arithmetic: 8.17 us -> 11.5 us  [convolve(): return jax.nn.silu(summed).astype(jnp.bfloat16)]
    reshape x0 -> x2, local copies, waits for them, and re-layouts: none -> 2 us  [run_correct(): l_tiles = jnp.transpose(l_t.reshape(rows, tiles, heads_per), (1, 0, 2))]
    convert_element_type x3 -> x2, other arithmetic: 3.25 us -> 1.47 us  [relay(): (total_decay * incoming.astype(jnp.float32) + local_end).astype(jnp.bfloa...]
    unnamed x10 -> x16, local copies, waits for them, and re-layouts: 0.02 us -> 1.49 us
    ppermute x3, starting transfers between devices: 12.9 us -> 11.9 us  [shifted(): lax.ppermute(value, axis, [(source, source + steps) for source in range(i...]
  transfers between devices with their start and end apart: 4 -> 4, of which waited for: 2 -> 1; matrix products, arithmetic and copies ran while one was open for 15% -> 24% of each run, Pallas kernels for 0% -> 17%
where the time goes in v6:
time: 81.3 us; the launch traced here: 80.4 us
  Pallas kernels  31 us (38%)
  other arithmetic  18.1 us (22%)
  starting transfers between devices  12 us (15%)
  local copies, waits for them, and re-layouts  9.77 us (12%)
  waiting for transfers between devices  9.27 us (11%)
    pallas_call x1, Pallas kernels, run_blocks(): pl.pallas_call(kernel, grid=(block_count,), in_specs=[row_block(width), r...  13.8 us
    ppermute x3, starting transfers between devices, shifted(): lax.ppermute(value, axis, [(source, source + steps) for source in range(i...  11.9 us
    convert_element_type x2, other arithmetic, convolve(): return jax.nn.silu(summed).astype(jnp.bfloat16)  11.5 us
    pallas_call x1, Pallas kernels, run_state(): pl.pallas_call(functools.partial(state_kernel, width // head_count), grid...  9.86 us
    ppermute x3, waiting for transfers between devices, shifted(): lax.ppermute(value, axis, [(source, source + steps) for source in range(i...  9.26 us
    pallas_call x1, Pallas kernels, run_correct(): pl.pallas_call(functools.partial(correct_kernel, head_width), grid=(tiles...  7.36 us
    reshape x2, local copies, waits for them, and re-layouts, run_correct(): l_tiles = jnp.transpose(l_t.reshape(rows, tiles, heads_per), (1, 0, 2))  2 us
  transfers between devices with their start and end apart: 4, of which 1 were waited for; matrix products, arithmetic and copies ran while one was open for 24% of the time, Pallas kernels for 17%

profile of v6, /device:TPU:0, one launch (start us, length us, event | category | flops | bytes accessed | tf_op | source)
XLA Modules:
  0.0 80.4 jit_solution(14169507441169416950)
XLA Ops:
  0.0 0.7 slice.111
  0.7 0.7 slice_bitcast_fusion.4
  1.4 4.9 %collective-permute-start = (bf16[3,1280]{1,0:T(4,128)(2,1)S(1)}, bf16[3,1280]{1,0:T(4,128)(2,1)S(1)}, u32[]{:S(2)}, u32[]{:S(2)}) collective-permute-start(bf16[3,1280]{1,0:T(4,128)(2,1)S(1)} %pad_maximum_fusion.2), channel_id=1, source_target_pairs={{0,4},{4,8},{8,12},{1,5},{5,9},{9,13},{2,6},{6,10},{10,14},{3,7},{... | collective-permute-start | bytes 23048 | tf_op jit(solution)/shard_map/ppermute | solution.py:16
  6.4 0.8 %reduce-window.9 = s32[3,1]{0,1:T(1,128)S(1)} reduce-window(s32[3,1]{0,1:T(1,128)} %bitcast.54, s32[]{:T(128)} %constant.34.clone.1), window={size=3x1 pad=2_0x0_0}, to_apply=%region_0.0 | reduce-window | flops 6 | bytes 28 | tf_op jit(solution)/shard_map/reduce-window.4
  7.2 0.7 bitcast_subtract_fusion
  7.9 0.1 convert_reduce_fusion
  8.0 0.1 slice_bitcast_fusion.2
  8.0 0.0 copy-start.5
  8.0 0.1 slice_reduce_fusion
  8.2 0.1 fusion.4
  8.2 0.8 %slice_convert_fusion.7 = (f32[1,2,128]{2,0,1:T(1,128)S(1)}, f32[1,2,128]{2,0,1:T(1,128)S(1)}, f32[1,2,128]{2,0,1:T(1,128)S(1)}, f32[1,2,128]{2,0,1:T(1,128)S(1)}) fusion(bf16[4,2,128]{2,0,1:T(4,128)(2,1)} %bitcast.48), kind=kLoop, calls=%fused_computation.53 | loop fusion | flops 1024 | bytes 6144 | tf_op jit(solution)/shard_map/convert_element_type | solution.py:43
  9.1 0.9 %slice_convert_fusion.3 = (f32[1,1024]{1,0:T(1,128)S(1)}, f32[1,1024]{1,0:T(1,128)S(1)}, f32[1,1024]{1,0:T(1,128)S(1)}, f32[1,1024]{1,0:T(1,128)S(1)}) fusion(bf16[4,1024]{1,0:T(4,128)(2,1)} %param.12), kind=kLoop, calls=%fused_computation.41 | loop fusion | flops 4096 | bytes 24576 | tf_op jit(solution)/shard_map/mul | solution.py:43
  10.0 1.1 %copy.26.entry_ref.refs_7_ = f32[1024,1]{1,0:T(8,128)} copy(f32[1024,1]{0,1:T(1,128)S(1)} %bitcast.43) | data formatting | bytes 8192 | tf_op jit(solution)/shard_map/convert_element_type | solution.py:302
  11.0 1.0 %copy.25.segc_ref.refs_6_ = s32[1024,1]{1,0:T(8,128)} copy(s32[1024,1]{0,1:T(1,128)S(1)} %bitcast.39) | data formatting | bytes 8192 | tf_op jit(solution)/shard_map/reshape | solution.py:301
  12.0 0.7 broadcast_in_dim.7
  12.8 0.7 reshape_reshape.3.refs_9_
  13.4 0.0 collective-permute-done
  13.4 2.6 %multiply_convert_fusion.1 = bf16[2,1024,128]{2,1,0:T(8,128)(2,1)S(1)} fusion(bf16[2,1024,128]{2,1,0:T(8,128)(2,1)} %param.11, bf16[2,3,128]{2,1,0:T(4,128)(2,1)S(1)} %slice_bitcast_fusion.3, f32[2,128]{1,0:T(2,128)S(1)} %bitcast.50, f32[1024]{0:T(1024)S(1)} %get-tuple-element.24, f32[2,128]{1,0:T(2,128)S(1)} %bitcast.51, f32[1024]{0:T(1024)S(1)} %get-tuple-element.25, ...), kind=kLoop, calls=%fused_computation.9 | loop fusion | flops 7602176 | bytes 1067520 | tf_op jit(solution)/shard_map/convert_element_type | solution.py:44
  16.0 0.1 collective-permute-start.1
  16.1 8.9 %multiply_convert_fusion.x_ref.refs_0_ = bf16[1024,1024]{1,0:T(8,128)(2,1)} fusion(bf16[1024,1024]{1,0:T(8,128)(2,1)} %param.10, bf16[3,1024]{1,0:T(4,128)(2,1)S(1)} %slice.142, f32[1024]{0:T(1024)S(1)} %bitcast.46, f32[1024]{0:T(1024)S(1)} %get-tuple-element.24, f32[1024]{0:T(1024)S(1)} %bitcast.47, f32[1024]{0:T(1024)S(1)} %get-tuple-element.25, ...), kind=kLoop, calls=%fused_computation | loop fusion | flops 30408704 | bytes 4233216 | tf_op jit(solution)/shard_map/convert_element_type | solution.py:44
  25.0 0.0 collective-permute-done.1
  25.0 0.4 maximum_select_fusion
  25.4 0.0 copy-done.5
  25.4 1.0 %slice_bitcast_fusion = (bf16[1024,256]{1,0:T(8,128)(2,1)}, bf16[1024,256]{1,0:T(8,128)(2,1)}) fusion(bf16[2,1024,256]{2,1,0:T(8,128)(2,1)S(1)} %maximum_select_fusion), kind=kLoop, calls=%fused_computation.14 | loop fusion | bytes 2097152 | tf_op jit(solution)/shard_map/squeeze | solution.py:294
  26.5 9.9 %shard_map.100 = (f32[256,1024]{1,0:T(8,128)}, f32[1024,16]{1,0:T(8,128)}, f32[1024,16]{1,0:T(8,128)}, f32[8,1,1024]{2,1,0:T(1,128)}, f32[1,1024]{1,0:T(1,128)}) custom-call(bf16[1024,1024]{1,0:T(8,128)(2,1)} %multiply_convert_fusion.x_ref.refs_0_, bf16[1024,256]{1,0:T(8,128)(2,1)} %get-tuple-element.22.b_ref.refs_1_, f32[16,1024]{1,0:T(8,128)} %dt_ref.1, ...), custom_call_target="tpu_custom_call" | custom-call | tf_op jit(solution)/shard_map/pallas_call | solution.py:161
  36.3 0.7 broadcast_multiply_fusion
  37.0 1.3 %add_convert_fusion.1 = bf16[256,1024]{1,0:T(8,128)(2,1)S(1)} fusion(f32[256,1024]{1,0:T(8,128)} %get-tuple-element.13, f32[1024]{0:T(1024)S(1)} %broadcast_multiply_fusion), kind=kLoop, calls=%fused_computation.8 | loop fusion | flops 524288 | bytes 1576960 | tf_op jit(solution)/shard_map/convert_element_type | solution.py:317
  38.3 3.5 %collective-permute-start.2 = (bf16[256,1024]{1,0:T(8,128)(2,1)S(1)}, bf16[256,1024]{1,0:T(8,128)(2,1)S(1)}, u32[]{:S(2)}, u32[]{:S(2)}) collective-permute-start(bf16[256,1024]{1,0:T(8,128)(2,1)S(1)} %add_convert_fusion.1), channel_id=1, source_target_pairs={{0,4},{4,8},{8,12},{1,5},{5,9},{9,13},{2,6},{6,10},{10,14},{3,7},{... | collective-permute-start | bytes 1572872 | tf_op jit(solution)/shard_map/ppermute | solution.py:16
  41.8 0.7 constant_dynamic-update-slice_fusion.6
  42.5 0.7 constant_dynamic-update-slice_fusion.5
  43.2 0.0 copy-start.3
  43.2 0.0 copy-start.6
  43.2 0.0 copy-start.1
  43.3 13.8 %shard_map.101.y_ref = f32[1024,1024]{1,0:T(8,128)} custom-call(bf16[1024,1024]{1,0:T(8,128)(2,1)} %multiply_convert_fusion.x_ref.refs_0_, bf16[1024,256]{1,0:T(8,128)(2,1)} %get-tuple-element.22.b_ref.refs_1_, bf16[1024,256]{1,0:T(8,128)(2,1)} %get-tuple-element.21.refs_2_.c_ref, f32[1024,16]{1,0:T(8,128)} %get-tuple-element.14.refs_3_, ...), custom_call_target="tpu_custom_call" | custom-call | tf_op jit(solution)/shard_map/pallas_call | solution.py:227
  57.1 0.0 copy-done.3
  57.1 0.0 collective-permute-done.2
  57.1 0.0 copy-done
  57.1 0.0 copy-done.6
  57.1 0.2 add_convert_fusion
  57.3 3.5 %collective-permute-start.3 = (bf16[256,1024]{1,0:T(8,128)(2,1)S(1)}, bf16[256,1024]{1,0:T(8,128)(2,1)S(1)}, u32[]{:S(2)}, u32[]{:S(2)}) collective-permute-start(bf16[256,1024]{1,0:T(8,128)(2,1)S(1)} %add_convert_fusion), channel_id=1, source_target_pairs={{0,4},{4,8},{8,12},{1,5},{5,9},{9,13},{2,6},{6,10},{10,14},{3,7},{... | collective-permute-start | bytes 1572872 | tf_op jit(solution)/shard_map/ppermute | solution.py:16
  60.8 0.0 copy-done.1
  60.8 0.2 copy.29
  61.0 2.0 %copy.30 = f32[1024,4,4]{2,0,1:T(8,128)} copy(f32[1024,4,4]{0,2,1:T(4,128)S(1)} %reshape.123) | data formatting | bytes 131072 | tf_op jit(solution)/shard_map/reshape | solution.py:195
  63.0 0.0 copy-start.4
  63.0 9.3 %collective-permute-done.3.ein_ref = bf16[256,1024]{1,0:T(8,128)(2,1)S(1)} collective-permute-done((bf16[256,1024]{1,0:T(8,128)(2,1)S(1)}, bf16[256,1024]{1,0:T(8,128)(2,1)S(1)}, u32[]{:S(2)}, u32[]{:S(2)}) %collective-permute-start.3) | collective-permute-done | bytes 524320 | tf_op jit(solution)/shard_map/ppermute | solution.py:16
  72.3 0.0 copy-done.4
  72.3 0.8 copy-done.2
  73.1 7.4 %shard_map.102 = bf16[1024,1024]{1,0:T(8,128)(2,1)} custom-call(f32[1024,1024]{1,0:T(8,128)} %shard_map.101.y_ref, bf16[1024,256]{1,0:T(8,128)(2,1)} %get-tuple-element.21.refs_2_.c_ref, f32[4,1024,4]{2,1,0:T(8,128)} %bitcast.38, f32[1024,1]{1,0:T(8,128)} %copy.26.entry_ref.refs_7_, f32[8,1,1024]{2,1,0:T(1,128)} %copy-done.4, bf16[256,1024]{1,0:T(8,128)(2,1)} %copy-done.2), custom_call_target="tpu_custom_call" | custom-call | tf_op jit(solution)/shard_map/pallas_call | solution.py:197
  (14 shorter events, 0.1 us)
Async XLA Ops:
  1.4 12.0 %collective-permute-start = (bf16[3,1280]{1,0:T(4,128)(2,1)S(1)}, bf16[3,1280]{1,0:T(4,128)(2,1)S(1)}, u32[]{:S(2)}, u32[]{:S(2)}) collective-permute-start(bf16[3,1280]{1,0:T(4,128)(2,1)S(1)} %pad_maximum_fusion.2), channel_id=1, source_target_pairs={{0,4},{4,8},{8,12},{1,5},{5,9},{9,13},{2,6},{6,10},{10,14},{3,7},{... | collective-permute-start | bytes 23048 | tf_op jit(solution)/shard_map/ppermute | solution.py:16
  8.0 17.4 %copy-start.5 = (s32[1024]{0:T(1024)}, s32[1024]{0:T(1024)S(1)}, u32[]{:S(2)}) copy-start(s32[1024]{0:T(1024)S(1)} %get-tuple-element.28) | copy-start | bytes 12292
  16.0 9.0 %collective-permute-start.1 = (bf16[2,1024,128]{2,1,0:T(8,128)(2,1)S(1)}, bf16[2,1024,128]{2,1,0:T(8,128)(2,1)S(1)}, u32[]{:S(2)}, u32[]{:S(2)}) collective-permute-start(bf16[2,1024,128]{2,1,0:T(8,128)(2,1)S(1)} %multiply_convert_fusion.1), channel_id=1, source_target_pairs={{0,1},{1,0},{2,3},{3,2},{4,5},{5,4},{6,7},{7,6},{8,9},{9,8},{10,11... | collective-permute-start | bytes 1572872 | tf_op jit(solution)/shard_map/ppermute | solution.py:26
  38.3 18.8 %collective-permute-start.2 = (bf16[256,1024]{1,0:T(8,128)(2,1)S(1)}, bf16[256,1024]{1,0:T(8,128)(2,1)S(1)}, u32[]{:S(2)}, u32[]{:S(2)}) collective-permute-start(bf16[256,1024]{1,0:T(8,128)(2,1)S(1)} %add_convert_fusion.1), channel_id=1, source_target_pairs={{0,4},{4,8},{8,12},{1,5},{5,9},{9,13},{2,6},{6,10},{10,14},{3,7},{... | collective-permute-start | bytes 1572872 | tf_op jit(solution)/shard_map/ppermute | solution.py:16
  43.2 13.8 %copy-start.3 = (f32[8,1,1024]{2,1,0:T(1,128)S(1)}, f32[8,1,1024]{2,1,0:T(1,128)}, u32[]{:S(2)}) copy-start(f32[8,1,1024]{2,1,0:T(1,128)} %get-tuple-element.16.refs_8_) | copy-start | bytes 98308
  43.2 13.9 %copy-start = (f32[256,1024]{1,0:T(8,128)S(1)}, f32[256,1024]{1,0:T(8,128)}, u32[]{:S(2)}) copy-start(f32[256,1024]{1,0:T(8,128)} %get-tuple-element.13) | copy-start | bytes 3145732
  43.2 13.9 %copy-start.6 = (f32[1,1024]{1,0:T(1,128)S(1)}, f32[1,1024]{1,0:T(1,128)}, u32[]{:S(2)}) copy-start(f32[1,1024]{1,0:T(1,128)} %get-tuple-element.12) | copy-start | bytes 12292
  43.2 17.6 %copy-start.1 = (f32[1024,16]{1,0:T(8,128)S(1)}, f32[1024,16]{1,0:T(8,128)}, u32[]{:S(2)}) copy-start(f32[1024,16]{1,0:T(8,128)} %get-tuple-element.14.refs_3_) | copy-start | bytes 196612
  57.3 15.0 %collective-permute-start.3 = (bf16[256,1024]{1,0:T(8,128)(2,1)S(1)}, bf16[256,1024]{1,0:T(8,128)(2,1)S(1)}, u32[]{:S(2)}, u32[]{:S(2)}) collective-permute-start(bf16[256,1024]{1,0:T(8,128)(2,1)S(1)} %add_convert_fusion), channel_id=1, source_target_pairs={{0,4},{4,8},{8,12},{1,5},{5,9},{9,13},{2,6},{6,10},{10,14},{3,7},{... | collective-permute-start | bytes 1572872 | tf_op jit(solution)/shard_map/ppermute | solution.py:16
  63.0 9.3 %copy-start.4 = (f32[8,1,1024]{2,1,0:T(1,128)}, f32[8,1,1024]{2,1,0:T(1,128)S(1)}, u32[]{:S(2)}) copy-start(f32[8,1,1024]{2,1,0:T(1,128)S(1)} %constant_dynamic-update-slice_fusion.prefix_ref) | copy-start | bytes 98308
  72.3 0.8 copy-start.2

commit v7 on v5

--- a/solution.py
+++ b/solution.py
@@ -68,7 +68,7 @@
 
 def block_kernel(with_y, head_width, *refs):
     if with_y:
-        (x_ref, b_ref, c_ref, l_ref, dt_ref, segr_ref, segc_ref, entry_ref, decay_ref,
+        (x_ref, b_ref, c_ref, l_ref, dt_ref, segr_ref, info_ref, decay_ref,
          skip_ref, ein_ref, out_ref, state_ref) = refs
     else:
         (x_ref, b_ref, l_ref, dt_ref, segc_ref, decay_ref, state_ref) = refs
@@ -81,7 +81,8 @@
         else:
             state_ref[...] = jnp.zeros(state_ref.shape, jnp.float32)
 
-    seg_col = segc_ref[...]
+    info = info_ref[...]
+    seg_col = info[:, 0:1]
     end_col = (seg_col == seg_col[BLOCK - 1 : BLOCK, :]).astype(jnp.float32)
     l_small = l_ref[...]
     dt_small = dt_ref[...]
@@ -100,7 +101,7 @@
         rising = expand_heads(jnp.exp(l_small), head_width)
         falling = expand_heads(jnp.exp(-l_small) * dt_small, head_width)
         intra = split_dot(masked, x * falling) * rising
-        inter = split_dot(c_mat, state) * (rising * entry_ref[...])
+        inter = split_dot(c_mat, state) * (rising * info[:, 1:2])
         out_ref[...] = (intra + inter + skip_ref[...] * x).astype(jnp.bfloat16)
     ending = expand_heads(
         jnp.exp(l_small[BLOCK - 1 : BLOCK, :] - l_small) * dt_small * end_col, head_width
@@ -111,14 +112,33 @@
     )
 
 
-def state_kernel(head_width, x_ref, b_ref, dt_ref, rate_ref, segc_ref, entry_ref, state_ref, l_ref,
-                 dtt_ref, decay_ref, total_ref):
+def state_kernel(head_width, x_ref, tail_ref, wconv_ref, bias_ref, b_ref, dt_ref, rate_ref,
+                 info_ref, state_ref, l_ref, dtt_ref, decay_ref, total_ref, xc_ref, prev_ref):
     blk = pl.program_id(0)
 
     @pl.when(blk == 0)
     def _():
         state_ref[...] = jnp.zeros(state_ref.shape, jnp.float32)
         total_ref[...] = jnp.ones(total_ref.shape, jnp.float32)
+        prev_ref[...] = tail_ref[...].astype(jnp.float32)
+
+    info = info_ref[...]
+    raw = x_ref[...].astype(jnp.float32)
+    prev = prev_ref[...]
+    top_row = lax.broadcasted_iota(jnp.int32, prev.shape, 0)
+    summed = jnp.zeros(raw.shape, jnp.float32) + bias_ref[...]
+    for offset in range(4):
+        back = 3 - offset
+        if back == 0:
+            window = raw
+        else:
+            rolled = pltpu.roll(raw, back, 0)
+            top = jnp.where(top_row < back, pltpu.roll(prev, back, 0), rolled[:8])
+            window = jnp.concatenate([top, rolled[8:]], 0) * info[:, 1 + back : 2 + back]
+        summed = summed + wconv_ref[offset : offset + 1, :] * window
+    prev_ref[...] = raw[BLOCK - 8 :]
+    xc = jax.nn.silu(summed).astype(jnp.bfloat16)
+    xc_ref[...] = xc
 
     rows = lax.broadcasted_iota(jnp.int32, (2 * BLOCK, BLOCK), 0)
     cols = lax.broadcasted_iota(jnp.int32, (2 * BLOCK, BLOCK), 1)
@@ -126,35 +146,35 @@
         ((rows < BLOCK) & (rows >= cols)) | (rows - BLOCK == cols), 1.0, 0.0
     ).astype(jnp.bfloat16)
     rest = dt_ref[...]
-    summed = None
+    cum = None
     for _ in range(3):
         piece = rest.astype(jnp.bfloat16)
         part = lax.dot_general(
             picker, piece, (((1,), (1,)), ((), ())), preferred_element_type=jnp.float32
         )
-        summed = part if summed is None else summed + part
+        cum = part if cum is None else cum + part
         rest = rest - piece.astype(jnp.float32)
-    l_small = -summed[:BLOCK] * rate_ref[...]
-    dt_small = summed[BLOCK:]
+    l_small = -cum[:BLOCK] * rate_ref[...]
+    dt_small = cum[BLOCK:]
     l_ref[...] = l_small
     dtt_ref[...] = dt_small
-    seg_col = segc_ref[...]
+    seg_col = info[:, 0:1]
     end_col = (seg_col == seg_col[BLOCK - 1 : BLOCK, :]).astype(jnp.float32)
     decay_x = expand_heads(
-        jnp.exp(l_small[BLOCK - 1 : BLOCK, :]) * entry_ref[BLOCK - 1 : BLOCK, :], head_width
+        jnp.exp(l_small[BLOCK - 1 : BLOCK, :]) * info[BLOCK - 1 : BLOCK, 1:2], head_width
     )
     decay_ref[0] = decay_x
     total_ref[...] = total_ref[...] * decay_x
     ending = expand_heads(
         jnp.exp(l_small[BLOCK - 1 : BLOCK, :] - l_small) * dt_small * end_col, head_width
     )
-    weighted = (x_ref[...].astype(jnp.float32) * ending).astype(jnp.bfloat16)
+    weighted = (xc.astype(jnp.float32) * ending).astype(jnp.bfloat16)
     state_ref[...] = decay_x * state_ref[...] + lax.dot_general(
         b_ref[...], weighted, (((0,), (0,)), ((), ())), preferred_element_type=jnp.float32
     )
 
 
-def run_state(x, b_full, step_size, rate_row, seg_col, entry_col):
+def run_state(x, tail8, wconv, bias_row, b_full, step_size, rate_row, info):
     rows, width = x.shape
     head_count = step_size.shape[0]
     n_size = b_full.shape[1]
@@ -164,18 +184,21 @@
     return pl.pallas_call(
         functools.partial(state_kernel, width // head_count),
         grid=(block_count,),
-        in_specs=[row_block(width), row_block(n_size),
-                  pl.BlockSpec((head_count, BLOCK), lambda b: (0, b)), whole((1, head_count)),
-                  row_block(1), row_block(1)],
+        in_specs=[row_block(width), whole((8, width)), whole((4, width)), whole((1, width)),
+                  row_block(n_size), pl.BlockSpec((head_count, BLOCK), lambda b: (0, b)),
+                  whole((1, head_count)), row_block(info.shape[1])],
         out_specs=[whole((n_size, width)), row_block(head_count), row_block(head_count),
-                   pl.BlockSpec((1, 1, width), lambda b: (b, 0, 0)), whole((1, width))],
+                   pl.BlockSpec((1, 1, width), lambda b: (b, 0, 0)), whole((1, width)),
+                   row_block(width)],
         out_shape=[jax.ShapeDtypeStruct((n_size, width), jnp.float32),
                    jax.ShapeDtypeStruct((rows, head_count), jnp.float32),
                    jax.ShapeDtypeStruct((rows, head_count), jnp.float32),
                    jax.ShapeDtypeStruct((block_count, 1, width), jnp.float32),
-                   jax.ShapeDtypeStruct((1, width), jnp.float32)],
+                   jax.ShapeDtypeStruct((1, width), jnp.float32),
+                   jax.ShapeDtypeStruct((rows, width), jnp.bfloat16)],
+        scratch_shapes=[pltpu.VMEM((8, width), jnp.float32)],
         compiler_params=pltpu.CompilerParams(dimension_semantics=("arbitrary",)),
-    )(x, b_full, step_size, rate_row, seg_col, entry_col)
+    )(x, tail8, wconv, bias_row, b_full, step_size, rate_row, info)
 
 
 def run_blocks(with_y, x, b_full, c_full, l_t, dt_t, seg_row, seg_col, entry_col, decay_x,
@@ -198,14 +221,13 @@
             grid=(block_count,),
             in_specs=[row_block(width), row_block(n_size), row_block(n_size),
                       row_block(head_count), row_block(head_count),
-                      pl.BlockSpec((1, BLOCK), lambda b: (0, b)), row_block(1), row_block(1),
+                      pl.BlockSpec((1, BLOCK), lambda b: (0, b)), row_block(seg_col.shape[1]),
                       decay_spec, pl.BlockSpec((1, width), lambda b: (0, 0)), state_spec],
             out_specs=row_block(width),
             out_shape=jax.ShapeDtypeStruct((rows, width), jnp.bfloat16),
             scratch_shapes=[pltpu.VMEM((n_size, width), jnp.float32)],
             compiler_params=params,
-        )(x, b_full, c_full, l_t, dt_t, seg_row, seg_col, entry_col, decay_x, skip_x,
-          entering)
+        )(x, b_full, c_full, l_t, dt_t, seg_row, seg_col, decay_x, skip_x, entering)
     return pl.pallas_call(
         kernel,
         grid=(block_count,),
@@ -251,9 +273,6 @@
         own_rows,
     )
     partner = from_partner(state_half, "head", 0)
-    inner_conv = convolve(
-        jnp.concatenate([inner_tail, inner_input], 0), conv_inner, bias_inner, seg_ext, own_rows
-    )
     lower_half = lax.axis_index("head") % 2 == 0
     state_full = jnp.where(
         lower_half,
@@ -267,12 +286,21 @@
     skip_x = spread(skip_gain).reshape(1, -1)
     seg_own = seg_ext[3:].reshape(block_count, BLOCK)
     seg_prev = seg_ext[2 : 2 + own_rows].reshape(block_count, BLOCK)[:, 0]
-    seg_row = seg_ext[3:].reshape(1, own_rows)
-    seg_col = seg_ext[3:].reshape(own_rows, 1)
-    entry_col = (seg_own == seg_prev[:, None]).astype(jnp.float32).reshape(own_rows, 1)
-
-    local_end, l_t, dt_t, decay_x, total_decay = run_state(
-        inner_conv, b_full, step_size, decay_rate.reshape(1, -1), seg_col, entry_col
+    seg_row = seg_ext[3:].reshape(1, own_rows).astype(jnp.float32)
+    own_seg = seg_ext[3:]
+    entry_col = (seg_own == seg_prev[:, None]).reshape(own_rows)
+    keeps = [(seg_ext[3 - back : 3 - back + own_rows] == own_seg) for back in (1, 2, 3)]
+    info = jnp.stack(
+        [own_seg.astype(jnp.float32), entry_col.astype(jnp.float32)]
+        + [keep.astype(jnp.float32) for keep in keeps]
+        + [jnp.zeros((own_rows,), jnp.float32)] * 3,
+        1,
+    )
+    tail8 = jnp.concatenate([jnp.zeros((5, inner_tail.shape[1]), inner_tail.dtype), inner_tail], 0)
+
+    local_end, l_t, dt_t, decay_x, total_decay, inner_conv = run_state(
+        inner_input, tail8, conv_inner.astype(jnp.float32), bias_inner.reshape(1, -1), b_full,
+        step_size, decay_rate.reshape(1, -1), info
     )
 
     def relay(step_num, incoming):
@@ -286,8 +314,8 @@
     for step_num in range(hops):
         incoming = relay(step_num, incoming)
     return run_blocks(
-        True, inner_conv, b_full, c_full, l_t, dt_t, seg_row, seg_col, entry_col, decay_x,
-        skip_x, incoming
+        True, inner_conv, b_full, c_full, l_t, dt_t, seg_row, info, None, decay_x, skip_x,
+        incoming
     )
 
 

time: 81.4 us -> 75.9 us (0.932)
  other arithmetic: 15.9 us -> 10.9 us
    convert_element_type x2 -> x1, other arithmetic: 8.17 us -> 2.63 us  [convolve(): return jax.nn.silu(summed).astype(jnp.bfloat16)]
    convert_element_type x1, other arithmetic: 0.08 us -> 1.3 us  [body(): conv_inner.astype(jnp.float32)]
    reshape x2 -> x0, local copies, waits for them, and re-layouts: 1.11 us -> none  [the longest x1 1.03 us: body(): seg_col = seg_ext[3:].reshape(own_rows, 1)]
    another operation x0 -> x4, local copies, waits for them, and re-layouts: none -> 1.06 us  [body(): jnp.stack([own_seg.astype(jnp.float32), entry_col.astype(jnp.float32)] +...]
    convert_element_type x1 -> x0, local copies, waits for them, and re-layouts: 1.03 us -> none  [body(): (seg_own == seg_prev[:, None]).astype(jnp.float32).reshape(own_rows, 1)]
    mul x1 -> x0, other arithmetic: 0.86 us -> none  [convolve(): summed = summed + weight[offset].astype(jnp.float32) * window * kept_mask]
  transfers between devices with their start and end apart: 4 -> 4, of which waited for: 2 -> 2; matrix products, arithmetic and copies ran while one was open for 15% -> 9% of each run, Pallas kernels for 0% -> 0%
where the time goes in v7:
time: 75.9 us; the launch traced here: 75.3 us
  Pallas kernels  24.3 us (32%)
  waiting for transfers between devices  22 us (29%)
  starting transfers between devices  12.9 us (17%)
  other arithmetic  10.9 us (14%)
  local copies, waits for them, and re-layouts  5.01 us (7%)
    ppermute x3, waiting for transfers between devices, shifted(): lax.ppermute(value, axis, [(source, source + steps) for source in range(i...  22 us
    pallas_call x1, Pallas kernels, run_blocks(): pl.pallas_call(kernel, grid=(block_count,), in_specs=[row_block(width), r...  14.2 us
    ppermute x3, starting transfers between devices, shifted(): lax.ppermute(value, axis, [(source, source + steps) for source in range(i...  12.9 us
    pallas_call x1, Pallas kernels, run_state(): pl.pallas_call(functools.partial(state_kernel, width // head_count), grid...  10.1 us
    convert_element_type x1, other arithmetic, convolve(): return jax.nn.silu(summed).astype(jnp.bfloat16)  2.63 us
    convert_element_type x2, other arithmetic, relay(): (total_decay * incoming + local_end).astype(jnp.bfloat16)  2.15 us
  transfers between devices with their start and end apart: 4, of which 2 were waited for; matrix products, arithmetic and copies ran while one was open for 9% of the time, Pallas kernels for 0%

profile of v7, /device:TPU:0, one launch (start us, length us, event | category | flops | bytes accessed | tf_op | source)
XLA Modules:
  0.0 75.3 jit_solution(17586209358103794317)
XLA Ops:
  0.0 0.7 slice_bitcast_fusion.4
  0.7 0.7 slice.66
  1.4 4.9 %collective-permute-start = (bf16[3,1280]{1,0:T(4,128)(2,1)S(1)}, bf16[3,1280]{1,0:T(4,128)(2,1)S(1)}, u32[]{:S(2)}, u32[]{:S(2)}) collective-permute-start(bf16[3,1280]{1,0:T(4,128)(2,1)S(1)} %pad_maximum_fusion.1), channel_id=1, source_target_pairs={{0,4},{4,8},{8,12},{1,5},{5,9},{9,13},{2,6},{6,10},{10,14},{3,7},{... | collective-permute-start | bytes 23048 | tf_op jit(solution)/shard_map/ppermute | solution.py:16
  6.4 0.8 %reduce-window.9 = s32[3,1]{0,1:T(1,128)S(1)} reduce-window(s32[3,1]{0,1:T(1,128)} %bitcast.50, s32[]{:T(128)} %constant.34.clone.1), window={size=3x1 pad=2_0x0_0}, to_apply=%region_0.0 | reduce-window | flops 6 | bytes 28 | tf_op jit(solution)/shard_map/reduce-window.4
  7.2 0.7 bitcast_subtract_fusion
  7.9 0.1 convert_reduce_fusion
  8.0 0.1 slice_bitcast_fusion.2
  8.0 0.0 copy-start.1
  8.0 0.1 slice_reduce_fusion
  8.2 0.1 fusion.2
  8.2 0.8 %slice_convert_fusion.4 = (f32[1,2,128]{2,0,1:T(1,128)S(1)}, f32[1,2,128]{2,0,1:T(1,128)S(1)}, f32[1,2,128]{2,0,1:T(1,128)S(1)}, f32[1,2,128]{2,0,1:T(1,128)S(1)}) fusion(bf16[4,2,128]{2,0,1:T(4,128)(2,1)} %bitcast.43), kind=kLoop, calls=%fused_computation.31 | loop fusion | flops 1024 | bytes 6144 | tf_op jit(solution)/shard_map/convert_element_type | solution.py:43
  9.1 0.0 collective-permute-done
  9.1 2.6 %multiply_convert_fusion = bf16[2,1024,128]{2,1,0:T(8,128)(2,1)S(1)} fusion(bf16[2,1024,128]{2,1,0:T(8,128)(2,1)} %param.11, bf16[2,3,128]{2,1,0:T(4,128)(2,1)S(1)} %slice_bitcast_fusion.3, f32[2,128]{1,0:T(2,128)S(1)} %bitcast.46, f32[1024]{0:T(1024)S(1)} %get-tuple-element.20, f32[2,128]{1,0:T(2,128)S(1)} %bitcast.47, f32[1024]{0:T(1024)S(1)} %get-tuple-element.21, ...), kind=kLoop, calls=%fused_computation.3 | loop fusion | flops 7602176 | bytes 1067520 | tf_op jit(solution)/shard_map/convert_element_type | solution.py:44
  11.7 0.1 collective-permute-start.1
  11.8 1.3 %convert_element_type.99.wconv_ref = f32[4,1024]{1,0:T(4,128)} convert(bf16[4,1024]{1,0:T(4,128)(2,1)} %param.12) | non-fusion elementwise | flops 4096 | bytes 24576 | tf_op jit(solution)/shard_map/convert_element_type | solution.py:302
  13.1 0.1 stack.31
  13.2 1.0 %copy.23.info_ref.refs_6_ = f32[1024,8]{1,0:T(8,128)} copy(f32[1024,8]{0,1:T(8,128)S(1)} %stack.31) | data formatting | bytes 65536 | tf_op jit(solution)/shard_map/stack | solution.py:293
  14.2 0.6 concatenate.16.tail_ref
  14.8 0.0 collective-permute-done.1
  14.8 0.4 maximum_select_fusion
  15.2 1.0 %slice_bitcast_fusion = (bf16[1024,256]{1,0:T(8,128)(2,1)}, bf16[1024,256]{1,0:T(8,128)(2,1)}) fusion(bf16[2,1024,256]{2,1,0:T(8,128)(2,1)S(1)} %maximum_select_fusion), kind=kLoop, calls=%fused_computation.8 | loop fusion | bytes 2097152 | tf_op jit(solution)/shard_map/squeeze | solution.py:283
  16.2 0.0 copy-done.1
  16.2 10.1 %shard_map.100 = (f32[256,1024]{1,0:T(8,128)}, f32[1024,16]{1,0:T(8,128)}, f32[1024,16]{1,0:T(8,128)}, f32[8,1,1024]{2,1,0:T(1,128)}, f32[1,1024]{1,0:T(1,128)}, /*index=5*/bf16[1024,1024]{1,0:T(8,128)(2,1)}) custom-call(bf16[1024,1024]{1,0:T(8,128)(2,1)} %x_ref.1, bf16[8,1024]{1,0:T(8,128)(2,1)} %concatenate.16.tail_ref, ...), custom_call_target="tpu_custom_call" | custom-call | tf_op jit(solution)/shard_map/pallas_call | solution.py:184
  26.3 0.0 copy-start
  26.3 0.0 copy-start.2
  26.3 0.8 %broadcast_multiply_fusion = f32[1024]{0:T(1024)S(1)} fusion(f32[1024]{0:T(1024)} %bitcast.40), kind=kLoop, calls=%fused_computation.26 | loop fusion | flops 1024 | bytes 8192 | tf_op jit(solution)/shard_map/mul | solution.py:307
  27.1 1.3 %add_convert_fusion.1 = bf16[256,1024]{1,0:T(8,128)(2,1)S(1)} fusion(f32[256,1024]{1,0:T(8,128)} %get-tuple-element.16, f32[1024]{0:T(1024)S(1)} %broadcast_multiply_fusion), kind=kLoop, calls=%fused_computation.2 | loop fusion | flops 524288 | bytes 1576960 | tf_op jit(solution)/shard_map/convert_element_type | solution.py:307
  28.4 3.5 %collective-permute-start.2 = (bf16[256,1024]{1,0:T(8,128)(2,1)S(1)}, bf16[256,1024]{1,0:T(8,128)(2,1)S(1)}, u32[]{:S(2)}, u32[]{:S(2)}) collective-permute-start(bf16[256,1024]{1,0:T(8,128)(2,1)S(1)} %add_convert_fusion.1), channel_id=1, source_target_pairs={{0,4},{4,8},{8,12},{1,5},{5,9},{9,13},{2,6},{6,10},{10,14},{3,7},{... | collective-permute-start | bytes 1572872 | tf_op jit(solution)/shard_map/ppermute | solution.py:16
  31.9 11.8 %collective-permute-done.2 = bf16[256,1024]{1,0:T(8,128)(2,1)S(1)} collective-permute-done((bf16[256,1024]{1,0:T(8,128)(2,1)S(1)}, bf16[256,1024]{1,0:T(8,128)(2,1)S(1)}, u32[]{:S(2)}, u32[]{:S(2)}) %collective-permute-start.2) | collective-permute-done | bytes 524320 | tf_op jit(solution)/shard_map/ppermute | solution.py:16
  43.7 0.0 copy-done
  43.7 0.8 %add_convert_fusion = bf16[256,1024]{1,0:T(8,128)(2,1)S(1)} fusion(f32[256,1024]{1,0:T(8,128)S(1)} %copy-done, bf16[256,1024]{1,0:T(8,128)(2,1)S(1)} %collective-permute-done.2, f32[1024]{0:T(1024)} %bitcast.41), kind=kLoop, calls=%fused_computation.1 | loop fusion | flops 1048576 | bytes 2101248 | tf_op jit(solution)/shard_map/convert_element_type | solution.py:307
  44.5 4.4 %collective-permute-start.3 = (bf16[256,1024]{1,0:T(8,128)(2,1)S(1)}, bf16[256,1024]{1,0:T(8,128)(2,1)S(1)}, u32[]{:S(2)}, u32[]{:S(2)}) collective-permute-start(bf16[256,1024]{1,0:T(8,128)(2,1)S(1)} %add_convert_fusion), channel_id=1, source_target_pairs={{0,4},{4,8},{8,12},{1,5},{5,9},{9,13},{2,6},{6,10},{10,14},{3,7},{... | collective-permute-start | bytes 1572872 | tf_op jit(solution)/shard_map/ppermute | solution.py:16
  49.0 0.0 copy-done.2
  49.0 0.1 broadcast_in_dim.4
  49.0 0.7 reshape_reshape.3.refs_8_
  49.7 10.2 %collective-permute-done.3 = bf16[256,1024]{1,0:T(8,128)(2,1)S(1)} collective-permute-done((bf16[256,1024]{1,0:T(8,128)(2,1)S(1)}, bf16[256,1024]{1,0:T(8,128)(2,1)S(1)}, u32[]{:S(2)}, u32[]{:S(2)}) %collective-permute-start.3) | collective-permute-done | bytes 524320 | tf_op jit(solution)/shard_map/ppermute | solution.py:16
  60.0 1.1 %convert_element_type.122.refs_9_ = f32[256,1024]{1,0:T(8,128)} convert(bf16[256,1024]{1,0:T(8,128)(2,1)S(1)} %collective-permute-done.3) | non-fusion elementwise | flops 262144 | bytes 1572864 | tf_op jit(solution)/shard_map/convert_element_type | solution.py:307
  61.1 14.2 %shard_map.101 = bf16[1024,1024]{1,0:T(8,128)(2,1)} custom-call(bf16[1024,1024]{1,0:T(8,128)(2,1)} %get-tuple-element.11.refs_0_, bf16[1024,256]{1,0:T(8,128)(2,1)} %get-tuple-element.18.b_ref.refs_1_, bf16[1024,256]{1,0:T(8,128)(2,1)} %get-tuple-element.17.refs_2_, f32[1024,16]{1,0:T(8,128)} %get-tuple-element.12.refs_3_, ...), custom_call_target="tpu_custom_call" | custom-call | tf_op jit(solution)/shard_map/pallas_call | solution.py:219
  (7 shorter events, 0.0 us)
Async XLA Ops:
  1.4 7.6 %collective-permute-start = (bf16[3,1280]{1,0:T(4,128)(2,1)S(1)}, bf16[3,1280]{1,0:T(4,128)(2,1)S(1)}, u32[]{:S(2)}, u32[]{:S(2)}) collective-permute-start(bf16[3,1280]{1,0:T(4,128)(2,1)S(1)} %pad_maximum_fusion.1), channel_id=1, source_target_pairs={{0,4},{4,8},{8,12},{1,5},{5,9},{9,13},{2,6},{6,10},{10,14},{3,7},{... | collective-permute-start | bytes 23048 | tf_op jit(solution)/shard_map/ppermute | solution.py:16
  8.0 8.2 %copy-start.1 = (f32[1024]{0:T(1024)}, f32[1024]{0:T(1024)S(1)}, u32[]{:S(2)}) copy-start(f32[1024]{0:T(1024)S(1)} %get-tuple-element.24) | copy-start | bytes 12292
  11.7 3.1 %collective-permute-start.1 = (bf16[2,1024,128]{2,1,0:T(8,128)(2,1)S(1)}, bf16[2,1024,128]{2,1,0:T(8,128)(2,1)S(1)}, u32[]{:S(2)}, u32[]{:S(2)}) collective-permute-start(bf16[2,1024,128]{2,1,0:T(8,128)(2,1)S(1)} %multiply_convert_fusion), channel_id=1, source_target_pairs={{0,1},{1,0},{2,3},{3,2},{4,5},{5,4},{6,7},{7,6},{8,9},{9,8},{10,11... | collective-permute-start | bytes 1572872 | tf_op jit(solution)/shard_map/ppermute | solution.py:26
  26.3 17.4 %copy-start = (f32[256,1024]{1,0:T(8,128)S(1)}, f32[256,1024]{1,0:T(8,128)}, u32[]{:S(2)}) copy-start(f32[256,1024]{1,0:T(8,128)} %get-tuple-element.16) | copy-start | bytes 3145732
  26.3 22.7 %copy-start.2 = (f32[16]{0:T(128)S(1)}, f32[16]{0:T(128)}, u32[]{:S(2)}) copy-start(f32[16]{0:T(128)} %param.18) | copy-start | bytes 196
  28.4 15.3 %collective-permute-start.2 = (bf16[256,1024]{1,0:T(8,128)(2,1)S(1)}, bf16[256,1024]{1,0:T(8,128)(2,1)S(1)}, u32[]{:S(2)}, u32[]{:S(2)}) collective-permute-start(bf16[256,1024]{1,0:T(8,128)(2,1)S(1)} %add_convert_fusion.1), channel_id=1, source_target_pairs={{0,4},{4,8},{8,12},{1,5},{5,9},{9,13},{2,6},{6,10},{10,14},{3,7},{... | collective-permute-start | bytes 1572872 | tf_op jit(solution)/shard_map/ppermute | solution.py:16
  44.5 15.4 %collective-permute-start.3 = (bf16[256,1024]{1,0:T(8,128)(2,1)S(1)}, bf16[256,1024]{1,0:T(8,128)(2,1)S(1)}, u32[]{:S(2)}, u32[]{:S(2)}) collective-permute-start(bf16[256,1024]{1,0:T(8,128)(2,1)S(1)} %add_convert_fusion), channel_id=1, source_target_pairs={{0,4},{4,8},{8,12},{1,5},{5,9},{9,13},{2,6},{6,10},{10,14},{3,7},{... | collective-permute-start | bytes 1572872 | tf_op jit(solution)/shard_map/ppermute | solution.py:16

commit v8 on v7

--- a/solution.py
+++ b/solution.py
@@ -77,7 +77,7 @@
     @pl.when(blk == 0)
     def _():
         if with_y:
-            state_ref[...] = ein_ref[...]
+            state_ref[...] = ein_ref[...].astype(jnp.float32)
         else:
             state_ref[...] = jnp.zeros(state_ref.shape, jnp.float32)
 
@@ -113,7 +113,8 @@
 
 
 def state_kernel(head_width, x_ref, tail_ref, wconv_ref, bias_ref, b_ref, dt_ref, rate_ref,
-                 info_ref, state_ref, l_ref, dtt_ref, decay_ref, total_ref, xc_ref, prev_ref):
+                 info_ref, state_ref, l_ref, dtt_ref, decay_ref, total_ref, xc_ref, sent_ref,
+                 prev_ref):
     blk = pl.program_id(0)
 
     @pl.when(blk == 0)
@@ -126,6 +127,7 @@
     raw = x_ref[...].astype(jnp.float32)
     prev = prev_ref[...]
     top_row = lax.broadcasted_iota(jnp.int32, prev.shape, 0)
+    taps = wconv_ref[...].astype(jnp.float32)
     summed = jnp.zeros(raw.shape, jnp.float32) + bias_ref[...]
     for offset in range(4):
         back = 3 - offset
@@ -135,7 +137,7 @@
             rolled = pltpu.roll(raw, back, 0)
             top = jnp.where(top_row < back, pltpu.roll(prev, back, 0), rolled[:8])
             window = jnp.concatenate([top, rolled[8:]], 0) * info[:, 1 + back : 2 + back]
-        summed = summed + wconv_ref[offset : offset + 1, :] * window
+        summed = summed + taps[offset : offset + 1, :] * window
     prev_ref[...] = raw[BLOCK - 8 :]
     xc = jax.nn.silu(summed).astype(jnp.bfloat16)
     xc_ref[...] = xc
@@ -169,9 +171,14 @@
         jnp.exp(l_small[BLOCK - 1 : BLOCK, :] - l_small) * dt_small * end_col, head_width
     )
     weighted = (xc.astype(jnp.float32) * ending).astype(jnp.bfloat16)
-    state_ref[...] = decay_x * state_ref[...] + lax.dot_general(
+    new_state = decay_x * state_ref[...] + lax.dot_general(
         b_ref[...], weighted, (((0,), (0,)), ((), ())), preferred_element_type=jnp.float32
     )
+    state_ref[...] = new_state
+
+    @pl.when(blk == pl.num_programs(0) - 1)
+    def _():
+        sent_ref[...] = new_state.astype(jnp.bfloat16)
 
 
 def run_state(x, tail8, wconv, bias_row, b_full, step_size, rate_row, info):
@@ -189,13 +196,14 @@
                   whole((1, head_count)), row_block(info.shape[1])],
         out_specs=[whole((n_size, width)), row_block(head_count), row_block(head_count),
                    pl.BlockSpec((1, 1, width), lambda b: (b, 0, 0)), whole((1, width)),
-                   row_block(width)],
+                   row_block(width), whole((n_size, width))],
         out_shape=[jax.ShapeDtypeStruct((n_size, width), jnp.float32),
                    jax.ShapeDtypeStruct((rows, head_count), jnp.float32),
                    jax.ShapeDtypeStruct((rows, head_count), jnp.float32),
                    jax.ShapeDtypeStruct((block_count, 1, width), jnp.float32),
                    jax.ShapeDtypeStruct((1, width), jnp.float32),
-                   jax.ShapeDtypeStruct((rows, width), jnp.bfloat16)],
+                   jax.ShapeDtypeStruct((rows, width), jnp.bfloat16),
+                   jax.ShapeDtypeStruct((n_size, width), jnp.bfloat16)],
         scratch_shapes=[pltpu.VMEM((8, width), jnp.float32)],
         compiler_params=pltpu.CompilerParams(dimension_semantics=("arbitrary",)),
     )(x, tail8, wconv, bias_row, b_full, step_size, rate_row, info)
@@ -259,11 +267,11 @@
     seg_ext = segment_of(lengths, positions)
     width = inner_input.shape[1]
     tails = jnp.concatenate(
-        [inner_input[-3:], jnp.transpose(state_input[:, -3:], (1, 0, 2)).reshape(3, -1)], 1
+        [inner_input[-8:], jnp.transpose(state_input[:, -8:], (1, 0, 2)).reshape(8, -1)], 1
     )
     tails = shifted(tails, "seq", 1)
-    inner_tail = tails[:, :width]
-    state_tail = jnp.transpose(tails[:, width:].reshape(3, 2, group_half), (1, 0, 2))
+    tail8 = tails[:, :width]
+    state_tail = jnp.transpose(tails[5:, width:].reshape(3, 2, group_half), (1, 0, 2))
     weight_state = jnp.swapaxes(conv_state, 0, 1)[:, :, None, :]
     state_half = convolve(
         jnp.concatenate([state_tail, state_input], 1),
@@ -296,22 +304,21 @@
         + [jnp.zeros((own_rows,), jnp.float32)] * 3,
         1,
     )
-    tail8 = jnp.concatenate([jnp.zeros((5, inner_tail.shape[1]), inner_tail.dtype), inner_tail], 0)
-
-    local_end, l_t, dt_t, decay_x, total_decay, inner_conv = run_state(
-        inner_input, tail8, conv_inner.astype(jnp.float32), bias_inner.reshape(1, -1), b_full,
+
+    local_end, l_t, dt_t, decay_x, total_decay, inner_conv, end_sent = run_state(
+        inner_input, tail8, conv_inner, bias_inner.reshape(1, -1), b_full,
         step_size, decay_rate.reshape(1, -1), info
     )
 
     def relay(step_num, incoming):
-        return shifted((total_decay * incoming + local_end).astype(jnp.bfloat16), "seq", 1).astype(
-            jnp.float32
+        return shifted(
+            (total_decay * incoming.astype(jnp.float32) + local_end).astype(jnp.bfloat16), "seq", 1
         )
 
     part_rows = own_rows * lax.axis_size("seq")
     hops = min(lax.axis_size("seq") - 1, -(-(part_rows // 2) // own_rows))
-    incoming = jnp.zeros_like(local_end)
-    for step_num in range(hops):
+    incoming = shifted(end_sent, "seq", 1)
+    for step_num in range(1, hops):
         incoming = relay(step_num, incoming)
     return run_blocks(
         True, inner_conv, b_full, c_full, l_t, dt_t, seg_row, info, None, decay_x, skip_x,

time: 75.9 us -> 73.1 us (0.963)
  other arithmetic: 10.9 us -> 6.91 us
  local copies, waits for them, and re-layouts: 5.01 us -> 5.82 us
    convert_element_type x4 -> x1, other arithmetic: 4.56 us -> 1.38 us  [relay(): (total_decay * incoming.astype(jnp.float32) + local_end).astype(jnp.bfloa...]
    unnamed x6, local copies, waits for them, and re-layouts: 0.02 us -> 0.82 us
    mul x1 -> x0, other arithmetic: 0.77 us -> none  [relay(): total_decay * incoming + local_end]
  transfers between devices with their start and end apart: 4 -> 4, of which waited for: 2 -> 3; matrix products, arithmetic and copies ran while one was open for 9% -> 7% of each run, Pallas kernels for 0% -> 0%
where the time goes in v8:
time: 73.1 us; the launch traced here: 72.6 us
  Pallas kernels  24.8 us (34%)
  waiting for transfers between devices  22.1 us (30%)
  starting transfers between devices  12.8 us (18%)
  other arithmetic  6.91 us (9%)
  local copies, waits for them, and re-layouts  5.82 us (8%)
    ppermute x3, waiting for transfers between devices, shifted(): lax.ppermute(value, axis, [(source, source + steps) for source in range(i...  21.9 us
    pallas_call x1, Pallas kernels, run_blocks(): pl.pallas_call(kernel, grid=(block_count,), in_specs=[row_block(width), r...  14 us
    ppermute x3, starting transfers between devices, shifted(): lax.ppermute(value, axis, [(source, source + steps) for source in range(i...  12.7 us
    pallas_call x1, Pallas kernels, run_state(): pl.pallas_call(functools.partial(state_kernel, width // head_count), grid...  10.8 us
    convert_element_type x1, other arithmetic, convolve(): return jax.nn.silu(summed).astype(jnp.bfloat16)  2.59 us
  transfers between devices with their start and end apart: 4, of which 3 were waited for; matrix products, arithmetic and copies ran while one was open for 7% of the time, Pallas kernels for 0%

profile of v8, /device:TPU:0, one launch (start us, length us, event | category | flops | bytes accessed | tf_op | source)
XLA Modules:
  0.0 72.6 jit_solution(17663196805714930135)
XLA Ops:
  0.0 0.7 slice_bitcast_fusion.2
  0.7 0.7 slice.66
  1.4 4.9 %collective-permute-start = (bf16[8,1280]{1,0:T(8,128)(2,1)S(1)}, bf16[8,1280]{1,0:T(8,128)(2,1)S(1)}, u32[]{:S(2)}, u32[]{:S(2)}) collective-permute-start(bf16[8,1280]{1,0:T(8,128)(2,1)S(1)} %pad_maximum_fusion.1), channel_id=1, source_target_pairs={{0,4},{4,8},{8,12},{1,5},{5,9},{9,13},{2,6},{6,10},{10,14},{3,7},{... | collective-permute-start | bytes 61448 | tf_op jit(solution)/shard_map/ppermute | solution.py:16
  6.4 0.8 %reduce-window.9 = s32[3,1]{0,1:T(1,128)S(1)} reduce-window(s32[3,1]{0,1:T(1,128)} %bitcast.49, s32[]{:T(128)} %constant.31.clone.1), window={size=3x1 pad=2_0x0_0}, to_apply=%region_0.0 | reduce-window | flops 6 | bytes 28 | tf_op jit(solution)/shard_map/reduce-window.4
  7.2 0.7 bitcast_subtract_fusion
  7.8 0.1 convert_reduce_fusion
  7.9 0.1 slice_bitcast_fusion.3
  8.0 0.0 copy-start.1
  8.0 0.1 slice_reduce_fusion
  8.1 0.1 fusion.2
  8.2 0.8 %slice_convert_fusion.4 = (f32[1,2,128]{2,0,1:T(1,128)S(1)}, f32[1,2,128]{2,0,1:T(1,128)S(1)}, f32[1,2,128]{2,0,1:T(1,128)S(1)}, f32[1,2,128]{2,0,1:T(1,128)S(1)}) fusion(bf16[4,2,128]{2,0,1:T(4,128)(2,1)} %bitcast.41), kind=kLoop, calls=%fused_computation.29 | loop fusion | flops 1024 | bytes 6144 | tf_op jit(solution)/shard_map/convert_element_type | solution.py:43
  9.1 0.0 collective-permute-done
  9.1 2.6 %multiply_convert_fusion = bf16[2,1024,128]{2,1,0:T(8,128)(2,1)S(1)} fusion(bf16[2,1024,128]{2,1,0:T(8,128)(2,1)} %param.11, bf16[2,3,128]{2,1,0:T(4,128)(2,1)S(1)} %slice_bitcast_fusion.4, f32[2,128]{1,0:T(2,128)S(1)} %bitcast.45, f32[1024]{0:T(1024)S(1)} %get-tuple-element.22, f32[2,128]{1,0:T(2,128)S(1)} %bitcast.46, f32[1024]{0:T(1024)S(1)} %get-tuple-element.23, ...), kind=kLoop, calls=%fused_computation.2 | loop fusion | flops 7602176 | bytes 1067520 | tf_op jit(solution)/shard_map/convert_element_type | solution.py:44
  11.7 0.1 collective-permute-start.1
  11.8 0.1 stack.31
  11.8 1.0 %copy.23.info_ref.refs_6_ = f32[1024,8]{1,0:T(8,128)} copy(f32[1024,8]{0,1:T(8,128)S(1)} %stack.31) | data formatting | bytes 65536 | tf_op jit(solution)/shard_map/stack | solution.py:301
  12.8 0.6 slice.84.tail_ref
  13.4 0.2 collective-permute-done.1
  13.6 0.4 maximum_select_fusion
  14.0 1.1 %slice_bitcast_fusion = (bf16[1024,256]{1,0:T(8,128)(2,1)}, bf16[1024,256]{1,0:T(8,128)(2,1)}) fusion(bf16[2,1024,256]{2,1,0:T(8,128)(2,1)S(1)} %maximum_select_fusion), kind=kLoop, calls=%fused_computation.7 | loop fusion | bytes 2097152 | tf_op jit(solution)/shard_map/squeeze | solution.py:291
  15.1 0.0 copy-done.1
  15.1 0.0 copy-start.2
  15.1 10.8 %shard_map.100 = (f32[256,1024]{1,0:T(8,128)}, f32[1024,16]{1,0:T(8,128)}, f32[1024,16]{1,0:T(8,128)}, f32[8,1,1024]{2,1,0:T(1,128)}, f32[1,1024]{1,0:T(1,128)},...) custom-call(bf16[1024,1024]{1,0:T(8,128)(2,1)} %x_ref.1, bf16[8,1024]{1,0:T(8,128)(2,1)} %slice.84.tail_ref, ...), custom_call_target="tpu_custom_call" | custom-call | tf_op jit(solution)/shard_map/pallas_call | solution.py:191
  25.9 3.5 %collective-permute-start.2 = (bf16[256,1024]{1,0:T(8,128)(2,1)}, bf16[256,1024]{1,0:T(8,128)(2,1)S(1)}, u32[]{:S(2)}, u32[]{:S(2)}) collective-permute-start(bf16[256,1024]{1,0:T(8,128)(2,1)} %get-tuple-element.17), channel_id=1, source_target_pairs={{0,4},{4,8},{8,12},{1,5},{5,9},{9,13},{2,6},{6,10},{10,14},{3,7},{... | collective-permute-start | bytes 1572872 | tf_op jit(solution)/shard_map/ppermute | solution.py:16
  29.4 11.9 %collective-permute-done.2 = bf16[256,1024]{1,0:T(8,128)(2,1)S(1)} collective-permute-done((bf16[256,1024]{1,0:T(8,128)(2,1)}, bf16[256,1024]{1,0:T(8,128)(2,1)S(1)}, u32[]{:S(2)}, u32[]{:S(2)}) %collective-permute-start.2) | collective-permute-done | bytes 524320 | tf_op jit(solution)/shard_map/ppermute | solution.py:16
  41.3 1.4 %add_convert_fusion = bf16[256,1024]{1,0:T(8,128)(2,1)S(1)} fusion(f32[256,1024]{1,0:T(8,128)} %get-tuple-element.18, bf16[256,1024]{1,0:T(8,128)(2,1)S(1)} %collective-permute-done.2, f32[1024]{0:T(1024)} %bitcast.43), kind=kLoop, calls=%fused_computation.1 | loop fusion | flops 1048576 | bytes 2101248 | tf_op jit(solution)/shard_map/convert_element_type | solution.py:315
  42.6 4.3 %collective-permute-start.3 = (bf16[256,1024]{1,0:T(8,128)(2,1)S(1)}, bf16[256,1024]{1,0:T(8,128)(2,1)S(1)}, u32[]{:S(2)}, u32[]{:S(2)}) collective-permute-start(bf16[256,1024]{1,0:T(8,128)(2,1)S(1)} %add_convert_fusion), channel_id=1, source_target_pairs={{0,4},{4,8},{8,12},{1,5},{5,9},{9,13},{2,6},{6,10},{10,14},{3,7},{... | collective-permute-start | bytes 1572872 | tf_op jit(solution)/shard_map/ppermute | solution.py:16
  47.0 0.0 copy-done.2
  47.0 0.1 broadcast_in_dim.2
  47.1 0.7 reshape_reshape.3.refs_8_
  47.7 10.0 %collective-permute-done.3.refs_9_ = bf16[256,1024]{1,0:T(8,128)(2,1)S(1)} collective-permute-done((bf16[256,1024]{1,0:T(8,128)(2,1)S(1)}, bf16[256,1024]{1,0:T(8,128)(2,1)S(1)}, u32[]{:S(2)}, u32[]{:S(2)}) %collective-permute-start.3) | collective-permute-done | bytes 524320 | tf_op jit(solution)/shard_map/ppermute | solution.py:16
  57.7 0.0 copy-start
  57.7 0.8 %copy-done = bf16[256,1024]{1,0:T(8,128)(2,1)} copy-done((bf16[256,1024]{1,0:T(8,128)(2,1)}, bf16[256,1024]{1,0:T(8,128)(2,1)S(1)}, u32[]{:S(2)}) %copy-start) | copy-done | bytes 524312
  58.5 14.0 %shard_map.101 = bf16[1024,1024]{1,0:T(8,128)(2,1)} custom-call(bf16[1024,1024]{1,0:T(8,128)(2,1)} %get-tuple-element.12.refs_0_, bf16[1024,256]{1,0:T(8,128)(2,1)} %get-tuple-element.20.b_ref.refs_1_, bf16[1024,256]{1,0:T(8,128)(2,1)} %get-tuple-element.19.refs_2_, f32[1024,16]{1,0:T(8,128)} %get-tuple-element.13.refs_3_, ...), custom_call_target="tpu_custom_call" | custom-call | tf_op jit(solution)/shard_map/pallas_call | solution.py:227
  (6 shorter events, 0.0 us)
Async XLA Ops:
  1.4 7.6 %collective-permute-start = (bf16[8,1280]{1,0:T(8,128)(2,1)S(1)}, bf16[8,1280]{1,0:T(8,128)(2,1)S(1)}, u32[]{:S(2)}, u32[]{:S(2)}) collective-permute-start(bf16[8,1280]{1,0:T(8,128)(2,1)S(1)} %pad_maximum_fusion.1), channel_id=1, source_target_pairs={{0,4},{4,8},{8,12},{1,5},{5,9},{9,13},{2,6},{6,10},{10,14},{3,7},{... | collective-permute-start | bytes 61448 | tf_op jit(solution)/shard_map/ppermute | solution.py:16
  8.0 7.1 %copy-start.1 = (f32[1024]{0:T(1024)}, f32[1024]{0:T(1024)S(1)}, u32[]{:S(2)}) copy-start(f32[1024]{0:T(1024)S(1)} %get-tuple-element.26) | copy-start | bytes 12292
  11.7 2.0 %collective-permute-start.1 = (bf16[2,1024,128]{2,1,0:T(8,128)(2,1)S(1)}, bf16[2,1024,128]{2,1,0:T(8,128)(2,1)S(1)}, u32[]{:S(2)}, u32[]{:S(2)}) collective-permute-start(bf16[2,1024,128]{2,1,0:T(8,128)(2,1)S(1)} %multiply_convert_fusion), channel_id=1, source_target_pairs={{0,1},{1,0},{2,3},{3,2},{4,5},{5,4},{6,7},{7,6},{8,9},{9,8},{10,11... | collective-permute-start | bytes 1572872 | tf_op jit(solution)/shard_map/ppermute | solution.py:26
  15.1 31.9 %copy-start.2 = (f32[16]{0:T(128)S(1)}, f32[16]{0:T(128)}, u32[]{:S(2)}) copy-start(f32[16]{0:T(128)} %param.18) | copy-start | bytes 196
  25.9 15.4 %collective-permute-start.2 = (bf16[256,1024]{1,0:T(8,128)(2,1)}, bf16[256,1024]{1,0:T(8,128)(2,1)S(1)}, u32[]{:S(2)}, u32[]{:S(2)}) collective-permute-start(bf16[256,1024]{1,0:T(8,128)(2,1)} %get-tuple-element.17), channel_id=1, source_target_pairs={{0,4},{4,8},{8,12},{1,5},{5,9},{9,13},{2,6},{6,10},{10,14},{3,7},{... | collective-permute-start | bytes 1572872 | tf_op jit(solution)/shard_map/ppermute | solution.py:16
  42.6 15.1 %collective-permute-start.3 = (bf16[256,1024]{1,0:T(8,128)(2,1)S(1)}, bf16[256,1024]{1,0:T(8,128)(2,1)S(1)}, u32[]{:S(2)}, u32[]{:S(2)}) collective-permute-start(bf16[256,1024]{1,0:T(8,128)(2,1)S(1)} %add_convert_fusion), channel_id=1, source_target_pairs={{0,4},{4,8},{8,12},{1,5},{5,9},{9,13},{2,6},{6,10},{10,14},{3,7},{... | collective-permute-start | bytes 1572872 | tf_op jit(solution)/shard_map/ppermute | solution.py:16
  57.7 0.8 %copy-start = (bf16[256,1024]{1,0:T(8,128)(2,1)}, bf16[256,1024]{1,0:T(8,128)(2,1)S(1)}, u32[]{:S(2)}) copy-start(bf16[256,1024]{1,0:T(8,128)(2,1)S(1)} %collective-permute-done.3.refs_9_) | copy-start | bytes 1572868

commit v9 on v8

--- a/solution.py
+++ b/solution.py
@@ -100,7 +100,8 @@
         masked = jnp.where(allowed, scores, 0.0).astype(jnp.bfloat16)
         rising = expand_heads(jnp.exp(l_small), head_width)
         falling = expand_heads(jnp.exp(-l_small) * dt_small, head_width)
-        intra = split_dot(masked, x * falling) * rising
+        scaled = (x * falling).astype(jnp.bfloat16)
+        intra = jnp.dot(masked, scaled, preferred_element_type=jnp.float32) * rising
         inter = split_dot(c_mat, state) * (rising * info[:, 1:2])
         out_ref[...] = (intra + inter + skip_ref[...] * x).astype(jnp.bfloat16)
     ending = expand_heads(

time: 73.1 us -> 72.3 us (0.989)
  Pallas kernels: 24.8 us -> 23.9 us
    pallas_call x1, Pallas kernels: 14 us -> 13.2 us  [run_blocks(): pl.pallas_call(kernel, grid=(block_count,), in_specs=[row_block(width), r...]
where the time goes in v9:
time: 72.3 us; the launch traced here: 71.7 us
  Pallas kernels  23.9 us (33%)
  waiting for transfers between devices  22.1 us (31%)
  starting transfers between devices  12.8 us (18%)
  other arithmetic  6.91 us (10%)
  local copies, waits for them, and re-layouts  5.82 us (8%)
    ppermute x3, waiting for transfers between devices, shifted(): lax.ppermute(value, axis, [(source, source + steps) for source in range(i...  21.9 us
    pallas_call x1, Pallas kernels, run_blocks(): pl.pallas_call(kernel, grid=(block_count,), in_specs=[row_block(width), r...  13.2 us
    ppermute x3, starting transfers between devices, shifted(): lax.ppermute(value, axis, [(source, source + steps) for source in range(i...  12.7 us
    pallas_call x1, Pallas kernels, run_state(): pl.pallas_call(functools.partial(state_kernel, width // head_count), grid...  10.8 us
    convert_element_type x1, other arithmetic, convolve(): return jax.nn.silu(summed).astype(jnp.bfloat16)  2.59 us
  transfers between devices with their start and end apart: 4, of which 3 were waited for; matrix products, arithmetic and copies ran while one was open for 7% of the time, Pallas kernels for 0%

profile of v9, /device:TPU:0, one launch (start us, length us, event | category | flops | bytes accessed | tf_op | source)
XLA Modules:
  0.0 71.7 jit_solution(15764336063002298913)
XLA Ops:
  0.0 0.7 slice_bitcast_fusion.2
  0.7 0.7 %slice.66 = bf16[8,1024]{1,0:T(8,128)(2,1)S(1)} slice(bf16[1024,1024]{1,0:T(8,128)(2,1)} %x_ref.1), slice={[1016:1024], [0:1024]} | slice | bytes 32768 | tf_op jit(solution)/shard_map/slice | solution.py:271
  1.4 4.9 %collective-permute-start = (bf16[8,1280]{1,0:T(8,128)(2,1)S(1)}, bf16[8,1280]{1,0:T(8,128)(2,1)S(1)}, u32[]{:S(2)}, u32[]{:S(2)}) collective-permute-start(bf16[8,1280]{1,0:T(8,128)(2,1)S(1)} %pad_maximum_fusion.1), channel_id=1, source_target_pairs={{0,4},{4,8},{8,12},{1,5},{5,9},{9,13},{2,6},{6,10},{10,14},{3,7},{... | collective-permute-start | bytes 61448 | tf_op jit(solution)/shard_map/ppermute | solution.py:16
  6.4 0.8 %reduce-window.9 = s32[3,1]{0,1:T(1,128)S(1)} reduce-window(s32[3,1]{0,1:T(1,128)} %bitcast.49, s32[]{:T(128)} %constant.31.clone.1), window={size=3x1 pad=2_0x0_0}, to_apply=%region_0.0 | reduce-window | flops 6 | bytes 28 | tf_op jit(solution)/shard_map/reduce-window.4
  7.2 0.7 bitcast_subtract_fusion
  7.8 0.1 convert_reduce_fusion
  7.9 0.1 slice_bitcast_fusion.3
  8.0 0.0 copy-start.1
  8.0 0.1 slice_reduce_fusion
  8.1 0.1 fusion.2
  8.2 0.8 %slice_convert_fusion.4 = (f32[1,2,128]{2,0,1:T(1,128)S(1)}, f32[1,2,128]{2,0,1:T(1,128)S(1)}, f32[1,2,128]{2,0,1:T(1,128)S(1)}, f32[1,2,128]{2,0,1:T(1,128)S(1)}) fusion(bf16[4,2,128]{2,0,1:T(4,128)(2,1)} %bitcast.41), kind=kLoop, calls=%fused_computation.29 | loop fusion | flops 1024 | bytes 6144 | tf_op jit(solution)/shard_map/convert_element_type | solution.py:43
  9.1 0.0 collective-permute-done
  9.1 2.6 %multiply_convert_fusion = bf16[2,1024,128]{2,1,0:T(8,128)(2,1)S(1)} fusion(bf16[2,1024,128]{2,1,0:T(8,128)(2,1)} %param.11, bf16[2,3,128]{2,1,0:T(4,128)(2,1)S(1)} %slice_bitcast_fusion.4, f32[2,128]{1,0:T(2,128)S(1)} %bitcast.45, f32[1024]{0:T(1024)S(1)} %get-tuple-element.22, f32[2,128]{1,0:T(2,128)S(1)} %bitcast.46, f32[1024]{0:T(1024)S(1)} %get-tuple-element.23, ...), kind=kLoop, calls=%fused_computation.2 | loop fusion | flops 7602176 | bytes 1067520 | tf_op jit(solution)/shard_map/convert_element_type | solution.py:44
  11.7 0.1 collective-permute-start.1
  11.8 0.1 stack.31
  11.8 1.0 %copy.23.info_ref.refs_6_ = f32[1024,8]{1,0:T(8,128)} copy(f32[1024,8]{0,1:T(8,128)S(1)} %stack.31) | data formatting | bytes 65536 | tf_op jit(solution)/shard_map/stack | solution.py:302
  12.8 0.6 slice.84.tail_ref
  13.4 0.2 collective-permute-done.1
  13.6 0.4 maximum_select_fusion
  14.0 1.1 %slice_bitcast_fusion = (bf16[1024,256]{1,0:T(8,128)(2,1)}, bf16[1024,256]{1,0:T(8,128)(2,1)}) fusion(bf16[2,1024,256]{2,1,0:T(8,128)(2,1)S(1)} %maximum_select_fusion), kind=kLoop, calls=%fused_computation.7 | loop fusion | bytes 2097152 | tf_op jit(solution)/shard_map/squeeze | solution.py:292
  15.1 0.0 copy-done.1
  15.1 0.0 copy-start.2
  15.1 10.8 %shard_map.100 = (f32[256,1024]{1,0:T(8,128)}, f32[1024,16]{1,0:T(8,128)}, f32[1024,16]{1,0:T(8,128)}, f32[8,1,1024]{2,1,0:T(1,128)}, f32[1,1024]{1,0:T(1,128)},...) custom-call(bf16[1024,1024]{1,0:T(8,128)(2,1)} %x_ref.1, bf16[8,1024]{1,0:T(8,128)(2,1)} %slice.84.tail_ref, ...), custom_call_target="tpu_custom_call" | custom-call | tf_op jit(solution)/shard_map/pallas_call | solution.py:192
  25.9 3.5 %collective-permute-start.2 = (bf16[256,1024]{1,0:T(8,128)(2,1)}, bf16[256,1024]{1,0:T(8,128)(2,1)S(1)}, u32[]{:S(2)}, u32[]{:S(2)}) collective-permute-start(bf16[256,1024]{1,0:T(8,128)(2,1)} %get-tuple-element.17), channel_id=1, source_target_pairs={{0,4},{4,8},{8,12},{1,5},{5,9},{9,13},{2,6},{6,10},{10,14},{3,7},{... | collective-permute-start | bytes 1572872 | tf_op jit(solution)/shard_map/ppermute | solution.py:16
  29.4 11.9 %collective-permute-done.2 = bf16[256,1024]{1,0:T(8,128)(2,1)S(1)} collective-permute-done((bf16[256,1024]{1,0:T(8,128)(2,1)}, bf16[256,1024]{1,0:T(8,128)(2,1)S(1)}, u32[]{:S(2)}, u32[]{:S(2)}) %collective-permute-start.2) | collective-permute-done | bytes 524320 | tf_op jit(solution)/shard_map/ppermute | solution.py:16
  41.3 1.4 %add_convert_fusion = bf16[256,1024]{1,0:T(8,128)(2,1)S(1)} fusion(f32[256,1024]{1,0:T(8,128)} %get-tuple-element.18, bf16[256,1024]{1,0:T(8,128)(2,1)S(1)} %collective-permute-done.2, f32[1024]{0:T(1024)} %bitcast.43), kind=kLoop, calls=%fused_computation.1 | loop fusion | flops 1048576 | bytes 2101248 | tf_op jit(solution)/shard_map/convert_element_type | solution.py:316
  42.6 4.3 %collective-permute-start.3 = (bf16[256,1024]{1,0:T(8,128)(2,1)S(1)}, bf16[256,1024]{1,0:T(8,128)(2,1)S(1)}, u32[]{:S(2)}, u32[]{:S(2)}) collective-permute-start(bf16[256,1024]{1,0:T(8,128)(2,1)S(1)} %add_convert_fusion), channel_id=1, source_target_pairs={{0,4},{4,8},{8,12},{1,5},{5,9},{9,13},{2,6},{6,10},{10,14},{3,7},{... | collective-permute-start | bytes 1572872 | tf_op jit(solution)/shard_map/ppermute | solution.py:16
  47.0 0.0 copy-done.2
  47.0 0.1 broadcast_in_dim.2
  47.1 0.7 reshape_reshape.3.refs_8_
  47.7 10.0 %collective-permute-done.3.refs_9_ = bf16[256,1024]{1,0:T(8,128)(2,1)S(1)} collective-permute-done((bf16[256,1024]{1,0:T(8,128)(2,1)S(1)}, bf16[256,1024]{1,0:T(8,128)(2,1)S(1)}, u32[]{:S(2)}, u32[]{:S(2)}) %collective-permute-start.3) | collective-permute-done | bytes 524320 | tf_op jit(solution)/shard_map/ppermute | solution.py:16
  57.7 0.0 copy-start
  57.7 0.8 %copy-done = bf16[256,1024]{1,0:T(8,128)(2,1)} copy-done((bf16[256,1024]{1,0:T(8,128)(2,1)}, bf16[256,1024]{1,0:T(8,128)(2,1)S(1)}, u32[]{:S(2)}) %copy-start) | copy-done | bytes 524312
  58.5 13.2 %shard_map.101 = bf16[1024,1024]{1,0:T(8,128)(2,1)} custom-call(bf16[1024,1024]{1,0:T(8,128)(2,1)} %get-tuple-element.12.refs_0_, bf16[1024,256]{1,0:T(8,128)(2,1)} %get-tuple-element.20.b_ref.refs_1_, bf16[1024,256]{1,0:T(8,128)(2,1)} %get-tuple-element.19.refs_2_, f32[1024,16]{1,0:T(8,128)} %get-tuple-element.13.refs_3_, ...), custom_call_target="tpu_custom_call" | custom-call | tf_op jit(solution)/shard_map/pallas_call | solution.py:228
  (6 shorter events, 0.0 us)
Async XLA Ops:
  1.4 7.6 %collective-permute-start = (bf16[8,1280]{1,0:T(8,128)(2,1)S(1)}, bf16[8,1280]{1,0:T(8,128)(2,1)S(1)}, u32[]{:S(2)}, u32[]{:S(2)}) collective-permute-start(bf16[8,1280]{1,0:T(8,128)(2,1)S(1)} %pad_maximum_fusion.1), channel_id=1, source_target_pairs={{0,4},{4,8},{8,12},{1,5},{5,9},{9,13},{2,6},{6,10},{10,14},{3,7},{... | collective-permute-start | bytes 61448 | tf_op jit(solution)/shard_map/ppermute | solution.py:16
  8.0 7.1 %copy-start.1 = (f32[1024]{0:T(1024)}, f32[1024]{0:T(1024)S(1)}, u32[]{:S(2)}) copy-start(f32[1024]{0:T(1024)S(1)} %get-tuple-element.26) | copy-start | bytes 12292
  11.7 2.0 %collective-permute-start.1 = (bf16[2,1024,128]{2,1,0:T(8,128)(2,1)S(1)}, bf16[2,1024,128]{2,1,0:T(8,128)(2,1)S(1)}, u32[]{:S(2)}, u32[]{:S(2)}) collective-permute-start(bf16[2,1024,128]{2,1,0:T(8,128)(2,1)S(1)} %multiply_convert_fusion), channel_id=1, source_target_pairs={{0,1},{1,0},{2,3},{3,2},{4,5},{5,4},{6,7},{7,6},{8,9},{9,8},{10,11... | collective-permute-start | bytes 1572872 | tf_op jit(solution)/shard_map/ppermute | solution.py:26
  15.1 31.9 %copy-start.2 = (f32[16]{0:T(128)S(1)}, f32[16]{0:T(128)}, u32[]{:S(2)}) copy-start(f32[16]{0:T(128)} %param.18) | copy-start | bytes 196
  25.9 15.4 %collective-permute-start.2 = (bf16[256,1024]{1,0:T(8,128)(2,1)}, bf16[256,1024]{1,0:T(8,128)(2,1)S(1)}, u32[]{:S(2)}, u32[]{:S(2)}) collective-permute-start(bf16[256,1024]{1,0:T(8,128)(2,1)} %get-tuple-element.17), channel_id=1, source_target_pairs={{0,4},{4,8},{8,12},{1,5},{5,9},{9,13},{2,6},{6,10},{10,14},{3,7},{... | collective-permute-start | bytes 1572872 | tf_op jit(solution)/shard_map/ppermute | solution.py:16
  42.6 15.1 %collective-permute-start.3 = (bf16[256,1024]{1,0:T(8,128)(2,1)S(1)}, bf16[256,1024]{1,0:T(8,128)(2,1)S(1)}, u32[]{:S(2)}, u32[]{:S(2)}) collective-permute-start(bf16[256,1024]{1,0:T(8,128)(2,1)S(1)} %add_convert_fusion), channel_id=1, source_target_pairs={{0,4},{4,8},{8,12},{1,5},{5,9},{9,13},{2,6},{6,10},{10,14},{3,7},{... | collective-permute-start | bytes 1572872 | tf_op jit(solution)/shard_map/ppermute | solution.py:16
  57.7 0.8 %copy-start = (bf16[256,1024]{1,0:T(8,128)(2,1)}, bf16[256,1024]{1,0:T(8,128)(2,1)S(1)}, u32[]{:S(2)}) copy-start(bf16[256,1024]{1,0:T(8,128)(2,1)S(1)} %collective-permute-done.3.refs_9_) | copy-start | bytes 1572868

commit v10 on v8

--- a/solution.py
+++ b/solution.py
@@ -112,23 +112,9 @@
     )
 
 
-def state_kernel(head_width, x_ref, tail_ref, wconv_ref, bias_ref, b_ref, dt_ref, rate_ref,
-                 info_ref, state_ref, l_ref, dtt_ref, decay_ref, total_ref, xc_ref, sent_ref,
-                 prev_ref):
-    blk = pl.program_id(0)
-
-    @pl.when(blk == 0)
-    def _():
-        state_ref[...] = jnp.zeros(state_ref.shape, jnp.float32)
-        total_ref[...] = jnp.ones(total_ref.shape, jnp.float32)
-        prev_ref[...] = tail_ref[...].astype(jnp.float32)
-
-    info = info_ref[...]
-    raw = x_ref[...].astype(jnp.float32)
-    prev = prev_ref[...]
+def causal_conv(raw, prev, taps, bias, info):
     top_row = lax.broadcasted_iota(jnp.int32, prev.shape, 0)
-    taps = wconv_ref[...].astype(jnp.float32)
-    summed = jnp.zeros(raw.shape, jnp.float32) + bias_ref[...]
+    summed = jnp.zeros(raw.shape, jnp.float32) + bias
     for offset in range(4):
         back = 3 - offset
         if back == 0:
@@ -138,9 +124,35 @@
             top = jnp.where(top_row < back, pltpu.roll(prev, back, 0), rolled[:8])
             window = jnp.concatenate([top, rolled[8:]], 0) * info[:, 1 + back : 2 + back]
         summed = summed + taps[offset : offset + 1, :] * window
+    return jax.nn.silu(summed).astype(jnp.bfloat16)
+
+
+def state_kernel(head_width, x_ref, tail_ref, wconv_ref, bias_ref, bc_ref, bcx_ref, dt_ref,
+                 rate_ref, info_ref, state_ref, l_ref, dtt_ref, decay_ref, total_ref, xc_ref,
+                 bo_ref, co_ref, sent_ref, prev_ref, bcprev_ref):
+    blk = pl.program_id(0)
+
+    @pl.when(blk == 0)
+    def _():
+        state_ref[...] = jnp.zeros(state_ref.shape, jnp.float32)
+        total_ref[...] = jnp.ones(total_ref.shape, jnp.float32)
+        prev_ref[...] = tail_ref[...].astype(jnp.float32)
+        bcprev_ref[...] = bcx_ref[:, 0:8, :]
+
+    info = info_ref[...]
+    raw = x_ref[...].astype(jnp.float32)
+    xc = causal_conv(raw, prev_ref[...], wconv_ref[...].astype(jnp.float32), bias_ref[...], info)
     prev_ref[...] = raw[BLOCK - 8 :]
-    xc = jax.nn.silu(summed).astype(jnp.bfloat16)
     xc_ref[...] = xc
+    convolved = []
+    for which in range(2):
+        raw_bc = bc_ref[which].astype(jnp.float32)
+        extra = bcx_ref[which]
+        convolved.append(causal_conv(raw_bc, bcprev_ref[which], extra[8:12], extra[12:13], info))
+        bcprev_ref[which] = raw_bc[BLOCK - 8 :]
+    b_mat, c_mat = convolved
+    bo_ref[...] = b_mat
+    co_ref[...] = c_mat
 
     rows = lax.broadcasted_iota(jnp.int32, (2 * BLOCK, BLOCK), 0)
     cols = lax.broadcasted_iota(jnp.int32, (2 * BLOCK, BLOCK), 1)
@@ -172,7 +184,7 @@
     )
     weighted = (xc.astype(jnp.float32) * ending).astype(jnp.bfloat16)
     new_state = decay_x * state_ref[...] + lax.dot_general(
-        b_ref[...], weighted, (((0,), (0,)), ((), ())), preferred_element_type=jnp.float32
+        b_mat, weighted, (((0,), (0,)), ((), ())), preferred_element_type=jnp.float32
     )
     state_ref[...] = new_state
 
@@ -181,10 +193,10 @@
         sent_ref[...] = new_state.astype(jnp.bfloat16)
 
 
-def run_state(x, tail8, wconv, bias_row, b_full, step_size, rate_row, info):
+def run_state(x, tail8, wconv, bias_row, bc_raw, bc_extra, step_size, rate_row, info):
     rows, width = x.shape
     head_count = step_size.shape[0]
-    n_size = b_full.shape[1]
+    n_size = bc_raw.shape[2]
     block_count = rows // BLOCK
     row_block = lambda cols: pl.BlockSpec((BLOCK, cols), lambda b: (b, 0))
     whole = lambda shape: pl.BlockSpec(shape, lambda b: (0,) * len(shape))
@@ -192,21 +204,26 @@
         functools.partial(state_kernel, width // head_count),
         grid=(block_count,),
         in_specs=[row_block(width), whole((8, width)), whole((4, width)), whole((1, width)),
-                  row_block(n_size), pl.BlockSpec((head_count, BLOCK), lambda b: (0, b)),
+                  pl.BlockSpec((2, BLOCK, n_size), lambda b: (0, b, 0)), whole(bc_extra.shape),
+                  pl.BlockSpec((head_count, BLOCK), lambda b: (0, b)),
                   whole((1, head_count)), row_block(info.shape[1])],
         out_specs=[whole((n_size, width)), row_block(head_count), row_block(head_count),
                    pl.BlockSpec((1, 1, width), lambda b: (b, 0, 0)), whole((1, width)),
-                   row_block(width), whole((n_size, width))],
+                   row_block(width), row_block(n_size), row_block(n_size),
+                   whole((n_size, width))],
         out_shape=[jax.ShapeDtypeStruct((n_size, width), jnp.float32),
                    jax.ShapeDtypeStruct((rows, head_count), jnp.float32),
                    jax.ShapeDtypeStruct((rows, head_count), jnp.float32),
                    jax.ShapeDtypeStruct((block_count, 1, width), jnp.float32),
                    jax.ShapeDtypeStruct((1, width), jnp.float32),
                    jax.ShapeDtypeStruct((rows, width), jnp.bfloat16),
+                   jax.ShapeDtypeStruct((rows, n_size), jnp.bfloat16),
+                   jax.ShapeDtypeStruct((rows, n_size), jnp.bfloat16),
                    jax.ShapeDtypeStruct((n_size, width), jnp.bfloat16)],
-        scratch_shapes=[pltpu.VMEM((8, width), jnp.float32)],
+        scratch_shapes=[pltpu.VMEM((8, width), jnp.float32),
+                        pltpu.VMEM((2, 8, n_size), jnp.float32)],
         compiler_params=pltpu.CompilerParams(dimension_semantics=("arbitrary",)),
-    )(x, tail8, wconv, bias_row, b_full, step_size, rate_row, info)
+    )(x, tail8, wconv, bias_row, bc_raw, bc_extra, step_size, rate_row, info)
 
 
 def run_blocks(with_y, x, b_full, c_full, l_t, dt_t, seg_row, seg_col, entry_col, decay_x,
@@ -271,24 +288,19 @@
     )
     tails = shifted(tails, "seq", 1)
     tail8 = tails[:, :width]
-    state_tail = jnp.transpose(tails[5:, width:].reshape(3, 2, group_half), (1, 0, 2))
-    weight_state = jnp.swapaxes(conv_state, 0, 1)[:, :, None, :]
-    state_half = convolve(
-        jnp.concatenate([state_tail, state_input], 1),
-        weight_state,
-        bias_state[:, None, :],
-        seg_ext,
-        own_rows,
-    )
-    partner = from_partner(state_half, "head", 0)
+    state_tail = tails[:, width:].reshape(8, 2, group_half)
+    extra = jnp.concatenate(
+        [jnp.transpose(state_tail, (1, 0, 2)).astype(jnp.float32),
+         conv_state.astype(jnp.float32), bias_state[:, None, :]],
+        1,
+    )
+    partner_raw, partner_extra = from_partner((state_input, extra), "head", 0)
     lower_half = lax.axis_index("head") % 2 == 0
-    state_full = jnp.where(
-        lower_half,
-        jnp.concatenate([state_half, partner], 2),
-        jnp.concatenate([partner, state_half], 2),
-    )
-    b_full = state_full[0]
-    c_full = state_full[1]
+    pair = lambda own, other: jnp.where(
+        lower_half, jnp.concatenate([own, other], 2), jnp.concatenate([other, own], 2)
+    )
+    bc_raw = pair(state_input, partner_raw)
+    bc_extra = pair(extra, partner_extra)
     head_width = inner_input.shape[1] // head_count
     spread = lambda v: jnp.repeat(v, head_width, axis=-1)
     skip_x = spread(skip_gain).reshape(1, -1)
@@ -305,8 +317,8 @@
         1,
     )
 
-    local_end, l_t, dt_t, decay_x, total_decay, inner_conv, end_sent = run_state(
-        inner_input, tail8, conv_inner, bias_inner.reshape(1, -1), b_full,
+    local_end, l_t, dt_t, decay_x, total_decay, inner_conv, b_full, c_full, end_sent = run_state(
+        inner_input, tail8, conv_inner, bias_inner.reshape(1, -1), bc_raw, bc_extra,
         step_size, decay_rate.reshape(1, -1), info
     )
 

time: 73.1 us -> 74.1 us (1.014)
  other arithmetic: 6.91 us -> 8.41 us
  local copies, waits for them, and re-layouts: 5.82 us -> 4.72 us
    select_n x1 -> x2, other arithmetic: 0.36 us -> 3.92 us  [body(): jnp.where(lower_half, jnp.concatenate([own, other], 2), jnp.concatenate([...]
    convert_element_type x2, other arithmetic: 3.43 us -> 0.69 us  [the longest x1 0.69 us: body(): conv_state.astype(jnp.float32)]
    squeeze x1 -> x0, local copies, waits for them, and re-layouts: 1.06 us -> none  [body(): c_full = state_full[1]]
  transfers between devices with their start and end apart: 4 -> 5, of which waited for: 3 -> 2; matrix products, arithmetic and copies ran while one was open for 7% -> 11% of each run, Pallas kernels for 0% -> 0%
where the time goes in v10:
time: 74.1 us; the launch traced here: 73.5 us
  Pallas kernels  25.4 us (34%)
  waiting for transfers between devices  21.9 us (30%)
  starting transfers between devices  13 us (18%)
  other arithmetic  8.41 us (11%)
  local copies, waits for them, and re-layouts  4.72 us (6%)
    ppermute x3, waiting for transfers between devices, shifted(): lax.ppermute(value, axis, [(source, source + steps) for source in range(i...  21.9 us
    pallas_call x1, Pallas kernels, run_blocks(): pl.pallas_call(kernel, grid=(block_count,), in_specs=[row_block(width), r...  14 us
    ppermute x3, starting transfers between devices, shifted(): lax.ppermute(value, axis, [(source, source + steps) for source in range(i...  12.3 us
    pallas_call x1, Pallas kernels, run_state(): pl.pallas_call(functools.partial(state_kernel, width // head_count), grid...  11.3 us
    select_n x2, other arithmetic, body(): jnp.where(lower_half, jnp.concatenate([own, other], 2), jnp.concatenate([...  3.92 us
  transfers between devices with their start and end apart: 5, of which 2 were waited for; matrix products, arithmetic and copies ran while one was open for 11% of the time, Pallas kernels for 0%

profile of v10, /device:TPU:0, one launch (start us, length us, event | category | flops | bytes accessed | tf_op | source)
XLA Modules:
  0.0 73.5 jit_solution(7995831787569964654)
XLA Ops:
  0.0 0.5 collective-permute-start.1
  0.5 0.7 slice_bitcast_fusion.1
  1.1 0.7 slice.30
  1.9 4.5 %collective-permute-start = (bf16[8,1280]{1,0:T(8,128)(2,1)S(1)}, bf16[8,1280]{1,0:T(8,128)(2,1)S(1)}, u32[]{:S(2)}, u32[]{:S(2)}) collective-permute-start(bf16[8,1280]{1,0:T(8,128)(2,1)S(1)} %pad_maximum_fusion), channel_id=1, source_target_pairs={{0,4},{4,8},{8,12},{1,5},{5,9},{9,13},{2,6},{6,10},{10,14},{3,7},{... | collective-permute-start | bytes 61448 | tf_op jit(solution)/shard_map/ppermute | solution.py:16
  6.4 0.8 %reduce-window.9 = s32[3,1]{0,1:T(1,128)S(1)} reduce-window(s32[3,1]{0,1:T(1,128)} %bitcast.41, s32[]{:T(128)} %constant.27.clone.1), window={size=3x1 pad=2_0x0_0}, to_apply=%region_0.0 | reduce-window | flops 6 | bytes 28 | tf_op jit(solution)/shard_map/reduce-window.4
  7.2 0.7 bitcast_subtract_fusion
  7.8 0.1 convert_reduce_fusion
  7.9 0.1 slice_bitcast_fusion.2
  8.0 0.0 copy-start.1
  8.0 0.1 slice_reduce_fusion
  8.1 0.7 convert_element_type.34
  8.8 0.0 collective-permute-done
  8.8 0.7 pad_maximum_fusion.1
  9.5 0.2 collective-permute-start.2
  9.8 0.1 fusion.2
  9.8 0.1 stack.43
  9.9 1.0 %copy.23.info_ref.refs_6_ = f32[1024,8]{1,0:T(8,128)} copy(f32[1024,8]{0,1:T(8,128)S(1)} %stack.43) | data formatting | bytes 65536 | tf_op jit(solution)/shard_map/stack | solution.py:313
  10.9 0.6 slice.39.tail_ref
  11.5 0.0 collective-permute-done.2
  11.5 1.4 %maximum_select_fusion.1.bcx_ref = f32[2,13,256]{2,1,0:T(8,128)} fusion(f32[2,13,128]{2,1,0:T(8,128)S(1)} %collective-permute-done.2, f32[2,1,128]{2,1,0:T(1,128)} %bitcast.39, f32[2,4,128]{2,1,0:T(4,128)S(1)} %convert_element_type.34, f32[2,8,128]{2,1,0:T(8,128)S(1)} %convert_bitcast_fusion, pred[]{:T(512)S(6)} %eq.27), kind=kLoop, calls=%fused_computation.2 | loop fusion | flops 46592 | bytes 53249 | tf_op jit(solution)/shard_map/jit(_where)/select_n | solution.py:299
  12.9 0.0 collective-permute-done.1
  12.9 2.5 %maximum_select_fusion.bc_ref = bf16[2,1024,256]{2,1,0:T(8,128)(2,1)} fusion(bf16[2,1024,128]{2,1,0:T(8,128)(2,1)S(1)} %collective-permute-done.1, bf16[2,1024,128]{2,1,0:T(8,128)(2,1)} %param.11, pred[]{:T(512)S(6)} %eq.27), kind=kLoop, calls=%fused_computation | loop fusion | flops 4718592 | bytes 2097153 | tf_op jit(solution)/shard_map/jit(_where)/select_n | solution.py:299
  15.4 0.0 copy-start.2
  15.4 11.3 %shard_map.100 = (f32[256,1024]{1,0:T(8,128)}, f32[1024,16]{1,0:T(8,128)}, f32[1024,16]{1,0:T(8,128)}, f32[8,1,1024]{2,1,0:T(1,128)}, f32[1,1024]{1,0:T(1,128)},...) custom-call(bf16[1024,1024]{1,0:T(8,128)(2,1)} %x_ref.1, ...), custom_call_target="tpu_custom_call" | custom-call | tf_op jit(solution)/shard_map/pallas_call | solution.py:203
  26.8 0.0 copy-done.1
  26.8 3.5 %collective-permute-start.3 = (bf16[256,1024]{1,0:T(8,128)(2,1)}, bf16[256,1024]{1,0:T(8,128)(2,1)S(1)}, u32[]{:S(2)}, u32[]{:S(2)}) collective-permute-start(bf16[256,1024]{1,0:T(8,128)(2,1)} %get-tuple-element.21), channel_id=1, source_target_pairs={{0,4},{4,8},{8,12},{1,5},{5,9},{9,13},{2,6},{6,10},{10,14},{3,7},{... | collective-permute-start | bytes 1572872 | tf_op jit(solution)/shard_map/ppermute | solution.py:16
  30.3 11.9 %collective-permute-done.3 = bf16[256,1024]{1,0:T(8,128)(2,1)S(1)} collective-permute-done((bf16[256,1024]{1,0:T(8,128)(2,1)}, bf16[256,1024]{1,0:T(8,128)(2,1)S(1)}, u32[]{:S(2)}, u32[]{:S(2)}) %collective-permute-start.3) | collective-permute-done | bytes 524320 | tf_op jit(solution)/shard_map/ppermute | solution.py:16
  42.2 1.4 %add_convert_fusion = bf16[256,1024]{1,0:T(8,128)(2,1)S(1)} fusion(f32[256,1024]{1,0:T(8,128)} %get-tuple-element.22, bf16[256,1024]{1,0:T(8,128)(2,1)S(1)} %collective-permute-done.3, f32[1024]{0:T(1024)} %bitcast.37), kind=kLoop, calls=%fused_computation.1 | loop fusion | flops 1048576 | bytes 2101248 | tf_op jit(solution)/shard_map/convert_element_type | solution.py:327
  43.6 4.3 %collective-permute-start.4 = (bf16[256,1024]{1,0:T(8,128)(2,1)S(1)}, bf16[256,1024]{1,0:T(8,128)(2,1)S(1)}, u32[]{:S(2)}, u32[]{:S(2)}) collective-permute-start(bf16[256,1024]{1,0:T(8,128)(2,1)S(1)} %add_convert_fusion), channel_id=1, source_target_pairs={{0,4},{4,8},{8,12},{1,5},{5,9},{9,13},{2,6},{6,10},{10,14},{3,7},{... | collective-permute-start | bytes 1572872 | tf_op jit(solution)/shard_map/ppermute | solution.py:16
  47.9 0.0 copy-done.2
  47.9 0.1 broadcast_in_dim.9
  48.0 0.7 reshape_reshape.3.refs_8_
  48.7 10.0 %collective-permute-done.4.refs_9_ = bf16[256,1024]{1,0:T(8,128)(2,1)S(1)} collective-permute-done((bf16[256,1024]{1,0:T(8,128)(2,1)S(1)}, bf16[256,1024]{1,0:T(8,128)(2,1)S(1)}, u32[]{:S(2)}, u32[]{:S(2)}) %collective-permute-start.4) | collective-permute-done | bytes 524320 | tf_op jit(solution)/shard_map/ppermute | solution.py:16
  58.7 0.0 copy-start
  58.7 0.8 %copy-done = bf16[256,1024]{1,0:T(8,128)(2,1)} copy-done((bf16[256,1024]{1,0:T(8,128)(2,1)}, bf16[256,1024]{1,0:T(8,128)(2,1)S(1)}, u32[]{:S(2)}) %copy-start) | copy-done | bytes 524312
  59.5 14.0 %shard_map.101 = bf16[1024,1024]{1,0:T(8,128)(2,1)} custom-call(bf16[1024,1024]{1,0:T(8,128)(2,1)} %get-tuple-element.14.refs_0_, bf16[1024,256]{1,0:T(8,128)(2,1)} %get-tuple-element.15.refs_1_, bf16[1024,256]{1,0:T(8,128)(2,1)} %get-tuple-element.16.refs_2_, f32[1024,16]{1,0:T(8,128)} %get-tuple-element.17.refs_3_, f32[1024,16]{1,0:T(8,128)} %get-tuple-element.18.refs_4_, ...), custom_call_target="tpu_custom_call" | custom-call | tf_op jit(solution)/shard_map/pallas_call | solution.py:244
  (6 shorter events, 0.0 us)
Async XLA Ops:
  0.0 12.9 %collective-permute-start.1 = (bf16[2,1024,128]{2,1,0:T(8,128)(2,1)}, bf16[2,1024,128]{2,1,0:T(8,128)(2,1)S(1)}, u32[]{:S(2)}, u32[]{:S(2)}) collective-permute-start(bf16[2,1024,128]{2,1,0:T(8,128)(2,1)} %param.11), channel_id=1, source_target_pairs={{0,1},{1,0},{2,3},{3,2},{4,5},{5,4},{6,7},{7,6},{8,9},{9,8},{10,11... | collective-permute-start | bytes 1572872 | tf_op jit(solution)/shard_map/ppermute | solution.py:26
  1.9 7.0 %collective-permute-start = (bf16[8,1280]{1,0:T(8,128)(2,1)S(1)}, bf16[8,1280]{1,0:T(8,128)(2,1)S(1)}, u32[]{:S(2)}, u32[]{:S(2)}) collective-permute-start(bf16[8,1280]{1,0:T(8,128)(2,1)S(1)} %pad_maximum_fusion), channel_id=1, source_target_pairs={{0,4},{4,8},{8,12},{1,5},{5,9},{9,13},{2,6},{6,10},{10,14},{3,7},{... | collective-permute-start | bytes 61448 | tf_op jit(solution)/shard_map/ppermute | solution.py:16
  8.0 18.8 %copy-start.1 = (f32[1024]{0:T(1024)}, f32[1024]{0:T(1024)S(1)}, u32[]{:S(2)}) copy-start(f32[1024]{0:T(1024)S(1)} %get-tuple-element.28) | copy-start | bytes 12292
  9.5 2.0 %collective-permute-start.2 = (f32[2,13,128]{2,1,0:T(8,128)S(1)}, f32[2,13,128]{2,1,0:T(8,128)S(1)}, u32[]{:S(2)}, u32[]{:S(2)}) collective-permute-start(f32[2,13,128]{2,1,0:T(8,128)S(1)} %pad_maximum_fusion.1), channel_id=1, source_target_pairs={{0,1},{1,0},{2,3},{3,2},{4,5},{5,4},{6,7},{7,6},{8,9},{9,8},{10,11... | collective-permute-start | bytes 39944 | tf_op jit(solution)/shard_map/ppermute | solution.py:26
  15.4 32.5 %copy-start.2 = (f32[16]{0:T(128)S(1)}, f32[16]{0:T(128)}, u32[]{:S(2)}) copy-start(f32[16]{0:T(128)} %param.18) | copy-start | bytes 196
  26.8 15.4 %collective-permute-start.3 = (bf16[256,1024]{1,0:T(8,128)(2,1)}, bf16[256,1024]{1,0:T(8,128)(2,1)S(1)}, u32[]{:S(2)}, u32[]{:S(2)}) collective-permute-start(bf16[256,1024]{1,0:T(8,128)(2,1)} %get-tuple-element.21), channel_id=1, source_target_pairs={{0,4},{4,8},{8,12},{1,5},{5,9},{9,13},{2,6},{6,10},{10,14},{3,7},{... | collective-permute-start | bytes 1572872 | tf_op jit(solution)/shard_map/ppermute | solution.py:16
  43.6 15.1 %collective-permute-start.4 = (bf16[256,1024]{1,0:T(8,128)(2,1)S(1)}, bf16[256,1024]{1,0:T(8,128)(2,1)S(1)}, u32[]{:S(2)}, u32[]{:S(2)}) collective-permute-start(bf16[256,1024]{1,0:T(8,128)(2,1)S(1)} %add_convert_fusion), channel_id=1, source_target_pairs={{0,4},{4,8},{8,12},{1,5},{5,9},{9,13},{2,6},{6,10},{10,14},{3,7},{... | collective-permute-start | bytes 1572872 | tf_op jit(solution)/shard_map/ppermute | solution.py:16
  58.7 0.8 %copy-start = (bf16[256,1024]{1,0:T(8,128)(2,1)}, bf16[256,1024]{1,0:T(8,128)(2,1)S(1)}, u32[]{:S(2)}) copy-start(bf16[256,1024]{1,0:T(8,128)(2,1)S(1)} %collective-permute-done.4.refs_9_) | copy-start | bytes 1572868

commit v11 on v10

--- a/solution.py
+++ b/solution.py
@@ -127,9 +127,9 @@
     return jax.nn.silu(summed).astype(jnp.bfloat16)
 
 
-def state_kernel(head_width, x_ref, tail_ref, wconv_ref, bias_ref, bc_ref, bcx_ref, dt_ref,
-                 rate_ref, info_ref, state_ref, l_ref, dtt_ref, decay_ref, total_ref, xc_ref,
-                 bo_ref, co_ref, sent_ref, prev_ref, bcprev_ref):
+def state_kernel(head_width, x_ref, tail_ref, wconv_ref, bias_ref, own_ref, other_ref, ownx_ref,
+                 otherx_ref, flag_ref, dt_ref, rate_ref, info_ref, state_ref, l_ref, dtt_ref,
+                 decay_ref, total_ref, xc_ref, bo_ref, co_ref, sent_ref, prev_ref, bcprev_ref):
     blk = pl.program_id(0)
 
     @pl.when(blk == 0)
@@ -137,19 +137,28 @@
         state_ref[...] = jnp.zeros(state_ref.shape, jnp.float32)
         total_ref[...] = jnp.ones(total_ref.shape, jnp.float32)
         prev_ref[...] = tail_ref[...].astype(jnp.float32)
-        bcprev_ref[...] = bcx_ref[:, 0:8, :]
+        bcprev_ref[0] = ownx_ref[:, 0:8, :]
+        bcprev_ref[1] = otherx_ref[:, 0:8, :]
 
     info = info_ref[...]
     raw = x_ref[...].astype(jnp.float32)
     xc = causal_conv(raw, prev_ref[...], wconv_ref[...].astype(jnp.float32), bias_ref[...], info)
     prev_ref[...] = raw[BLOCK - 8 :]
     xc_ref[...] = xc
+    lower = flag_ref[...][:, 0:1] > 0.5
     convolved = []
     for which in range(2):
-        raw_bc = bc_ref[which].astype(jnp.float32)
-        extra = bcx_ref[which]
-        convolved.append(causal_conv(raw_bc, bcprev_ref[which], extra[8:12], extra[12:13], info))
-        bcprev_ref[which] = raw_bc[BLOCK - 8 :]
+        halves = []
+        for side, (raw_ref, extra_ref) in enumerate(((own_ref, ownx_ref), (other_ref, otherx_ref))):
+            raw_bc = raw_ref[which].astype(jnp.float32)
+            extra = extra_ref[which]
+            halves.append(
+                causal_conv(raw_bc, bcprev_ref[side, which], extra[8:12], extra[12:13], info)
+            )
+            bcprev_ref[side, which] = raw_bc[BLOCK - 8 :]
+        convolved.append(jnp.where(
+            lower, jnp.concatenate(halves, 1), jnp.concatenate(halves[::-1], 1)
+        ))
     b_mat, c_mat = convolved
     bo_ref[...] = b_mat
     co_ref[...] = c_mat
@@ -193,10 +202,12 @@
         sent_ref[...] = new_state.astype(jnp.bfloat16)
 
 
-def run_state(x, tail8, wconv, bias_row, bc_raw, bc_extra, step_size, rate_row, info):
+def run_state(x, tail8, wconv, bias_row, own_raw, other_raw, own_extra, other_extra, flag,
+              step_size, rate_row, info):
     rows, width = x.shape
     head_count = step_size.shape[0]
-    n_size = bc_raw.shape[2]
+    half = own_raw.shape[2]
+    n_size = 2 * half
     block_count = rows // BLOCK
     row_block = lambda cols: pl.BlockSpec((BLOCK, cols), lambda b: (b, 0))
     whole = lambda shape: pl.BlockSpec(shape, lambda b: (0,) * len(shape))
@@ -204,7 +215,9 @@
         functools.partial(state_kernel, width // head_count),
         grid=(block_count,),
         in_specs=[row_block(width), whole((8, width)), whole((4, width)), whole((1, width)),
-                  pl.BlockSpec((2, BLOCK, n_size), lambda b: (0, b, 0)), whole(bc_extra.shape),
+                  pl.BlockSpec((2, BLOCK, half), lambda b: (0, b, 0)),
+                  pl.BlockSpec((2, BLOCK, half), lambda b: (0, b, 0)),
+                  whole(own_extra.shape), whole(own_extra.shape), whole(flag.shape),
                   pl.BlockSpec((head_count, BLOCK), lambda b: (0, b)),
                   whole((1, head_count)), row_block(info.shape[1])],
         out_specs=[whole((n_size, width)), row_block(head_count), row_block(head_count),
@@ -221,9 +234,10 @@
                    jax.ShapeDtypeStruct((rows, n_size), jnp.bfloat16),
                    jax.ShapeDtypeStruct((n_size, width), jnp.bfloat16)],
         scratch_shapes=[pltpu.VMEM((8, width), jnp.float32),
-                        pltpu.VMEM((2, 8, n_size), jnp.float32)],
+                        pltpu.VMEM((2, 2, 8, half), jnp.float32)],
         compiler_params=pltpu.CompilerParams(dimension_semantics=("arbitrary",)),
-    )(x, tail8, wconv, bias_row, bc_raw, bc_extra, step_size, rate_row, info)
+    )(x, tail8, wconv, bias_row, own_raw, other_raw, own_extra, other_extra, flag, step_size,
+      rate_row, info)
 
 
 def run_blocks(with_y, x, b_full, c_full, l_t, dt_t, seg_row, seg_col, entry_col, decay_x,
@@ -295,12 +309,8 @@
         1,
     )
     partner_raw, partner_extra = from_partner((state_input, extra), "head", 0)
-    lower_half = lax.axis_index("head") % 2 == 0
-    pair = lambda own, other: jnp.where(
-        lower_half, jnp.concatenate([own, other], 2), jnp.concatenate([other, own], 2)
-    )
-    bc_raw = pair(state_input, partner_raw)
-    bc_extra = pair(extra, partner_extra)
+    lower_half = (lax.axis_index("head") % 2 == 0).astype(jnp.float32)
+    flag = jnp.full((1, 128), lower_half, jnp.float32)
     head_width = inner_input.shape[1] // head_count
     spread = lambda v: jnp.repeat(v, head_width, axis=-1)
     skip_x = spread(skip_gain).reshape(1, -1)
@@ -318,7 +328,8 @@
     )
 
     local_end, l_t, dt_t, decay_x, total_decay, inner_conv, b_full, c_full, end_sent = run_state(
-        inner_input, tail8, conv_inner, bias_inner.reshape(1, -1), bc_raw, bc_extra,
+        inner_input, tail8, conv_inner, bias_inner.reshape(1, -1), state_input, partner_raw,
+        extra, partner_extra, flag,
         step_size, decay_rate.reshape(1, -1), info
     )
 

time: 74.1 us -> 70.9 us (0.957)
  other arithmetic: 8.41 us -> 4.49 us
  local copies, waits for them, and re-layouts: 4.72 us -> 5.54 us
    select_n x2 -> x0, other arithmetic: 3.92 us -> none  [body(): jnp.where(lower_half, jnp.concatenate([own, other], 2), jnp.concatenate([...]
  transfers between devices with their start and end apart: 5 -> 5, of which waited for: 2 -> 2; matrix products, arithmetic and copies ran while one was open for 11% -> 10% of each run, Pallas kernels for 0% -> 0%
where the time goes in v11:
time: 70.9 us; the launch traced here: 70.4 us
  Pallas kernels  25.3 us (36%)
  waiting for transfers between devices  21.9 us (31%)
  starting transfers between devices  13 us (18%)
  local copies, waits for them, and re-layouts  5.54 us (8%)
  other arithmetic  4.49 us (6%)
    ppermute x3, waiting for transfers between devices, shifted(): lax.ppermute(value, axis, [(source, source + steps) for source in range(i...  21.9 us
    pallas_call x1, Pallas kernels, run_blocks(): pl.pallas_call(kernel, grid=(block_count,), in_specs=[row_block(width), r...  14 us
    ppermute x3, starting transfers between devices, shifted(): lax.ppermute(value, axis, [(source, source + steps) for source in range(i...  12.3 us
    pallas_call x1, Pallas kernels, run_state(): pl.pallas_call(functools.partial(state_kernel, width // head_count), grid...  11.3 us
  transfers between devices with their start and end apart: 5, of which 2 were waited for; matrix products, arithmetic and copies ran while one was open for 10% of the time, Pallas kernels for 0%

profile of v11, /device:TPU:0, one launch (start us, length us, event | category | flops | bytes accessed | tf_op | source)
XLA Modules:
  0.0 70.4 jit_solution(6558978760602902028)
XLA Ops:
  0.0 0.5 collective-permute-start.1
  0.5 0.7 slice_bitcast_fusion.1
  1.1 0.7 %slice.30 = bf16[8,1024]{1,0:T(8,128)(2,1)S(1)} slice(bf16[1024,1024]{1,0:T(8,128)(2,1)} %x_ref.1), slice={[1016:1024], [0:1024]} | slice | bytes 32768 | tf_op jit(solution)/shard_map/slice | solution.py:301
  1.9 4.5 %collective-permute-start = (bf16[8,1280]{1,0:T(8,128)(2,1)S(1)}, bf16[8,1280]{1,0:T(8,128)(2,1)S(1)}, u32[]{:S(2)}, u32[]{:S(2)}) collective-permute-start(bf16[8,1280]{1,0:T(8,128)(2,1)S(1)} %pad_maximum_fusion), channel_id=1, source_target_pairs={{0,4},{4,8},{8,12},{1,5},{5,9},{9,13},{2,6},{6,10},{10,14},{3,7},{... | collective-permute-start | bytes 61448 | tf_op jit(solution)/shard_map/ppermute | solution.py:16
  6.3 0.8 %reduce-window.9 = s32[3,1]{0,1:T(1,128)S(1)} reduce-window(s32[3,1]{0,1:T(1,128)} %bitcast.40, s32[]{:T(128)} %constant.27.clone.1), window={size=3x1 pad=2_0x0_0}, to_apply=%region_0.0 | reduce-window | flops 6 | bytes 28 | tf_op jit(solution)/shard_map/reduce-window.4
  7.2 0.7 bitcast_subtract_fusion
  7.8 0.1 convert_reduce_fusion
  7.9 0.1 slice_bitcast_fusion.2
  8.0 0.0 copy-start.3
  8.0 0.1 slice_reduce_fusion
  8.1 0.7 convert_element_type.37
  8.8 0.0 collective-permute-done
  8.8 0.7 pad_maximum_fusion.1.ownx_ref
  9.5 0.0 copy-start.2
  9.5 0.2 collective-permute-start.2
  9.7 0.1 fusion.2
  9.8 0.1 stack.43
  9.9 1.0 %copy.23.info_ref.refs_6_ = f32[1024,8]{1,0:T(8,128)} copy(f32[1024,8]{0,1:T(8,128)S(1)} %stack.43) | data formatting | bytes 65536 | tf_op jit(solution)/shard_map/stack | solution.py:323
  10.9 0.6 slice.39.tail_ref
  11.5 0.0 collective-permute-done.2.otherx_ref
  11.5 0.0 copy-start.4
  11.5 0.0 collective-permute-done.1.other_ref
  11.5 0.0 copy-start
  11.5 0.6 broadcast_in_dim.12.flag_ref
  12.1 0.0 copy-done.2
  12.1 0.0 copy-done.4
  12.1 0.2 copy-done
  12.3 0.0 copy-start.5
  12.3 11.3 %shard_map.100 = (f32[256,1024]{1,0:T(8,128)}, f32[1024,16]{1,0:T(8,128)}, f32[1024,16]{1,0:T(8,128)}, f32[8,1,1024]{2,1,0:T(1,128)}, f32[1,1024]{1,0:T(1,128)},...) custom-call(bf16[1024,1024]{1,0:T(8,128)(2,1)} %x_ref.1, ...), custom_call_target="tpu_custom_call" | custom-call | tf_op jit(solution)/shard_map/pallas_call | solution.py:214
  23.6 0.0 copy-done.3
  23.7 3.5 %collective-permute-start.3 = (bf16[256,1024]{1,0:T(8,128)(2,1)}, bf16[256,1024]{1,0:T(8,128)(2,1)S(1)}, u32[]{:S(2)}, u32[]{:S(2)}) collective-permute-start(bf16[256,1024]{1,0:T(8,128)(2,1)} %get-tuple-element.21), channel_id=1, source_target_pairs={{0,4},{4,8},{8,12},{1,5},{5,9},{9,13},{2,6},{6,10},{10,14},{3,7},{... | collective-permute-start | bytes 1572872 | tf_op jit(solution)/shard_map/ppermute | solution.py:16
  27.2 11.9 %collective-permute-done.3 = bf16[256,1024]{1,0:T(8,128)(2,1)S(1)} collective-permute-done((bf16[256,1024]{1,0:T(8,128)(2,1)}, bf16[256,1024]{1,0:T(8,128)(2,1)S(1)}, u32[]{:S(2)}, u32[]{:S(2)}) %collective-permute-start.3) | collective-permute-done | bytes 524320 | tf_op jit(solution)/shard_map/ppermute | solution.py:16
  39.1 1.4 %add_convert_fusion = bf16[256,1024]{1,0:T(8,128)(2,1)S(1)} fusion(f32[256,1024]{1,0:T(8,128)} %get-tuple-element.22, bf16[256,1024]{1,0:T(8,128)(2,1)S(1)} %collective-permute-done.3, f32[1024]{0:T(1024)} %bitcast.37), kind=kLoop, calls=%fused_computation | loop fusion | flops 1048576 | bytes 2101248 | tf_op jit(solution)/shard_map/convert_element_type | solution.py:338
  40.5 4.3 %collective-permute-start.4 = (bf16[256,1024]{1,0:T(8,128)(2,1)S(1)}, bf16[256,1024]{1,0:T(8,128)(2,1)S(1)}, u32[]{:S(2)}, u32[]{:S(2)}) collective-permute-start(bf16[256,1024]{1,0:T(8,128)(2,1)S(1)} %add_convert_fusion), channel_id=1, source_target_pairs={{0,4},{4,8},{8,12},{1,5},{5,9},{9,13},{2,6},{6,10},{10,14},{3,7},{... | collective-permute-start | bytes 1572872 | tf_op jit(solution)/shard_map/ppermute | solution.py:16
  44.8 0.0 copy-done.5
  44.8 0.1 broadcast_in_dim.13
  44.9 0.7 reshape_reshape.3.refs_8_
  45.5 10.0 %collective-permute-done.4.refs_9_ = bf16[256,1024]{1,0:T(8,128)(2,1)S(1)} collective-permute-done((bf16[256,1024]{1,0:T(8,128)(2,1)S(1)}, bf16[256,1024]{1,0:T(8,128)(2,1)S(1)}, u32[]{:S(2)}, u32[]{:S(2)}) %collective-permute-start.4) | collective-permute-done | bytes 524320 | tf_op jit(solution)/shard_map/ppermute | solution.py:16
  55.6 0.0 copy-start.1
  55.6 0.8 %copy-done.1 = bf16[256,1024]{1,0:T(8,128)(2,1)} copy-done((bf16[256,1024]{1,0:T(8,128)(2,1)}, bf16[256,1024]{1,0:T(8,128)(2,1)S(1)}, u32[]{:S(2)}) %copy-start.1) | copy-done | bytes 524312
  56.4 14.0 %shard_map.101 = bf16[1024,1024]{1,0:T(8,128)(2,1)} custom-call(bf16[1024,1024]{1,0:T(8,128)(2,1)} %get-tuple-element.14.refs_0_, bf16[1024,256]{1,0:T(8,128)(2,1)} %get-tuple-element.15.refs_1_, bf16[1024,256]{1,0:T(8,128)(2,1)} %get-tuple-element.16.refs_2_, f32[1024,16]{1,0:T(8,128)} %get-tuple-element.17.refs_3_, f32[1024,16]{1,0:T(8,128)} %get-tuple-element.18.refs_4_, ...), custom_call_target="tpu_custom_call" | custom-call | tf_op jit(solution)/shard_map/pallas_call | solution.py:258
  (6 shorter events, 0.0 us)
Async XLA Ops:
  0.0 11.5 %collective-permute-start.1 = (bf16[2,1024,128]{2,1,0:T(8,128)(2,1)}, bf16[2,1024,128]{2,1,0:T(8,128)(2,1)S(1)}, u32[]{:S(2)}, u32[]{:S(2)}) collective-permute-start(bf16[2,1024,128]{2,1,0:T(8,128)(2,1)} %own_ref.1), channel_id=1, source_target_pairs={{0,1},{1,0},{2,3},{3,2},{4,5},{5,4},{6,7},{7,6},{8,9},{9,8},{10,11... | collective-permute-start | bytes 1572872 | tf_op jit(solution)/shard_map/ppermute | solution.py:26
  1.9 7.0 %collective-permute-start = (bf16[8,1280]{1,0:T(8,128)(2,1)S(1)}, bf16[8,1280]{1,0:T(8,128)(2,1)S(1)}, u32[]{:S(2)}, u32[]{:S(2)}) collective-permute-start(bf16[8,1280]{1,0:T(8,128)(2,1)S(1)} %pad_maximum_fusion), channel_id=1, source_target_pairs={{0,4},{4,8},{8,12},{1,5},{5,9},{9,13},{2,6},{6,10},{10,14},{3,7},{... | collective-permute-start | bytes 61448 | tf_op jit(solution)/shard_map/ppermute | solution.py:16
  8.0 15.6 %copy-start.3 = (f32[1024]{0:T(1024)}, f32[1024]{0:T(1024)S(1)}, u32[]{:S(2)}) copy-start(f32[1024]{0:T(1024)S(1)} %get-tuple-element.28) | copy-start | bytes 12292
  9.5 2.6 %copy-start.2 = (f32[2,13,128]{2,1,0:T(8,128)}, f32[2,13,128]{2,1,0:T(8,128)S(1)}, u32[]{:S(2)}) copy-start(f32[2,13,128]{2,1,0:T(8,128)S(1)} %pad_maximum_fusion.1.ownx_ref) | copy-start | bytes 39940
  9.5 2.0 %collective-permute-start.2 = (f32[2,13,128]{2,1,0:T(8,128)S(1)}, f32[2,13,128]{2,1,0:T(8,128)S(1)}, u32[]{:S(2)}, u32[]{:S(2)}) collective-permute-start(f32[2,13,128]{2,1,0:T(8,128)S(1)} %pad_maximum_fusion.1.ownx_ref), channel_id=1, source_target_pairs={{0,1},{1,0},{2,3},{3,2},{4,5},{5,4},{6,7},{7,6},{8,9},{9,8},{10,11... | collective-permute-start | bytes 39944 | tf_op jit(solution)/shard_map/ppermute | solution.py:26
  11.5 0.6 copy-start.4
  11.5 0.8 %copy-start = (bf16[2,1024,128]{2,1,0:T(8,128)(2,1)}, bf16[2,1024,128]{2,1,0:T(8,128)(2,1)S(1)}, u32[]{:S(2)}) copy-start(bf16[2,1024,128]{2,1,0:T(8,128)(2,1)S(1)} %collective-permute-done.1.other_ref) | copy-start | bytes 1572868
  12.3 32.5 %copy-start.5 = (f32[16]{0:T(128)S(1)}, f32[16]{0:T(128)}, u32[]{:S(2)}) copy-start(f32[16]{0:T(128)} %param.18) | copy-start | bytes 196
  23.7 15.4 %collective-permute-start.3 = (bf16[256,1024]{1,0:T(8,128)(2,1)}, bf16[256,1024]{1,0:T(8,128)(2,1)S(1)}, u32[]{:S(2)}, u32[]{:S(2)}) collective-permute-start(bf16[256,1024]{1,0:T(8,128)(2,1)} %get-tuple-element.21), channel_id=1, source_target_pairs={{0,4},{4,8},{8,12},{1,5},{5,9},{9,13},{2,6},{6,10},{10,14},{3,7},{... | collective-permute-start | bytes 1572872 | tf_op jit(solution)/shard_map/ppermute | solution.py:16
  40.5 15.1 %collective-permute-start.4 = (bf16[256,1024]{1,0:T(8,128)(2,1)S(1)}, bf16[256,1024]{1,0:T(8,128)(2,1)S(1)}, u32[]{:S(2)}, u32[]{:S(2)}) collective-permute-start(bf16[256,1024]{1,0:T(8,128)(2,1)S(1)} %add_convert_fusion), channel_id=1, source_target_pairs={{0,4},{4,8},{8,12},{1,5},{5,9},{9,13},{2,6},{6,10},{10,14},{3,7},{... | collective-permute-start | bytes 1572872 | tf_op jit(solution)/shard_map/ppermute | solution.py:16
  55.6 0.8 %copy-start.1 = (bf16[256,1024]{1,0:T(8,128)(2,1)}, bf16[256,1024]{1,0:T(8,128)(2,1)S(1)}, u32[]{:S(2)}) copy-start(bf16[256,1024]{1,0:T(8,128)(2,1)S(1)} %collective-permute-done.4.refs_9_) | copy-start | bytes 1572868

commit v12 on v11

--- a/solution.py
+++ b/solution.py
@@ -129,7 +129,8 @@
 
 def state_kernel(head_width, x_ref, tail_ref, wconv_ref, bias_ref, own_ref, other_ref, ownx_ref,
                  otherx_ref, flag_ref, dt_ref, rate_ref, info_ref, state_ref, l_ref, dtt_ref,
-                 decay_ref, total_ref, xc_ref, bo_ref, co_ref, sent_ref, prev_ref, bcprev_ref):
+                 decay_ref, total_ref, xc_ref, bo_ref, co_ref, sent_ref, prefix_ref, prev_ref,
+                 bcprev_ref):
     blk = pl.program_id(0)
 
     @pl.when(blk == 0)
@@ -187,6 +188,7 @@
         jnp.exp(l_small[BLOCK - 1 : BLOCK, :]) * info[BLOCK - 1 : BLOCK, 1:2], head_width
     )
     decay_ref[0] = decay_x
+    prefix_ref[0] = total_ref[...]
     total_ref[...] = total_ref[...] * decay_x
     ending = expand_heads(
         jnp.exp(l_small[BLOCK - 1 : BLOCK, :] - l_small) * dt_small * end_col, head_width
@@ -223,7 +225,7 @@
         out_specs=[whole((n_size, width)), row_block(head_count), row_block(head_count),
                    pl.BlockSpec((1, 1, width), lambda b: (b, 0, 0)), whole((1, width)),
                    row_block(width), row_block(n_size), row_block(n_size),
-                   whole((n_size, width))],
+                   whole((n_size, width)), pl.BlockSpec((1, 1, width), lambda b: (b, 0, 0))],
         out_shape=[jax.ShapeDtypeStruct((n_size, width), jnp.float32),
                    jax.ShapeDtypeStruct((rows, head_count), jnp.float32),
                    jax.ShapeDtypeStruct((rows, head_count), jnp.float32),
@@ -232,12 +234,131 @@
                    jax.ShapeDtypeStruct((rows, width), jnp.bfloat16),
                    jax.ShapeDtypeStruct((rows, n_size), jnp.bfloat16),
                    jax.ShapeDtypeStruct((rows, n_size), jnp.bfloat16),
-                   jax.ShapeDtypeStruct((n_size, width), jnp.bfloat16)],
+                   jax.ShapeDtypeStruct((n_size, width), jnp.bfloat16),
+                   jax.ShapeDtypeStruct((block_count, 1, width), jnp.float32)],
         scratch_shapes=[pltpu.VMEM((8, width), jnp.float32),
                         pltpu.VMEM((2, 2, 8, half), jnp.float32)],
         compiler_params=pltpu.CompilerParams(dimension_semantics=("arbitrary",)),
     )(x, tail8, wconv, bias_row, own_raw, other_raw, own_extra, other_extra, flag, step_size,
       rate_row, info)
+
+
+def partial_kernel(head_width, from_zero, *refs):
+    if from_zero:
+        (x_ref, b_ref, c_ref, l_ref, dt_ref, segr_ref, info_ref, decay_ref, skip_ref, out_ref,
+         end_ref, state_ref) = refs
+    else:
+        (x_ref, b_ref, c_ref, l_ref, dt_ref, segr_ref, info_ref, decay_ref, skip_ref, init_ref,
+         after_ref, buf_ref, out_ref, end_ref, state_ref) = refs
+    blk = pl.program_id(0)
+
+    @pl.when(blk == 0)
+    def _():
+        if from_zero:
+            state_ref[...] = jnp.zeros(state_ref.shape, jnp.float32)
+        else:
+            state_ref[...] = init_ref[...]
+
+    info = info_ref[...]
+    seg_col = info[:, 0:1]
+    end_col = (seg_col == seg_col[BLOCK - 1 : BLOCK, :]).astype(jnp.float32)
+    l_small = l_ref[...]
+    dt_small = dt_ref[...]
+    x = x_ref[...].astype(jnp.float32)
+    state = state_ref[...]
+    c_mat = c_ref[...]
+    b_mat = b_ref[...]
+    scores = lax.dot_general(
+        c_mat, b_mat, (((1,), (1,)), ((), ())), preferred_element_type=jnp.float32
+    )
+    rows = lax.broadcasted_iota(jnp.int32, (BLOCK, BLOCK), 0)
+    cols = lax.broadcasted_iota(jnp.int32, (BLOCK, BLOCK), 1)
+    allowed = (rows >= cols) & (seg_col == segr_ref[...])
+    masked = jnp.where(allowed, scores, 0.0).astype(jnp.bfloat16)
+    rising = expand_heads(jnp.exp(l_small), head_width)
+    falling = expand_heads(jnp.exp(-l_small) * dt_small, head_width)
+    intra = split_dot(masked, x * falling) * rising
+    inter = split_dot(c_mat, state) * (rising * info[:, 1:2])
+    out_ref[...] = intra + inter + skip_ref[...] * x
+    ending = expand_heads(
+        jnp.exp(l_small[BLOCK - 1 : BLOCK, :] - l_small) * dt_small * end_col, head_width
+    )
+    weighted = (x * ending).astype(jnp.bfloat16)
+    new_state = decay_ref[0] * state + lax.dot_general(
+        b_mat, weighted, (((0,), (0,)), ((), ())), preferred_element_type=jnp.float32
+    )
+    state_ref[...] = new_state
+
+    @pl.when(blk == pl.num_programs(0) - 1)
+    def _():
+        end_ref[...] = new_state
+
+
+def run_partial(first, count, x, b_full, c_full, l_t, dt_t, seg_row, info, decay_x, skip_x,
+                init=None, after=None, buf=None):
+    rows, width = x.shape
+    head_count = l_t.shape[1]
+    n_size = b_full.shape[1]
+    row_block = lambda cols: pl.BlockSpec((BLOCK, cols), lambda b: (b + first, 0))
+    whole = lambda shape: pl.BlockSpec(shape, lambda b: (0,) * len(shape))
+    from_zero = init is None
+    in_specs = [row_block(width), row_block(n_size), row_block(n_size), row_block(head_count),
+                row_block(head_count), pl.BlockSpec((1, BLOCK), lambda b: (0, b + first)),
+                row_block(info.shape[1]), pl.BlockSpec((1, 1, width), lambda b: (b + first, 0, 0)),
+                whole((1, width))]
+    args = [x, b_full, c_full, l_t, dt_t, seg_row, info, decay_x, skip_x]
+    aliases = {}
+    if not from_zero:
+        any_spec = pl.BlockSpec(memory_space=pl.ANY)
+        in_specs += [whole((n_size, width)), any_spec, any_spec]
+        args += [init, after, buf]
+        aliases = {len(args) - 1: 0}
+    return pl.pallas_call(
+        functools.partial(partial_kernel, width // head_count, from_zero),
+        grid=(count,),
+        in_specs=in_specs,
+        out_specs=[row_block(width), whole((n_size, width))],
+        out_shape=[jax.ShapeDtypeStruct((rows, width), jnp.float32),
+                   jax.ShapeDtypeStruct((n_size, width), jnp.float32)],
+        scratch_shapes=[pltpu.VMEM((n_size, width), jnp.float32)],
+        input_output_aliases=aliases,
+        compiler_params=pltpu.CompilerParams(dimension_semantics=("arbitrary",)),
+    )(*args)
+
+
+def correct_kernel(head_width, y_ref, c_ref, l_ref, info_ref, prefix_ref, ein_ref, out_ref):
+    rows, cols = y_ref.shape
+    rising = expand_heads(jnp.exp(l_ref[0]), head_width)
+    blocks = prefix_ref.shape[0]
+    prefix = jnp.broadcast_to(prefix_ref[...], (blocks, BLOCK, cols)).reshape(rows, cols)
+    carried = jnp.dot(c_ref[...], ein_ref[...], preferred_element_type=jnp.float32)
+    factor = rising * info_ref[...][:, 1:2] * prefix
+    out_ref[...] = (y_ref[...] + carried * factor).astype(jnp.bfloat16)
+
+
+def run_correct(partial, c_full, l_t, info, prefix_x, entering):
+    rows, width = partial.shape
+    head_count = l_t.shape[1]
+    head_width = width // head_count
+    n_size = c_full.shape[1]
+    tile = 256
+    tiles = width // tile
+    heads_per = tile // head_width
+    l_tiles = jnp.transpose(l_t.reshape(rows, tiles, heads_per), (1, 0, 2))
+    block_count = prefix_x.shape[0]
+    return pl.pallas_call(
+        functools.partial(correct_kernel, head_width),
+        grid=(tiles,),
+        in_specs=[pl.BlockSpec((rows, tile), lambda j: (0, j)),
+                  pl.BlockSpec((rows, n_size), lambda j: (0, 0)),
+                  pl.BlockSpec((1, rows, heads_per), lambda j: (j, 0, 0)),
+                  pl.BlockSpec((rows, info.shape[1]), lambda j: (0, 0)),
+                  pl.BlockSpec((block_count, 1, tile), lambda j: (0, 0, j)),
+                  pl.BlockSpec((n_size, tile), lambda j: (0, j))],
+        out_specs=pl.BlockSpec((rows, tile), lambda j: (0, j)),
+        out_shape=jax.ShapeDtypeStruct((rows, width), jnp.bfloat16),
+        compiler_params=pltpu.CompilerParams(dimension_semantics=("arbitrary",)),
+    )(partial, c_full, l_tiles, info, prefix_x, entering)
 
 
 def run_blocks(with_y, x, b_full, c_full, l_t, dt_t, seg_row, seg_col, entry_col, decay_x,
@@ -327,7 +448,8 @@
         1,
     )
 
-    local_end, l_t, dt_t, decay_x, total_decay, inner_conv, b_full, c_full, end_sent = run_state(
+    (local_end, l_t, dt_t, decay_x, total_decay, inner_conv, b_full, c_full, end_sent,
+     prefix_x) = run_state(
         inner_input, tail8, conv_inner, bias_inner.reshape(1, -1), state_input, partner_raw,
         extra, partner_extra, flag,
         step_size, decay_rate.reshape(1, -1), info
@@ -340,13 +462,19 @@
 
     part_rows = own_rows * lax.axis_size("seq")
     hops = min(lax.axis_size("seq") - 1, -(-(part_rows // 2) // own_rows))
+    half_blocks = block_count // 2
+    operands = (inner_conv, b_full, c_full, l_t, dt_t, seg_row, info, decay_x, skip_x)
     incoming = shifted(end_sent, "seq", 1)
+    partial, middle = run_partial(0, half_blocks, *operands)
+    incoming, partial, middle = lax.optimization_barrier((incoming, partial, middle))
+    first_hop = incoming
     for step_num in range(1, hops):
         incoming = relay(step_num, incoming)
-    return run_blocks(
-        True, inner_conv, b_full, c_full, l_t, dt_t, seg_row, info, None, decay_x, skip_x,
-        incoming
-    )
+    partial, _ = run_partial(
+        half_blocks, block_count - half_blocks, *operands, init=middle, after=first_hop,
+        buf=partial
+    )
+    return run_correct(partial, c_full, l_t, info, prefix_x, incoming)
 
 
 def solution(mesh):

time: 70.9 us -> 63.6 us (0.90)
  waiting for transfers between devices: 21.9 us -> 2.61 us
  Pallas kernels: 25.3 us -> 36.2 us
  local copies, waits for them, and re-layouts: 5.54 us -> 7.73 us
  other arithmetic: 4.49 us -> 3.27 us
    ppermute x3, waiting for transfers between devices: 21.9 us -> 2.6 us  [shifted(): lax.ppermute(value, axis, [(source, source + steps) for source in range(i...]
    pallas_call x1 -> x3, Pallas kernels: 14 us -> 24.8 us  [the longest x2 17.4 us: run_partial(): pl.pallas_call(functools.partial(partial_kernel, width // head_count, fro...]
    reshape x0 -> x2, local copies, waits for them, and re-layouts: none -> 2.01 us  [run_correct(): l_tiles = jnp.transpose(l_t.reshape(rows, tiles, heads_per), (1, 0, 2))]
    convert_element_type x1, other arithmetic: 1.38 us -> 0.15 us  [relay(): (total_decay * incoming.astype(jnp.float32) + local_end).astype(jnp.bfloa...]
  transfers between devices with their start and end apart: 5 -> 5, of which waited for: 2 -> 1; matrix products, arithmetic and copies ran while one was open for 10% -> 15% of each run, Pallas kernels for 0% -> 28%
where the time goes in v12:
time: 63.6 us; the launch traced here: 63 us
  Pallas kernels  36.2 us (57%)
  starting transfers between devices  13 us (20%)
  local copies, waits for them, and re-layouts  7.73 us (12%)
  other arithmetic  3.27 us (5%)
  waiting for transfers between devices  2.61 us (4%)
    pallas_call x2, Pallas kernels, run_partial(): pl.pallas_call(functools.partial(partial_kernel, width // head_count, fro...  17.4 us
    ppermute x3, starting transfers between devices, shifted(): lax.ppermute(value, axis, [(source, source + steps) for source in range(i...  12.3 us
    pallas_call x1, Pallas kernels, run_state(): pl.pallas_call(functools.partial(state_kernel, width // head_count), grid...  11.4 us
    pallas_call x1, Pallas kernels, run_correct(): pl.pallas_call(functools.partial(correct_kernel, head_width), grid=(tiles...  7.38 us
    ppermute x3, waiting for transfers between devices, shifted(): lax.ppermute(value, axis, [(source, source + steps) for source in range(i...  2.6 us
    reshape x2, local copies, waits for them, and re-layouts, run_correct(): l_tiles = jnp.transpose(l_t.reshape(rows, tiles, heads_per), (1, 0, 2))  2.01 us
  transfers between devices with their start and end apart: 5, of which 1 were waited for; matrix products, arithmetic and copies ran while one was open for 15% of the time, Pallas kernels for 28%

profile of v12, /device:TPU:0, one launch (start us, length us, event | category | flops | bytes accessed | tf_op | source)
XLA Modules:
  0.0 63.0 jit_solution(4845900318883542291)
XLA Ops:
  0.0 0.5 collective-permute-start.1
  0.5 0.7 %slice_bitcast_fusion.1 = bf16[8,256]{1,0:T(8,128)(2,1)S(1)} fusion(bf16[2,1024,128]{2,1,0:T(8,128)(2,1)} %own_ref.1), kind=kLoop, calls=%fused_computation.12 | loop fusion | bytes 8192 | tf_op jit(solution)/shard_map/reshape | solution.py:422
  1.1 0.7 %slice.30 = bf16[8,1024]{1,0:T(8,128)(2,1)S(1)} slice(bf16[1024,1024]{1,0:T(8,128)(2,1)} %x_ref.1), slice={[1016:1024], [0:1024]} | slice | bytes 32768 | tf_op jit(solution)/shard_map/slice | solution.py:422
  1.9 4.5 %collective-permute-start = (bf16[8,1280]{1,0:T(8,128)(2,1)S(1)}, bf16[8,1280]{1,0:T(8,128)(2,1)S(1)}, u32[]{:S(2)}, u32[]{:S(2)}) collective-permute-start(bf16[8,1280]{1,0:T(8,128)(2,1)S(1)} %pad_maximum_fusion), channel_id=1, source_target_pairs={{0,4},{4,8},{8,12},{1,5},{5,9},{9,13},{2,6},{6,10},{10,14},{3,7},{... | collective-permute-start | bytes 61448 | tf_op jit(solution)/shard_map/ppermute | solution.py:16
  6.4 0.8 %reduce-window.9 = s32[3,1]{0,1:T(1,128)S(1)} reduce-window(s32[3,1]{0,1:T(1,128)} %bitcast.45, s32[]{:T(128)} %constant.27.clone.1), window={size=3x1 pad=2_0x0_0}, to_apply=%region_0.0 | reduce-window | flops 6 | bytes 28 | tf_op jit(solution)/shard_map/reduce-window.4
  7.2 0.7 %bitcast_subtract_fusion = s32[3]{0:T(128)S(1)} fusion(s32[3]{0:T(128)} %param.19, s32[3,1]{0,1:T(1,128)S(1)} %reduce-window.9), kind=kLoop, calls=%fused_computation.19 | loop fusion | flops 3 | bytes 36 | tf_op jit(solution)/shard_map/sub | solution.py:30
  7.8 0.1 convert_reduce_fusion
  7.9 0.1 slice_bitcast_fusion.2
  8.0 0.0 copy-start.6
  8.0 0.1 slice_reduce_fusion
  8.1 0.7 %convert_element_type.37 = f32[2,4,128]{2,1,0:T(4,128)S(1)} convert(bf16[2,4,128]{2,1,0:T(4,128)(2,1)} %param.14) | non-fusion elementwise | flops 1024 | bytes 6144 | tf_op jit(solution)/shard_map/convert_element_type | solution.py:429
  8.8 0.0 collective-permute-done
  8.8 0.7 %pad_maximum_fusion.1.ownx_ref = f32[2,13,128]{2,1,0:T(8,128)S(1)} fusion(f32[2,1,128]{2,1,0:T(1,128)} %bitcast.43, f32[2,4,128]{2,1,0:T(4,128)S(1)} %convert_element_type.37, f32[2,8,128]{2,1,0:T(8,128)S(1)} %convert_bitcast_fusion), kind=kLoop, calls=%fused_computation.3 | loop fusion | flops 6656 | bytes 26624 | tf_op jit(solution)/shard_map/concatenate | solution.py:427
  9.5 0.2 collective-permute-start.2
  9.8 0.1 fusion.2
  9.8 0.1 stack.43
  9.9 0.0 copy-start.9
  9.9 1.0 %copy.32.info_ref.refs_6_ = f32[1024,8]{1,0:T(8,128)} copy(f32[1024,8]{0,1:T(8,128)S(1)} %stack.43) | data formatting | bytes 65536 | tf_op jit(solution)/shard_map/stack | solution.py:444
  10.9 0.6 slice.39.tail_ref
  11.5 0.0 collective-permute-done.2.otherx_ref
  11.5 0.0 collective-permute-done.1.other_ref
  11.5 0.0 copy-start.3
  11.6 0.6 broadcast_in_dim.12.flag_ref
  12.2 0.0 copy-done.5
  12.2 0.0 copy-done.7
  12.2 0.1 copy-done.3
  12.3 11.4 %shard_map.100 = (f32[256,1024]{1,0:T(8,128)}, f32[1024,16]{1,0:T(8,128)}, f32[1024,16]{1,0:T(8,128)}, f32[8,1,1024]{2,1,0:T(1,128)}, f32[1,1024]{1,0:T(1,128)},...) custom-call(bf16[1024,1024]{1,0:T(8,128)(2,1)} %x_ref.1, ...), custom_call_target="tpu_custom_call" | custom-call | tf_op jit(solution)/shard_map/pallas_call | solution.py:216
  23.7 0.0 copy-done.6
  23.7 3.5 %collective-permute-start.3 = (bf16[256,1024]{1,0:T(8,128)(2,1)}, bf16[256,1024]{1,0:T(8,128)(2,1)S(1)}, u32[]{:S(2)}, u32[]{:S(2)}) collective-permute-start(bf16[256,1024]{1,0:T(8,128)(2,1)} %get-tuple-element.27), channel_id=1, source_target_pairs={{0,4},{4,8},{8,12},{1,5},{5,9},{9,13},{2,6},{6,10},{10,14},{3,7},{... | collective-permute-start | bytes 1572872 | tf_op jit(solution)/shard_map/ppermute | solution.py:16
  27.3 0.0 copy-done.9
  27.3 0.1 broadcast_in_dim.13
  27.3 0.7 %reshape_reshape.3.refs_8_ = f32[1,1024]{1,0:T(1,128)} reshape(f32[16,64]{1,0:T(8,128)S(1)} %broadcast_in_dim.13) | data formatting | bytes 8192 | tf_op jit(solution)/shard_map/reshape;reshape | solution.py:437
  28.0 8.5 %shard_map.101 = (f32[1024,1024]{1,0:T(8,128)}, f32[256,1024]{1,0:T(8,128)}) custom-call(bf16[1024,1024]{1,0:T(8,128)(2,1)} %get-tuple-element.21.refs_0_, bf16[1024,256]{1,0:T(8,128)(2,1)} %get-tuple-element.22.refs_1_, bf16[1024,256]{1,0:T(8,128)(2,1)} %get-tuple-element.23.refs_2_.c_ref, f32[1024,16]{1,0:T(8,128)} %get-tuple-element.24.refs_3_, ...), custom_call_target="tpu_custom_call" | custom-call | tf_op jit(solution)/shard_map/pallas_call | solution.py:316
  36.5 0.0 copy-start
  36.6 2.6 %collective-permute-done.3.refs_10_ = bf16[256,1024]{1,0:T(8,128)(2,1)S(1)} collective-permute-done((bf16[256,1024]{1,0:T(8,128)(2,1)}, bf16[256,1024]{1,0:T(8,128)(2,1)S(1)}, u32[]{:S(2)}, u32[]{:S(2)}) %collective-permute-start.3) | collective-permute-done | bytes 524320 | tf_op jit(solution)/shard_map/ppermute | solution.py:16
  39.2 0.0 copy-done.2
  39.2 0.0 copy-done.8
  39.2 0.2 add_convert_fusion
  39.3 4.3 %collective-permute-start.4 = (bf16[256,1024]{1,0:T(8,128)(2,1)S(1)}, bf16[256,1024]{1,0:T(8,128)(2,1)S(1)}, u32[]{:S(2)}, u32[]{:S(2)}) collective-permute-start(bf16[256,1024]{1,0:T(8,128)(2,1)S(1)} %add_convert_fusion), channel_id=1, source_target_pairs={{0,4},{4,8},{8,12},{1,5},{5,9},{9,13},{2,6},{6,10},{10,14},{3,7},{... | collective-permute-start | bytes 1572872 | tf_op jit(solution)/shard_map/ppermute | solution.py:16
  43.6 0.0 copy-done
  43.7 0.2 copy.35
  43.9 2.0 %copy.36 = f32[1024,4,4]{2,0,1:T(8,128)} copy(f32[1024,4,4]{0,2,1:T(4,128)S(1)} %reshape.61) | data formatting | bytes 131072 | tf_op jit(solution)/shard_map/reshape | solution.py:347
  45.8 0.0 copy-done.1
  45.8 8.9 %shard_map.102 = (f32[1024,1024]{1,0:T(8,128)}, f32[256,1024]{1,0:T(8,128)}) custom-call(bf16[1024,1024]{1,0:T(8,128)(2,1)} %get-tuple-element.21.refs_0_, bf16[1024,256]{1,0:T(8,128)(2,1)} %get-tuple-element.22.refs_1_, bf16[1024,256]{1,0:T(8,128)(2,1)} %get-tuple-element.23.refs_2_.c_ref, ...), custom_call_target="tpu_custom_call", output_to_operand_aliasing={{0}: (11, {})} | custom-call | tf_op jit(solution)/shard_map/pallas_call | solution.py:316
  54.8 0.0 collective-permute-done.4.ein_ref
  54.8 0.0 copy-start.4
  54.8 0.8 %copy-done.4 = bf16[256,1024]{1,0:T(8,128)(2,1)} copy-done((bf16[256,1024]{1,0:T(8,128)(2,1)}, bf16[256,1024]{1,0:T(8,128)(2,1)S(1)}, u32[]{:S(2)}) %copy-start.4) | copy-done | bytes 524312
  55.6 7.4 %shard_map.103 = bf16[1024,1024]{1,0:T(8,128)(2,1)} custom-call(f32[1024,1024]{1,0:T(8,128)} %get-tuple-element.33.y_ref, bf16[1024,256]{1,0:T(8,128)(2,1)} %get-tuple-element.23.refs_2_.c_ref, f32[4,1024,4]{2,1,0:T(8,128)} %bitcast.33, f32[1024,8]{1,0:T(8,128)} %copy.32.info_ref.refs_6_, f32[8,1,1024]{2,1,0:T(1,128)} %get-tuple-element.34.prefix_ref, ...), custom_call_target="tpu_custom_call" | custom-call | tf_op jit(solution)/shard_map/pallas_call | solution.py:349
  (12 shorter events, 0.1 us)
Async XLA Ops:
  0.0 11.5 %collective-permute-start.1 = (bf16[2,1024,128]{2,1,0:T(8,128)(2,1)}, bf16[2,1024,128]{2,1,0:T(8,128)(2,1)S(1)}, u32[]{:S(2)}, u32[]{:S(2)}) collective-permute-start(bf16[2,1024,128]{2,1,0:T(8,128)(2,1)} %own_ref.1), channel_id=1, source_target_pairs={{0,1},{1,0},{2,3},{3,2},{4,5},{5,4},{6,7},{7,6},{8,9},{9,8},{10,11... | collective-permute-start | bytes 1572872 | tf_op jit(solution)/shard_map/ppermute | solution.py:26
  1.9 7.0 %collective-permute-start = (bf16[8,1280]{1,0:T(8,128)(2,1)S(1)}, bf16[8,1280]{1,0:T(8,128)(2,1)S(1)}, u32[]{:S(2)}, u32[]{:S(2)}) collective-permute-start(bf16[8,1280]{1,0:T(8,128)(2,1)S(1)} %pad_maximum_fusion), channel_id=1, source_target_pairs={{0,4},{4,8},{8,12},{1,5},{5,9},{9,13},{2,6},{6,10},{10,14},{3,7},{... | collective-permute-start | bytes 61448 | tf_op jit(solution)/shard_map/ppermute | solution.py:16
  8.0 15.7 %copy-start.6 = (f32[1024]{0:T(1024)}, f32[1024]{0:T(1024)S(1)}, u32[]{:S(2)}) copy-start(f32[1024]{0:T(1024)S(1)} %get-tuple-element.42) | copy-start | bytes 12292
  9.5 2.7 %copy-start.5 = (f32[2,13,128]{2,1,0:T(8,128)}, f32[2,13,128]{2,1,0:T(8,128)S(1)}, u32[]{:S(2)}) copy-start(f32[2,13,128]{2,1,0:T(8,128)S(1)} %pad_maximum_fusion.1.ownx_ref) | copy-start | bytes 39940
  9.5 2.0 %collective-permute-start.2 = (f32[2,13,128]{2,1,0:T(8,128)S(1)}, f32[2,13,128]{2,1,0:T(8,128)S(1)}, u32[]{:S(2)}, u32[]{:S(2)}) collective-permute-start(f32[2,13,128]{2,1,0:T(8,128)S(1)} %pad_maximum_fusion.1.ownx_ref), channel_id=1, source_target_pairs={{0,1},{1,0},{2,3},{3,2},{4,5},{5,4},{6,7},{7,6},{8,9},{9,8},{10,11... | collective-permute-start | bytes 39944 | tf_op jit(solution)/shard_map/ppermute | solution.py:26
  9.9 17.4 %copy-start.9 = (f32[16]{0:T(128)S(1)}, f32[16]{0:T(128)}, u32[]{:S(2)}) copy-start(f32[16]{0:T(128)} %param.18) | copy-start | bytes 196
  11.5 0.7 %copy-start.7 = (f32[2,13,128]{2,1,0:T(8,128)}, f32[2,13,128]{2,1,0:T(8,128)S(1)}, u32[]{:S(2)}) copy-start(f32[2,13,128]{2,1,0:T(8,128)S(1)} %collective-permute-done.2.otherx_ref) | copy-start | bytes 39940
  11.5 0.8 %copy-start.3 = (bf16[2,1024,128]{2,1,0:T(8,128)(2,1)}, bf16[2,1024,128]{2,1,0:T(8,128)(2,1)S(1)}, u32[]{:S(2)}) copy-start(bf16[2,1024,128]{2,1,0:T(8,128)(2,1)S(1)} %collective-permute-done.1.other_ref) | copy-start | bytes 1572868
  23.7 15.4 %collective-permute-start.3 = (bf16[256,1024]{1,0:T(8,128)(2,1)}, bf16[256,1024]{1,0:T(8,128)(2,1)S(1)}, u32[]{:S(2)}, u32[]{:S(2)}) collective-permute-start(bf16[256,1024]{1,0:T(8,128)(2,1)} %get-tuple-element.27), channel_id=1, source_target_pairs={{0,4},{4,8},{8,12},{1,5},{5,9},{9,13},{2,6},{6,10},{10,14},{3,7},{... | collective-permute-start | bytes 1572872 | tf_op jit(solution)/shard_map/ppermute | solution.py:16
  28.0 11.1 %copy-start.2 = (f32[256,1024]{1,0:T(8,128)S(1)}, f32[256,1024]{1,0:T(8,128)}, u32[]{:S(2)}) copy-start(f32[256,1024]{1,0:T(8,128)} %get-tuple-element.36) | copy-start | bytes 3145732
  28.0 11.1 %copy-start.8 = (f32[1,1024]{1,0:T(1,128)S(1)}, f32[1,1024]{1,0:T(1,128)}, u32[]{:S(2)}) copy-start(f32[1,1024]{1,0:T(1,128)} %get-tuple-element.35) | copy-start | bytes 12292
  36.5 7.1 %copy-start = (f32[1024,16]{1,0:T(8,128)S(1)}, f32[1024,16]{1,0:T(8,128)}, u32[]{:S(2)}) copy-start(f32[1024,16]{1,0:T(8,128)} %get-tuple-element.24.refs_3_) | copy-start | bytes 196612
  39.2 6.7 %copy-start.1 = (bf16[256,1024]{1,0:T(8,128)(2,1)}, bf16[256,1024]{1,0:T(8,128)(2,1)S(1)}, u32[]{:S(2)}) copy-start(bf16[256,1024]{1,0:T(8,128)(2,1)S(1)} %collective-permute-done.3.refs_10_) | copy-start | bytes 1572868
  39.3 15.4 %collective-permute-start.4 = (bf16[256,1024]{1,0:T(8,128)(2,1)S(1)}, bf16[256,1024]{1,0:T(8,128)(2,1)S(1)}, u32[]{:S(2)}, u32[]{:S(2)}) collective-permute-start(bf16[256,1024]{1,0:T(8,128)(2,1)S(1)} %add_convert_fusion), channel_id=1, source_target_pairs={{0,4},{4,8},{8,12},{1,5},{5,9},{9,13},{2,6},{6,10},{10,14},{3,7},{... | collective-permute-start | bytes 1572872 | tf_op jit(solution)/shard_map/ppermute | solution.py:16
  54.8 0.8 %copy-start.4 = (bf16[256,1024]{1,0:T(8,128)(2,1)}, bf16[256,1024]{1,0:T(8,128)(2,1)S(1)}, u32[]{:S(2)}) copy-start(bf16[256,1024]{1,0:T(8,128)(2,1)S(1)} %collective-permute-done.4.ein_ref) | copy-start | bytes 1572868

commit v13 on v12

--- a/solution.py
+++ b/solution.py
@@ -8,6 +8,7 @@
 from jax.sharding import PartitionSpec as P
 
 BLOCK = 128
+CORRECT_TILE = 256
 
 
 def shifted(value, axis, steps):
@@ -129,8 +130,8 @@
 
 def state_kernel(head_width, x_ref, tail_ref, wconv_ref, bias_ref, own_ref, other_ref, ownx_ref,
                  otherx_ref, flag_ref, dt_ref, rate_ref, info_ref, state_ref, l_ref, dtt_ref,
-                 decay_ref, total_ref, xc_ref, bo_ref, co_ref, sent_ref, prefix_ref, prev_ref,
-                 bcprev_ref):
+                 decay_ref, total_ref, xc_ref, bo_ref, co_ref, sent_ref, prefix_ref, ltile_ref,
+                 prev_ref, bcprev_ref):
     blk = pl.program_id(0)
 
     @pl.when(blk == 0)
@@ -182,6 +183,9 @@
     dt_small = cum[BLOCK:]
     l_ref[...] = l_small
     dtt_ref[...] = dt_small
+    tile_heads = ltile_ref.shape[2]
+    for tile in range(ltile_ref.shape[0]):
+        ltile_ref[tile] = l_small[:, tile * tile_heads : (tile + 1) * tile_heads]
     seg_col = info[:, 0:1]
     end_col = (seg_col == seg_col[BLOCK - 1 : BLOCK, :]).astype(jnp.float32)
     decay_x = expand_heads(
@@ -211,6 +215,8 @@
     half = own_raw.shape[2]
     n_size = 2 * half
     block_count = rows // BLOCK
+    tiles = width // CORRECT_TILE
+    tile_heads = head_count // tiles
     row_block = lambda cols: pl.BlockSpec((BLOCK, cols), lambda b: (b, 0))
     whole = lambda shape: pl.BlockSpec(shape, lambda b: (0,) * len(shape))
     return pl.pallas_call(
@@ -225,7 +231,8 @@
         out_specs=[whole((n_size, width)), row_block(head_count), row_block(head_count),
                    pl.BlockSpec((1, 1, width), lambda b: (b, 0, 0)), whole((1, width)),
                    row_block(width), row_block(n_size), row_block(n_size),
-                   whole((n_size, width)), pl.BlockSpec((1, 1, width), lambda b: (b, 0, 0))],
+                   whole((n_size, width)), pl.BlockSpec((1, 1, width), lambda b: (b, 0, 0)),
+                   pl.BlockSpec((tiles, BLOCK, tile_heads), lambda b: (0, b, 0))],
         out_shape=[jax.ShapeDtypeStruct((n_size, width), jnp.float32),
                    jax.ShapeDtypeStruct((rows, head_count), jnp.float32),
                    jax.ShapeDtypeStruct((rows, head_count), jnp.float32),
@@ -235,7 +242,8 @@
                    jax.ShapeDtypeStruct((rows, n_size), jnp.bfloat16),
                    jax.ShapeDtypeStruct((rows, n_size), jnp.bfloat16),
                    jax.ShapeDtypeStruct((n_size, width), jnp.bfloat16),
-                   jax.ShapeDtypeStruct((block_count, 1, width), jnp.float32)],
+                   jax.ShapeDtypeStruct((block_count, 1, width), jnp.float32),
+                   jax.ShapeDtypeStruct((tiles, rows, tile_heads), jnp.float32)],
         scratch_shapes=[pltpu.VMEM((8, width), jnp.float32),
                         pltpu.VMEM((2, 2, 8, half), jnp.float32)],
         compiler_params=pltpu.CompilerParams(dimension_semantics=("arbitrary",)),
@@ -249,7 +257,7 @@
          end_ref, state_ref) = refs
     else:
         (x_ref, b_ref, c_ref, l_ref, dt_ref, segr_ref, info_ref, decay_ref, skip_ref, init_ref,
-         after_ref, buf_ref, out_ref, end_ref, state_ref) = refs
+         after_ref, out_ref, end_ref, state_ref) = refs
     blk = pl.program_id(0)
 
     @pl.when(blk == 0)
@@ -295,7 +303,7 @@
 
 
 def run_partial(first, count, x, b_full, c_full, l_t, dt_t, seg_row, info, decay_x, skip_x,
-                init=None, after=None, buf=None):
+                init=None, after=None):
     rows, width = x.shape
     head_count = l_t.shape[1]
     n_size = b_full.shape[1]
@@ -307,49 +315,45 @@
                 row_block(info.shape[1]), pl.BlockSpec((1, 1, width), lambda b: (b + first, 0, 0)),
                 whole((1, width))]
     args = [x, b_full, c_full, l_t, dt_t, seg_row, info, decay_x, skip_x]
-    aliases = {}
     if not from_zero:
-        any_spec = pl.BlockSpec(memory_space=pl.ANY)
-        in_specs += [whole((n_size, width)), any_spec, any_spec]
-        args += [init, after, buf]
-        aliases = {len(args) - 1: 0}
+        in_specs += [whole((n_size, width)), pl.BlockSpec(memory_space=pl.ANY)]
+        args += [init, after]
     return pl.pallas_call(
         functools.partial(partial_kernel, width // head_count, from_zero),
         grid=(count,),
         in_specs=in_specs,
-        out_specs=[row_block(width), whole((n_size, width))],
-        out_shape=[jax.ShapeDtypeStruct((rows, width), jnp.float32),
+        out_specs=[pl.BlockSpec((BLOCK, width), lambda b: (b, 0)), whole((n_size, width))],
+        out_shape=[jax.ShapeDtypeStruct((count * BLOCK, width), jnp.float32),
                    jax.ShapeDtypeStruct((n_size, width), jnp.float32)],
         scratch_shapes=[pltpu.VMEM((n_size, width), jnp.float32)],
-        input_output_aliases=aliases,
         compiler_params=pltpu.CompilerParams(dimension_semantics=("arbitrary",)),
     )(*args)
 
 
-def correct_kernel(head_width, y_ref, c_ref, l_ref, info_ref, prefix_ref, ein_ref, out_ref):
-    rows, cols = y_ref.shape
+def correct_kernel(head_width, y_ref, z_ref, c_ref, l_ref, info_ref, prefix_ref, ein_ref, out_ref):
+    rows, cols = out_ref.shape
     rising = expand_heads(jnp.exp(l_ref[0]), head_width)
     blocks = prefix_ref.shape[0]
     prefix = jnp.broadcast_to(prefix_ref[...], (blocks, BLOCK, cols)).reshape(rows, cols)
     carried = jnp.dot(c_ref[...], ein_ref[...], preferred_element_type=jnp.float32)
     factor = rising * info_ref[...][:, 1:2] * prefix
-    out_ref[...] = (y_ref[...] + carried * factor).astype(jnp.bfloat16)
-
-
-def run_correct(partial, c_full, l_t, info, prefix_x, entering):
-    rows, width = partial.shape
-    head_count = l_t.shape[1]
-    head_width = width // head_count
+    partial = jnp.concatenate([y_ref[...], z_ref[...]], 0)
+    out_ref[...] = (partial + carried * factor).astype(jnp.bfloat16)
+
+
+def run_correct(first, second, c_full, l_tiles, info, prefix_x, entering):
+    rows = first.shape[0] + second.shape[0]
+    width = first.shape[1]
+    tiles, _, heads_per = l_tiles.shape
+    tile = CORRECT_TILE
+    head_width = tile // heads_per
     n_size = c_full.shape[1]
-    tile = 256
-    tiles = width // tile
-    heads_per = tile // head_width
-    l_tiles = jnp.transpose(l_t.reshape(rows, tiles, heads_per), (1, 0, 2))
     block_count = prefix_x.shape[0]
     return pl.pallas_call(
         functools.partial(correct_kernel, head_width),
         grid=(tiles,),
-        in_specs=[pl.BlockSpec((rows, tile), lambda j: (0, j)),
+        in_specs=[pl.BlockSpec((first.shape[0], tile), lambda j: (0, j)),
+                  pl.BlockSpec((second.shape[0], tile), lambda j: (0, j)),
                   pl.BlockSpec((rows, n_size), lambda j: (0, 0)),
                   pl.BlockSpec((1, rows, heads_per), lambda j: (j, 0, 0)),
                   pl.BlockSpec((rows, info.shape[1]), lambda j: (0, 0)),
@@ -358,7 +362,7 @@
         out_specs=pl.BlockSpec((rows, tile), lambda j: (0, j)),
         out_shape=jax.ShapeDtypeStruct((rows, width), jnp.bfloat16),
         compiler_params=pltpu.CompilerParams(dimension_semantics=("arbitrary",)),
-    )(partial, c_full, l_tiles, info, prefix_x, entering)
+    )(first, second, c_full, l_tiles, info, prefix_x, entering)
 
 
 def run_blocks(with_y, x, b_full, c_full, l_t, dt_t, seg_row, seg_col, entry_col, decay_x,
@@ -449,7 +453,7 @@
     )
 
     (local_end, l_t, dt_t, decay_x, total_decay, inner_conv, b_full, c_full, end_sent,
-     prefix_x) = run_state(
+     prefix_x, l_tiles) = run_state(
         inner_input, tail8, conv_inner, bias_inner.reshape(1, -1), state_input, partner_raw,
         extra, partner_extra, flag,
         step_size, decay_rate.reshape(1, -1), info
@@ -470,11 +474,10 @@
     first_hop = incoming
     for step_num in range(1, hops):
         incoming = relay(step_num, incoming)
-    partial, _ = run_partial(
-        half_blocks, block_count - half_blocks, *operands, init=middle, after=first_hop,
-        buf=partial
-    )
-    return run_correct(partial, c_full, l_t, info, prefix_x, incoming)
+    second, _ = run_partial(
+        half_blocks, block_count - half_blocks, *operands, init=middle, after=first_hop
+    )
+    return run_correct(partial, second, c_full, l_tiles, info, prefix_x, incoming)
 
 
 def solution(mesh):

time: 63.6 us -> 63.5 us (level)
  local copies, waits for them, and re-layouts: 7.73 us -> 5.6 us
  waiting for transfers between devices: 2.61 us -> 4.46 us
    reshape x2 -> x0, local copies, waits for them, and re-layouts: 2.01 us -> none  [run_correct(): l_tiles = jnp.transpose(l_t.reshape(rows, tiles, heads_per), (1, 0, 2))]
    ppermute x3, waiting for transfers between devices: 2.6 us -> 4.45 us  [shifted(): lax.ppermute(value, axis, [(source, source + steps) for source in range(i...]
  transfers between devices with their start and end apart: 5 -> 5, of which waited for: 1 -> 2; matrix products, arithmetic and copies ran while one was open for 15% -> 11% of each run, Pallas kernels for 28% -> 28%
where the time goes in v13:
time: 63.5 us; the launch traced here: 62.8 us
  Pallas kernels  36.4 us (57%)
  starting transfers between devices  13 us (20%)
  local copies, waits for them, and re-layouts  5.6 us (9%)
  waiting for transfers between devices  4.46 us (7%)
  other arithmetic  3.27 us (5%)
    pallas_call x2, Pallas kernels, run_partial(): pl.pallas_call(functools.partial(partial_kernel, width // head_count, fro...  17.4 us
    ppermute x3, starting transfers between devices, shifted(): lax.ppermute(value, axis, [(source, source + steps) for source in range(i...  12.3 us
    pallas_call x1, Pallas kernels, run_state(): pl.pallas_call(functools.partial(state_kernel, width // head_count), grid...  11.7 us
    pallas_call x1, Pallas kernels, run_correct(): pl.pallas_call(functools.partial(correct_kernel, head_width), grid=(tiles...  7.24 us
    ppermute x3, waiting for transfers between devices, shifted(): lax.ppermute(value, axis, [(source, source + steps) for source in range(i...  4.45 us
  transfers between devices with their start and end apart: 5, of which 2 were waited for; matrix products, arithmetic and copies ran while one was open for 11% of the time, Pallas kernels for 28%

profile of v13, /device:TPU:0, one launch (start us, length us, event | category | flops | bytes accessed | tf_op | source)
XLA Modules:
  0.0 62.8 jit_solution(11639659719894639930)
XLA Ops:
  0.0 0.5 collective-permute-start.1
  0.5 0.7 %slice_bitcast_fusion.1 = bf16[8,256]{1,0:T(8,128)(2,1)S(1)} fusion(bf16[2,1024,128]{2,1,0:T(8,128)(2,1)} %own_ref.1), kind=kLoop, calls=%fused_computation.12 | loop fusion | bytes 8192 | tf_op jit(solution)/shard_map/reshape | solution.py:426
  1.1 0.7 %slice.30 = bf16[8,1024]{1,0:T(8,128)(2,1)S(1)} slice(bf16[1024,1024]{1,0:T(8,128)(2,1)} %x_ref.1), slice={[1016:1024], [0:1024]} | slice | bytes 32768 | tf_op jit(solution)/shard_map/slice | solution.py:426
  1.9 4.5 %collective-permute-start = (bf16[8,1280]{1,0:T(8,128)(2,1)S(1)}, bf16[8,1280]{1,0:T(8,128)(2,1)S(1)}, u32[]{:S(2)}, u32[]{:S(2)}) collective-permute-start(bf16[8,1280]{1,0:T(8,128)(2,1)S(1)} %pad_maximum_fusion), channel_id=1, source_target_pairs={{0,4},{4,8},{8,12},{1,5},{5,9},{9,13},{2,6},{6,10},{10,14},{3,7},{... | collective-permute-start | bytes 61448 | tf_op jit(solution)/shard_map/ppermute | solution.py:17
  6.3 0.8 %reduce-window.9 = s32[3,1]{0,1:T(1,128)S(1)} reduce-window(s32[3,1]{0,1:T(1,128)} %bitcast.41, s32[]{:T(128)} %constant.27.clone.1), window={size=3x1 pad=2_0x0_0}, to_apply=%region_0.0 | reduce-window | flops 6 | bytes 28 | tf_op jit(solution)/shard_map/reduce-window.4
  7.2 0.7 %bitcast_subtract_fusion = s32[3]{0:T(128)S(1)} fusion(s32[3]{0:T(128)} %param.19, s32[3,1]{0,1:T(1,128)S(1)} %reduce-window.9), kind=kLoop, calls=%fused_computation.19 | loop fusion | flops 3 | bytes 36 | tf_op jit(solution)/shard_map/sub | solution.py:31
  7.8 0.1 convert_reduce_fusion
  7.9 0.1 slice_bitcast_fusion.2
  8.0 0.0 copy-start.5
  8.0 0.1 slice_reduce_fusion
  8.1 0.7 %convert_element_type.37 = f32[2,4,128]{2,1,0:T(4,128)S(1)} convert(bf16[2,4,128]{2,1,0:T(4,128)(2,1)} %param.14) | non-fusion elementwise | flops 1024 | bytes 6144 | tf_op jit(solution)/shard_map/convert_element_type | solution.py:433
  8.8 0.0 collective-permute-done
  8.8 0.7 %pad_maximum_fusion.1.ownx_ref = f32[2,13,128]{2,1,0:T(8,128)S(1)} fusion(f32[2,1,128]{2,1,0:T(1,128)} %bitcast.39, f32[2,4,128]{2,1,0:T(4,128)S(1)} %convert_element_type.37, f32[2,8,128]{2,1,0:T(8,128)S(1)} %convert_bitcast_fusion), kind=kLoop, calls=%fused_computation.3 | loop fusion | flops 6656 | bytes 26624 | tf_op jit(solution)/shard_map/concatenate | solution.py:431
  9.5 0.0 copy-start.4
  9.5 0.2 collective-permute-start.2
  9.7 0.1 fusion.2
  9.8 0.1 stack.43
  9.9 0.0 copy-start.8
  9.9 1.0 %copy.25.info_ref.refs_6_ = f32[1024,8]{1,0:T(8,128)} copy(f32[1024,8]{0,1:T(8,128)S(1)} %stack.43) | data formatting | bytes 65536 | tf_op jit(solution)/shard_map/stack | solution.py:448
  10.9 0.6 slice.39.tail_ref
  11.5 0.0 collective-permute-done.2.otherx_ref
  11.6 0.0 copy-start.6
  11.6 0.0 collective-permute-done.1.other_ref
  11.6 0.0 copy-start.2
  11.6 0.6 broadcast_in_dim.12.flag_ref
  12.2 0.0 copy-done.4
  12.2 0.0 copy-done.6
  12.2 0.2 copy-done.2
  12.4 11.7 %shard_map.100 = (f32[256,1024]{1,0:T(8,128)}, f32[1024,16]{1,0:T(8,128)}, f32[1024,16]{1,0:T(8,128)}, f32[8,1,1024]{2,1,0:T(1,128)}, f32[1,1024]{1,0:T(1,128)},...) custom-call(bf16[1024,1024]{1,0:T(8,128)(2,1)} %x_ref.1, ...), custom_call_target="tpu_custom_call" | custom-call | tf_op jit(solution)/shard_map/pallas_call | solution.py:222
  24.1 0.0 copy-done.5
  24.1 3.5 %collective-permute-start.3 = (bf16[256,1024]{1,0:T(8,128)(2,1)}, bf16[256,1024]{1,0:T(8,128)(2,1)S(1)}, u32[]{:S(2)}, u32[]{:S(2)}) collective-permute-start(bf16[256,1024]{1,0:T(8,128)(2,1)} %get-tuple-element.22), channel_id=1, source_target_pairs={{0,4},{4,8},{8,12},{1,5},{5,9},{9,13},{2,6},{6,10},{10,14},{3,7},{... | collective-permute-start | bytes 1572872 | tf_op jit(solution)/shard_map/ppermute | solution.py:17
  27.6 0.0 copy-done.8
  27.6 0.1 broadcast_in_dim.13
  27.7 0.7 %reshape_reshape.3.refs_8_ = f32[1,1024]{1,0:T(1,128)} reshape(f32[16,64]{1,0:T(8,128)S(1)} %broadcast_in_dim.13) | data formatting | bytes 8192 | tf_op jit(solution)/shard_map/reshape;reshape | solution.py:441
  28.3 0.0 copy-start.1
  28.3 0.0 copy-start.7
  28.4 8.5 %shard_map.101 = (f32[512,1024]{1,0:T(8,128)}, f32[256,1024]{1,0:T(8,128)}) custom-call(bf16[1024,1024]{1,0:T(8,128)(2,1)} %get-tuple-element.23.refs_0_, bf16[1024,256]{1,0:T(8,128)(2,1)} %get-tuple-element.24.refs_1_, bf16[1024,256]{1,0:T(8,128)(2,1)} %get-tuple-element.25.refs_2_.c_ref, f32[1024,16]{1,0:T(8,128)} %get-tuple-element.26.refs_3_, ...), custom_call_target="tpu_custom_call" | custom-call | tf_op jit(solution)/shard_map/pallas_call | solution.py:321
  36.8 2.7 %collective-permute-done.3.refs_10_ = bf16[256,1024]{1,0:T(8,128)(2,1)S(1)} collective-permute-done((bf16[256,1024]{1,0:T(8,128)(2,1)}, bf16[256,1024]{1,0:T(8,128)(2,1)S(1)}, u32[]{:S(2)}, u32[]{:S(2)}) %collective-permute-start.3) | collective-permute-done | bytes 524320 | tf_op jit(solution)/shard_map/ppermute | solution.py:17
  39.5 0.0 copy-start
  39.5 0.0 copy-done.1
  39.5 0.0 copy-done.7
  39.5 0.2 add_convert_fusion
  39.7 4.3 %collective-permute-start.4 = (bf16[256,1024]{1,0:T(8,128)(2,1)S(1)}, bf16[256,1024]{1,0:T(8,128)(2,1)S(1)}, u32[]{:S(2)}, u32[]{:S(2)}) collective-permute-start(bf16[256,1024]{1,0:T(8,128)(2,1)S(1)} %add_convert_fusion), channel_id=1, source_target_pairs={{0,4},{4,8},{8,12},{1,5},{5,9},{9,13},{2,6},{6,10},{10,14},{3,7},{... | collective-permute-start | bytes 1572872 | tf_op jit(solution)/shard_map/ppermute | solution.py:17
  44.0 0.0 copy-done
  44.0 9.0 %shard_map.102 = (f32[512,1024]{1,0:T(8,128)}, f32[256,1024]{1,0:T(8,128)}) custom-call(bf16[1024,1024]{1,0:T(8,128)(2,1)} %get-tuple-element.23.refs_0_, bf16[1024,256]{1,0:T(8,128)(2,1)} %get-tuple-element.24.refs_1_, bf16[1024,256]{1,0:T(8,128)(2,1)} %get-tuple-element.25.refs_2_.c_ref, f32[1024,16]{1,0:T(8,128)} %get-tuple-element.26.refs_3_, ...), custom_call_target="tpu_custom_call" | custom-call | tf_op jit(solution)/shard_map/pallas_call | solution.py:321
  53.0 1.8 %collective-permute-done.4.ein_ref = bf16[256,1024]{1,0:T(8,128)(2,1)S(1)} collective-permute-done((bf16[256,1024]{1,0:T(8,128)(2,1)S(1)}, bf16[256,1024]{1,0:T(8,128)(2,1)S(1)}, u32[]{:S(2)}, u32[]{:S(2)}) %collective-permute-start.4) | collective-permute-done | bytes 524320 | tf_op jit(solution)/shard_map/ppermute | solution.py:17
  54.8 0.8 %copy-done.3 = bf16[256,1024]{1,0:T(8,128)(2,1)} copy-done((bf16[256,1024]{1,0:T(8,128)(2,1)}, bf16[256,1024]{1,0:T(8,128)(2,1)S(1)}, u32[]{:S(2)}) %copy-start.3) | copy-done | bytes 524312
  55.6 7.2 %shard_map.103 = bf16[1024,1024]{1,0:T(8,128)(2,1)} custom-call(f32[512,1024]{1,0:T(8,128)} %get-tuple-element.31.y_ref, f32[512,1024]{1,0:T(8,128)} %get-tuple-element.34.z_ref, bf16[1024,256]{1,0:T(8,128)(2,1)} %get-tuple-element.25.refs_2_.c_ref, f32[4,1024,4]{2,1,0:T(8,128)} %get-tuple-element.35.l_ref, f32[1024,8]{1,0:T(8,128)} %copy.25.info_ref.refs_6_, ...), custom_call_target="tpu_custom_call" | custom-call | tf_op jit(solution)/shard_map/pallas_call | solution.py:352
  (7 shorter events, 0.0 us)
Async XLA Ops:
  0.0 11.6 %collective-permute-start.1 = (bf16[2,1024,128]{2,1,0:T(8,128)(2,1)}, bf16[2,1024,128]{2,1,0:T(8,128)(2,1)S(1)}, u32[]{:S(2)}, u32[]{:S(2)}) collective-permute-start(bf16[2,1024,128]{2,1,0:T(8,128)(2,1)} %own_ref.1), channel_id=1, source_target_pairs={{0,1},{1,0},{2,3},{3,2},{4,5},{5,4},{6,7},{7,6},{8,9},{9,8},{10,11... | collective-permute-start | bytes 1572872 | tf_op jit(solution)/shard_map/ppermute | solution.py:27
  1.9 7.0 %collective-permute-start = (bf16[8,1280]{1,0:T(8,128)(2,1)S(1)}, bf16[8,1280]{1,0:T(8,128)(2,1)S(1)}, u32[]{:S(2)}, u32[]{:S(2)}) collective-permute-start(bf16[8,1280]{1,0:T(8,128)(2,1)S(1)} %pad_maximum_fusion), channel_id=1, source_target_pairs={{0,4},{4,8},{8,12},{1,5},{5,9},{9,13},{2,6},{6,10},{10,14},{3,7},{... | collective-permute-start | bytes 61448 | tf_op jit(solution)/shard_map/ppermute | solution.py:17
  8.0 16.1 %copy-start.5 = (f32[1024]{0:T(1024)}, f32[1024]{0:T(1024)S(1)}, u32[]{:S(2)}) copy-start(f32[1024]{0:T(1024)S(1)} %get-tuple-element.44) | copy-start | bytes 12292
  9.5 2.6 %copy-start.4 = (f32[2,13,128]{2,1,0:T(8,128)}, f32[2,13,128]{2,1,0:T(8,128)S(1)}, u32[]{:S(2)}) copy-start(f32[2,13,128]{2,1,0:T(8,128)S(1)} %pad_maximum_fusion.1.ownx_ref) | copy-start | bytes 39940
  9.5 2.0 %collective-permute-start.2 = (f32[2,13,128]{2,1,0:T(8,128)S(1)}, f32[2,13,128]{2,1,0:T(8,128)S(1)}, u32[]{:S(2)}, u32[]{:S(2)}) collective-permute-start(f32[2,13,128]{2,1,0:T(8,128)S(1)} %pad_maximum_fusion.1.ownx_ref), channel_id=1, source_target_pairs={{0,1},{1,0},{2,3},{3,2},{4,5},{5,4},{6,7},{7,6},{8,9},{9,8},{10,11... | collective-permute-start | bytes 39944 | tf_op jit(solution)/shard_map/ppermute | solution.py:27
  9.9 17.7 %copy-start.8 = (f32[16]{0:T(128)S(1)}, f32[16]{0:T(128)}, u32[]{:S(2)}) copy-start(f32[16]{0:T(128)} %param.18) | copy-start | bytes 196
  11.6 0.6 copy-start.6
  11.6 0.8 %copy-start.2 = (bf16[2,1024,128]{2,1,0:T(8,128)(2,1)}, bf16[2,1024,128]{2,1,0:T(8,128)(2,1)S(1)}, u32[]{:S(2)}) copy-start(bf16[2,1024,128]{2,1,0:T(8,128)(2,1)S(1)} %collective-permute-done.1.other_ref) | copy-start | bytes 1572868
  24.1 15.4 %collective-permute-start.3 = (bf16[256,1024]{1,0:T(8,128)(2,1)}, bf16[256,1024]{1,0:T(8,128)(2,1)S(1)}, u32[]{:S(2)}, u32[]{:S(2)}) collective-permute-start(bf16[256,1024]{1,0:T(8,128)(2,1)} %get-tuple-element.22), channel_id=1, source_target_pairs={{0,4},{4,8},{8,12},{1,5},{5,9},{9,13},{2,6},{6,10},{10,14},{3,7},{... | collective-permute-start | bytes 1572872 | tf_op jit(solution)/shard_map/ppermute | solution.py:17
  28.3 11.2 %copy-start.1 = (f32[256,1024]{1,0:T(8,128)S(1)}, f32[256,1024]{1,0:T(8,128)}, u32[]{:S(2)}) copy-start(f32[256,1024]{1,0:T(8,128)} %get-tuple-element.38) | copy-start | bytes 3145732
  28.3 11.2 %copy-start.7 = (f32[1,1024]{1,0:T(1,128)S(1)}, f32[1,1024]{1,0:T(1,128)}, u32[]{:S(2)}) copy-start(f32[1,1024]{1,0:T(1,128)} %get-tuple-element.37) | copy-start | bytes 12292
  39.5 4.5 %copy-start = (bf16[256,1024]{1,0:T(8,128)(2,1)}, bf16[256,1024]{1,0:T(8,128)(2,1)S(1)}, u32[]{:S(2)}) copy-start(bf16[256,1024]{1,0:T(8,128)(2,1)S(1)} %collective-permute-done.3.refs_10_) | copy-start | bytes 1572868
  39.7 15.1 %collective-permute-start.4 = (bf16[256,1024]{1,0:T(8,128)(2,1)S(1)}, bf16[256,1024]{1,0:T(8,128)(2,1)S(1)}, u32[]{:S(2)}, u32[]{:S(2)}) collective-permute-start(bf16[256,1024]{1,0:T(8,128)(2,1)S(1)} %add_convert_fusion), channel_id=1, source_target_pairs={{0,4},{4,8},{8,12},{1,5},{5,9},{9,13},{2,6},{6,10},{10,14},{3,7},{... | collective-permute-start | bytes 1572872 | tf_op jit(solution)/shard_map/ppermute | solution.py:17
  54.8 0.8 %copy-start.3 = (bf16[256,1024]{1,0:T(8,128)(2,1)}, bf16[256,1024]{1,0:T(8,128)(2,1)S(1)}, u32[]{:S(2)}) copy-start(bf16[256,1024]{1,0:T(8,128)(2,1)S(1)} %collective-permute-done.4.ein_ref) | copy-start | bytes 1572868

commit v14 on v13

--- a/solution.py
+++ b/solution.py
@@ -129,16 +129,17 @@
 
 
 def state_kernel(head_width, x_ref, tail_ref, wconv_ref, bias_ref, own_ref, other_ref, ownx_ref,
-                 otherx_ref, flag_ref, dt_ref, rate_ref, info_ref, state_ref, l_ref, dtt_ref,
+                 otherx_ref, dt_ref, rate_ref, info_ref, state_ref, l_ref, dtt_ref,
                  decay_ref, total_ref, xc_ref, bo_ref, co_ref, sent_ref, prefix_ref, ltile_ref,
-                 prev_ref, bcprev_ref):
+                 prev_ref, bcprev_ref, small_ref):
     blk = pl.program_id(0)
 
     @pl.when(blk == 0)
     def _():
         state_ref[...] = jnp.zeros(state_ref.shape, jnp.float32)
         total_ref[...] = jnp.ones(total_ref.shape, jnp.float32)
-        prev_ref[...] = tail_ref[...].astype(jnp.float32)
+        prev_ref[...] = tail_ref[:, : x_ref.shape[1]].astype(jnp.float32)
+        small_ref[...] = jnp.ones(small_ref.shape, jnp.float32)
         bcprev_ref[0] = ownx_ref[:, 0:8, :]
         bcprev_ref[1] = otherx_ref[:, 0:8, :]
 
@@ -147,7 +148,7 @@
     xc = causal_conv(raw, prev_ref[...], wconv_ref[...].astype(jnp.float32), bias_ref[...], info)
     prev_ref[...] = raw[BLOCK - 8 :]
     xc_ref[...] = xc
-    lower = flag_ref[...][:, 0:1] > 0.5
+    lower = info_ref[0:1, 5:6] > 0.5
     convolved = []
     for which in range(2):
         halves = []
@@ -183,9 +184,6 @@
     dt_small = cum[BLOCK:]
     l_ref[...] = l_small
     dtt_ref[...] = dt_small
-    tile_heads = ltile_ref.shape[2]
-    for tile in range(ltile_ref.shape[0]):
-        ltile_ref[tile] = l_small[:, tile * tile_heads : (tile + 1) * tile_heads]
     seg_col = info[:, 0:1]
     end_col = (seg_col == seg_col[BLOCK - 1 : BLOCK, :]).astype(jnp.float32)
     decay_x = expand_heads(
@@ -194,6 +192,13 @@
     decay_ref[0] = decay_x
     prefix_ref[0] = total_ref[...]
     total_ref[...] = total_ref[...] * decay_x
+    carry = (jnp.exp(l_small) * info[:, 1:2]) * small_ref[...]
+    small_ref[...] = small_ref[...] * (
+        jnp.exp(l_small[BLOCK - 1 : BLOCK, :]) * info[BLOCK - 1 : BLOCK, 1:2]
+    )
+    tile_heads = ltile_ref.shape[2]
+    for tile in range(ltile_ref.shape[0]):
+        ltile_ref[tile] = carry[:, tile * tile_heads : (tile + 1) * tile_heads]
     ending = expand_heads(
         jnp.exp(l_small[BLOCK - 1 : BLOCK, :] - l_small) * dt_small * end_col, head_width
     )
@@ -208,7 +213,7 @@
         sent_ref[...] = new_state.astype(jnp.bfloat16)
 
 
-def run_state(x, tail8, wconv, bias_row, own_raw, other_raw, own_extra, other_extra, flag,
+def run_state(x, tails, wconv, bias_row, own_raw, other_raw, own_extra, other_extra,
               step_size, rate_row, info):
     rows, width = x.shape
     head_count = step_size.shape[0]
@@ -222,10 +227,10 @@
     return pl.pallas_call(
         functools.partial(state_kernel, width // head_count),
         grid=(block_count,),
-        in_specs=[row_block(width), whole((8, width)), whole((4, width)), whole((1, width)),
+        in_specs=[row_block(width), whole(tails.shape), whole((4, width)), whole((1, width)),
                   pl.BlockSpec((2, BLOCK, half), lambda b: (0, b, 0)),
                   pl.BlockSpec((2, BLOCK, half), lambda b: (0, b, 0)),
-                  whole(own_extra.shape), whole(own_extra.shape), whole(flag.shape),
+                  whole(own_extra.shape), whole(own_extra.shape),
                   pl.BlockSpec((head_count, BLOCK), lambda b: (0, b)),
                   whole((1, head_count)), row_block(info.shape[1])],
         out_specs=[whole((n_size, width)), row_block(head_count), row_block(head_count),
@@ -245,9 +250,10 @@
                    jax.ShapeDtypeStruct((block_count, 1, width), jnp.float32),
                    jax.ShapeDtypeStruct((tiles, rows, tile_heads), jnp.float32)],
         scratch_shapes=[pltpu.VMEM((8, width), jnp.float32),
-                        pltpu.VMEM((2, 2, 8, half), jnp.float32)],
+                        pltpu.VMEM((2, 2, 8, half), jnp.float32),
+                        pltpu.VMEM((1, head_count), jnp.float32)],
         compiler_params=pltpu.CompilerParams(dimension_semantics=("arbitrary",)),
-    )(x, tail8, wconv, bias_row, own_raw, other_raw, own_extra, other_extra, flag, step_size,
+    )(x, tails, wconv, bias_row, own_raw, other_raw, own_extra, other_extra, step_size,
       rate_row, info)
 
 
@@ -330,25 +336,20 @@
     )(*args)
 
 
-def correct_kernel(head_width, y_ref, z_ref, c_ref, l_ref, info_ref, prefix_ref, ein_ref, out_ref):
-    rows, cols = out_ref.shape
-    rising = expand_heads(jnp.exp(l_ref[0]), head_width)
-    blocks = prefix_ref.shape[0]
-    prefix = jnp.broadcast_to(prefix_ref[...], (blocks, BLOCK, cols)).reshape(rows, cols)
+def correct_kernel(head_width, y_ref, z_ref, c_ref, g_ref, ein_ref, out_ref):
+    factor = expand_heads(g_ref[0], head_width)
     carried = jnp.dot(c_ref[...], ein_ref[...], preferred_element_type=jnp.float32)
-    factor = rising * info_ref[...][:, 1:2] * prefix
     partial = jnp.concatenate([y_ref[...], z_ref[...]], 0)
     out_ref[...] = (partial + carried * factor).astype(jnp.bfloat16)
 
 
-def run_correct(first, second, c_full, l_tiles, info, prefix_x, entering):
+def run_correct(first, second, c_full, g_tiles, entering):
     rows = first.shape[0] + second.shape[0]
     width = first.shape[1]
-    tiles, _, heads_per = l_tiles.shape
+    tiles, _, heads_per = g_tiles.shape
     tile = CORRECT_TILE
     head_width = tile // heads_per
     n_size = c_full.shape[1]
-    block_count = prefix_x.shape[0]
     return pl.pallas_call(
         functools.partial(correct_kernel, head_width),
         grid=(tiles,),
@@ -356,13 +357,11 @@
                   pl.BlockSpec((second.shape[0], tile), lambda j: (0, j)),
                   pl.BlockSpec((rows, n_size), lambda j: (0, 0)),
                   pl.BlockSpec((1, rows, heads_per), lambda j: (j, 0, 0)),
-                  pl.BlockSpec((rows, info.shape[1]), lambda j: (0, 0)),
-                  pl.BlockSpec((block_count, 1, tile), lambda j: (0, 0, j)),
                   pl.BlockSpec((n_size, tile), lambda j: (0, j))],
         out_specs=pl.BlockSpec((rows, tile), lambda j: (0, j)),
         out_shape=jax.ShapeDtypeStruct((rows, width), jnp.bfloat16),
         compiler_params=pltpu.CompilerParams(dimension_semantics=("arbitrary",)),
-    )(first, second, c_full, l_tiles, info, prefix_x, entering)
+    )(first, second, c_full, g_tiles, entering)
 
 
 def run_blocks(with_y, x, b_full, c_full, l_t, dt_t, seg_row, seg_col, entry_col, decay_x,
@@ -426,7 +425,6 @@
         [inner_input[-8:], jnp.transpose(state_input[:, -8:], (1, 0, 2)).reshape(8, -1)], 1
     )
     tails = shifted(tails, "seq", 1)
-    tail8 = tails[:, :width]
     state_tail = tails[:, width:].reshape(8, 2, group_half)
     extra = jnp.concatenate(
         [jnp.transpose(state_tail, (1, 0, 2)).astype(jnp.float32),
@@ -435,7 +433,6 @@
     )
     partner_raw, partner_extra = from_partner((state_input, extra), "head", 0)
     lower_half = (lax.axis_index("head") % 2 == 0).astype(jnp.float32)
-    flag = jnp.full((1, 128), lower_half, jnp.float32)
     head_width = inner_input.shape[1] // head_count
     spread = lambda v: jnp.repeat(v, head_width, axis=-1)
     skip_x = spread(skip_gain).reshape(1, -1)
@@ -448,14 +445,15 @@
     info = jnp.stack(
         [own_seg.astype(jnp.float32), entry_col.astype(jnp.float32)]
         + [keep.astype(jnp.float32) for keep in keeps]
-        + [jnp.zeros((own_rows,), jnp.float32)] * 3,
+        + [jnp.zeros((own_rows,), jnp.float32), jnp.full((own_rows,), lower_half, jnp.float32),
+           jnp.zeros((own_rows,), jnp.float32)],
         1,
     )
 
     (local_end, l_t, dt_t, decay_x, total_decay, inner_conv, b_full, c_full, end_sent,
-     prefix_x, l_tiles) = run_state(
-        inner_input, tail8, conv_inner, bias_inner.reshape(1, -1), state_input, partner_raw,
-        extra, partner_extra, flag,
+     prefix_x, g_tiles) = run_state(
+        inner_input, tails, conv_inner, bias_inner.reshape(1, -1), state_input, partner_raw,
+        extra, partner_extra,
         step_size, decay_rate.reshape(1, -1), info
     )
 
@@ -477,7 +475,7 @@
     second, _ = run_partial(
         half_blocks, block_count - half_blocks, *operands, init=middle, after=first_hop
     )
-    return run_correct(partial, second, c_full, l_tiles, info, prefix_x, incoming)
+    return run_correct(partial, second, c_full, g_tiles, incoming)
 
 
 def solution(mesh):

time: 63.5 us -> 62.2 us (0.980)
  Pallas kernels: 36.4 us -> 35.7 us
    pallas_call x1, Pallas kernels: 7.24 us -> 6.46 us  [run_correct(): pl.pallas_call(functools.partial(correct_kernel, head_width), grid=(tiles...]
    unnamed x18 -> x20, local copies, waits for them, and re-layouts: 1.05 us -> 1.62 us
where the time goes in v14:
time: 62.2 us; the launch traced here: 61.5 us
  Pallas kernels  35.7 us (57%)
  starting transfers between devices  13 us (21%)
  local copies, waits for them, and re-layouts  4.97 us (8%)
  waiting for transfers between devices  4.44 us (7%)
  other arithmetic  3.27 us (5%)
    pallas_call x2, Pallas kernels, run_partial(): pl.pallas_call(functools.partial(partial_kernel, width // head_count, fro...  17.5 us
    ppermute x3, starting transfers between devices, shifted(): lax.ppermute(value, axis, [(source, source + steps) for source in range(i...  12.3 us
    pallas_call x1, Pallas kernels, run_state(): pl.pallas_call(functools.partial(state_kernel, width // head_count), grid...  11.8 us
    pallas_call x1, Pallas kernels, run_correct(): pl.pallas_call(functools.partial(correct_kernel, head_width), grid=(tiles...  6.46 us
    ppermute x3, waiting for transfers between devices, shifted(): lax.ppermute(value, axis, [(source, source + steps) for source in range(i...  4.44 us
    unnamed x20, local copies, waits for them, and re-layouts  1.62 us
  transfers between devices with their start and end apart: 5, of which 2 were waited for; matrix products, arithmetic and copies ran while one was open for 11% of the time, Pallas kernels for 28%

profile of v14, /device:TPU:0, one launch (start us, length us, event | category | flops | bytes accessed | tf_op | source)
XLA Modules:
  0.0 61.5 jit_solution(12224029191599055205)
XLA Ops:
  0.0 0.5 collective-permute-start.1
  0.5 0.7 %slice_bitcast_fusion.1 = bf16[8,256]{1,0:T(8,128)(2,1)S(1)} fusion(bf16[2,1024,128]{2,1,0:T(8,128)(2,1)} %own_ref.1), kind=kLoop, calls=%fused_computation.12 | loop fusion | bytes 8192 | tf_op jit(solution)/shard_map/reshape | solution.py:425
  1.1 0.7 %slice.27 = bf16[8,1024]{1,0:T(8,128)(2,1)S(1)} slice(bf16[1024,1024]{1,0:T(8,128)(2,1)} %x_ref.1), slice={[1016:1024], [0:1024]} | slice | bytes 32768 | tf_op jit(solution)/shard_map/slice | solution.py:425
  1.9 4.5 %collective-permute-start = (bf16[8,1280]{1,0:T(8,128)(2,1)S(1)}, bf16[8,1280]{1,0:T(8,128)(2,1)S(1)}, u32[]{:S(2)}, u32[]{:S(2)}) collective-permute-start(bf16[8,1280]{1,0:T(8,128)(2,1)S(1)} %pad_maximum_fusion), channel_id=1, source_target_pairs={{0,4},{4,8},{8,12},{1,5},{5,9},{9,13},{2,6},{6,10},{10,14},{3,7},{... | collective-permute-start | bytes 61448 | tf_op jit(solution)/shard_map/ppermute | solution.py:17
  6.3 0.8 %reduce-window.9 = s32[3,1]{0,1:T(1,128)S(1)} reduce-window(s32[3,1]{0,1:T(1,128)} %bitcast.41, s32[]{:T(128)} %constant.25.clone.1), window={size=3x1 pad=2_0x0_0}, to_apply=%region_0.0 | reduce-window | flops 6 | bytes 28 | tf_op jit(solution)/shard_map/reduce-window.4
  7.2 0.7 %bitcast_subtract_fusion = s32[3]{0:T(128)S(1)} fusion(s32[3]{0:T(128)} %param.19, s32[3,1]{0,1:T(1,128)S(1)} %reduce-window.9), kind=kLoop, calls=%fused_computation.19 | loop fusion | flops 3 | bytes 36 | tf_op jit(solution)/shard_map/sub | solution.py:31
  7.8 0.1 convert_reduce_fusion
  7.9 0.1 slice_bitcast_fusion.2
  8.0 0.0 copy-start.5
  8.0 0.1 slice_reduce_fusion
  8.1 0.7 %convert_element_type.37 = f32[2,4,128]{2,1,0:T(4,128)S(1)} convert(bf16[2,4,128]{2,1,0:T(4,128)(2,1)} %param.14) | non-fusion elementwise | flops 1024 | bytes 6144 | tf_op jit(solution)/shard_map/convert_element_type | solution.py:431
  8.8 0.0 collective-permute-done.tail_ref
  8.8 0.0 copy-start.6
  8.8 0.7 %pad_maximum_fusion.1.ownx_ref = f32[2,13,128]{2,1,0:T(8,128)S(1)} fusion(f32[2,1,128]{2,1,0:T(1,128)} %bitcast.39, f32[2,4,128]{2,1,0:T(4,128)S(1)} %convert_element_type.37, f32[2,8,128]{2,1,0:T(8,128)S(1)} %convert_bitcast_fusion), kind=kLoop, calls=%fused_computation.3 | loop fusion | flops 6656 | bytes 26624 | tf_op jit(solution)/shard_map/concatenate | solution.py:429
  9.5 0.0 copy-start.4
  9.5 0.2 collective-permute-start.2
  9.8 0.1 fusion.2
  9.8 0.1 stack.39
  9.9 0.0 copy-start.9
  9.9 1.0 %copy.24.info_ref.refs_6_ = f32[1024,8]{1,0:T(8,128)} copy(f32[1024,8]{0,1:T(8,128)S(1)} %stack.39) | data formatting | bytes 65536 | tf_op jit(solution)/shard_map/stack | solution.py:445
  10.9 0.0 collective-permute-done.2.otherx_ref
  10.9 0.0 copy-start.7
  11.0 0.0 collective-permute-done.1.other_ref
  11.0 0.0 copy-start.3
  11.0 0.0 copy-done.6
  11.0 0.0 copy-done.4
  11.0 0.6 copy-done.7
  11.5 0.2 copy-done.3
  11.8 11.8 %shard_map.100 = (f32[256,1024]{1,0:T(8,128)}, f32[1024,16]{1,0:T(8,128)}, f32[1024,16]{1,0:T(8,128)}, f32[8,1,1024]{2,1,0:T(1,128)}, f32[1,1024]{1,0:T(1,128)},...) custom-call(bf16[1024,1024]{1,0:T(8,128)(2,1)} %x_ref.1, ...), custom_call_target="tpu_custom_call" | custom-call | tf_op jit(solution)/shard_map/pallas_call | solution.py:227
  23.5 0.0 copy-done.5
  23.6 3.5 %collective-permute-start.3 = (bf16[256,1024]{1,0:T(8,128)(2,1)}, bf16[256,1024]{1,0:T(8,128)(2,1)S(1)}, u32[]{:S(2)}, u32[]{:S(2)}) collective-permute-start(bf16[256,1024]{1,0:T(8,128)(2,1)} %get-tuple-element.21), channel_id=1, source_target_pairs={{0,4},{4,8},{8,12},{1,5},{5,9},{9,13},{2,6},{6,10},{10,14},{3,7},{... | collective-permute-start | bytes 1572872 | tf_op jit(solution)/shard_map/ppermute | solution.py:17
  27.1 0.0 copy-done.9
  27.1 0.1 broadcast_in_dim.9
  27.2 0.7 %reshape_reshape.3.refs_8_ = f32[1,1024]{1,0:T(1,128)} reshape(f32[16,64]{1,0:T(8,128)S(1)} %broadcast_in_dim.9) | data formatting | bytes 8192 | tf_op jit(solution)/shard_map/reshape;reshape | solution.py:438
  27.8 0.0 copy-start.1
  27.8 0.0 copy-start.8
  27.8 8.5 %shard_map.101 = (f32[512,1024]{1,0:T(8,128)}, f32[256,1024]{1,0:T(8,128)}) custom-call(bf16[1024,1024]{1,0:T(8,128)(2,1)} %get-tuple-element.22.refs_0_, bf16[1024,256]{1,0:T(8,128)(2,1)} %get-tuple-element.23.refs_1_, bf16[1024,256]{1,0:T(8,128)(2,1)} %get-tuple-element.24.refs_2_.c_ref, f32[1024,16]{1,0:T(8,128)} %get-tuple-element.25.refs_3_, ...), custom_call_target="tpu_custom_call" | custom-call | tf_op jit(solution)/shard_map/pallas_call | solution.py:327
  36.3 2.7 %collective-permute-done.3.refs_10_ = bf16[256,1024]{1,0:T(8,128)(2,1)S(1)} collective-permute-done((bf16[256,1024]{1,0:T(8,128)(2,1)}, bf16[256,1024]{1,0:T(8,128)(2,1)S(1)}, u32[]{:S(2)}, u32[]{:S(2)}) %collective-permute-start.3) | collective-permute-done | bytes 524320 | tf_op jit(solution)/shard_map/ppermute | solution.py:17
  39.0 0.0 copy-start
  39.0 0.0 copy-done.1
  39.0 0.0 copy-done.8
  39.0 0.2 add_convert_fusion
  39.1 4.3 %collective-permute-start.4 = (bf16[256,1024]{1,0:T(8,128)(2,1)S(1)}, bf16[256,1024]{1,0:T(8,128)(2,1)S(1)}, u32[]{:S(2)}, u32[]{:S(2)}) collective-permute-start(bf16[256,1024]{1,0:T(8,128)(2,1)S(1)} %add_convert_fusion), channel_id=1, source_target_pairs={{0,4},{4,8},{8,12},{1,5},{5,9},{9,13},{2,6},{6,10},{10,14},{3,7},{... | collective-permute-start | bytes 1572872 | tf_op jit(solution)/shard_map/ppermute | solution.py:17
  43.5 0.0 copy-done
  43.5 9.0 %shard_map.102 = (f32[512,1024]{1,0:T(8,128)}, f32[256,1024]{1,0:T(8,128)}) custom-call(bf16[1024,1024]{1,0:T(8,128)(2,1)} %get-tuple-element.22.refs_0_, bf16[1024,256]{1,0:T(8,128)(2,1)} %get-tuple-element.23.refs_1_, bf16[1024,256]{1,0:T(8,128)(2,1)} %get-tuple-element.24.refs_2_.c_ref, f32[1024,16]{1,0:T(8,128)} %get-tuple-element.25.refs_3_, ...), custom_call_target="tpu_custom_call" | custom-call | tf_op jit(solution)/shard_map/pallas_call | solution.py:327
  52.4 1.8 %collective-permute-done.4.ein_ref = bf16[256,1024]{1,0:T(8,128)(2,1)S(1)} collective-permute-done((bf16[256,1024]{1,0:T(8,128)(2,1)S(1)}, bf16[256,1024]{1,0:T(8,128)(2,1)S(1)}, u32[]{:S(2)}, u32[]{:S(2)}) %collective-permute-start.4) | collective-permute-done | bytes 524320 | tf_op jit(solution)/shard_map/ppermute | solution.py:17
  54.2 0.8 %copy-done.2 = bf16[256,1024]{1,0:T(8,128)(2,1)} copy-done((bf16[256,1024]{1,0:T(8,128)(2,1)}, bf16[256,1024]{1,0:T(8,128)(2,1)S(1)}, u32[]{:S(2)}) %copy-start.2) | copy-done | bytes 524312
  55.0 6.5 %shard_map.103 = bf16[1024,1024]{1,0:T(8,128)(2,1)} custom-call(f32[512,1024]{1,0:T(8,128)} %get-tuple-element.30.y_ref, f32[512,1024]{1,0:T(8,128)} %get-tuple-element.33.z_ref, bf16[1024,256]{1,0:T(8,128)(2,1)} %get-tuple-element.24.refs_2_.c_ref, f32[4,1024,4]{2,1,0:T(8,128)} %get-tuple-element.34.g_ref, bf16[256,1024]{1,0:T(8,128)(2,1)} %copy-done.2), custom_call_target="tpu_custom_call" | custom-call | tf_op jit(solution)/shard_map/pallas_call | solution.py:353
  (7 shorter events, 0.0 us)
Async XLA Ops:
  0.0 11.0 %collective-permute-start.1 = (bf16[2,1024,128]{2,1,0:T(8,128)(2,1)}, bf16[2,1024,128]{2,1,0:T(8,128)(2,1)S(1)}, u32[]{:S(2)}, u32[]{:S(2)}) collective-permute-start(bf16[2,1024,128]{2,1,0:T(8,128)(2,1)} %own_ref.1), channel_id=1, source_target_pairs={{0,1},{1,0},{2,3},{3,2},{4,5},{5,4},{6,7},{7,6},{8,9},{9,8},{10,11... | collective-permute-start | bytes 1572872 | tf_op jit(solution)/shard_map/ppermute | solution.py:27
  1.9 7.0 %collective-permute-start = (bf16[8,1280]{1,0:T(8,128)(2,1)S(1)}, bf16[8,1280]{1,0:T(8,128)(2,1)S(1)}, u32[]{:S(2)}, u32[]{:S(2)}) collective-permute-start(bf16[8,1280]{1,0:T(8,128)(2,1)S(1)} %pad_maximum_fusion), channel_id=1, source_target_pairs={{0,4},{4,8},{8,12},{1,5},{5,9},{9,13},{2,6},{6,10},{10,14},{3,7},{... | collective-permute-start | bytes 61448 | tf_op jit(solution)/shard_map/ppermute | solution.py:17
  8.0 15.5 %copy-start.5 = (f32[1024]{0:T(1024)}, f32[1024]{0:T(1024)S(1)}, u32[]{:S(2)}) copy-start(f32[1024]{0:T(1024)S(1)} %get-tuple-element.42) | copy-start | bytes 12292
  8.8 2.1 %copy-start.6 = (bf16[8,1280]{1,0:T(8,128)(2,1)}, bf16[8,1280]{1,0:T(8,128)(2,1)S(1)}, u32[]{:S(2)}) copy-start(bf16[8,1280]{1,0:T(8,128)(2,1)S(1)} %collective-permute-done.tail_ref) | copy-start | bytes 61444
  9.5 1.5 %copy-start.4 = (f32[2,13,128]{2,1,0:T(8,128)}, f32[2,13,128]{2,1,0:T(8,128)S(1)}, u32[]{:S(2)}) copy-start(f32[2,13,128]{2,1,0:T(8,128)S(1)} %pad_maximum_fusion.1.ownx_ref) | copy-start | bytes 39940
  9.5 1.4 %collective-permute-start.2 = (f32[2,13,128]{2,1,0:T(8,128)S(1)}, f32[2,13,128]{2,1,0:T(8,128)S(1)}, u32[]{:S(2)}, u32[]{:S(2)}) collective-permute-start(f32[2,13,128]{2,1,0:T(8,128)S(1)} %pad_maximum_fusion.1.ownx_ref), channel_id=1, source_target_pairs={{0,1},{1,0},{2,3},{3,2},{4,5},{5,4},{6,7},{7,6},{8,9},{9,8},{10,11... | collective-permute-start | bytes 39944 | tf_op jit(solution)/shard_map/ppermute | solution.py:27
  9.9 17.2 %copy-start.9 = (f32[16]{0:T(128)S(1)}, f32[16]{0:T(128)}, u32[]{:S(2)}) copy-start(f32[16]{0:T(128)} %param.18) | copy-start | bytes 196
  10.9 0.6 copy-start.7
  11.0 0.8 %copy-start.3 = (bf16[2,1024,128]{2,1,0:T(8,128)(2,1)}, bf16[2,1024,128]{2,1,0:T(8,128)(2,1)S(1)}, u32[]{:S(2)}) copy-start(bf16[2,1024,128]{2,1,0:T(8,128)(2,1)S(1)} %collective-permute-done.1.other_ref) | copy-start | bytes 1572868
  23.6 15.4 %collective-permute-start.3 = (bf16[256,1024]{1,0:T(8,128)(2,1)}, bf16[256,1024]{1,0:T(8,128)(2,1)S(1)}, u32[]{:S(2)}, u32[]{:S(2)}) collective-permute-start(bf16[256,1024]{1,0:T(8,128)(2,1)} %get-tuple-element.21), channel_id=1, source_target_pairs={{0,4},{4,8},{8,12},{1,5},{5,9},{9,13},{2,6},{6,10},{10,14},{3,7},{... | collective-permute-start | bytes 1572872 | tf_op jit(solution)/shard_map/ppermute | solution.py:17
  27.8 11.1 %copy-start.1 = (f32[256,1024]{1,0:T(8,128)S(1)}, f32[256,1024]{1,0:T(8,128)}, u32[]{:S(2)}) copy-start(f32[256,1024]{1,0:T(8,128)} %get-tuple-element.36) | copy-start | bytes 3145732
  27.8 11.2 %copy-start.8 = (f32[1,1024]{1,0:T(1,128)S(1)}, f32[1,1024]{1,0:T(1,128)}, u32[]{:S(2)}) copy-start(f32[1,1024]{1,0:T(1,128)} %get-tuple-element.35) | copy-start | bytes 12292
  39.0 4.5 %copy-start = (bf16[256,1024]{1,0:T(8,128)(2,1)}, bf16[256,1024]{1,0:T(8,128)(2,1)S(1)}, u32[]{:S(2)}) copy-start(bf16[256,1024]{1,0:T(8,128)(2,1)S(1)} %collective-permute-done.3.refs_10_) | copy-start | bytes 1572868
  39.1 15.1 %collective-permute-start.4 = (bf16[256,1024]{1,0:T(8,128)(2,1)S(1)}, bf16[256,1024]{1,0:T(8,128)(2,1)S(1)}, u32[]{:S(2)}, u32[]{:S(2)}) collective-permute-start(bf16[256,1024]{1,0:T(8,128)(2,1)S(1)} %add_convert_fusion), channel_id=1, source_target_pairs={{0,4},{4,8},{8,12},{1,5},{5,9},{9,13},{2,6},{6,10},{10,14},{3,7},{... | collective-permute-start | bytes 1572872 | tf_op jit(solution)/shard_map/ppermute | solution.py:17
  54.2 0.8 %copy-start.2 = (bf16[256,1024]{1,0:T(8,128)(2,1)}, bf16[256,1024]{1,0:T(8,128)(2,1)S(1)}, u32[]{:S(2)}) copy-start(bf16[256,1024]{1,0:T(8,128)(2,1)S(1)} %collective-permute-done.4.ein_ref) | copy-start | bytes 1572868

commit v15 on v14

--- a/solution.py
+++ b/solution.py
@@ -263,7 +263,7 @@
          end_ref, state_ref) = refs
     else:
         (x_ref, b_ref, c_ref, l_ref, dt_ref, segr_ref, info_ref, decay_ref, skip_ref, init_ref,
-         after_ref, out_ref, end_ref, state_ref) = refs
+         after_ref, out_ref, state_ref) = refs
     blk = pl.program_id(0)
 
     @pl.when(blk == 0)
@@ -294,18 +294,23 @@
     intra = split_dot(masked, x * falling) * rising
     inter = split_dot(c_mat, state) * (rising * info[:, 1:2])
     out_ref[...] = intra + inter + skip_ref[...] * x
-    ending = expand_heads(
-        jnp.exp(l_small[BLOCK - 1 : BLOCK, :] - l_small) * dt_small * end_col, head_width
-    )
-    weighted = (x * ending).astype(jnp.bfloat16)
-    new_state = decay_ref[0] * state + lax.dot_general(
-        b_mat, weighted, (((0,), (0,)), ((), ())), preferred_element_type=jnp.float32
-    )
-    state_ref[...] = new_state
-
-    @pl.when(blk == pl.num_programs(0) - 1)
+    last = blk == pl.num_programs(0) - 1
+
+    @pl.when(jnp.logical_or(jnp.logical_not(last), from_zero))
     def _():
-        end_ref[...] = new_state
+        ending = expand_heads(
+            jnp.exp(l_small[BLOCK - 1 : BLOCK, :] - l_small) * dt_small * end_col, head_width
+        )
+        weighted = (x * ending).astype(jnp.bfloat16)
+        new_state = decay_ref[0] * state + lax.dot_general(
+            b_mat, weighted, (((0,), (0,)), ((), ())), preferred_element_type=jnp.float32
+        )
+        state_ref[...] = new_state
+        if from_zero:
+
+            @pl.when(last)
+            def _():
+                end_ref[...] = new_state
 
 
 def run_partial(first, count, x, b_full, c_full, l_t, dt_t, seg_row, info, decay_x, skip_x,
@@ -324,13 +329,17 @@
     if not from_zero:
         in_specs += [whole((n_size, width)), pl.BlockSpec(memory_space=pl.ANY)]
         args += [init, after]
+    out_specs = [pl.BlockSpec((BLOCK, width), lambda b: (b, 0))]
+    out_shape = [jax.ShapeDtypeStruct((count * BLOCK, width), jnp.float32)]
+    if from_zero:
+        out_specs.append(whole((n_size, width)))
+        out_shape.append(jax.ShapeDtypeStruct((n_size, width), jnp.float32))
     return pl.pallas_call(
         functools.partial(partial_kernel, width // head_count, from_zero),
         grid=(count,),
         in_specs=in_specs,
-        out_specs=[pl.BlockSpec((BLOCK, width), lambda b: (b, 0)), whole((n_size, width))],
-        out_shape=[jax.ShapeDtypeStruct((count * BLOCK, width), jnp.float32),
-                   jax.ShapeDtypeStruct((n_size, width), jnp.float32)],
+        out_specs=out_specs,
+        out_shape=out_shape,
         scratch_shapes=[pltpu.VMEM((n_size, width), jnp.float32)],
         compiler_params=pltpu.CompilerParams(dimension_semantics=("arbitrary",)),
     )(*args)
@@ -339,8 +348,9 @@
 def correct_kernel(head_width, y_ref, z_ref, c_ref, g_ref, ein_ref, out_ref):
     factor = expand_heads(g_ref[0], head_width)
     carried = jnp.dot(c_ref[...], ein_ref[...], preferred_element_type=jnp.float32)
-    partial = jnp.concatenate([y_ref[...], z_ref[...]], 0)
-    out_ref[...] = (partial + carried * factor).astype(jnp.bfloat16)
+    split = y_ref.shape[0]
+    out_ref[:split] = (y_ref[...] + carried[:split] * factor[:split]).astype(jnp.bfloat16)
+    out_ref[split:] = (z_ref[...] + carried[split:] * factor[split:]).astype(jnp.bfloat16)
 
 
 def run_correct(first, second, c_full, g_tiles, entering):
@@ -472,7 +482,7 @@
     first_hop = incoming
     for step_num in range(1, hops):
         incoming = relay(step_num, incoming)
-    second, _ = run_partial(
+    (second,) = run_partial(
         half_blocks, block_count - half_blocks, *operands, init=middle, after=first_hop
     )
     return run_correct(partial, second, c_full, g_tiles, incoming)

time: 62.2 us -> 62.1 us (level)
  transfers between devices with their start and end apart: 5 -> 5, of which waited for: 2 -> 2; matrix products, arithmetic and copies ran while one was open for 11% -> 10% of each run, Pallas kernels for 28% -> 29%
where the time goes in v15:
time: 62.1 us; the launch traced here: 61.5 us
  Pallas kernels  36.1 us (58%)
  starting transfers between devices  13 us (21%)
  local copies, waits for them, and re-layouts  4.92 us (8%)
  waiting for transfers between devices  4.02 us (6%)
  other arithmetic  3.27 us (5%)
    pallas_call x2, Pallas kernels, run_partial(): pl.pallas_call(functools.partial(partial_kernel, width // head_count, fro...  17.9 us
    ppermute x3, starting transfers between devices, shifted(): lax.ppermute(value, axis, [(source, source + steps) for source in range(i...  12.3 us
    pallas_call x1, Pallas kernels, run_state(): pl.pallas_call(functools.partial(state_kernel, width // head_count), grid...  11.8 us
    pallas_call x1, Pallas kernels, run_correct(): pl.pallas_call(functools.partial(correct_kernel, head_width), grid=(tiles...  6.47 us
    ppermute x3, waiting for transfers between devices, shifted(): lax.ppermute(value, axis, [(source, source + steps) for source in range(i...  4.01 us
    unnamed x20, local copies, waits for them, and re-layouts  1.6 us
  transfers between devices with their start and end apart: 5, of which 2 were waited for; matrix products, arithmetic and copies ran while one was open for 10% of the time, Pallas kernels for 29%

profile of v15, /device:TPU:0, one launch (start us, length us, event | category | flops | bytes accessed | tf_op | source)
XLA Modules:
  0.0 61.5 jit_solution(15071997310464461502)
XLA Ops:
  0.0 0.5 collective-permute-start.1
  0.5 0.7 %slice_bitcast_fusion.1 = bf16[8,256]{1,0:T(8,128)(2,1)S(1)} fusion(bf16[2,1024,128]{2,1,0:T(8,128)(2,1)} %own_ref.1), kind=kLoop, calls=%fused_computation.12 | loop fusion | bytes 8192 | tf_op jit(solution)/shard_map/reshape | solution.py:435
  1.1 0.7 %slice.27 = bf16[8,1024]{1,0:T(8,128)(2,1)S(1)} slice(bf16[1024,1024]{1,0:T(8,128)(2,1)} %x_ref.1), slice={[1016:1024], [0:1024]} | slice | bytes 32768 | tf_op jit(solution)/shard_map/slice | solution.py:435
  1.9 4.5 %collective-permute-start = (bf16[8,1280]{1,0:T(8,128)(2,1)S(1)}, bf16[8,1280]{1,0:T(8,128)(2,1)S(1)}, u32[]{:S(2)}, u32[]{:S(2)}) collective-permute-start(bf16[8,1280]{1,0:T(8,128)(2,1)S(1)} %pad_maximum_fusion), channel_id=1, source_target_pairs={{0,4},{4,8},{8,12},{1,5},{5,9},{9,13},{2,6},{6,10},{10,14},{3,7},{... | collective-permute-start | bytes 61448 | tf_op jit(solution)/shard_map/ppermute | solution.py:17
  6.3 0.8 %reduce-window.9 = s32[3,1]{0,1:T(1,128)S(1)} reduce-window(s32[3,1]{0,1:T(1,128)} %bitcast.41, s32[]{:T(128)} %constant.25.clone.1), window={size=3x1 pad=2_0x0_0}, to_apply=%region_0.0 | reduce-window | flops 6 | bytes 28 | tf_op jit(solution)/shard_map/reduce-window.4
  7.2 0.7 %bitcast_subtract_fusion = s32[3]{0:T(128)S(1)} fusion(s32[3]{0:T(128)} %param.19, s32[3,1]{0,1:T(1,128)S(1)} %reduce-window.9), kind=kLoop, calls=%fused_computation.19 | loop fusion | flops 3 | bytes 36 | tf_op jit(solution)/shard_map/sub | solution.py:31
  7.8 0.1 convert_reduce_fusion
  7.9 0.1 slice_bitcast_fusion.2
  8.0 0.0 copy-start.4
  8.0 0.1 slice_reduce_fusion
  8.1 0.7 %convert_element_type.37 = f32[2,4,128]{2,1,0:T(4,128)S(1)} convert(bf16[2,4,128]{2,1,0:T(4,128)(2,1)} %param.14) | non-fusion elementwise | flops 1024 | bytes 6144 | tf_op jit(solution)/shard_map/convert_element_type | solution.py:441
  8.8 0.0 collective-permute-done.tail_ref
  8.8 0.0 copy-start.6
  8.8 0.7 %pad_maximum_fusion.1.ownx_ref = f32[2,13,128]{2,1,0:T(8,128)S(1)} fusion(f32[2,1,128]{2,1,0:T(1,128)} %bitcast.39, f32[2,4,128]{2,1,0:T(4,128)S(1)} %convert_element_type.37, f32[2,8,128]{2,1,0:T(8,128)S(1)} %convert_bitcast_fusion), kind=kLoop, calls=%fused_computation.3 | loop fusion | flops 6656 | bytes 26624 | tf_op jit(solution)/shard_map/concatenate | solution.py:439
  9.5 0.0 copy-start.5
  9.5 0.2 collective-permute-start.2
  9.8 0.1 fusion.2
  9.8 0.1 stack.39
  9.9 0.0 copy-start.9
  9.9 1.0 %copy.24.info_ref.refs_6_ = f32[1024,8]{1,0:T(8,128)} copy(f32[1024,8]{0,1:T(8,128)S(1)} %stack.39) | data formatting | bytes 65536 | tf_op jit(solution)/shard_map/stack | solution.py:455
  10.9 0.0 collective-permute-done.2.otherx_ref
  10.9 0.0 collective-permute-done.1.other_ref
  10.9 0.0 copy-start.3
  10.9 0.0 copy-done.6
  10.9 0.0 copy-done.5
  11.0 0.6 copy-done.7
  11.5 0.2 copy-done.3
  11.7 11.8 %shard_map.100 = (f32[256,1024]{1,0:T(8,128)}, f32[1024,16]{1,0:T(8,128)}, f32[1024,16]{1,0:T(8,128)}, f32[8,1,1024]{2,1,0:T(1,128)}, f32[1,1024]{1,0:T(1,128)},...) custom-call(bf16[1024,1024]{1,0:T(8,128)(2,1)} %x_ref.1, ...), custom_call_target="tpu_custom_call" | custom-call | tf_op jit(solution)/shard_map/pallas_call | solution.py:227
  23.5 0.0 copy-done.4
  23.5 3.5 %collective-permute-start.3 = (bf16[256,1024]{1,0:T(8,128)(2,1)}, bf16[256,1024]{1,0:T(8,128)(2,1)S(1)}, u32[]{:S(2)}, u32[]{:S(2)}) collective-permute-start(bf16[256,1024]{1,0:T(8,128)(2,1)} %get-tuple-element.20), channel_id=1, source_target_pairs={{0,4},{4,8},{8,12},{1,5},{5,9},{9,13},{2,6},{6,10},{10,14},{3,7},{... | collective-permute-start | bytes 1572872 | tf_op jit(solution)/shard_map/ppermute | solution.py:17
  27.0 0.0 copy-done.9
  27.1 0.1 broadcast_in_dim.9
  27.1 0.7 %reshape_reshape.3.refs_8_ = f32[1,1024]{1,0:T(1,128)} reshape(f32[16,64]{1,0:T(8,128)S(1)} %broadcast_in_dim.9) | data formatting | bytes 8192 | tf_op jit(solution)/shard_map/reshape;reshape | solution.py:448
  27.8 0.0 copy-start.1
  27.8 0.0 copy-start.8
  27.8 8.5 %shard_map.101 = (f32[512,1024]{1,0:T(8,128)}, f32[256,1024]{1,0:T(8,128)}) custom-call(bf16[1024,1024]{1,0:T(8,128)(2,1)} %get-tuple-element.21.refs_0_, bf16[1024,256]{1,0:T(8,128)(2,1)} %get-tuple-element.22.refs_1_, bf16[1024,256]{1,0:T(8,128)(2,1)} %get-tuple-element.23.refs_2_.c_ref, f32[1024,16]{1,0:T(8,128)} %get-tuple-element.24.refs_3_, ...), custom_call_target="tpu_custom_call" | custom-call | tf_op jit(solution)/shard_map/pallas_call | solution.py:337
  36.3 2.6 %collective-permute-done.3.refs_10_ = bf16[256,1024]{1,0:T(8,128)(2,1)S(1)} collective-permute-done((bf16[256,1024]{1,0:T(8,128)(2,1)}, bf16[256,1024]{1,0:T(8,128)(2,1)S(1)}, u32[]{:S(2)}, u32[]{:S(2)}) %collective-permute-start.3) | collective-permute-done | bytes 524320 | tf_op jit(solution)/shard_map/ppermute | solution.py:17
  38.9 0.0 copy-start
  38.9 0.0 copy-done.1
  38.9 0.0 copy-done.8
  38.9 0.2 add_convert_fusion
  39.1 4.3 %collective-permute-start.4 = (bf16[256,1024]{1,0:T(8,128)(2,1)S(1)}, bf16[256,1024]{1,0:T(8,128)(2,1)S(1)}, u32[]{:S(2)}, u32[]{:S(2)}) collective-permute-start(bf16[256,1024]{1,0:T(8,128)(2,1)S(1)} %add_convert_fusion), channel_id=1, source_target_pairs={{0,4},{4,8},{8,12},{1,5},{5,9},{9,13},{2,6},{6,10},{10,14},{3,7},{... | collective-permute-start | bytes 1572872 | tf_op jit(solution)/shard_map/ppermute | solution.py:17
  43.4 0.0 copy-done
  43.4 9.4 %shard_map.102.z_ref = f32[512,1024]{1,0:T(8,128)} custom-call(bf16[1024,1024]{1,0:T(8,128)(2,1)} %get-tuple-element.21.refs_0_, bf16[1024,256]{1,0:T(8,128)(2,1)} %get-tuple-element.22.refs_1_, bf16[1024,256]{1,0:T(8,128)(2,1)} %get-tuple-element.23.refs_2_.c_ref, f32[1024,16]{1,0:T(8,128)} %get-tuple-element.24.refs_3_, ...), custom_call_target="tpu_custom_call" | custom-call | tf_op jit(solution)/shard_map/pallas_call | solution.py:337
  52.8 1.4 %collective-permute-done.4.ein_ref = bf16[256,1024]{1,0:T(8,128)(2,1)S(1)} collective-permute-done((bf16[256,1024]{1,0:T(8,128)(2,1)S(1)}, bf16[256,1024]{1,0:T(8,128)(2,1)S(1)}, u32[]{:S(2)}, u32[]{:S(2)}) %collective-permute-start.4) | collective-permute-done | bytes 524320 | tf_op jit(solution)/shard_map/ppermute | solution.py:17
  54.2 0.0 copy-start.2
  54.2 0.8 %copy-done.2 = bf16[256,1024]{1,0:T(8,128)(2,1)} copy-done((bf16[256,1024]{1,0:T(8,128)(2,1)}, bf16[256,1024]{1,0:T(8,128)(2,1)S(1)}, u32[]{:S(2)}) %copy-start.2) | copy-done | bytes 524312
  55.0 6.5 %shard_map.103 = bf16[1024,1024]{1,0:T(8,128)(2,1)} custom-call(f32[512,1024]{1,0:T(8,128)} %get-tuple-element.29.y_ref, f32[512,1024]{1,0:T(8,128)} %shard_map.102.z_ref, bf16[1024,256]{1,0:T(8,128)(2,1)} %get-tuple-element.23.refs_2_.c_ref, f32[4,1024,4]{2,1,0:T(8,128)} %get-tuple-element.32.g_ref, bf16[256,1024]{1,0:T(8,128)(2,1)} %copy-done.2), custom_call_target="tpu_custom_call" | custom-call | tf_op jit(solution)/shard_map/pallas_call | solution.py:363
  (7 shorter events, 0.0 us)
Async XLA Ops:
  0.0 10.9 %collective-permute-start.1 = (bf16[2,1024,128]{2,1,0:T(8,128)(2,1)}, bf16[2,1024,128]{2,1,0:T(8,128)(2,1)S(1)}, u32[]{:S(2)}, u32[]{:S(2)}) collective-permute-start(bf16[2,1024,128]{2,1,0:T(8,128)(2,1)} %own_ref.1), channel_id=1, source_target_pairs={{0,1},{1,0},{2,3},{3,2},{4,5},{5,4},{6,7},{7,6},{8,9},{9,8},{10,11... | collective-permute-start | bytes 1572872 | tf_op jit(solution)/shard_map/ppermute | solution.py:27
  1.9 7.0 %collective-permute-start = (bf16[8,1280]{1,0:T(8,128)(2,1)S(1)}, bf16[8,1280]{1,0:T(8,128)(2,1)S(1)}, u32[]{:S(2)}, u32[]{:S(2)}) collective-permute-start(bf16[8,1280]{1,0:T(8,128)(2,1)S(1)} %pad_maximum_fusion), channel_id=1, source_target_pairs={{0,4},{4,8},{8,12},{1,5},{5,9},{9,13},{2,6},{6,10},{10,14},{3,7},{... | collective-permute-start | bytes 61448 | tf_op jit(solution)/shard_map/ppermute | solution.py:17
  8.0 15.5 %copy-start.4 = (f32[1024]{0:T(1024)}, f32[1024]{0:T(1024)S(1)}, u32[]{:S(2)}) copy-start(f32[1024]{0:T(1024)S(1)} %get-tuple-element.40) | copy-start | bytes 12292
  8.8 2.1 %copy-start.6 = (bf16[8,1280]{1,0:T(8,128)(2,1)}, bf16[8,1280]{1,0:T(8,128)(2,1)S(1)}, u32[]{:S(2)}) copy-start(bf16[8,1280]{1,0:T(8,128)(2,1)S(1)} %collective-permute-done.tail_ref) | copy-start | bytes 61444
  9.5 1.4 %copy-start.5 = (f32[2,13,128]{2,1,0:T(8,128)}, f32[2,13,128]{2,1,0:T(8,128)S(1)}, u32[]{:S(2)}) copy-start(f32[2,13,128]{2,1,0:T(8,128)S(1)} %pad_maximum_fusion.1.ownx_ref) | copy-start | bytes 39940
  9.5 1.4 %collective-permute-start.2 = (f32[2,13,128]{2,1,0:T(8,128)S(1)}, f32[2,13,128]{2,1,0:T(8,128)S(1)}, u32[]{:S(2)}, u32[]{:S(2)}) collective-permute-start(f32[2,13,128]{2,1,0:T(8,128)S(1)} %pad_maximum_fusion.1.ownx_ref), channel_id=1, source_target_pairs={{0,1},{1,0},{2,3},{3,2},{4,5},{5,4},{6,7},{7,6},{8,9},{9,8},{10,11... | collective-permute-start | bytes 39944 | tf_op jit(solution)/shard_map/ppermute | solution.py:27
  9.9 17.1 %copy-start.9 = (f32[16]{0:T(128)S(1)}, f32[16]{0:T(128)}, u32[]{:S(2)}) copy-start(f32[16]{0:T(128)} %param.18) | copy-start | bytes 196
  10.9 0.6 %copy-start.7 = (f32[2,13,128]{2,1,0:T(8,128)}, f32[2,13,128]{2,1,0:T(8,128)S(1)}, u32[]{:S(2)}) copy-start(f32[2,13,128]{2,1,0:T(8,128)S(1)} %collective-permute-done.2.otherx_ref) | copy-start | bytes 39940
  10.9 0.8 %copy-start.3 = (bf16[2,1024,128]{2,1,0:T(8,128)(2,1)}, bf16[2,1024,128]{2,1,0:T(8,128)(2,1)S(1)}, u32[]{:S(2)}) copy-start(bf16[2,1024,128]{2,1,0:T(8,128)(2,1)S(1)} %collective-permute-done.1.other_ref) | copy-start | bytes 1572868
  23.5 15.4 %collective-permute-start.3 = (bf16[256,1024]{1,0:T(8,128)(2,1)}, bf16[256,1024]{1,0:T(8,128)(2,1)S(1)}, u32[]{:S(2)}, u32[]{:S(2)}) collective-permute-start(bf16[256,1024]{1,0:T(8,128)(2,1)} %get-tuple-element.20), channel_id=1, source_target_pairs={{0,4},{4,8},{8,12},{1,5},{5,9},{9,13},{2,6},{6,10},{10,14},{3,7},{... | collective-permute-start | bytes 1572872 | tf_op jit(solution)/shard_map/ppermute | solution.py:17
  27.8 11.2 %copy-start.1 = (f32[256,1024]{1,0:T(8,128)S(1)}, f32[256,1024]{1,0:T(8,128)}, u32[]{:S(2)}) copy-start(f32[256,1024]{1,0:T(8,128)} %get-tuple-element.34) | copy-start | bytes 3145732
  27.8 11.2 %copy-start.8 = (f32[1,1024]{1,0:T(1,128)S(1)}, f32[1,1024]{1,0:T(1,128)}, u32[]{:S(2)}) copy-start(f32[1,1024]{1,0:T(1,128)} %get-tuple-element.33) | copy-start | bytes 12292
  38.9 4.5 %copy-start = (bf16[256,1024]{1,0:T(8,128)(2,1)}, bf16[256,1024]{1,0:T(8,128)(2,1)S(1)}, u32[]{:S(2)}) copy-start(bf16[256,1024]{1,0:T(8,128)(2,1)S(1)} %collective-permute-done.3.refs_10_) | copy-start | bytes 1572868
  39.1 15.1 %collective-permute-start.4 = (bf16[256,1024]{1,0:T(8,128)(2,1)S(1)}, bf16[256,1024]{1,0:T(8,128)(2,1)S(1)}, u32[]{:S(2)}, u32[]{:S(2)}) collective-permute-start(bf16[256,1024]{1,0:T(8,128)(2,1)S(1)} %add_convert_fusion), channel_id=1, source_target_pairs={{0,4},{4,8},{8,12},{1,5},{5,9},{9,13},{2,6},{6,10},{10,14},{3,7},{... | collective-permute-start | bytes 1572872 | tf_op jit(solution)/shard_map/ppermute | solution.py:17
  54.2 0.8 %copy-start.2 = (bf16[256,1024]{1,0:T(8,128)(2,1)}, bf16[256,1024]{1,0:T(8,128)(2,1)S(1)}, u32[]{:S(2)}) copy-start(bf16[256,1024]{1,0:T(8,128)(2,1)S(1)} %collective-permute-done.4.ein_ref) | copy-start | bytes 1572868

commit v16 on v15

--- a/solution.py
+++ b/solution.py
@@ -125,7 +125,7 @@
             top = jnp.where(top_row < back, pltpu.roll(prev, back, 0), rolled[:8])
             window = jnp.concatenate([top, rolled[8:]], 0) * info[:, 1 + back : 2 + back]
         summed = summed + taps[offset : offset + 1, :] * window
-    return jax.nn.silu(summed).astype(jnp.bfloat16)
+    return (summed * (0.5 + 0.5 * jnp.tanh(0.5 * summed))).astype(jnp.bfloat16)
 
 
 def state_kernel(head_width, x_ref, tail_ref, wconv_ref, bias_ref, own_ref, other_ref, ownx_ref,

time: 62.1 us -> 62.4 us (level)
  no operation moved by 1% of the time
where the time goes in v16:
time: 62.4 us; the launch traced here: 61.8 us
  Pallas kernels  36.5 us (58%)
  starting transfers between devices  13 us (21%)
  local copies, waits for them, and re-layouts  4.92 us (8%)
  waiting for transfers between devices  4.02 us (6%)
  other arithmetic  3.27 us (5%)
    pallas_call x2, Pallas kernels, run_partial(): pl.pallas_call(functools.partial(partial_kernel, width // head_count, fro...  17.9 us
    ppermute x3, starting transfers between devices, shifted(): lax.ppermute(value, axis, [(source, source + steps) for source in range(i...  12.3 us
    pallas_call x1, Pallas kernels, run_state(): pl.pallas_call(functools.partial(state_kernel, width // head_count), grid...  12.1 us
    pallas_call x1, Pallas kernels, run_correct(): pl.pallas_call(functools.partial(correct_kernel, head_width), grid=(tiles...  6.48 us
    ppermute x3, waiting for transfers between devices, shifted(): lax.ppermute(value, axis, [(source, source + steps) for source in range(i...  4.01 us
    unnamed x20, local copies, waits for them, and re-layouts  1.6 us
  transfers between devices with their start and end apart: 5, of which 2 were waited for; matrix products, arithmetic and copies ran while one was open for 10% of the time, Pallas kernels for 29%

profile of v16, /device:TPU:0, one launch (start us, length us, event | category | flops | bytes accessed | tf_op | source)
XLA Modules:
  0.0 61.8 jit_solution(313975394215569781)
XLA Ops:
  0.0 0.5 collective-permute-start.1
  0.5 0.7 %slice_bitcast_fusion.1 = bf16[8,256]{1,0:T(8,128)(2,1)S(1)} fusion(bf16[2,1024,128]{2,1,0:T(8,128)(2,1)} %own_ref.1), kind=kLoop, calls=%fused_computation.12 | loop fusion | bytes 8192 | tf_op jit(solution)/shard_map/reshape | solution.py:435
  1.1 0.7 %slice.27 = bf16[8,1024]{1,0:T(8,128)(2,1)S(1)} slice(bf16[1024,1024]{1,0:T(8,128)(2,1)} %x_ref.1), slice={[1016:1024], [0:1024]} | slice | bytes 32768 | tf_op jit(solution)/shard_map/slice | solution.py:435
  1.9 4.5 %collective-permute-start = (bf16[8,1280]{1,0:T(8,128)(2,1)S(1)}, bf16[8,1280]{1,0:T(8,128)(2,1)S(1)}, u32[]{:S(2)}, u32[]{:S(2)}) collective-permute-start(bf16[8,1280]{1,0:T(8,128)(2,1)S(1)} %pad_maximum_fusion), channel_id=1, source_target_pairs={{0,4},{4,8},{8,12},{1,5},{5,9},{9,13},{2,6},{6,10},{10,14},{3,7},{... | collective-permute-start | bytes 61448 | tf_op jit(solution)/shard_map/ppermute | solution.py:17
  6.3 0.8 %reduce-window.9 = s32[3,1]{0,1:T(1,128)S(1)} reduce-window(s32[3,1]{0,1:T(1,128)} %bitcast.41, s32[]{:T(128)} %constant.25.clone.1), window={size=3x1 pad=2_0x0_0}, to_apply=%region_0.0 | reduce-window | flops 6 | bytes 28 | tf_op jit(solution)/shard_map/reduce-window.4
  7.2 0.7 %bitcast_subtract_fusion = s32[3]{0:T(128)S(1)} fusion(s32[3]{0:T(128)} %param.19, s32[3,1]{0,1:T(1,128)S(1)} %reduce-window.9), kind=kLoop, calls=%fused_computation.19 | loop fusion | flops 3 | bytes 36 | tf_op jit(solution)/shard_map/sub | solution.py:31
  7.8 0.1 convert_reduce_fusion
  7.9 0.1 slice_bitcast_fusion.2
  8.0 0.0 copy-start.4
  8.0 0.1 slice_reduce_fusion
  8.1 0.7 %convert_element_type.37 = f32[2,4,128]{2,1,0:T(4,128)S(1)} convert(bf16[2,4,128]{2,1,0:T(4,128)(2,1)} %param.14) | non-fusion elementwise | flops 1024 | bytes 6144 | tf_op jit(solution)/shard_map/convert_element_type | solution.py:441
  8.8 0.0 collective-permute-done.tail_ref
  8.8 0.0 copy-start.6
  8.8 0.7 %pad_maximum_fusion.1.ownx_ref = f32[2,13,128]{2,1,0:T(8,128)S(1)} fusion(f32[2,1,128]{2,1,0:T(1,128)} %bitcast.39, f32[2,4,128]{2,1,0:T(4,128)S(1)} %convert_element_type.37, f32[2,8,128]{2,1,0:T(8,128)S(1)} %convert_bitcast_fusion), kind=kLoop, calls=%fused_computation.3 | loop fusion | flops 6656 | bytes 26624 | tf_op jit(solution)/shard_map/concatenate | solution.py:439
  9.5 0.0 copy-start.5
  9.5 0.2 collective-permute-start.2
  9.8 0.1 fusion.2
  9.8 0.1 stack.39
  9.9 0.0 copy-start.9
  9.9 1.0 %copy.24.info_ref.refs_6_ = f32[1024,8]{1,0:T(8,128)} copy(f32[1024,8]{0,1:T(8,128)S(1)} %stack.39) | data formatting | bytes 65536 | tf_op jit(solution)/shard_map/stack | solution.py:455
  10.9 0.0 collective-permute-done.2.otherx_ref
  10.9 0.0 copy-start.7
  10.9 0.0 collective-permute-done.1.other_ref
  10.9 0.0 copy-start.3
  10.9 0.0 copy-done.6
  10.9 0.0 copy-done.5
  11.0 0.6 copy-done.7
  11.5 0.2 copy-done.3
  11.7 12.1 %shard_map.100 = (f32[256,1024]{1,0:T(8,128)}, f32[1024,16]{1,0:T(8,128)}, f32[1024,16]{1,0:T(8,128)}, f32[8,1,1024]{2,1,0:T(1,128)}, f32[1,1024]{1,0:T(1,128)},...) custom-call(bf16[1024,1024]{1,0:T(8,128)(2,1)} %x_ref.1, ...), custom_call_target="tpu_custom_call" | custom-call | tf_op jit(solution)/shard_map/pallas_call | solution.py:227
  23.8 0.0 copy-done.4
  23.9 3.5 %collective-permute-start.3 = (bf16[256,1024]{1,0:T(8,128)(2,1)}, bf16[256,1024]{1,0:T(8,128)(2,1)S(1)}, u32[]{:S(2)}, u32[]{:S(2)}) collective-permute-start(bf16[256,1024]{1,0:T(8,128)(2,1)} %get-tuple-element.20), channel_id=1, source_target_pairs={{0,4},{4,8},{8,12},{1,5},{5,9},{9,13},{2,6},{6,10},{10,14},{3,7},{... | collective-permute-start | bytes 1572872 | tf_op jit(solution)/shard_map/ppermute | solution.py:17
  27.4 0.0 copy-done.9
  27.4 0.1 broadcast_in_dim.9
  27.5 0.7 %reshape_reshape.3.refs_8_ = f32[1,1024]{1,0:T(1,128)} reshape(f32[16,64]{1,0:T(8,128)S(1)} %broadcast_in_dim.9) | data formatting | bytes 8192 | tf_op jit(solution)/shard_map/reshape;reshape | solution.py:448
  28.1 0.0 copy-start.1
  28.1 0.0 copy-start.8
  28.1 8.5 %shard_map.101 = (f32[512,1024]{1,0:T(8,128)}, f32[256,1024]{1,0:T(8,128)}) custom-call(bf16[1024,1024]{1,0:T(8,128)(2,1)} %get-tuple-element.21.refs_0_, bf16[1024,256]{1,0:T(8,128)(2,1)} %get-tuple-element.22.refs_1_, bf16[1024,256]{1,0:T(8,128)(2,1)} %get-tuple-element.23.refs_2_.c_ref, f32[1024,16]{1,0:T(8,128)} %get-tuple-element.24.refs_3_, ...), custom_call_target="tpu_custom_call" | custom-call | tf_op jit(solution)/shard_map/pallas_call | solution.py:337
  36.6 2.6 %collective-permute-done.3.refs_10_ = bf16[256,1024]{1,0:T(8,128)(2,1)S(1)} collective-permute-done((bf16[256,1024]{1,0:T(8,128)(2,1)}, bf16[256,1024]{1,0:T(8,128)(2,1)S(1)}, u32[]{:S(2)}, u32[]{:S(2)}) %collective-permute-start.3) | collective-permute-done | bytes 524320 | tf_op jit(solution)/shard_map/ppermute | solution.py:17
  39.3 0.0 copy-start
  39.3 0.0 copy-done.1
  39.3 0.0 copy-done.8
  39.3 0.2 add_convert_fusion
  39.4 4.3 %collective-permute-start.4 = (bf16[256,1024]{1,0:T(8,128)(2,1)S(1)}, bf16[256,1024]{1,0:T(8,128)(2,1)S(1)}, u32[]{:S(2)}, u32[]{:S(2)}) collective-permute-start(bf16[256,1024]{1,0:T(8,128)(2,1)S(1)} %add_convert_fusion), channel_id=1, source_target_pairs={{0,4},{4,8},{8,12},{1,5},{5,9},{9,13},{2,6},{6,10},{10,14},{3,7},{... | collective-permute-start | bytes 1572872 | tf_op jit(solution)/shard_map/ppermute | solution.py:17
  43.8 0.0 copy-done
  43.8 9.4 %shard_map.102.z_ref = f32[512,1024]{1,0:T(8,128)} custom-call(bf16[1024,1024]{1,0:T(8,128)(2,1)} %get-tuple-element.21.refs_0_, bf16[1024,256]{1,0:T(8,128)(2,1)} %get-tuple-element.22.refs_1_, bf16[1024,256]{1,0:T(8,128)(2,1)} %get-tuple-element.23.refs_2_.c_ref, f32[1024,16]{1,0:T(8,128)} %get-tuple-element.24.refs_3_, ...), custom_call_target="tpu_custom_call" | custom-call | tf_op jit(solution)/shard_map/pallas_call | solution.py:337
  53.2 1.4 %collective-permute-done.4.ein_ref = bf16[256,1024]{1,0:T(8,128)(2,1)S(1)} collective-permute-done((bf16[256,1024]{1,0:T(8,128)(2,1)S(1)}, bf16[256,1024]{1,0:T(8,128)(2,1)S(1)}, u32[]{:S(2)}, u32[]{:S(2)}) %collective-permute-start.4) | collective-permute-done | bytes 524320 | tf_op jit(solution)/shard_map/ppermute | solution.py:17
  54.5 0.8 %copy-done.2 = bf16[256,1024]{1,0:T(8,128)(2,1)} copy-done((bf16[256,1024]{1,0:T(8,128)(2,1)}, bf16[256,1024]{1,0:T(8,128)(2,1)S(1)}, u32[]{:S(2)}) %copy-start.2) | copy-done | bytes 524312
  55.3 6.5 %shard_map.103 = bf16[1024,1024]{1,0:T(8,128)(2,1)} custom-call(f32[512,1024]{1,0:T(8,128)} %get-tuple-element.29.y_ref, f32[512,1024]{1,0:T(8,128)} %shard_map.102.z_ref, bf16[1024,256]{1,0:T(8,128)(2,1)} %get-tuple-element.23.refs_2_.c_ref, f32[4,1024,4]{2,1,0:T(8,128)} %get-tuple-element.32.g_ref, bf16[256,1024]{1,0:T(8,128)(2,1)} %copy-done.2), custom_call_target="tpu_custom_call" | custom-call | tf_op jit(solution)/shard_map/pallas_call | solution.py:363
  (7 shorter events, 0.0 us)
Async XLA Ops:
  0.0 10.9 %collective-permute-start.1 = (bf16[2,1024,128]{2,1,0:T(8,128)(2,1)}, bf16[2,1024,128]{2,1,0:T(8,128)(2,1)S(1)}, u32[]{:S(2)}, u32[]{:S(2)}) collective-permute-start(bf16[2,1024,128]{2,1,0:T(8,128)(2,1)} %own_ref.1), channel_id=1, source_target_pairs={{0,1},{1,0},{2,3},{3,2},{4,5},{5,4},{6,7},{7,6},{8,9},{9,8},{10,11... | collective-permute-start | bytes 1572872 | tf_op jit(solution)/shard_map/ppermute | solution.py:27
  1.9 7.0 %collective-permute-start = (bf16[8,1280]{1,0:T(8,128)(2,1)S(1)}, bf16[8,1280]{1,0:T(8,128)(2,1)S(1)}, u32[]{:S(2)}, u32[]{:S(2)}) collective-permute-start(bf16[8,1280]{1,0:T(8,128)(2,1)S(1)} %pad_maximum_fusion), channel_id=1, source_target_pairs={{0,4},{4,8},{8,12},{1,5},{5,9},{9,13},{2,6},{6,10},{10,14},{3,7},{... | collective-permute-start | bytes 61448 | tf_op jit(solution)/shard_map/ppermute | solution.py:17
  8.0 15.8 %copy-start.4 = (f32[1024]{0:T(1024)}, f32[1024]{0:T(1024)S(1)}, u32[]{:S(2)}) copy-start(f32[1024]{0:T(1024)S(1)} %get-tuple-element.40) | copy-start | bytes 12292
  8.8 2.1 %copy-start.6 = (bf16[8,1280]{1,0:T(8,128)(2,1)}, bf16[8,1280]{1,0:T(8,128)(2,1)S(1)}, u32[]{:S(2)}) copy-start(bf16[8,1280]{1,0:T(8,128)(2,1)S(1)} %collective-permute-done.tail_ref) | copy-start | bytes 61444
  9.5 1.4 %copy-start.5 = (f32[2,13,128]{2,1,0:T(8,128)}, f32[2,13,128]{2,1,0:T(8,128)S(1)}, u32[]{:S(2)}) copy-start(f32[2,13,128]{2,1,0:T(8,128)S(1)} %pad_maximum_fusion.1.ownx_ref) | copy-start | bytes 39940
  9.5 1.4 %collective-permute-start.2 = (f32[2,13,128]{2,1,0:T(8,128)S(1)}, f32[2,13,128]{2,1,0:T(8,128)S(1)}, u32[]{:S(2)}, u32[]{:S(2)}) collective-permute-start(f32[2,13,128]{2,1,0:T(8,128)S(1)} %pad_maximum_fusion.1.ownx_ref), channel_id=1, source_target_pairs={{0,1},{1,0},{2,3},{3,2},{4,5},{5,4},{6,7},{7,6},{8,9},{9,8},{10,11... | collective-permute-start | bytes 39944 | tf_op jit(solution)/shard_map/ppermute | solution.py:27
  9.9 17.5 %copy-start.9 = (f32[16]{0:T(128)S(1)}, f32[16]{0:T(128)}, u32[]{:S(2)}) copy-start(f32[16]{0:T(128)} %param.18) | copy-start | bytes 196
  10.9 0.6 copy-start.7
  10.9 0.8 %copy-start.3 = (bf16[2,1024,128]{2,1,0:T(8,128)(2,1)}, bf16[2,1024,128]{2,1,0:T(8,128)(2,1)S(1)}, u32[]{:S(2)}) copy-start(bf16[2,1024,128]{2,1,0:T(8,128)(2,1)S(1)} %collective-permute-done.1.other_ref) | copy-start | bytes 1572868
  23.9 15.4 %collective-permute-start.3 = (bf16[256,1024]{1,0:T(8,128)(2,1)}, bf16[256,1024]{1,0:T(8,128)(2,1)S(1)}, u32[]{:S(2)}, u32[]{:S(2)}) collective-permute-start(bf16[256,1024]{1,0:T(8,128)(2,1)} %get-tuple-element.20), channel_id=1, source_target_pairs={{0,4},{4,8},{8,12},{1,5},{5,9},{9,13},{2,6},{6,10},{10,14},{3,7},{... | collective-permute-start | bytes 1572872 | tf_op jit(solution)/shard_map/ppermute | solution.py:17
  28.1 11.2 %copy-start.1 = (f32[256,1024]{1,0:T(8,128)S(1)}, f32[256,1024]{1,0:T(8,128)}, u32[]{:S(2)}) copy-start(f32[256,1024]{1,0:T(8,128)} %get-tuple-element.34) | copy-start | bytes 3145732
  28.1 11.2 %copy-start.8 = (f32[1,1024]{1,0:T(1,128)S(1)}, f32[1,1024]{1,0:T(1,128)}, u32[]{:S(2)}) copy-start(f32[1,1024]{1,0:T(1,128)} %get-tuple-element.33) | copy-start | bytes 12292
  39.3 4.5 %copy-start = (bf16[256,1024]{1,0:T(8,128)(2,1)}, bf16[256,1024]{1,0:T(8,128)(2,1)S(1)}, u32[]{:S(2)}) copy-start(bf16[256,1024]{1,0:T(8,128)(2,1)S(1)} %collective-permute-done.3.refs_10_) | copy-start | bytes 1572868
  39.4 15.1 %collective-permute-start.4 = (bf16[256,1024]{1,0:T(8,128)(2,1)S(1)}, bf16[256,1024]{1,0:T(8,128)(2,1)S(1)}, u32[]{:S(2)}, u32[]{:S(2)}) collective-permute-start(bf16[256,1024]{1,0:T(8,128)(2,1)S(1)} %add_convert_fusion), channel_id=1, source_target_pairs={{0,4},{4,8},{8,12},{1,5},{5,9},{9,13},{2,6},{6,10},{10,14},{3,7},{... | collective-permute-start | bytes 1572872 | tf_op jit(solution)/shard_map/ppermute | solution.py:17
  54.5 0.8 %copy-start.2 = (bf16[256,1024]{1,0:T(8,128)(2,1)}, bf16[256,1024]{1,0:T(8,128)(2,1)S(1)}, u32[]{:S(2)}) copy-start(bf16[256,1024]{1,0:T(8,128)(2,1)S(1)} %collective-permute-done.4.ein_ref) | copy-start | bytes 1572868

commit v17 on v15

--- a/solution.py
+++ b/solution.py
@@ -28,9 +28,12 @@
 
 
 def segment_of(lengths, positions):
-    starts = jnp.cumsum(lengths, dtype=jnp.int32) - lengths
-    covered = (starts[None, :] <= positions[:, None]).astype(jnp.int32)
-    return jnp.sum(covered, axis=1, dtype=jnp.int32) - 1
+    start = jnp.zeros((), jnp.int32)
+    count = jnp.full(positions.shape, -1, jnp.int32)
+    for req in range(lengths.shape[0]):
+        count = count + (start <= positions).astype(jnp.int32)
+        start = start + lengths[req]
+    return count
 
 
 def convolve(extended, weight, bias_row, seg_ext, row_count):
@@ -452,13 +455,13 @@
     own_seg = seg_ext[3:]
     entry_col = (seg_own == seg_prev[:, None]).reshape(own_rows)
     keeps = [(seg_ext[3 - back : 3 - back + own_rows] == own_seg) for back in (1, 2, 3)]
-    info = jnp.stack(
-        [own_seg.astype(jnp.float32), entry_col.astype(jnp.float32)]
-        + [keep.astype(jnp.float32) for keep in keeps]
-        + [jnp.zeros((own_rows,), jnp.float32), jnp.full((own_rows,), lower_half, jnp.float32),
-           jnp.zeros((own_rows,), jnp.float32)],
-        1,
-    )
+    columns = [own_seg.astype(jnp.float32), entry_col.astype(jnp.float32)]
+    columns += [keep.astype(jnp.float32) for keep in keeps]
+    columns += [jnp.zeros((own_rows,), jnp.float32), jnp.full((own_rows,), lower_half, jnp.float32)]
+    column_id = lax.broadcasted_iota(jnp.int32, (own_rows, 8), 1)
+    info = jnp.zeros((own_rows, 8), jnp.float32)
+    for place, column in enumerate(columns):
+        info = jnp.where(column_id == place, column[:, None], info)
 
     (local_end, l_t, dt_t, decay_x, total_decay, inner_conv, b_full, c_full, end_sent,
      prefix_x, g_tiles) = run_state(

time: 62.1 us -> 64.2 us (1.034)
  between operations: 0.14 us -> 1.35 us
    select_n x0 -> x1, other arithmetic: none -> 1.58 us  [body(): info = jnp.where(column_id == place, column[:, None], info)]
    slice x0 -> x1, local copies, waits for them, and re-layouts: none -> 1.31 us  [segment_of(): start = start + lengths[req]]
    another operation x4 -> x0, local copies, waits for them, and re-layouts: 1.06 us -> none  [the longest x3 1.06 us: body(): jnp.stack([own_seg.astype(jnp.float32), entry_col.astype(jnp.float32)] +...]
    another operation x2 -> x0, other arithmetic: 0.9 us -> none
    sub x3 -> x0, other arithmetic: 0.67 us -> none  [the longest x1 0.66 us: segment_of(): starts = jnp.cumsum(lengths, dtype=jnp.int32) - lengths]
  transfers between devices with their start and end apart: 5 -> 5, of which waited for: 2 -> 2; matrix products, arithmetic and copies ran while one was open for 10% -> 11% of each run, Pallas kernels for 29% -> 28%
where the time goes in v17:
time: 64.2 us; the launch traced here: 63.5 us
  Pallas kernels  36.1 us (56%)
  starting transfers between devices  13 us (20%)
  local copies, waits for them, and re-layouts  5.17 us (8%)
  waiting for transfers between devices  4.02 us (6%)
  other arithmetic  3.86 us (6%)
  between operations  1.35 us (2%)
    pallas_call x2, Pallas kernels, run_partial(): pl.pallas_call(functools.partial(partial_kernel, width // head_count, fro...  17.9 us
    ppermute x3, starting transfers between devices, shifted(): lax.ppermute(value, axis, [(source, source + steps) for source in range(i...  12.3 us
    pallas_call x1, Pallas kernels, run_state(): pl.pallas_call(functools.partial(state_kernel, width // head_count), grid...  11.8 us
    pallas_call x1, Pallas kernels, run_correct(): pl.pallas_call(functools.partial(correct_kernel, head_width), grid=(tiles...  6.46 us
    ppermute x3, waiting for transfers between devices, shifted(): lax.ppermute(value, axis, [(source, source + steps) for source in range(i...  4.01 us
    unnamed x20, local copies, waits for them, and re-layouts  1.59 us
    select_n x1, other arithmetic, body(): info = jnp.where(column_id == place, column[:, None], info)  1.58 us
    slice x1, local copies, waits for them, and re-layouts, segment_of(): start = start + lengths[req]  1.31 us
  transfers between devices with their start and end apart: 5, of which 2 were waited for; matrix products, arithmetic and copies ran while one was open for 11% of the time, Pallas kernels for 28%

profile of v17, /device:TPU:0, one launch (start us, length us, event | category | flops | bytes accessed | tf_op | source)
XLA Modules:
  0.0 63.5 jit_solution(11447141793211968467)
XLA Ops:
  0.0 0.5 collective-permute-start.1
  0.5 0.7 %slice_bitcast_fusion.1 = bf16[8,256]{1,0:T(8,128)(2,1)S(1)} fusion(bf16[2,1024,128]{2,1,0:T(8,128)(2,1)} %own_ref.1), kind=kLoop, calls=%fused_computation.15 | loop fusion | bytes 8192 | tf_op jit(solution)/shard_map/reshape | solution.py:438
  1.1 0.7 %slice.33 = bf16[8,1024]{1,0:T(8,128)(2,1)S(1)} slice(bf16[1024,1024]{1,0:T(8,128)(2,1)} %x_ref.1), slice={[1016:1024], [0:1024]} | slice | bytes 32768 | tf_op jit(solution)/shard_map/slice | solution.py:438
  1.9 4.5 %collective-permute-start = (bf16[8,1280]{1,0:T(8,128)(2,1)S(1)}, bf16[8,1280]{1,0:T(8,128)(2,1)S(1)}, u32[]{:S(2)}, u32[]{:S(2)}) collective-permute-start(bf16[8,1280]{1,0:T(8,128)(2,1)S(1)} %pad_maximum_fusion), channel_id=1, source_target_pairs={{0,4},{4,8},{8,12},{1,5},{5,9},{9,13},{2,6},{6,10},{10,14},{3,7},{... | collective-permute-start | bytes 61448 | tf_op jit(solution)/shard_map/ppermute | solution.py:17
  6.4 1.3 %fusion.6 = (s32[1]{0:T(128)}, s32[1]{0:T(128)}) fusion(s32[3]{0:T(128)} %param.19), kind=kLoop, calls=%fused_computation.29 | loop fusion | bytes 16 | tf_op jit(solution)/shard_map/slice | solution.py:35
  8.9 0.6 convert_add_fusion
  9.5 0.1 slice_bitcast_fusion.2
  9.6 0.0 copy-start.4
  9.6 0.1 slice_reduce_fusion
  9.7 0.1 fusion.4
  9.8 0.7 %convert_element_type.51 = f32[2,4,128]{2,1,0:T(4,128)S(1)} convert(bf16[2,4,128]{2,1,0:T(4,128)(2,1)} %param.14) | non-fusion elementwise | flops 1024 | bytes 6144 | tf_op jit(solution)/shard_map/convert_element_type | solution.py:444
  10.5 0.0 collective-permute-done.tail_ref
  10.5 0.0 copy-start.6
  10.5 0.7 %pad_maximum_fusion.1.ownx_ref = f32[2,13,128]{2,1,0:T(8,128)S(1)} fusion(f32[2,1,128]{2,1,0:T(1,128)} %bitcast.28, f32[2,4,128]{2,1,0:T(4,128)S(1)} %convert_element_type.51, f32[2,8,128]{2,1,0:T(8,128)S(1)} %convert_bitcast_fusion), kind=kLoop, calls=%fused_computation.3 | loop fusion | flops 6656 | bytes 26624 | tf_op jit(solution)/shard_map/concatenate | solution.py:442
  11.2 0.0 copy-start.5
  11.2 0.2 collective-permute-start.2
  11.4 0.0 copy-start.9
  11.4 1.6 %select_select_fusion.info_ref.refs_6_ = f32[1024,8]{1,0:T(8,128)} fusion(f32[1024]{0:T(1024)S(1)} %get-tuple-element.40, f32[1024]{0:T(1024)S(1)} %get-tuple-element.38, f32[1024]{0:T(1024)S(1)} %get-tuple-element.36, f32[1024]{0:T(1024)S(1)} %get-tuple-element.37, f32[1024]{0:T(1024)S(1)} %get-tuple-element.35, f32[]{:T(128)S(6)} %convert_element_type.52, ...), kind=kLoop, calls=%fused_computation.1 | loop fusion | flops 57344 | bytes 53308 | tf_op jit(solution)/shard_map/jit(_where)/select_n | solution.py:464
  13.0 0.0 collective-permute-done.2.otherx_ref
  13.0 0.0 copy-start.7
  13.0 0.0 collective-permute-done.1.other_ref
  13.0 0.0 copy-start.3
  13.0 0.0 copy-done.6
  13.0 0.0 copy-done.5
  13.0 0.6 copy-done.7
  13.6 0.2 copy-done.3
  13.8 11.8 %shard_map.100 = (f32[256,1024]{1,0:T(8,128)}, f32[1024,16]{1,0:T(8,128)}, f32[1024,16]{1,0:T(8,128)}, f32[8,1,1024]{2,1,0:T(1,128)}, f32[1,1024]{1,0:T(1,128)},...) custom-call(bf16[1024,1024]{1,0:T(8,128)(2,1)} %x_ref.1, ...), custom_call_target="tpu_custom_call" | custom-call | tf_op jit(solution)/shard_map/pallas_call | solution.py:230
  25.6 0.0 copy-done.4
  25.6 3.5 %collective-permute-start.3 = (bf16[256,1024]{1,0:T(8,128)(2,1)}, bf16[256,1024]{1,0:T(8,128)(2,1)S(1)}, u32[]{:S(2)}, u32[]{:S(2)}) collective-permute-start(bf16[256,1024]{1,0:T(8,128)(2,1)} %get-tuple-element.20), channel_id=1, source_target_pairs={{0,4},{4,8},{8,12},{1,5},{5,9},{9,13},{2,6},{6,10},{10,14},{3,7},{... | collective-permute-start | bytes 1572872 | tf_op jit(solution)/shard_map/ppermute | solution.py:17
  29.1 0.0 copy-done.9
  29.1 0.1 broadcast_in_dim.62
  29.2 0.7 %reshape_reshape.3.refs_8_ = f32[1,1024]{1,0:T(1,128)} reshape(f32[16,64]{1,0:T(8,128)S(1)} %broadcast_in_dim.62) | data formatting | bytes 8192 | tf_op jit(solution)/shard_map/reshape;reshape | solution.py:451
  29.9 0.0 copy-start.1
  29.9 0.0 copy-start.8
  29.9 8.5 %shard_map.101 = (f32[512,1024]{1,0:T(8,128)}, f32[256,1024]{1,0:T(8,128)}) custom-call(bf16[1024,1024]{1,0:T(8,128)(2,1)} %get-tuple-element.21.refs_0_, bf16[1024,256]{1,0:T(8,128)(2,1)} %get-tuple-element.22.refs_1_, bf16[1024,256]{1,0:T(8,128)(2,1)} %get-tuple-element.23.refs_2_.c_ref, f32[1024,16]{1,0:T(8,128)} %get-tuple-element.24.refs_3_, ...), custom_call_target="tpu_custom_call" | custom-call | tf_op jit(solution)/shard_map/pallas_call | solution.py:340
  38.3 2.7 %collective-permute-done.3.refs_10_ = bf16[256,1024]{1,0:T(8,128)(2,1)S(1)} collective-permute-done((bf16[256,1024]{1,0:T(8,128)(2,1)}, bf16[256,1024]{1,0:T(8,128)(2,1)S(1)}, u32[]{:S(2)}, u32[]{:S(2)}) %collective-permute-start.3) | collective-permute-done | bytes 524320 | tf_op jit(solution)/shard_map/ppermute | solution.py:17
  41.0 0.0 copy-start
  41.0 0.0 copy-done.1
  41.0 0.0 copy-done.8
  41.0 0.2 add_convert_fusion
  41.2 4.3 %collective-permute-start.4 = (bf16[256,1024]{1,0:T(8,128)(2,1)S(1)}, bf16[256,1024]{1,0:T(8,128)(2,1)S(1)}, u32[]{:S(2)}, u32[]{:S(2)}) collective-permute-start(bf16[256,1024]{1,0:T(8,128)(2,1)S(1)} %add_convert_fusion), channel_id=1, source_target_pairs={{0,4},{4,8},{8,12},{1,5},{5,9},{9,13},{2,6},{6,10},{10,14},{3,7},{... | collective-permute-start | bytes 1572872 | tf_op jit(solution)/shard_map/ppermute | solution.py:17
  45.5 0.0 copy-done
  45.5 9.4 %shard_map.102.z_ref = f32[512,1024]{1,0:T(8,128)} custom-call(bf16[1024,1024]{1,0:T(8,128)(2,1)} %get-tuple-element.21.refs_0_, bf16[1024,256]{1,0:T(8,128)(2,1)} %get-tuple-element.22.refs_1_, bf16[1024,256]{1,0:T(8,128)(2,1)} %get-tuple-element.23.refs_2_.c_ref, f32[1024,16]{1,0:T(8,128)} %get-tuple-element.24.refs_3_, ...), custom_call_target="tpu_custom_call" | custom-call | tf_op jit(solution)/shard_map/pallas_call | solution.py:340
  54.9 1.3 %collective-permute-done.4.ein_ref = bf16[256,1024]{1,0:T(8,128)(2,1)S(1)} collective-permute-done((bf16[256,1024]{1,0:T(8,128)(2,1)S(1)}, bf16[256,1024]{1,0:T(8,128)(2,1)S(1)}, u32[]{:S(2)}, u32[]{:S(2)}) %collective-permute-start.4) | collective-permute-done | bytes 524320 | tf_op jit(solution)/shard_map/ppermute | solution.py:17
  56.3 0.0 copy-start.2
  56.3 0.8 %copy-done.2 = bf16[256,1024]{1,0:T(8,128)(2,1)} copy-done((bf16[256,1024]{1,0:T(8,128)(2,1)}, bf16[256,1024]{1,0:T(8,128)(2,1)S(1)}, u32[]{:S(2)}) %copy-start.2) | copy-done | bytes 524312
  57.0 6.5 %shard_map.103 = bf16[1024,1024]{1,0:T(8,128)(2,1)} custom-call(f32[512,1024]{1,0:T(8,128)} %get-tuple-element.29.y_ref, f32[512,1024]{1,0:T(8,128)} %shard_map.102.z_ref, bf16[1024,256]{1,0:T(8,128)(2,1)} %get-tuple-element.23.refs_2_.c_ref, f32[4,1024,4]{2,1,0:T(8,128)} %get-tuple-element.32.g_ref, bf16[256,1024]{1,0:T(8,128)(2,1)} %copy-done.2), custom_call_target="tpu_custom_call" | custom-call | tf_op jit(solution)/shard_map/pallas_call | solution.py:366
  (6 shorter events, 0.0 us)
Async XLA Ops:
  0.0 13.0 %collective-permute-start.1 = (bf16[2,1024,128]{2,1,0:T(8,128)(2,1)}, bf16[2,1024,128]{2,1,0:T(8,128)(2,1)S(1)}, u32[]{:S(2)}, u32[]{:S(2)}) collective-permute-start(bf16[2,1024,128]{2,1,0:T(8,128)(2,1)} %own_ref.1), channel_id=1, source_target_pairs={{0,1},{1,0},{2,3},{3,2},{4,5},{5,4},{6,7},{7,6},{8,9},{9,8},{10,11... | collective-permute-start | bytes 1572872 | tf_op jit(solution)/shard_map/ppermute | solution.py:27
  1.9 8.6 %collective-permute-start = (bf16[8,1280]{1,0:T(8,128)(2,1)S(1)}, bf16[8,1280]{1,0:T(8,128)(2,1)S(1)}, u32[]{:S(2)}, u32[]{:S(2)}) collective-permute-start(bf16[8,1280]{1,0:T(8,128)(2,1)S(1)} %pad_maximum_fusion), channel_id=1, source_target_pairs={{0,4},{4,8},{8,12},{1,5},{5,9},{9,13},{2,6},{6,10},{10,14},{3,7},{... | collective-permute-start | bytes 61448 | tf_op jit(solution)/shard_map/ppermute | solution.py:17
  9.6 16.0 %copy-start.4 = (f32[1024]{0:T(1024)}, f32[1024]{0:T(1024)S(1)}, u32[]{:S(2)}) copy-start(f32[1024]{0:T(1024)S(1)} %get-tuple-element.40) | copy-start | bytes 12292
  10.5 2.5 %copy-start.6 = (bf16[8,1280]{1,0:T(8,128)(2,1)}, bf16[8,1280]{1,0:T(8,128)(2,1)S(1)}, u32[]{:S(2)}) copy-start(bf16[8,1280]{1,0:T(8,128)(2,1)S(1)} %collective-permute-done.tail_ref) | copy-start | bytes 61444
  11.2 1.8 %copy-start.5 = (f32[2,13,128]{2,1,0:T(8,128)}, f32[2,13,128]{2,1,0:T(8,128)S(1)}, u32[]{:S(2)}) copy-start(f32[2,13,128]{2,1,0:T(8,128)S(1)} %pad_maximum_fusion.1.ownx_ref) | copy-start | bytes 39940
  11.2 1.8 %collective-permute-start.2 = (f32[2,13,128]{2,1,0:T(8,128)S(1)}, f32[2,13,128]{2,1,0:T(8,128)S(1)}, u32[]{:S(2)}, u32[]{:S(2)}) collective-permute-start(f32[2,13,128]{2,1,0:T(8,128)S(1)} %pad_maximum_fusion.1.ownx_ref), channel_id=1, source_target_pairs={{0,1},{1,0},{2,3},{3,2},{4,5},{5,4},{6,7},{7,6},{8,9},{9,8},{10,11... | collective-permute-start | bytes 39944 | tf_op jit(solution)/shard_map/ppermute | solution.py:27
  11.4 17.7 %copy-start.9 = (f32[16]{0:T(128)S(1)}, f32[16]{0:T(128)}, u32[]{:S(2)}) copy-start(f32[16]{0:T(128)} %param.18) | copy-start | bytes 196
  13.0 0.6 copy-start.7
  13.0 0.8 %copy-start.3 = (bf16[2,1024,128]{2,1,0:T(8,128)(2,1)}, bf16[2,1024,128]{2,1,0:T(8,128)(2,1)S(1)}, u32[]{:S(2)}) copy-start(bf16[2,1024,128]{2,1,0:T(8,128)(2,1)S(1)} %collective-permute-done.1.other_ref) | copy-start | bytes 1572868
  25.6 15.4 %collective-permute-start.3 = (bf16[256,1024]{1,0:T(8,128)(2,1)}, bf16[256,1024]{1,0:T(8,128)(2,1)S(1)}, u32[]{:S(2)}, u32[]{:S(2)}) collective-permute-start(bf16[256,1024]{1,0:T(8,128)(2,1)} %get-tuple-element.20), channel_id=1, source_target_pairs={{0,4},{4,8},{8,12},{1,5},{5,9},{9,13},{2,6},{6,10},{10,14},{3,7},{... | collective-permute-start | bytes 1572872 | tf_op jit(solution)/shard_map/ppermute | solution.py:17
  29.9 11.1 %copy-start.1 = (f32[256,1024]{1,0:T(8,128)S(1)}, f32[256,1024]{1,0:T(8,128)}, u32[]{:S(2)}) copy-start(f32[256,1024]{1,0:T(8,128)} %get-tuple-element.34) | copy-start | bytes 3145732
  29.9 11.1 %copy-start.8 = (f32[1,1024]{1,0:T(1,128)S(1)}, f32[1,1024]{1,0:T(1,128)}, u32[]{:S(2)}) copy-start(f32[1,1024]{1,0:T(1,128)} %get-tuple-element.33) | copy-start | bytes 12292
  41.0 4.5 %copy-start = (bf16[256,1024]{1,0:T(8,128)(2,1)}, bf16[256,1024]{1,0:T(8,128)(2,1)S(1)}, u32[]{:S(2)}) copy-start(bf16[256,1024]{1,0:T(8,128)(2,1)S(1)} %collective-permute-done.3.refs_10_) | copy-start | bytes 1572868
  41.2 15.1 %collective-permute-start.4 = (bf16[256,1024]{1,0:T(8,128)(2,1)S(1)}, bf16[256,1024]{1,0:T(8,128)(2,1)S(1)}, u32[]{:S(2)}, u32[]{:S(2)}) collective-permute-start(bf16[256,1024]{1,0:T(8,128)(2,1)S(1)} %add_convert_fusion), channel_id=1, source_target_pairs={{0,4},{4,8},{8,12},{1,5},{5,9},{9,13},{2,6},{6,10},{10,14},{3,7},{... | collective-permute-start | bytes 1572872 | tf_op jit(solution)/shard_map/ppermute | solution.py:17
  56.3 0.8 %copy-start.2 = (bf16[256,1024]{1,0:T(8,128)(2,1)}, bf16[256,1024]{1,0:T(8,128)(2,1)S(1)}, u32[]{:S(2)}) copy-start(bf16[256,1024]{1,0:T(8,128)(2,1)S(1)} %collective-permute-done.4.ein_ref) | copy-start | bytes 1572868

commit v18 on v15

--- a/solution.py
+++ b/solution.py
@@ -55,16 +55,18 @@
 
 def expand_heads(small, head_width):
     rows, heads = small.shape
-    per_tile = 128 // head_width
-    lane = lax.broadcasted_iota(jnp.int32, (rows, 128), 1) // head_width
-    tiles = []
-    for tile in range(heads // per_tile):
-        picked = jnp.broadcast_to(small[:, tile * per_tile : tile * per_tile + 1], (rows, 128))
-        for k in range(1, per_tile):
-            column = small[:, tile * per_tile + k : tile * per_tile + k + 1]
-            picked = jnp.where(lane == k, jnp.broadcast_to(column, (rows, 128)), picked)
-        tiles.append(picked)
-    return jnp.concatenate(tiles, axis=1)
+    width = heads * head_width
+    owner = lax.broadcasted_iota(jnp.int32, (heads, width), 1) // head_width
+    spread = (owner == lax.broadcasted_iota(jnp.int32, (heads, width), 0)).astype(jnp.float32)
+    spread = spread.astype(jnp.bfloat16)
+    rest = small
+    out = None
+    for _ in range(3):
+        piece = rest.astype(jnp.bfloat16)
+        part = jnp.dot(piece, spread, preferred_element_type=jnp.float32)
+        out = part if out is None else out + part
+        rest = rest - piece.astype(jnp.float32)
+    return out
 
 
 def block_kernel(with_y, head_width, *refs):

time: 62.1 us -> 62.6 us (level)
  Pallas kernels: 36.1 us -> 36.8 us
where the time goes in v18:
time: 62.6 us; the launch traced here: 61.9 us
  Pallas kernels  36.8 us (59%)
  starting transfers between devices  13 us (21%)
  local copies, waits for them, and re-layouts  4.92 us (8%)
  waiting for transfers between devices  3.83 us (6%)
  other arithmetic  3.27 us (5%)
    pallas_call x2, Pallas kernels, run_partial(): pl.pallas_call(functools.partial(partial_kernel, width // head_count, fro...  18.1 us
    ppermute x3, starting transfers between devices, shifted(): lax.ppermute(value, axis, [(source, source + steps) for source in range(i...  12.3 us
    pallas_call x1, Pallas kernels, run_state(): pl.pallas_call(functools.partial(state_kernel, width // head_count), grid...  12.2 us
    pallas_call x1, Pallas kernels, run_correct(): pl.pallas_call(functools.partial(correct_kernel, head_width), grid=(tiles...  6.52 us
    ppermute x3, waiting for transfers between devices, shifted(): lax.ppermute(value, axis, [(source, source + steps) for source in range(i...  3.82 us
    unnamed x20, local copies, waits for them, and re-layouts  1.6 us
  transfers between devices with their start and end apart: 5, of which 2 were waited for; matrix products, arithmetic and copies ran while one was open for 10% of the time, Pallas kernels for 29%

profile of v18, /device:TPU:0, one launch (start us, length us, event | category | flops | bytes accessed | tf_op | source)
XLA Modules:
  0.0 61.9 jit_solution(8973257741367513986)
XLA Ops:
  0.0 0.5 collective-permute-start.1
  0.5 0.7 %slice_bitcast_fusion.1 = bf16[8,256]{1,0:T(8,128)(2,1)S(1)} fusion(bf16[2,1024,128]{2,1,0:T(8,128)(2,1)} %own_ref.1), kind=kLoop, calls=%fused_computation.12 | loop fusion | bytes 8192 | tf_op jit(solution)/shard_map/reshape | solution.py:437
  1.1 0.7 %slice.27 = bf16[8,1024]{1,0:T(8,128)(2,1)S(1)} slice(bf16[1024,1024]{1,0:T(8,128)(2,1)} %x_ref.1), slice={[1016:1024], [0:1024]} | slice | bytes 32768 | tf_op jit(solution)/shard_map/slice | solution.py:437
  1.9 4.5 %collective-permute-start = (bf16[8,1280]{1,0:T(8,128)(2,1)S(1)}, bf16[8,1280]{1,0:T(8,128)(2,1)S(1)}, u32[]{:S(2)}, u32[]{:S(2)}) collective-permute-start(bf16[8,1280]{1,0:T(8,128)(2,1)S(1)} %pad_maximum_fusion), channel_id=1, source_target_pairs={{0,4},{4,8},{8,12},{1,5},{5,9},{9,13},{2,6},{6,10},{10,14},{3,7},{... | collective-permute-start | bytes 61448 | tf_op jit(solution)/shard_map/ppermute | solution.py:17
  6.3 0.8 %reduce-window.9 = s32[3,1]{0,1:T(1,128)S(1)} reduce-window(s32[3,1]{0,1:T(1,128)} %bitcast.41, s32[]{:T(128)} %constant.25.clone.1), window={size=3x1 pad=2_0x0_0}, to_apply=%region_0.0 | reduce-window | flops 6 | bytes 28 | tf_op jit(solution)/shard_map/reduce-window.4
  7.2 0.7 %bitcast_subtract_fusion = s32[3]{0:T(128)S(1)} fusion(s32[3]{0:T(128)} %param.19, s32[3,1]{0,1:T(1,128)S(1)} %reduce-window.9), kind=kLoop, calls=%fused_computation.19 | loop fusion | flops 3 | bytes 36 | tf_op jit(solution)/shard_map/sub | solution.py:31
  7.8 0.1 convert_reduce_fusion
  7.9 0.1 slice_bitcast_fusion.2
  8.0 0.0 copy-start.4
  8.0 0.1 slice_reduce_fusion
  8.1 0.7 %convert_element_type.37 = f32[2,4,128]{2,1,0:T(4,128)S(1)} convert(bf16[2,4,128]{2,1,0:T(4,128)(2,1)} %param.14) | non-fusion elementwise | flops 1024 | bytes 6144 | tf_op jit(solution)/shard_map/convert_element_type | solution.py:443
  8.8 0.0 collective-permute-done.tail_ref
  8.8 0.0 copy-start.6
  8.8 0.7 %pad_maximum_fusion.1.ownx_ref = f32[2,13,128]{2,1,0:T(8,128)S(1)} fusion(f32[2,1,128]{2,1,0:T(1,128)} %bitcast.39, f32[2,4,128]{2,1,0:T(4,128)S(1)} %convert_element_type.37, f32[2,8,128]{2,1,0:T(8,128)S(1)} %convert_bitcast_fusion), kind=kLoop, calls=%fused_computation.3 | loop fusion | flops 6656 | bytes 26624 | tf_op jit(solution)/shard_map/concatenate | solution.py:441
  9.5 0.0 copy-start.5
  9.5 0.2 collective-permute-start.2
  9.8 0.1 fusion.2
  9.8 0.1 stack.39
  9.9 0.0 copy-start.9
  9.9 1.0 %copy.24.info_ref.refs_6_ = f32[1024,8]{1,0:T(8,128)} copy(f32[1024,8]{0,1:T(8,128)S(1)} %stack.39) | data formatting | bytes 65536 | tf_op jit(solution)/shard_map/stack | solution.py:457
  10.9 0.0 collective-permute-done.2.otherx_ref
  10.9 0.0 copy-start.7
  10.9 0.0 collective-permute-done.1.other_ref
  10.9 0.0 copy-start.3
  10.9 0.0 copy-done.6
  10.9 0.0 copy-done.5
  11.0 0.6 copy-done.7
  11.5 0.2 copy-done.3
  11.7 12.2 %shard_map.100 = (f32[256,1024]{1,0:T(8,128)}, f32[1024,16]{1,0:T(8,128)}, f32[1024,16]{1,0:T(8,128)}, f32[8,1,1024]{2,1,0:T(1,128)}, f32[1,1024]{1,0:T(1,128)},...) custom-call(bf16[1024,1024]{1,0:T(8,128)(2,1)} %x_ref.1, ...), custom_call_target="tpu_custom_call" | custom-call | tf_op jit(solution)/shard_map/pallas_call | solution.py:229
  23.9 0.0 copy-done.4
  23.9 3.5 %collective-permute-start.3 = (bf16[256,1024]{1,0:T(8,128)(2,1)}, bf16[256,1024]{1,0:T(8,128)(2,1)S(1)}, u32[]{:S(2)}, u32[]{:S(2)}) collective-permute-start(bf16[256,1024]{1,0:T(8,128)(2,1)} %get-tuple-element.20), channel_id=1, source_target_pairs={{0,4},{4,8},{8,12},{1,5},{5,9},{9,13},{2,6},{6,10},{10,14},{3,7},{... | collective-permute-start | bytes 1572872 | tf_op jit(solution)/shard_map/ppermute | solution.py:17
  27.4 0.0 copy-done.9
  27.4 0.1 broadcast_in_dim.9
  27.5 0.7 %reshape_reshape.3.refs_8_ = f32[1,1024]{1,0:T(1,128)} reshape(f32[16,64]{1,0:T(8,128)S(1)} %broadcast_in_dim.9) | data formatting | bytes 8192 | tf_op jit(solution)/shard_map/reshape;reshape | solution.py:450
  28.2 0.0 copy-start.1
  28.2 0.0 copy-start.8
  28.2 9.0 %shard_map.101 = (f32[512,1024]{1,0:T(8,128)}, f32[256,1024]{1,0:T(8,128)}) custom-call(bf16[1024,1024]{1,0:T(8,128)(2,1)} %get-tuple-element.21.refs_0_, bf16[1024,256]{1,0:T(8,128)(2,1)} %get-tuple-element.22.refs_1_, bf16[1024,256]{1,0:T(8,128)(2,1)} %get-tuple-element.23.refs_2_.c_ref, f32[1024,16]{1,0:T(8,128)} %get-tuple-element.24.refs_3_, ...), custom_call_target="tpu_custom_call" | custom-call | tf_op jit(solution)/shard_map/pallas_call | solution.py:339
  37.2 2.2 %collective-permute-done.3.refs_10_ = bf16[256,1024]{1,0:T(8,128)(2,1)S(1)} collective-permute-done((bf16[256,1024]{1,0:T(8,128)(2,1)}, bf16[256,1024]{1,0:T(8,128)(2,1)S(1)}, u32[]{:S(2)}, u32[]{:S(2)}) %collective-permute-start.3) | collective-permute-done | bytes 524320 | tf_op jit(solution)/shard_map/ppermute | solution.py:17
  39.3 0.0 copy-start
  39.3 0.0 copy-done.1
  39.3 0.0 copy-done.8
  39.3 0.2 add_convert_fusion
  39.5 4.3 %collective-permute-start.4 = (bf16[256,1024]{1,0:T(8,128)(2,1)S(1)}, bf16[256,1024]{1,0:T(8,128)(2,1)S(1)}, u32[]{:S(2)}, u32[]{:S(2)}) collective-permute-start(bf16[256,1024]{1,0:T(8,128)(2,1)S(1)} %add_convert_fusion), channel_id=1, source_target_pairs={{0,4},{4,8},{8,12},{1,5},{5,9},{9,13},{2,6},{6,10},{10,14},{3,7},{... | collective-permute-start | bytes 1572872 | tf_op jit(solution)/shard_map/ppermute | solution.py:17
  43.8 0.0 copy-done
  43.8 9.1 %shard_map.102.z_ref = f32[512,1024]{1,0:T(8,128)} custom-call(bf16[1024,1024]{1,0:T(8,128)(2,1)} %get-tuple-element.21.refs_0_, bf16[1024,256]{1,0:T(8,128)(2,1)} %get-tuple-element.22.refs_1_, bf16[1024,256]{1,0:T(8,128)(2,1)} %get-tuple-element.23.refs_2_.c_ref, f32[1024,16]{1,0:T(8,128)} %get-tuple-element.24.refs_3_, ...), custom_call_target="tpu_custom_call" | custom-call | tf_op jit(solution)/shard_map/pallas_call | solution.py:339
  53.0 1.6 %collective-permute-done.4.ein_ref = bf16[256,1024]{1,0:T(8,128)(2,1)S(1)} collective-permute-done((bf16[256,1024]{1,0:T(8,128)(2,1)S(1)}, bf16[256,1024]{1,0:T(8,128)(2,1)S(1)}, u32[]{:S(2)}, u32[]{:S(2)}) %collective-permute-start.4) | collective-permute-done | bytes 524320 | tf_op jit(solution)/shard_map/ppermute | solution.py:17
  54.6 0.8 %copy-done.2 = bf16[256,1024]{1,0:T(8,128)(2,1)} copy-done((bf16[256,1024]{1,0:T(8,128)(2,1)}, bf16[256,1024]{1,0:T(8,128)(2,1)S(1)}, u32[]{:S(2)}) %copy-start.2) | copy-done | bytes 524312
  55.4 6.5 %shard_map.103 = bf16[1024,1024]{1,0:T(8,128)(2,1)} custom-call(f32[512,1024]{1,0:T(8,128)} %get-tuple-element.29.y_ref, f32[512,1024]{1,0:T(8,128)} %shard_map.102.z_ref, bf16[1024,256]{1,0:T(8,128)(2,1)} %get-tuple-element.23.refs_2_.c_ref, f32[4,1024,4]{2,1,0:T(8,128)} %get-tuple-element.32.g_ref, bf16[256,1024]{1,0:T(8,128)(2,1)} %copy-done.2), custom_call_target="tpu_custom_call" | custom-call | tf_op jit(solution)/shard_map/pallas_call | solution.py:365
  (7 shorter events, 0.0 us)
Async XLA Ops:
  0.0 10.9 %collective-permute-start.1 = (bf16[2,1024,128]{2,1,0:T(8,128)(2,1)}, bf16[2,1024,128]{2,1,0:T(8,128)(2,1)S(1)}, u32[]{:S(2)}, u32[]{:S(2)}) collective-permute-start(bf16[2,1024,128]{2,1,0:T(8,128)(2,1)} %own_ref.1), channel_id=1, source_target_pairs={{0,1},{1,0},{2,3},{3,2},{4,5},{5,4},{6,7},{7,6},{8,9},{9,8},{10,11... | collective-permute-start | bytes 1572872 | tf_op jit(solution)/shard_map/ppermute | solution.py:27
  1.9 7.0 %collective-permute-start = (bf16[8,1280]{1,0:T(8,128)(2,1)S(1)}, bf16[8,1280]{1,0:T(8,128)(2,1)S(1)}, u32[]{:S(2)}, u32[]{:S(2)}) collective-permute-start(bf16[8,1280]{1,0:T(8,128)(2,1)S(1)} %pad_maximum_fusion), channel_id=1, source_target_pairs={{0,4},{4,8},{8,12},{1,5},{5,9},{9,13},{2,6},{6,10},{10,14},{3,7},{... | collective-permute-start | bytes 61448 | tf_op jit(solution)/shard_map/ppermute | solution.py:17
  8.0 15.9 %copy-start.4 = (f32[1024]{0:T(1024)}, f32[1024]{0:T(1024)S(1)}, u32[]{:S(2)}) copy-start(f32[1024]{0:T(1024)S(1)} %get-tuple-element.40) | copy-start | bytes 12292
  8.8 2.1 %copy-start.6 = (bf16[8,1280]{1,0:T(8,128)(2,1)}, bf16[8,1280]{1,0:T(8,128)(2,1)S(1)}, u32[]{:S(2)}) copy-start(bf16[8,1280]{1,0:T(8,128)(2,1)S(1)} %collective-permute-done.tail_ref) | copy-start | bytes 61444
  9.5 1.4 %copy-start.5 = (f32[2,13,128]{2,1,0:T(8,128)}, f32[2,13,128]{2,1,0:T(8,128)S(1)}, u32[]{:S(2)}) copy-start(f32[2,13,128]{2,1,0:T(8,128)S(1)} %pad_maximum_fusion.1.ownx_ref) | copy-start | bytes 39940
  9.5 1.4 %collective-permute-start.2 = (f32[2,13,128]{2,1,0:T(8,128)S(1)}, f32[2,13,128]{2,1,0:T(8,128)S(1)}, u32[]{:S(2)}, u32[]{:S(2)}) collective-permute-start(f32[2,13,128]{2,1,0:T(8,128)S(1)} %pad_maximum_fusion.1.ownx_ref), channel_id=1, source_target_pairs={{0,1},{1,0},{2,3},{3,2},{4,5},{5,4},{6,7},{7,6},{8,9},{9,8},{10,11... | collective-permute-start | bytes 39944 | tf_op jit(solution)/shard_map/ppermute | solution.py:27
  9.9 17.5 %copy-start.9 = (f32[16]{0:T(128)S(1)}, f32[16]{0:T(128)}, u32[]{:S(2)}) copy-start(f32[16]{0:T(128)} %param.18) | copy-start | bytes 196
  10.9 0.6 copy-start.7
  10.9 0.8 %copy-start.3 = (bf16[2,1024,128]{2,1,0:T(8,128)(2,1)}, bf16[2,1024,128]{2,1,0:T(8,128)(2,1)S(1)}, u32[]{:S(2)}) copy-start(bf16[2,1024,128]{2,1,0:T(8,128)(2,1)S(1)} %collective-permute-done.1.other_ref) | copy-start | bytes 1572868
  23.9 15.4 %collective-permute-start.3 = (bf16[256,1024]{1,0:T(8,128)(2,1)}, bf16[256,1024]{1,0:T(8,128)(2,1)S(1)}, u32[]{:S(2)}, u32[]{:S(2)}) collective-permute-start(bf16[256,1024]{1,0:T(8,128)(2,1)} %get-tuple-element.20), channel_id=1, source_target_pairs={{0,4},{4,8},{8,12},{1,5},{5,9},{9,13},{2,6},{6,10},{10,14},{3,7},{... | collective-permute-start | bytes 1572872 | tf_op jit(solution)/shard_map/ppermute | solution.py:17
  28.2 11.2 %copy-start.1 = (f32[256,1024]{1,0:T(8,128)S(1)}, f32[256,1024]{1,0:T(8,128)}, u32[]{:S(2)}) copy-start(f32[256,1024]{1,0:T(8,128)} %get-tuple-element.34) | copy-start | bytes 3145732
  28.2 11.2 %copy-start.8 = (f32[1,1024]{1,0:T(1,128)S(1)}, f32[1,1024]{1,0:T(1,128)}, u32[]{:S(2)}) copy-start(f32[1,1024]{1,0:T(1,128)} %get-tuple-element.33) | copy-start | bytes 12292
  39.3 4.5 %copy-start = (bf16[256,1024]{1,0:T(8,128)(2,1)}, bf16[256,1024]{1,0:T(8,128)(2,1)S(1)}, u32[]{:S(2)}) copy-start(bf16[256,1024]{1,0:T(8,128)(2,1)S(1)} %collective-permute-done.3.refs_10_) | copy-start | bytes 1572868
  39.5 15.1 %collective-permute-start.4 = (bf16[256,1024]{1,0:T(8,128)(2,1)S(1)}, bf16[256,1024]{1,0:T(8,128)(2,1)S(1)}, u32[]{:S(2)}, u32[]{:S(2)}) collective-permute-start(bf16[256,1024]{1,0:T(8,128)(2,1)S(1)} %add_convert_fusion), channel_id=1, source_target_pairs={{0,4},{4,8},{8,12},{1,5},{5,9},{9,13},{2,6},{6,10},{10,14},{3,7},{... | collective-permute-start | bytes 1572872 | tf_op jit(solution)/shard_map/ppermute | solution.py:17
  54.6 0.8 %copy-start.2 = (bf16[256,1024]{1,0:T(8,128)(2,1)}, bf16[256,1024]{1,0:T(8,128)(2,1)S(1)}, u32[]{:S(2)}) copy-start(bf16[256,1024]{1,0:T(8,128)(2,1)S(1)} %collective-permute-done.4.ein_ref) | copy-start | bytes 1572868

commit v19 on v15

--- a/solution.py
+++ b/solution.py
@@ -113,7 +113,7 @@
     )
 
 
-def causal_conv(raw, prev, taps, bias, info):
+def causal_conv(raw, prev, taps, bias, info, masked):
     top_row = lax.broadcasted_iota(jnp.int32, prev.shape, 0)
     summed = jnp.zeros(raw.shape, jnp.float32) + bias
     for offset in range(4):
@@ -123,13 +123,15 @@
         else:
             rolled = pltpu.roll(raw, back, 0)
             top = jnp.where(top_row < back, pltpu.roll(prev, back, 0), rolled[:8])
-            window = jnp.concatenate([top, rolled[8:]], 0) * info[:, 1 + back : 2 + back]
+            window = jnp.concatenate([top, rolled[8:]], 0)
+            if masked:
+                window = window * info[:, 1 + back : 2 + back]
         summed = summed + taps[offset : offset + 1, :] * window
     return jax.nn.silu(summed).astype(jnp.bfloat16)
 
 
-def state_kernel(head_width, x_ref, tail_ref, wconv_ref, bias_ref, own_ref, other_ref, ownx_ref,
-                 otherx_ref, dt_ref, rate_ref, info_ref, state_ref, l_ref, dtt_ref,
+def state_kernel(head_width, starts_ref, x_ref, tail_ref, wconv_ref, bias_ref, own_ref, other_ref,
+                 ownx_ref, otherx_ref, dt_ref, rate_ref, info_ref, state_ref, l_ref, dtt_ref,
                  decay_ref, total_ref, xc_ref, bo_ref, co_ref, sent_ref, prefix_ref, ltile_ref,
                  prev_ref, bcprev_ref, small_ref):
     blk = pl.program_id(0)
@@ -144,24 +146,39 @@
         bcprev_ref[1] = otherx_ref[:, 0:8, :]
 
     info = info_ref[...]
-    raw = x_ref[...].astype(jnp.float32)
-    xc = causal_conv(raw, prev_ref[...], wconv_ref[...].astype(jnp.float32), bias_ref[...], info)
-    prev_ref[...] = raw[BLOCK - 8 :]
-    xc_ref[...] = xc
     lower = info_ref[0:1, 5:6] > 0.5
-    convolved = []
-    for which in range(2):
-        halves = []
-        for side, (raw_ref, extra_ref) in enumerate(((own_ref, ownx_ref), (other_ref, otherx_ref))):
-            raw_bc = raw_ref[which].astype(jnp.float32)
-            extra = extra_ref[which]
-            halves.append(
-                causal_conv(raw_bc, bcprev_ref[side, which], extra[8:12], extra[12:13], info)
+
+    def convolve_block(masked):
+        raw = x_ref[...].astype(jnp.float32)
+        xc_ref[...] = causal_conv(
+            raw, prev_ref[...], wconv_ref[...].astype(jnp.float32), bias_ref[...], info, masked
+        )
+        prev_ref[...] = raw[BLOCK - 8 :]
+        outs = (bo_ref, co_ref)
+        for which in range(2):
+            halves = []
+            pairs = ((own_ref, ownx_ref), (other_ref, otherx_ref))
+            for side, (raw_ref, extra_ref) in enumerate(pairs):
+                raw_bc = raw_ref[which].astype(jnp.float32)
+                extra = extra_ref[which]
+                halves.append(causal_conv(
+                    raw_bc, bcprev_ref[side, which], extra[8:12], extra[12:13], info, masked
+                ))
+                bcprev_ref[side, which] = raw_bc[BLOCK - 8 :]
+            outs[which][...] = jnp.where(
+                lower, jnp.concatenate(halves, 1), jnp.concatenate(halves[::-1], 1)
             )
-            bcprev_ref[side, which] = raw_bc[BLOCK - 8 :]
-        convolved.append(jnp.where(
-            lower, jnp.concatenate(halves, 1), jnp.concatenate(halves[::-1], 1)
-        ))
+
+    @pl.when(starts_ref[blk] != 0)
+    def _():
+        convolve_block(True)
+
+    @pl.when(starts_ref[blk] == 0)
+    def _():
+        convolve_block(False)
+
+    xc = xc_ref[...]
+    convolved = [bo_ref[...], co_ref[...]]
     b_mat, c_mat = convolved
     bo_ref[...] = b_mat
     co_ref[...] = c_mat
@@ -213,7 +230,7 @@
         sent_ref[...] = new_state.astype(jnp.bfloat16)
 
 
-def run_state(x, tails, wconv, bias_row, own_raw, other_raw, own_extra, other_extra,
+def run_state(starts, x, tails, wconv, bias_row, own_raw, other_raw, own_extra, other_extra,
               step_size, rate_row, info):
     rows, width = x.shape
     head_count = step_size.shape[0]
@@ -227,7 +244,8 @@
     return pl.pallas_call(
         functools.partial(state_kernel, width // head_count),
         grid=(block_count,),
-        in_specs=[row_block(width), whole(tails.shape), whole((4, width)), whole((1, width)),
+        in_specs=[pl.BlockSpec(memory_space=pltpu.SMEM),
+                  row_block(width), whole(tails.shape), whole((4, width)), whole((1, width)),
                   pl.BlockSpec((2, BLOCK, half), lambda b: (0, b, 0)),
                   pl.BlockSpec((2, BLOCK, half), lambda b: (0, b, 0)),
                   whole(own_extra.shape), whole(own_extra.shape),
@@ -253,7 +271,7 @@
                         pltpu.VMEM((2, 2, 8, half), jnp.float32),
                         pltpu.VMEM((1, head_count), jnp.float32)],
         compiler_params=pltpu.CompilerParams(dimension_semantics=("arbitrary",)),
-    )(x, tails, wconv, bias_row, own_raw, other_raw, own_extra, other_extra, step_size,
+    )(starts, x, tails, wconv, bias_row, own_raw, other_raw, own_extra, other_extra, step_size,
       rate_row, info)
 
 
@@ -452,6 +470,8 @@
     own_seg = seg_ext[3:]
     entry_col = (seg_own == seg_prev[:, None]).reshape(own_rows)
     keeps = [(seg_ext[3 - back : 3 - back + own_rows] == own_seg) for back in (1, 2, 3)]
+    cut = jnp.logical_not(keeps[0] & keeps[1] & keeps[2])
+    block_starts = jnp.any(cut.reshape(block_count, BLOCK), axis=1).astype(jnp.int32)
     info = jnp.stack(
         [own_seg.astype(jnp.float32), entry_col.astype(jnp.float32)]
         + [keep.astype(jnp.float32) for keep in keeps]
@@ -462,6 +482,7 @@
 
     (local_end, l_t, dt_t, decay_x, total_decay, inner_conv, b_full, c_full, end_sent,
      prefix_x, g_tiles) = run_state(
+        block_starts,
         inner_input, tails, conv_inner, bias_inner.reshape(1, -1), state_input, partner_raw,
         extra, partner_extra,
         step_size, decay_rate.reshape(1, -1), info

time: 62.1 us -> 67.5 us (1.087)
  Pallas kernels: 36.1 us -> 40.9 us
  other arithmetic: 3.27 us -> 4.05 us
    pallas_call x1, Pallas kernels: 11.8 us -> 16.6 us  [run_state(): pl.pallas_call(functools.partial(state_kernel, width // head_count), grid...]
  transfers between devices with their start and end apart: 5 -> 5, of which waited for: 2 -> 2; matrix products, arithmetic and copies ran while one was open for 10% -> 11% of each run, Pallas kernels for 29% -> 27%
where the time goes in v19:
time: 67.5 us; the launch traced here: 67 us
  Pallas kernels  40.9 us (61%)
  starting transfers between devices  13 us (19%)
  local copies, waits for them, and re-layouts  4.91 us (7%)
  other arithmetic  4.05 us (6%)
  waiting for transfers between devices  4.05 us (6%)
    pallas_call x2, Pallas kernels, run_partial(): pl.pallas_call(functools.partial(partial_kernel, width // head_count, fro...  17.9 us
    pallas_call x1, Pallas kernels, run_state(): pl.pallas_call(functools.partial(state_kernel, width // head_count), grid...  16.6 us
    ppermute x3, starting transfers between devices, shifted(): lax.ppermute(value, axis, [(source, source + steps) for source in range(i...  12.3 us
    pallas_call x1, Pallas kernels, run_correct(): pl.pallas_call(functools.partial(correct_kernel, head_width), grid=(tiles...  6.46 us
    ppermute x3, waiting for transfers between devices, shifted(): lax.ppermute(value, axis, [(source, source + steps) for source in range(i...  4.05 us
    unnamed x20, local copies, waits for them, and re-layouts  1.6 us
  transfers between devices with their start and end apart: 5, of which 2 were waited for; matrix products, arithmetic and copies ran while one was open for 11% of the time, Pallas kernels for 27%

profile of v19, /device:TPU:0, one launch (start us, length us, event | category | flops | bytes accessed | tf_op | source)
XLA Modules:
  0.0 67.0 jit_solution(2933589299819271981)
XLA Ops:
  0.0 0.5 collective-permute-start.1
  0.5 0.7 %slice_bitcast_fusion.1 = bf16[8,256]{1,0:T(8,128)(2,1)S(1)} fusion(bf16[2,1024,128]{2,1,0:T(8,128)(2,1)} %own_ref.1), kind=kLoop, calls=%fused_computation.12 | loop fusion | bytes 8192 | tf_op jit(solution)/shard_map/reshape | solution.py:453
  1.1 0.7 %slice.43 = bf16[8,1024]{1,0:T(8,128)(2,1)S(1)} slice(bf16[1024,1024]{1,0:T(8,128)(2,1)} %x_ref.1), slice={[1016:1024], [0:1024]} | slice | bytes 32768 | tf_op jit(solution)/shard_map/slice | solution.py:453
  1.9 4.5 %collective-permute-start = (bf16[8,1280]{1,0:T(8,128)(2,1)S(1)}, bf16[8,1280]{1,0:T(8,128)(2,1)S(1)}, u32[]{:S(2)}, u32[]{:S(2)}) collective-permute-start(bf16[8,1280]{1,0:T(8,128)(2,1)S(1)} %pad_maximum_fusion), channel_id=1, source_target_pairs={{0,4},{4,8},{8,12},{1,5},{5,9},{9,13},{2,6},{6,10},{10,14},{3,7},{... | collective-permute-start | bytes 61448 | tf_op jit(solution)/shard_map/ppermute | solution.py:17
  6.3 0.8 %reduce-window.9 = s32[3,1]{0,1:T(1,128)S(1)} reduce-window(s32[3,1]{0,1:T(1,128)} %bitcast.71, s32[]{:T(128)} %constant.26.clone.1), window={size=3x1 pad=2_0x0_0}, to_apply=%region_0.0 | reduce-window | flops 6 | bytes 28 | tf_op jit(solution)/shard_map/reduce-window.4
  7.2 0.7 bitcast_subtract_fusion
  7.8 0.1 convert_reduce_fusion
  7.9 0.1 slice_bitcast_fusion.2
  8.0 0.0 copy-start.4
  8.0 0.1 slice_reduce_fusion
  8.1 0.1 compare_convert_fusion
  8.2 0.7 %convert_element_type.42 = f32[2,4,128]{2,1,0:T(4,128)S(1)} convert(bf16[2,4,128]{2,1,0:T(4,128)(2,1)} %param.14) | non-fusion elementwise | flops 1024 | bytes 6144 | tf_op jit(solution)/shard_map/convert_element_type | solution.py:459
  8.9 0.0 collective-permute-done.tail_ref
  8.9 0.0 copy-start.6
  8.9 0.7 %pad_maximum_fusion.1.ownx_ref = f32[2,13,128]{2,1,0:T(8,128)S(1)} fusion(f32[2,1,128]{2,1,0:T(1,128)} %bitcast.69, f32[2,4,128]{2,1,0:T(4,128)S(1)} %convert_element_type.42, f32[2,8,128]{2,1,0:T(8,128)S(1)} %convert_bitcast_fusion), kind=kLoop, calls=%fused_computation.3 | loop fusion | flops 6656 | bytes 26624 | tf_op jit(solution)/shard_map/concatenate | solution.py:457
  9.6 0.0 copy-start.5
  9.6 0.2 collective-permute-start.2
  9.8 0.2 fusion.4
  10.0 0.6 convert_element_type.38.starts_ref
  10.6 0.1 stack.39
  10.7 0.0 copy-start.9
  10.7 1.0 %copy.24.info_ref.refs_6_ = f32[1024,8]{1,0:T(8,128)} copy(f32[1024,8]{0,1:T(8,128)S(1)} %stack.39) | data formatting | bytes 65536 | tf_op jit(solution)/shard_map/stack | solution.py:475
  11.7 0.0 collective-permute-done.2.otherx_ref
  11.7 0.0 copy-start.7
  11.7 0.0 collective-permute-done.1.other_ref
  11.7 0.0 copy-start.3
  11.7 0.0 copy-done.6
  11.7 0.0 copy-done.5
  11.7 0.6 copy-done.7
  12.3 0.2 copy-done.3
  12.5 16.6 %shard_map.100 = (f32[256,1024]{1,0:T(8,128)}, f32[1024,16]{1,0:T(8,128)}, f32[1024,16]{1,0:T(8,128)}, f32[8,1,1024]{2,1,0:T(1,128)}, f32[1,1024]{1,0:T(1,128)},...) custom-call(s32[8]{0:T(128)} %convert_element_type.38.starts_ref, ...), custom_call_target="tpu_custom_call" | custom-call | tf_op jit(solution)/shard_map/pallas_call | solution.py:244
  29.1 0.0 copy-done.4
  29.1 3.5 %collective-permute-start.3 = (bf16[256,1024]{1,0:T(8,128)(2,1)}, bf16[256,1024]{1,0:T(8,128)(2,1)S(1)}, u32[]{:S(2)}, u32[]{:S(2)}) collective-permute-start(bf16[256,1024]{1,0:T(8,128)(2,1)} %get-tuple-element.20), channel_id=1, source_target_pairs={{0,4},{4,8},{8,12},{1,5},{5,9},{9,13},{2,6},{6,10},{10,14},{3,7},{... | collective-permute-start | bytes 1572872 | tf_op jit(solution)/shard_map/ppermute | solution.py:17
  32.6 0.0 copy-done.9
  32.6 0.1 broadcast_in_dim.9
  32.7 0.7 reshape_reshape.3.refs_8_
  33.4 0.0 copy-start.1
  33.4 8.5 %shard_map.101 = (f32[512,1024]{1,0:T(8,128)}, f32[256,1024]{1,0:T(8,128)}) custom-call(bf16[1024,1024]{1,0:T(8,128)(2,1)} %get-tuple-element.21.refs_0_, bf16[1024,256]{1,0:T(8,128)(2,1)} %get-tuple-element.22.refs_1_, bf16[1024,256]{1,0:T(8,128)(2,1)} %get-tuple-element.23.refs_2_.c_ref, f32[1024,16]{1,0:T(8,128)} %get-tuple-element.24.refs_3_, ...), custom_call_target="tpu_custom_call" | custom-call | tf_op jit(solution)/shard_map/pallas_call | solution.py:355
  41.9 2.6 %collective-permute-done.3.refs_10_ = bf16[256,1024]{1,0:T(8,128)(2,1)S(1)} collective-permute-done((bf16[256,1024]{1,0:T(8,128)(2,1)}, bf16[256,1024]{1,0:T(8,128)(2,1)S(1)}, u32[]{:S(2)}, u32[]{:S(2)}) %collective-permute-start.3) | collective-permute-done | bytes 524320 | tf_op jit(solution)/shard_map/ppermute | solution.py:17
  44.5 0.0 copy-done.1
  44.5 0.0 copy-done.8
  44.5 0.2 add_convert_fusion
  44.7 4.3 %collective-permute-start.4 = (bf16[256,1024]{1,0:T(8,128)(2,1)S(1)}, bf16[256,1024]{1,0:T(8,128)(2,1)S(1)}, u32[]{:S(2)}, u32[]{:S(2)}) collective-permute-start(bf16[256,1024]{1,0:T(8,128)(2,1)S(1)} %add_convert_fusion), channel_id=1, source_target_pairs={{0,4},{4,8},{8,12},{1,5},{5,9},{9,13},{2,6},{6,10},{10,14},{3,7},{... | collective-permute-start | bytes 1572872 | tf_op jit(solution)/shard_map/ppermute | solution.py:17
  49.0 0.0 copy-done
  49.0 9.3 %shard_map.102.z_ref = f32[512,1024]{1,0:T(8,128)} custom-call(bf16[1024,1024]{1,0:T(8,128)(2,1)} %get-tuple-element.21.refs_0_, bf16[1024,256]{1,0:T(8,128)(2,1)} %get-tuple-element.22.refs_1_, bf16[1024,256]{1,0:T(8,128)(2,1)} %get-tuple-element.23.refs_2_.c_ref, f32[1024,16]{1,0:T(8,128)} %get-tuple-element.24.refs_3_, ...), custom_call_target="tpu_custom_call" | custom-call | tf_op jit(solution)/shard_map/pallas_call | solution.py:355
  58.4 1.4 %collective-permute-done.4.ein_ref = bf16[256,1024]{1,0:T(8,128)(2,1)S(1)} collective-permute-done((bf16[256,1024]{1,0:T(8,128)(2,1)S(1)}, bf16[256,1024]{1,0:T(8,128)(2,1)S(1)}, u32[]{:S(2)}, u32[]{:S(2)}) %collective-permute-start.4) | collective-permute-done | bytes 524320 | tf_op jit(solution)/shard_map/ppermute | solution.py:17
  59.8 0.8 %copy-done.2 = bf16[256,1024]{1,0:T(8,128)(2,1)} copy-done((bf16[256,1024]{1,0:T(8,128)(2,1)}, bf16[256,1024]{1,0:T(8,128)(2,1)S(1)}, u32[]{:S(2)}) %copy-start.2) | copy-done | bytes 524312
  60.6 6.5 %shard_map.103 = bf16[1024,1024]{1,0:T(8,128)(2,1)} custom-call(f32[512,1024]{1,0:T(8,128)} %get-tuple-element.29.y_ref, f32[512,1024]{1,0:T(8,128)} %shard_map.102.z_ref, bf16[1024,256]{1,0:T(8,128)(2,1)} %get-tuple-element.23.refs_2_.c_ref, f32[4,1024,4]{2,1,0:T(8,128)} %get-tuple-element.32.g_ref, bf16[256,1024]{1,0:T(8,128)(2,1)} %copy-done.2), custom_call_target="tpu_custom_call" | custom-call | tf_op jit(solution)/shard_map/pallas_call | solution.py:381
  (9 shorter events, 0.0 us)
Async XLA Ops:
  0.0 11.7 %collective-permute-start.1 = (bf16[2,1024,128]{2,1,0:T(8,128)(2,1)}, bf16[2,1024,128]{2,1,0:T(8,128)(2,1)S(1)}, u32[]{:S(2)}, u32[]{:S(2)}) collective-permute-start(bf16[2,1024,128]{2,1,0:T(8,128)(2,1)} %own_ref.1), channel_id=1, source_target_pairs={{0,1},{1,0},{2,3},{3,2},{4,5},{5,4},{6,7},{7,6},{8,9},{9,8},{10,11... | collective-permute-start | bytes 1572872 | tf_op jit(solution)/shard_map/ppermute | solution.py:27
  1.9 7.0 %collective-permute-start = (bf16[8,1280]{1,0:T(8,128)(2,1)S(1)}, bf16[8,1280]{1,0:T(8,128)(2,1)S(1)}, u32[]{:S(2)}, u32[]{:S(2)}) collective-permute-start(bf16[8,1280]{1,0:T(8,128)(2,1)S(1)} %pad_maximum_fusion), channel_id=1, source_target_pairs={{0,4},{4,8},{8,12},{1,5},{5,9},{9,13},{2,6},{6,10},{10,14},{3,7},{... | collective-permute-start | bytes 61448 | tf_op jit(solution)/shard_map/ppermute | solution.py:17
  8.0 21.0 %copy-start.4 = (f32[1024]{0:T(1024)}, f32[1024]{0:T(1024)S(1)}, u32[]{:S(2)}) copy-start(f32[1024]{0:T(1024)S(1)} %get-tuple-element.40) | copy-start | bytes 12292
  8.9 2.8 %copy-start.6 = (bf16[8,1280]{1,0:T(8,128)(2,1)}, bf16[8,1280]{1,0:T(8,128)(2,1)S(1)}, u32[]{:S(2)}) copy-start(bf16[8,1280]{1,0:T(8,128)(2,1)S(1)} %collective-permute-done.tail_ref) | copy-start | bytes 61444
  9.6 2.1 %copy-start.5 = (f32[2,13,128]{2,1,0:T(8,128)}, f32[2,13,128]{2,1,0:T(8,128)S(1)}, u32[]{:S(2)}) copy-start(f32[2,13,128]{2,1,0:T(8,128)S(1)} %pad_maximum_fusion.1.ownx_ref) | copy-start | bytes 39940
  9.6 2.1 %collective-permute-start.2 = (f32[2,13,128]{2,1,0:T(8,128)S(1)}, f32[2,13,128]{2,1,0:T(8,128)S(1)}, u32[]{:S(2)}, u32[]{:S(2)}) collective-permute-start(f32[2,13,128]{2,1,0:T(8,128)S(1)} %pad_maximum_fusion.1.ownx_ref), channel_id=1, source_target_pairs={{0,1},{1,0},{2,3},{3,2},{4,5},{5,4},{6,7},{7,6},{8,9},{9,8},{10,11... | collective-permute-start | bytes 39944 | tf_op jit(solution)/shard_map/ppermute | solution.py:27
  10.7 21.9 %copy-start.9 = (f32[16]{0:T(128)S(1)}, f32[16]{0:T(128)}, u32[]{:S(2)}) copy-start(f32[16]{0:T(128)} %param.18) | copy-start | bytes 196
  11.7 0.6 copy-start.7
  11.7 0.8 %copy-start.3 = (bf16[2,1024,128]{2,1,0:T(8,128)(2,1)}, bf16[2,1024,128]{2,1,0:T(8,128)(2,1)S(1)}, u32[]{:S(2)}) copy-start(bf16[2,1024,128]{2,1,0:T(8,128)(2,1)S(1)} %collective-permute-done.1.other_ref) | copy-start | bytes 1572868
  29.1 15.5 %collective-permute-start.3 = (bf16[256,1024]{1,0:T(8,128)(2,1)}, bf16[256,1024]{1,0:T(8,128)(2,1)S(1)}, u32[]{:S(2)}, u32[]{:S(2)}) collective-permute-start(bf16[256,1024]{1,0:T(8,128)(2,1)} %get-tuple-element.20), channel_id=1, source_target_pairs={{0,4},{4,8},{8,12},{1,5},{5,9},{9,13},{2,6},{6,10},{10,14},{3,7},{... | collective-permute-start | bytes 1572872 | tf_op jit(solution)/shard_map/ppermute | solution.py:17
  33.4 11.2 %copy-start.1 = (f32[256,1024]{1,0:T(8,128)S(1)}, f32[256,1024]{1,0:T(8,128)}, u32[]{:S(2)}) copy-start(f32[256,1024]{1,0:T(8,128)} %get-tuple-element.34) | copy-start | bytes 3145732
  33.4 11.2 %copy-start.8 = (f32[1,1024]{1,0:T(1,128)S(1)}, f32[1,1024]{1,0:T(1,128)}, u32[]{:S(2)}) copy-start(f32[1,1024]{1,0:T(1,128)} %get-tuple-element.33) | copy-start | bytes 12292
  44.5 4.5 %copy-start = (bf16[256,1024]{1,0:T(8,128)(2,1)}, bf16[256,1024]{1,0:T(8,128)(2,1)S(1)}, u32[]{:S(2)}) copy-start(bf16[256,1024]{1,0:T(8,128)(2,1)S(1)} %collective-permute-done.3.refs_10_) | copy-start | bytes 1572868
  44.7 15.1 %collective-permute-start.4 = (bf16[256,1024]{1,0:T(8,128)(2,1)S(1)}, bf16[256,1024]{1,0:T(8,128)(2,1)S(1)}, u32[]{:S(2)}, u32[]{:S(2)}) collective-permute-start(bf16[256,1024]{1,0:T(8,128)(2,1)S(1)} %add_convert_fusion), channel_id=1, source_target_pairs={{0,4},{4,8},{8,12},{1,5},{5,9},{9,13},{2,6},{6,10},{10,14},{3,7},{... | collective-permute-start | bytes 1572872 | tf_op jit(solution)/shard_map/ppermute | solution.py:17
  59.8 0.8 %copy-start.2 = (bf16[256,1024]{1,0:T(8,128)(2,1)}, bf16[256,1024]{1,0:T(8,128)(2,1)S(1)}, u32[]{:S(2)}) copy-start(bf16[256,1024]{1,0:T(8,128)(2,1)S(1)} %collective-permute-done.4.ein_ref) | copy-start | bytes 1572868

commit v20 on v15

--- a/solution.py
+++ b/solution.py
@@ -130,7 +130,7 @@
 
 def state_kernel(head_width, x_ref, tail_ref, wconv_ref, bias_ref, own_ref, other_ref, ownx_ref,
                  otherx_ref, dt_ref, rate_ref, info_ref, state_ref, l_ref, dtt_ref,
-                 decay_ref, total_ref, xc_ref, bo_ref, co_ref, sent_ref, prefix_ref, ltile_ref,
+                 decay_ref, total_ref, xc_ref, bo_ref, sent_ref, prefix_ref, ltile_ref,
                  prev_ref, bcprev_ref, small_ref):
     blk = pl.program_id(0)
 
@@ -150,7 +150,7 @@
     xc_ref[...] = xc
     lower = info_ref[0:1, 5:6] > 0.5
     convolved = []
-    for which in range(2):
+    for which in range(1):
         halves = []
         for side, (raw_ref, extra_ref) in enumerate(((own_ref, ownx_ref), (other_ref, otherx_ref))):
             raw_bc = raw_ref[which].astype(jnp.float32)
@@ -162,9 +162,8 @@
         convolved.append(jnp.where(
             lower, jnp.concatenate(halves, 1), jnp.concatenate(halves[::-1], 1)
         ))
-    b_mat, c_mat = convolved
+    b_mat = convolved[0]
     bo_ref[...] = b_mat
-    co_ref[...] = c_mat
 
     rows = lax.broadcasted_iota(jnp.int32, (2 * BLOCK, BLOCK), 0)
     cols = lax.broadcasted_iota(jnp.int32, (2 * BLOCK, BLOCK), 1)
@@ -235,7 +234,7 @@
                   whole((1, head_count)), row_block(info.shape[1])],
         out_specs=[whole((n_size, width)), row_block(head_count), row_block(head_count),
                    pl.BlockSpec((1, 1, width), lambda b: (b, 0, 0)), whole((1, width)),
-                   row_block(width), row_block(n_size), row_block(n_size),
+                   row_block(width), row_block(n_size),
                    whole((n_size, width)), pl.BlockSpec((1, 1, width), lambda b: (b, 0, 0)),
                    pl.BlockSpec((tiles, BLOCK, tile_heads), lambda b: (0, b, 0))],
         out_shape=[jax.ShapeDtypeStruct((n_size, width), jnp.float32),
@@ -244,7 +243,6 @@
                    jax.ShapeDtypeStruct((block_count, 1, width), jnp.float32),
                    jax.ShapeDtypeStruct((1, width), jnp.float32),
                    jax.ShapeDtypeStruct((rows, width), jnp.bfloat16),
-                   jax.ShapeDtypeStruct((rows, n_size), jnp.bfloat16),
                    jax.ShapeDtypeStruct((rows, n_size), jnp.bfloat16),
                    jax.ShapeDtypeStruct((n_size, width), jnp.bfloat16),
                    jax.ShapeDtypeStruct((block_count, 1, width), jnp.float32),
@@ -259,19 +257,24 @@
 
 def partial_kernel(head_width, from_zero, *refs):
     if from_zero:
-        (x_ref, b_ref, c_ref, l_ref, dt_ref, segr_ref, info_ref, decay_ref, skip_ref, out_ref,
-         end_ref, state_ref) = refs
+        (x_ref, b_ref, cown_ref, cother_ref, ownx_ref, otherx_ref, l_ref, dt_ref, segr_ref,
+         info_ref, decay_ref, skip_ref, out_ref, cout_ref, end_ref, state_ref, cprev_ref) = refs
     else:
-        (x_ref, b_ref, c_ref, l_ref, dt_ref, segr_ref, info_ref, decay_ref, skip_ref, init_ref,
-         after_ref, out_ref, state_ref) = refs
+        (x_ref, b_ref, cown_ref, cother_ref, ownx_ref, otherx_ref, l_ref, dt_ref, segr_ref,
+         info_ref, decay_ref, skip_ref, init_ref, after_ref, pown_ref, pother_ref, out_ref,
+         cout_ref, state_ref, cprev_ref) = refs
     blk = pl.program_id(0)
 
     @pl.when(blk == 0)
     def _():
         if from_zero:
             state_ref[...] = jnp.zeros(state_ref.shape, jnp.float32)
+            cprev_ref[0] = ownx_ref[1, 0:8, :]
+            cprev_ref[1] = otherx_ref[1, 0:8, :]
         else:
             state_ref[...] = init_ref[...]
+            cprev_ref[0] = pown_ref[0, 8:16, :].astype(jnp.float32)
+            cprev_ref[1] = pother_ref[0, 8:16, :].astype(jnp.float32)
 
     info = info_ref[...]
     seg_col = info[:, 0:1]
@@ -280,7 +283,15 @@
     dt_small = dt_ref[...]
     x = x_ref[...].astype(jnp.float32)
     state = state_ref[...]
-    c_mat = c_ref[...]
+    halves = []
+    for side, (raw_ref, extra_ref) in enumerate(((cown_ref, ownx_ref), (cother_ref, otherx_ref))):
+        raw_c = raw_ref[0].astype(jnp.float32)
+        extra = extra_ref[1]
+        halves.append(causal_conv(raw_c, cprev_ref[side], extra[8:12], extra[12:13], info))
+        cprev_ref[side] = raw_c[BLOCK - 8 :]
+    lower = info_ref[0:1, 5:6] > 0.5
+    c_mat = jnp.where(lower, jnp.concatenate(halves, 1), jnp.concatenate(halves[::-1], 1))
+    cout_ref[...] = c_mat
     b_mat = b_ref[...]
     scores = lax.dot_general(
         c_mat, b_mat, (((1,), (1,)), ((), ())), preferred_element_type=jnp.float32
@@ -313,24 +324,32 @@
                 end_ref[...] = new_state
 
 
-def run_partial(first, count, x, b_full, c_full, l_t, dt_t, seg_row, info, decay_x, skip_x,
+def run_partial(first, count, x, b_full, c_raws, l_t, dt_t, seg_row, info, decay_x, skip_x,
                 init=None, after=None):
     rows, width = x.shape
     head_count = l_t.shape[1]
     n_size = b_full.shape[1]
+    own_raw, other_raw, own_extra, other_extra = c_raws
+    half = own_raw.shape[2]
     row_block = lambda cols: pl.BlockSpec((BLOCK, cols), lambda b: (b + first, 0))
     whole = lambda shape: pl.BlockSpec(shape, lambda b: (0,) * len(shape))
     from_zero = init is None
-    in_specs = [row_block(width), row_block(n_size), row_block(n_size), row_block(head_count),
+    plane = pl.BlockSpec((1, BLOCK, half), lambda b: (1, b + first, 0))
+    in_specs = [row_block(width), row_block(n_size), plane, plane, whole(own_extra.shape),
+                whole(own_extra.shape), row_block(head_count),
                 row_block(head_count), pl.BlockSpec((1, BLOCK), lambda b: (0, b + first)),
                 row_block(info.shape[1]), pl.BlockSpec((1, 1, width), lambda b: (b + first, 0, 0)),
                 whole((1, width))]
-    args = [x, b_full, c_full, l_t, dt_t, seg_row, info, decay_x, skip_x]
+    args = [x, b_full, own_raw, other_raw, own_extra, other_extra, l_t, dt_t, seg_row, info,
+            decay_x, skip_x]
     if not from_zero:
-        in_specs += [whole((n_size, width)), pl.BlockSpec(memory_space=pl.ANY)]
-        args += [init, after]
-    out_specs = [pl.BlockSpec((BLOCK, width), lambda b: (b, 0))]
-    out_shape = [jax.ShapeDtypeStruct((count * BLOCK, width), jnp.float32)]
+        before = pl.BlockSpec((1, 16, half), lambda b: (1, first * (BLOCK // 16) - 1, 0))
+        in_specs += [whole((n_size, width)), pl.BlockSpec(memory_space=pl.ANY), before, before]
+        args += [init, after, own_raw, other_raw]
+    out_specs = [pl.BlockSpec((BLOCK, width), lambda b: (b, 0)),
+                 pl.BlockSpec((BLOCK, n_size), lambda b: (b, 0))]
+    out_shape = [jax.ShapeDtypeStruct((count * BLOCK, width), jnp.float32),
+                 jax.ShapeDtypeStruct((count * BLOCK, n_size), jnp.bfloat16)]
     if from_zero:
         out_specs.append(whole((n_size, width)))
         out_shape.append(jax.ShapeDtypeStruct((n_size, width), jnp.float32))
@@ -340,38 +359,42 @@
         in_specs=in_specs,
         out_specs=out_specs,
         out_shape=out_shape,
-        scratch_shapes=[pltpu.VMEM((n_size, width), jnp.float32)],
+        scratch_shapes=[pltpu.VMEM((n_size, width), jnp.float32),
+                        pltpu.VMEM((2, 8, half), jnp.float32)],
         compiler_params=pltpu.CompilerParams(dimension_semantics=("arbitrary",)),
     )(*args)
 
 
-def correct_kernel(head_width, y_ref, z_ref, c_ref, g_ref, ein_ref, out_ref):
+def correct_kernel(head_width, y_ref, z_ref, c_ref, d_ref, g_ref, ein_ref, out_ref):
     factor = expand_heads(g_ref[0], head_width)
-    carried = jnp.dot(c_ref[...], ein_ref[...], preferred_element_type=jnp.float32)
+    ein = ein_ref[...]
     split = y_ref.shape[0]
-    out_ref[:split] = (y_ref[...] + carried[:split] * factor[:split]).astype(jnp.bfloat16)
-    out_ref[split:] = (z_ref[...] + carried[split:] * factor[split:]).astype(jnp.bfloat16)
-
-
-def run_correct(first, second, c_full, g_tiles, entering):
+    carried = jnp.dot(c_ref[...], ein, preferred_element_type=jnp.float32)
+    out_ref[:split] = (y_ref[...] + carried * factor[:split]).astype(jnp.bfloat16)
+    carried = jnp.dot(d_ref[...], ein, preferred_element_type=jnp.float32)
+    out_ref[split:] = (z_ref[...] + carried * factor[split:]).astype(jnp.bfloat16)
+
+
+def run_correct(first, second, c_first, c_second, g_tiles, entering):
     rows = first.shape[0] + second.shape[0]
     width = first.shape[1]
     tiles, _, heads_per = g_tiles.shape
     tile = CORRECT_TILE
     head_width = tile // heads_per
-    n_size = c_full.shape[1]
+    n_size = c_first.shape[1]
     return pl.pallas_call(
         functools.partial(correct_kernel, head_width),
         grid=(tiles,),
         in_specs=[pl.BlockSpec((first.shape[0], tile), lambda j: (0, j)),
                   pl.BlockSpec((second.shape[0], tile), lambda j: (0, j)),
-                  pl.BlockSpec((rows, n_size), lambda j: (0, 0)),
+                  pl.BlockSpec((first.shape[0], n_size), lambda j: (0, 0)),
+                  pl.BlockSpec((second.shape[0], n_size), lambda j: (0, 0)),
                   pl.BlockSpec((1, rows, heads_per), lambda j: (j, 0, 0)),
                   pl.BlockSpec((n_size, tile), lambda j: (0, j))],
         out_specs=pl.BlockSpec((rows, tile), lambda j: (0, j)),
         out_shape=jax.ShapeDtypeStruct((rows, width), jnp.bfloat16),
         compiler_params=pltpu.CompilerParams(dimension_semantics=("arbitrary",)),
-    )(first, second, c_full, g_tiles, entering)
+    )(first, second, c_first, c_second, g_tiles, entering)
 
 
 def run_blocks(with_y, x, b_full, c_full, l_t, dt_t, seg_row, seg_col, entry_col, decay_x,
@@ -460,7 +483,7 @@
         1,
     )
 
-    (local_end, l_t, dt_t, decay_x, total_decay, inner_conv, b_full, c_full, end_sent,
+    (local_end, l_t, dt_t, decay_x, total_decay, inner_conv, b_full, end_sent,
      prefix_x, g_tiles) = run_state(
         inner_input, tails, conv_inner, bias_inner.reshape(1, -1), state_input, partner_raw,
         extra, partner_extra,
@@ -475,17 +498,20 @@
     part_rows = own_rows * lax.axis_size("seq")
     hops = min(lax.axis_size("seq") - 1, -(-(part_rows // 2) // own_rows))
     half_blocks = block_count // 2
-    operands = (inner_conv, b_full, c_full, l_t, dt_t, seg_row, info, decay_x, skip_x)
+    c_raws = (state_input, partner_raw, extra, partner_extra)
+    operands = (inner_conv, b_full, c_raws, l_t, dt_t, seg_row, info, decay_x, skip_x)
     incoming = shifted(end_sent, "seq", 1)
-    partial, middle = run_partial(0, half_blocks, *operands)
-    incoming, partial, middle = lax.optimization_barrier((incoming, partial, middle))
+    partial, c_first, middle = run_partial(0, half_blocks, *operands)
+    incoming, partial, c_first, middle = lax.optimization_barrier(
+        (incoming, partial, c_first, middle)
+    )
     first_hop = incoming
     for step_num in range(1, hops):
         incoming = relay(step_num, incoming)
-    (second,) = run_partial(
+    second, c_second = run_partial(
         half_blocks, block_count - half_blocks, *operands, init=middle, after=first_hop
     )
-    return run_correct(partial, second, c_full, g_tiles, incoming)
+    return run_correct(partial, second, c_first, c_second, g_tiles, incoming)
 
 
 def solution(mesh):

time: 62.1 us -> 61.6 us (level)
  waiting for transfers between devices: 4.02 us -> 3.16 us
    ppermute x3, waiting for transfers between devices: 4.01 us -> 3.16 us  [shifted(): lax.ppermute(value, axis, [(source, source + steps) for source in range(i...]
    pallas_call x2, Pallas kernels: 17.9 us -> 18.7 us  [run_partial(): pl.pallas_call(functools.partial(partial_kernel, width // head_count, fro...]
  transfers between devices with their start and end apart: 5 -> 5, of which waited for: 2 -> 2; matrix products, arithmetic and copies ran while one was open for 10% -> 11% of each run, Pallas kernels for 29% -> 31%
where the time goes in v20:
time: 61.6 us; the launch traced here: 61 us
  Pallas kernels  36.4 us (59%)
  starting transfers between devices  13 us (21%)
  local copies, waits for them, and re-layouts  5 us (8%)
  other arithmetic  3.28 us (5%)
  waiting for transfers between devices  3.16 us (5%)
    pallas_call x2, Pallas kernels, run_partial(): pl.pallas_call(functools.partial(partial_kernel, width // head_count, fro...  18.7 us
    ppermute x3, starting transfers between devices, shifted(): lax.ppermute(value, axis, [(source, source + steps) for source in range(i...  12.3 us
    pallas_call x1, Pallas kernels, run_state(): pl.pallas_call(functools.partial(state_kernel, width // head_count), grid...  11.4 us
    pallas_call x1, Pallas kernels, run_correct(): pl.pallas_call(functools.partial(correct_kernel, head_width), grid=(tiles...  6.29 us
    ppermute x3, waiting for transfers between devices, shifted(): lax.ppermute(value, axis, [(source, source + steps) for source in range(i...  3.16 us
    unnamed x20, local copies, waits for them, and re-layouts  1.61 us
  transfers between devices with their start and end apart: 5, of which 2 were waited for; matrix products, arithmetic and copies ran while one was open for 11% of the time, Pallas kernels for 31%

profile of v20, /device:TPU:0, one launch (start us, length us, event | category | flops | bytes accessed | tf_op | source)
XLA Modules:
  0.0 61.0 jit_solution(7002081578904248231)
XLA Ops:
  0.0 0.5 collective-permute-start.1
  0.5 0.7 %slice_bitcast_fusion.1 = bf16[8,256]{1,0:T(8,128)(2,1)S(1)} fusion(bf16[2,1024,128]{2,1,0:T(8,128)(2,1)} %refs_14_.1), kind=kLoop, calls=%fused_computation.12 | loop fusion | bytes 8192 | tf_op jit(solution)/shard_map/reshape | solution.py:458
  1.1 0.7 %slice.27 = bf16[8,1024]{1,0:T(8,128)(2,1)S(1)} slice(bf16[1024,1024]{1,0:T(8,128)(2,1)} %x_ref.1), slice={[1016:1024], [0:1024]} | slice | bytes 32768 | tf_op jit(solution)/shard_map/slice | solution.py:458
  1.9 4.5 %collective-permute-start = (bf16[8,1280]{1,0:T(8,128)(2,1)S(1)}, bf16[8,1280]{1,0:T(8,128)(2,1)S(1)}, u32[]{:S(2)}, u32[]{:S(2)}) collective-permute-start(bf16[8,1280]{1,0:T(8,128)(2,1)S(1)} %pad_maximum_fusion), channel_id=1, source_target_pairs={{0,4},{4,8},{8,12},{1,5},{5,9},{9,13},{2,6},{6,10},{10,14},{3,7},{... | collective-permute-start | bytes 61448 | tf_op jit(solution)/shard_map/ppermute | solution.py:17
  6.3 0.8 %reduce-window.9 = s32[3,1]{0,1:T(1,128)S(1)} reduce-window(s32[3,1]{0,1:T(1,128)} %bitcast.41, s32[]{:T(128)} %constant.25.clone.1), window={size=3x1 pad=2_0x0_0}, to_apply=%region_0.0 | reduce-window | flops 6 | bytes 28 | tf_op jit(solution)/shard_map/reduce-window.4
  7.2 0.7 %bitcast_subtract_fusion = s32[3]{0:T(128)S(1)} fusion(s32[3]{0:T(128)} %param.19, s32[3,1]{0,1:T(1,128)S(1)} %reduce-window.9), kind=kLoop, calls=%fused_computation.19 | loop fusion | flops 3 | bytes 36 | tf_op jit(solution)/shard_map/sub | solution.py:31
  7.8 0.1 convert_reduce_fusion
  7.9 0.1 slice_bitcast_fusion.2
  8.0 0.0 copy-start.6
  8.0 0.1 slice_reduce_fusion
  8.1 0.7 %convert_element_type.37 = f32[2,4,128]{2,1,0:T(4,128)S(1)} convert(bf16[2,4,128]{2,1,0:T(4,128)(2,1)} %param.14) | non-fusion elementwise | flops 1024 | bytes 6144 | tf_op jit(solution)/shard_map/convert_element_type | solution.py:464
  8.8 0.0 collective-permute-done.tail_ref
  8.8 0.0 copy-start.7
  8.8 0.7 %pad_maximum_fusion.1.ownx_ref.refs_4_ = f32[2,13,128]{2,1,0:T(8,128)S(1)} fusion(f32[2,1,128]{2,1,0:T(1,128)} %bitcast.39, f32[2,4,128]{2,1,0:T(4,128)S(1)} %convert_element_type.37, f32[2,8,128]{2,1,0:T(8,128)S(1)} %convert_bitcast_fusion), kind=kLoop, calls=%fused_computation.3 | loop fusion | flops 6656 | bytes 26624 | tf_op jit(solution)/shard_map/concatenate | solution.py:462
  9.5 0.0 copy-start.4
  9.5 0.2 collective-permute-start.2
  9.8 0.1 fusion.2
  9.8 0.1 stack.39
  9.9 0.0 copy-start.9
  9.9 1.1 %copy.24.info_ref.refs_9_ = f32[1024,8]{1,0:T(8,128)} copy(f32[1024,8]{0,1:T(8,128)S(1)} %stack.39) | data formatting | bytes 65536 | tf_op jit(solution)/shard_map/stack | solution.py:478
  11.0 0.0 collective-permute-done.2.otherx_ref.refs_5_
  11.0 0.0 copy-start.5
  11.0 0.0 collective-permute-done.1.other_ref.refs_3_.refs_15_
  11.0 0.0 copy-start
  11.0 0.0 copy-done.7
  11.0 0.0 copy-done.4
  11.0 0.6 copy-done.5
  11.6 0.2 copy-done
  11.8 11.4 %shard_map.100 = (f32[256,1024]{1,0:T(8,128)}, f32[1024,16]{1,0:T(8,128)}, f32[1024,16]{1,0:T(8,128)}, f32[8,1,1024]{2,1,0:T(1,128)}, f32[1,1024]{1,0:T(1,128)},...) custom-call(bf16[1024,1024]{1,0:T(8,128)(2,1)} %x_ref.1, ...), custom_call_target="tpu_custom_call" | custom-call | tf_op jit(solution)/shard_map/pallas_call | solution.py:226
  23.2 0.0 copy-done.6
  23.2 3.5 %collective-permute-start.3 = (bf16[256,1024]{1,0:T(8,128)(2,1)}, bf16[256,1024]{1,0:T(8,128)(2,1)S(1)}, u32[]{:S(2)}, u32[]{:S(2)}) collective-permute-start(bf16[256,1024]{1,0:T(8,128)(2,1)} %get-tuple-element.23), channel_id=1, source_target_pairs={{0,4},{4,8},{8,12},{1,5},{5,9},{9,13},{2,6},{6,10},{10,14},{3,7},{... | collective-permute-start | bytes 1572872 | tf_op jit(solution)/shard_map/ppermute | solution.py:17
  26.7 0.0 copy-done.9
  26.7 0.1 broadcast_in_dim.9
  26.8 0.7 %reshape_reshape.3.refs_11_ = f32[1,1024]{1,0:T(1,128)} reshape(f32[16,64]{1,0:T(8,128)S(1)} %broadcast_in_dim.9) | data formatting | bytes 8192 | tf_op jit(solution)/shard_map/reshape;reshape | solution.py:471
  27.5 0.0 copy-start.2
  27.5 0.0 copy-start.8
  27.5 9.0 %shard_map.101 = (f32[512,1024]{1,0:T(8,128)}, bf16[512,256]{1,0:T(8,128)(2,1)}, f32[256,1024]{1,0:T(8,128)}) custom-call(bf16[1024,1024]{1,0:T(8,128)(2,1)} %get-tuple-element.24.refs_0_, bf16[1024,256]{1,0:T(8,128)(2,1)} %get-tuple-element.25.refs_1_, bf16[2,1024,128]{2,1,0:T(8,128)(2,1)} %refs_14_.1, bf16[2,1024,128]{2,1,0:T(8,128)(2,1)} %copy-done, ...), custom_call_target="tpu_custom_call" | custom-call | tf_op jit(solution)/shard_map/pallas_call | solution.py:356
  36.4 2.2 %collective-permute-done.3.refs_13_ = bf16[256,1024]{1,0:T(8,128)(2,1)S(1)} collective-permute-done((bf16[256,1024]{1,0:T(8,128)(2,1)}, bf16[256,1024]{1,0:T(8,128)(2,1)S(1)}, u32[]{:S(2)}, u32[]{:S(2)}) %collective-permute-start.3) | collective-permute-done | bytes 524320 | tf_op jit(solution)/shard_map/ppermute | solution.py:17
  38.6 0.0 copy-start.1
  38.6 0.0 copy-done.2
  38.6 0.0 copy-done.8
  38.6 0.2 add_convert_fusion
  38.8 4.3 %collective-permute-start.4 = (bf16[256,1024]{1,0:T(8,128)(2,1)S(1)}, bf16[256,1024]{1,0:T(8,128)(2,1)S(1)}, u32[]{:S(2)}, u32[]{:S(2)}) collective-permute-start(bf16[256,1024]{1,0:T(8,128)(2,1)S(1)} %add_convert_fusion), channel_id=1, source_target_pairs={{0,4},{4,8},{8,12},{1,5},{5,9},{9,13},{2,6},{6,10},{10,14},{3,7},{... | collective-permute-start | bytes 1572872 | tf_op jit(solution)/shard_map/ppermute | solution.py:17
  43.1 0.0 copy-done.1
  43.1 9.7 %shard_map.102 = (f32[512,1024]{1,0:T(8,128)}, bf16[512,256]{1,0:T(8,128)(2,1)}) custom-call(bf16[1024,1024]{1,0:T(8,128)(2,1)} %get-tuple-element.24.refs_0_, bf16[1024,256]{1,0:T(8,128)(2,1)} %get-tuple-element.25.refs_1_, bf16[2,1024,128]{2,1,0:T(8,128)(2,1)} %refs_14_.1, bf16[2,1024,128]{2,1,0:T(8,128)(2,1)} %copy-done, f32[2,13,128]{2,1,0:T(8,128)} %copy-done.4, ...), custom_call_target="tpu_custom_call" | custom-call | tf_op jit(solution)/shard_map/pallas_call | solution.py:356
  52.8 1.0 %collective-permute-done.4.ein_ref = bf16[256,1024]{1,0:T(8,128)(2,1)S(1)} collective-permute-done((bf16[256,1024]{1,0:T(8,128)(2,1)S(1)}, bf16[256,1024]{1,0:T(8,128)(2,1)S(1)}, u32[]{:S(2)}, u32[]{:S(2)}) %collective-permute-start.4) | collective-permute-done | bytes 524320 | tf_op jit(solution)/shard_map/ppermute | solution.py:17
  53.8 0.8 %copy-done.3 = bf16[256,1024]{1,0:T(8,128)(2,1)} copy-done((bf16[256,1024]{1,0:T(8,128)(2,1)}, bf16[256,1024]{1,0:T(8,128)(2,1)S(1)}, u32[]{:S(2)}) %copy-start.3) | copy-done | bytes 524312
  54.7 6.3 %shard_map.103 = bf16[1024,1024]{1,0:T(8,128)(2,1)} custom-call(f32[512,1024]{1,0:T(8,128)} %get-tuple-element.32.y_ref, f32[512,1024]{1,0:T(8,128)} %get-tuple-element.35.z_ref, bf16[512,256]{1,0:T(8,128)(2,1)} %get-tuple-element.36.c_ref, bf16[512,256]{1,0:T(8,128)(2,1)} %get-tuple-element.37.d_ref, f32[4,1024,4]{2,1,0:T(8,128)} %get-tuple-element.38.g_ref, ...), custom_call_target="tpu_custom_call" | custom-call | tf_op jit(solution)/shard_map/pallas_call | solution.py:385
  (7 shorter events, 0.0 us)
Async XLA Ops:
  0.0 11.0 %collective-permute-start.1 = (bf16[2,1024,128]{2,1,0:T(8,128)(2,1)}, bf16[2,1024,128]{2,1,0:T(8,128)(2,1)S(1)}, u32[]{:S(2)}, u32[]{:S(2)}) collective-permute-start(bf16[2,1024,128]{2,1,0:T(8,128)(2,1)} %refs_14_.1), channel_id=1, source_target_pairs={{0,1},{1,0},{2,3},{3,2},{4,5},{5,4},{6,7},{7,6},{8,9},{9,8},{10,11... | collective-permute-start | bytes 1572872 | tf_op jit(solution)/shard_map/ppermute | solution.py:27
  1.9 7.0 %collective-permute-start = (bf16[8,1280]{1,0:T(8,128)(2,1)S(1)}, bf16[8,1280]{1,0:T(8,128)(2,1)S(1)}, u32[]{:S(2)}, u32[]{:S(2)}) collective-permute-start(bf16[8,1280]{1,0:T(8,128)(2,1)S(1)} %pad_maximum_fusion), channel_id=1, source_target_pairs={{0,4},{4,8},{8,12},{1,5},{5,9},{9,13},{2,6},{6,10},{10,14},{3,7},{... | collective-permute-start | bytes 61448 | tf_op jit(solution)/shard_map/ppermute | solution.py:17
  8.0 15.2 %copy-start.6 = (f32[1024]{0:T(1024)}, f32[1024]{0:T(1024)S(1)}, u32[]{:S(2)}) copy-start(f32[1024]{0:T(1024)S(1)} %get-tuple-element.46) | copy-start | bytes 12292
  8.8 2.2 %copy-start.7 = (bf16[8,1280]{1,0:T(8,128)(2,1)}, bf16[8,1280]{1,0:T(8,128)(2,1)S(1)}, u32[]{:S(2)}) copy-start(bf16[8,1280]{1,0:T(8,128)(2,1)S(1)} %collective-permute-done.tail_ref) | copy-start | bytes 61444
  9.5 1.5 %copy-start.4 = (f32[2,13,128]{2,1,0:T(8,128)}, f32[2,13,128]{2,1,0:T(8,128)S(1)}, u32[]{:S(2)}) copy-start(f32[2,13,128]{2,1,0:T(8,128)S(1)} %pad_maximum_fusion.1.ownx_ref.refs_4_) | copy-start | bytes 39940
  9.5 1.4 %collective-permute-start.2 = (f32[2,13,128]{2,1,0:T(8,128)S(1)}, f32[2,13,128]{2,1,0:T(8,128)S(1)}, u32[]{:S(2)}, u32[]{:S(2)}) collective-permute-start(f32[2,13,128]{2,1,0:T(8,128)S(1)} %pad_maximum_fusion.1.ownx_ref.refs_4_), channel_id=1, source_target_pairs={{0,1},{1,0},{2,3},{3,2},{4,5},{5,4},{6,7},{7,6},{8,9},{9,8},{10,11... | collective-permute-start | bytes 39944 | tf_op jit(solution)/shard_map/ppermute | solution.py:27
  9.9 16.8 %copy-start.9 = (f32[16]{0:T(128)S(1)}, f32[16]{0:T(128)}, u32[]{:S(2)}) copy-start(f32[16]{0:T(128)} %param.18) | copy-start | bytes 196
  11.0 0.6 copy-start.5
  11.0 0.8 %copy-start = (bf16[2,1024,128]{2,1,0:T(8,128)(2,1)}, bf16[2,1024,128]{2,1,0:T(8,128)(2,1)S(1)}, u32[]{:S(2)}) copy-start(bf16[2,1024,128]{2,1,0:T(8,128)(2,1)S(1)} %collective-permute-done.1.other_ref.refs_3_.refs_15_) | copy-start | bytes 1572868
  23.2 15.4 %collective-permute-start.3 = (bf16[256,1024]{1,0:T(8,128)(2,1)}, bf16[256,1024]{1,0:T(8,128)(2,1)S(1)}, u32[]{:S(2)}, u32[]{:S(2)}) collective-permute-start(bf16[256,1024]{1,0:T(8,128)(2,1)} %get-tuple-element.23), channel_id=1, source_target_pairs={{0,4},{4,8},{8,12},{1,5},{5,9},{9,13},{2,6},{6,10},{10,14},{3,7},{... | collective-permute-start | bytes 1572872 | tf_op jit(solution)/shard_map/ppermute | solution.py:17
  27.5 11.1 %copy-start.2 = (f32[256,1024]{1,0:T(8,128)S(1)}, f32[256,1024]{1,0:T(8,128)}, u32[]{:S(2)}) copy-start(f32[256,1024]{1,0:T(8,128)} %get-tuple-element.40) | copy-start | bytes 3145732
  27.5 11.1 %copy-start.8 = (f32[1,1024]{1,0:T(1,128)S(1)}, f32[1,1024]{1,0:T(1,128)}, u32[]{:S(2)}) copy-start(f32[1,1024]{1,0:T(1,128)} %get-tuple-element.39) | copy-start | bytes 12292
  38.6 4.5 %copy-start.1 = (bf16[256,1024]{1,0:T(8,128)(2,1)}, bf16[256,1024]{1,0:T(8,128)(2,1)S(1)}, u32[]{:S(2)}) copy-start(bf16[256,1024]{1,0:T(8,128)(2,1)S(1)} %collective-permute-done.3.refs_13_) | copy-start | bytes 1572868
  38.8 15.1 %collective-permute-start.4 = (bf16[256,1024]{1,0:T(8,128)(2,1)S(1)}, bf16[256,1024]{1,0:T(8,128)(2,1)S(1)}, u32[]{:S(2)}, u32[]{:S(2)}) collective-permute-start(bf16[256,1024]{1,0:T(8,128)(2,1)S(1)} %add_convert_fusion), channel_id=1, source_target_pairs={{0,4},{4,8},{8,12},{1,5},{5,9},{9,13},{2,6},{6,10},{10,14},{3,7},{... | collective-permute-start | bytes 1572872 | tf_op jit(solution)/shard_map/ppermute | solution.py:17
  53.8 0.8 %copy-start.3 = (bf16[256,1024]{1,0:T(8,128)(2,1)}, bf16[256,1024]{1,0:T(8,128)(2,1)S(1)}, u32[]{:S(2)}) copy-start(bf16[256,1024]{1,0:T(8,128)(2,1)S(1)} %collective-permute-done.4.ein_ref) | copy-start | bytes 1572868

commit v21 on v20

--- a/solution.py
+++ b/solution.py
@@ -8,7 +8,7 @@
 from jax.sharding import PartitionSpec as P
 
 BLOCK = 128
-CORRECT_TILE = 256
+CORRECT_TILE = 512
 
 
 def shifted(value, axis, steps):

time: 61.6 us -> 60.9 us (0.989)
  no operation moved by 1% of the time
where the time goes in v21:
time: 60.9 us; the launch traced here: 60.4 us
  Pallas kernels  35.8 us (59%)
  starting transfers between devices  13 us (21%)
  local copies, waits for them, and re-layouts  4.97 us (8%)
  other arithmetic  3.28 us (5%)
  waiting for transfers between devices  3.19 us (5%)
    pallas_call x2, Pallas kernels, run_partial(): pl.pallas_call(functools.partial(partial_kernel, width // head_count, fro...  18.7 us
    ppermute x3, starting transfers between devices, shifted(): lax.ppermute(value, axis, [(source, source + steps) for source in range(i...  12.3 us
    pallas_call x1, Pallas kernels, run_state(): pl.pallas_call(functools.partial(state_kernel, width // head_count), grid...  11.1 us
    pallas_call x1, Pallas kernels, run_correct(): pl.pallas_call(functools.partial(correct_kernel, head_width), grid=(tiles...  6.04 us
    ppermute x3, waiting for transfers between devices, shifted(): lax.ppermute(value, axis, [(source, source + steps) for source in range(i...  3.19 us
    unnamed x20, local copies, waits for them, and re-layouts  1.65 us
  transfers between devices with their start and end apart: 5, of which 2 were waited for; matrix products, arithmetic and copies ran while one was open for 11% of the time, Pallas kernels for 31%

profile of v21, /device:TPU:0, one launch (start us, length us, event | category | flops | bytes accessed | tf_op | source)
XLA Modules:
  0.0 60.4 jit_solution(4095757185260489045)
XLA Ops:
  0.0 0.5 collective-permute-start.1
  0.5 0.7 %slice_bitcast_fusion.1 = bf16[8,256]{1,0:T(8,128)(2,1)S(1)} fusion(bf16[2,1024,128]{2,1,0:T(8,128)(2,1)} %refs_14_.1), kind=kLoop, calls=%fused_computation.12 | loop fusion | bytes 8192 | tf_op jit(solution)/shard_map/reshape | solution.py:458
  1.1 0.7 %slice.27 = bf16[8,1024]{1,0:T(8,128)(2,1)S(1)} slice(bf16[1024,1024]{1,0:T(8,128)(2,1)} %x_ref.1), slice={[1016:1024], [0:1024]} | slice | bytes 32768 | tf_op jit(solution)/shard_map/slice | solution.py:458
  1.9 4.5 %collective-permute-start = (bf16[8,1280]{1,0:T(8,128)(2,1)S(1)}, bf16[8,1280]{1,0:T(8,128)(2,1)S(1)}, u32[]{:S(2)}, u32[]{:S(2)}) collective-permute-start(bf16[8,1280]{1,0:T(8,128)(2,1)S(1)} %pad_maximum_fusion), channel_id=1, source_target_pairs={{0,4},{4,8},{8,12},{1,5},{5,9},{9,13},{2,6},{6,10},{10,14},{3,7},{... | collective-permute-start | bytes 61448 | tf_op jit(solution)/shard_map/ppermute | solution.py:17
  6.3 0.8 %reduce-window.9 = s32[3,1]{0,1:T(1,128)S(1)} reduce-window(s32[3,1]{0,1:T(1,128)} %bitcast.41, s32[]{:T(128)} %constant.25.clone.1), window={size=3x1 pad=2_0x0_0}, to_apply=%region_0.0 | reduce-window | flops 6 | bytes 28 | tf_op jit(solution)/shard_map/reduce-window.4
  7.2 0.7 %bitcast_subtract_fusion = s32[3]{0:T(128)S(1)} fusion(s32[3]{0:T(128)} %param.19, s32[3,1]{0,1:T(1,128)S(1)} %reduce-window.9), kind=kLoop, calls=%fused_computation.19 | loop fusion | flops 3 | bytes 36 | tf_op jit(solution)/shard_map/sub | solution.py:31
  7.8 0.1 convert_reduce_fusion
  7.9 0.1 slice_bitcast_fusion.2
  8.0 0.0 copy-start.6
  8.0 0.1 slice_reduce_fusion
  8.1 0.7 %convert_element_type.37 = f32[2,4,128]{2,1,0:T(4,128)S(1)} convert(bf16[2,4,128]{2,1,0:T(4,128)(2,1)} %param.14) | non-fusion elementwise | flops 1024 | bytes 6144 | tf_op jit(solution)/shard_map/convert_element_type | solution.py:464
  8.8 0.0 collective-permute-done.tail_ref
  8.8 0.0 copy-start.7
  8.8 0.7 %pad_maximum_fusion.1.ownx_ref.refs_4_ = f32[2,13,128]{2,1,0:T(8,128)S(1)} fusion(f32[2,1,128]{2,1,0:T(1,128)} %bitcast.39, f32[2,4,128]{2,1,0:T(4,128)S(1)} %convert_element_type.37, f32[2,8,128]{2,1,0:T(8,128)S(1)} %convert_bitcast_fusion), kind=kLoop, calls=%fused_computation.3 | loop fusion | flops 6656 | bytes 26624 | tf_op jit(solution)/shard_map/concatenate | solution.py:462
  9.5 0.0 copy-start.4
  9.5 0.2 collective-permute-start.2
  9.8 0.1 fusion.2
  9.8 0.1 stack.39
  9.9 0.0 copy-start.9
  9.9 1.0 %copy.24.info_ref.refs_9_ = f32[1024,8]{1,0:T(8,128)} copy(f32[1024,8]{0,1:T(8,128)S(1)} %stack.39) | data formatting | bytes 65536 | tf_op jit(solution)/shard_map/stack | solution.py:478
  10.9 0.0 collective-permute-done.2.otherx_ref.refs_5_
  10.9 0.0 copy-start.5
  10.9 0.0 collective-permute-done.1.other_ref.refs_3_.refs_15_
  10.9 0.0 copy-start
  10.9 0.0 copy-done.7
  11.0 0.0 copy-done.4
  11.0 0.6 copy-done.5
  11.5 0.2 copy-done
  11.8 11.1 %shard_map.100 = (f32[256,1024]{1,0:T(8,128)}, f32[1024,16]{1,0:T(8,128)}, f32[1024,16]{1,0:T(8,128)}, f32[8,1,1024]{2,1,0:T(1,128)}, f32[1,1024]{1,0:T(1,128)},...) custom-call(bf16[1024,1024]{1,0:T(8,128)(2,1)} %x_ref.1, ...), custom_call_target="tpu_custom_call" | custom-call | tf_op jit(solution)/shard_map/pallas_call | solution.py:226
  22.8 0.0 copy-done.6
  22.8 3.5 %collective-permute-start.3 = (bf16[256,1024]{1,0:T(8,128)(2,1)}, bf16[256,1024]{1,0:T(8,128)(2,1)S(1)}, u32[]{:S(2)}, u32[]{:S(2)}) collective-permute-start(bf16[256,1024]{1,0:T(8,128)(2,1)} %get-tuple-element.23), channel_id=1, source_target_pairs={{0,4},{4,8},{8,12},{1,5},{5,9},{9,13},{2,6},{6,10},{10,14},{3,7},{... | collective-permute-start | bytes 1572872 | tf_op jit(solution)/shard_map/ppermute | solution.py:17
  26.4 0.0 copy-done.9
  26.4 0.1 broadcast_in_dim.9
  26.4 0.7 %reshape_reshape.3.refs_11_ = f32[1,1024]{1,0:T(1,128)} reshape(f32[16,64]{1,0:T(8,128)S(1)} %broadcast_in_dim.9) | data formatting | bytes 8192 | tf_op jit(solution)/shard_map/reshape;reshape | solution.py:471
  27.1 0.0 copy-start.2
  27.1 0.0 copy-start.8
  27.1 9.0 %shard_map.101 = (f32[512,1024]{1,0:T(8,128)}, bf16[512,256]{1,0:T(8,128)(2,1)}, f32[256,1024]{1,0:T(8,128)}) custom-call(bf16[1024,1024]{1,0:T(8,128)(2,1)} %get-tuple-element.24.refs_0_, bf16[1024,256]{1,0:T(8,128)(2,1)} %get-tuple-element.25.refs_1_, bf16[2,1024,128]{2,1,0:T(8,128)(2,1)} %refs_14_.1, bf16[2,1024,128]{2,1,0:T(8,128)(2,1)} %copy-done, ...), custom_call_target="tpu_custom_call" | custom-call | tf_op jit(solution)/shard_map/pallas_call | solution.py:356
  36.1 2.2 %collective-permute-done.3.refs_13_ = bf16[256,1024]{1,0:T(8,128)(2,1)S(1)} collective-permute-done((bf16[256,1024]{1,0:T(8,128)(2,1)}, bf16[256,1024]{1,0:T(8,128)(2,1)S(1)}, u32[]{:S(2)}, u32[]{:S(2)}) %collective-permute-start.3) | collective-permute-done | bytes 524320 | tf_op jit(solution)/shard_map/ppermute | solution.py:17
  38.3 0.0 copy-start.1
  38.3 0.0 copy-done.2
  38.3 0.0 copy-done.8
  38.3 0.2 add_convert_fusion
  38.4 4.3 %collective-permute-start.4 = (bf16[256,1024]{1,0:T(8,128)(2,1)S(1)}, bf16[256,1024]{1,0:T(8,128)(2,1)S(1)}, u32[]{:S(2)}, u32[]{:S(2)}) collective-permute-start(bf16[256,1024]{1,0:T(8,128)(2,1)S(1)} %add_convert_fusion), channel_id=1, source_target_pairs={{0,4},{4,8},{8,12},{1,5},{5,9},{9,13},{2,6},{6,10},{10,14},{3,7},{... | collective-permute-start | bytes 1572872 | tf_op jit(solution)/shard_map/ppermute | solution.py:17
  42.7 0.0 copy-done.1
  42.8 9.7 %shard_map.102 = (f32[512,1024]{1,0:T(8,128)}, bf16[512,256]{1,0:T(8,128)(2,1)}) custom-call(bf16[1024,1024]{1,0:T(8,128)(2,1)} %get-tuple-element.24.refs_0_, bf16[1024,256]{1,0:T(8,128)(2,1)} %get-tuple-element.25.refs_1_, bf16[2,1024,128]{2,1,0:T(8,128)(2,1)} %refs_14_.1, bf16[2,1024,128]{2,1,0:T(8,128)(2,1)} %copy-done, f32[2,13,128]{2,1,0:T(8,128)} %copy-done.4, ...), custom_call_target="tpu_custom_call" | custom-call | tf_op jit(solution)/shard_map/pallas_call | solution.py:356
  52.5 1.0 %collective-permute-done.4.ein_ref = bf16[256,1024]{1,0:T(8,128)(2,1)S(1)} collective-permute-done((bf16[256,1024]{1,0:T(8,128)(2,1)S(1)}, bf16[256,1024]{1,0:T(8,128)(2,1)S(1)}, u32[]{:S(2)}, u32[]{:S(2)}) %collective-permute-start.4) | collective-permute-done | bytes 524320 | tf_op jit(solution)/shard_map/ppermute | solution.py:17
  53.5 0.8 %copy-done.3 = bf16[256,1024]{1,0:T(8,128)(2,1)} copy-done((bf16[256,1024]{1,0:T(8,128)(2,1)}, bf16[256,1024]{1,0:T(8,128)(2,1)S(1)}, u32[]{:S(2)}) %copy-start.3) | copy-done | bytes 524312
  54.3 6.0 %shard_map.103 = bf16[1024,1024]{1,0:T(8,128)(2,1)} custom-call(f32[512,1024]{1,0:T(8,128)} %get-tuple-element.32.y_ref, f32[512,1024]{1,0:T(8,128)} %get-tuple-element.35.z_ref, bf16[512,256]{1,0:T(8,128)(2,1)} %get-tuple-element.36.c_ref, bf16[512,256]{1,0:T(8,128)(2,1)} %get-tuple-element.37.d_ref, f32[2,1024,8]{2,1,0:T(8,128)} %get-tuple-element.38.g_ref, ...), custom_call_target="tpu_custom_call" | custom-call | tf_op jit(solution)/shard_map/pallas_call | solution.py:385
  (7 shorter events, 0.0 us)
Async XLA Ops:
  0.0 10.9 %collective-permute-start.1 = (bf16[2,1024,128]{2,1,0:T(8,128)(2,1)}, bf16[2,1024,128]{2,1,0:T(8,128)(2,1)S(1)}, u32[]{:S(2)}, u32[]{:S(2)}) collective-permute-start(bf16[2,1024,128]{2,1,0:T(8,128)(2,1)} %refs_14_.1), channel_id=1, source_target_pairs={{0,1},{1,0},{2,3},{3,2},{4,5},{5,4},{6,7},{7,6},{8,9},{9,8},{10,11... | collective-permute-start | bytes 1572872 | tf_op jit(solution)/shard_map/ppermute | solution.py:27
  1.9 7.0 %collective-permute-start = (bf16[8,1280]{1,0:T(8,128)(2,1)S(1)}, bf16[8,1280]{1,0:T(8,128)(2,1)S(1)}, u32[]{:S(2)}, u32[]{:S(2)}) collective-permute-start(bf16[8,1280]{1,0:T(8,128)(2,1)S(1)} %pad_maximum_fusion), channel_id=1, source_target_pairs={{0,4},{4,8},{8,12},{1,5},{5,9},{9,13},{2,6},{6,10},{10,14},{3,7},{... | collective-permute-start | bytes 61448 | tf_op jit(solution)/shard_map/ppermute | solution.py:17
  8.0 14.8 %copy-start.6 = (f32[1024]{0:T(1024)}, f32[1024]{0:T(1024)S(1)}, u32[]{:S(2)}) copy-start(f32[1024]{0:T(1024)S(1)} %get-tuple-element.46) | copy-start | bytes 12292
  8.8 2.1 %copy-start.7 = (bf16[8,1280]{1,0:T(8,128)(2,1)}, bf16[8,1280]{1,0:T(8,128)(2,1)S(1)}, u32[]{:S(2)}) copy-start(bf16[8,1280]{1,0:T(8,128)(2,1)S(1)} %collective-permute-done.tail_ref) | copy-start | bytes 61444
  9.5 1.4 %copy-start.4 = (f32[2,13,128]{2,1,0:T(8,128)}, f32[2,13,128]{2,1,0:T(8,128)S(1)}, u32[]{:S(2)}) copy-start(f32[2,13,128]{2,1,0:T(8,128)S(1)} %pad_maximum_fusion.1.ownx_ref.refs_4_) | copy-start | bytes 39940
  9.5 1.4 %collective-permute-start.2 = (f32[2,13,128]{2,1,0:T(8,128)S(1)}, f32[2,13,128]{2,1,0:T(8,128)S(1)}, u32[]{:S(2)}, u32[]{:S(2)}) collective-permute-start(f32[2,13,128]{2,1,0:T(8,128)S(1)} %pad_maximum_fusion.1.ownx_ref.refs_4_), channel_id=1, source_target_pairs={{0,1},{1,0},{2,3},{3,2},{4,5},{5,4},{6,7},{7,6},{8,9},{9,8},{10,11... | collective-permute-start | bytes 39944 | tf_op jit(solution)/shard_map/ppermute | solution.py:27
  9.9 16.5 %copy-start.9 = (f32[16]{0:T(128)S(1)}, f32[16]{0:T(128)}, u32[]{:S(2)}) copy-start(f32[16]{0:T(128)} %param.18) | copy-start | bytes 196
  10.9 0.6 copy-start.5
  10.9 0.8 %copy-start = (bf16[2,1024,128]{2,1,0:T(8,128)(2,1)}, bf16[2,1024,128]{2,1,0:T(8,128)(2,1)S(1)}, u32[]{:S(2)}) copy-start(bf16[2,1024,128]{2,1,0:T(8,128)(2,1)S(1)} %collective-permute-done.1.other_ref.refs_3_.refs_15_) | copy-start | bytes 1572868
  22.8 15.4 %collective-permute-start.3 = (bf16[256,1024]{1,0:T(8,128)(2,1)}, bf16[256,1024]{1,0:T(8,128)(2,1)S(1)}, u32[]{:S(2)}, u32[]{:S(2)}) collective-permute-start(bf16[256,1024]{1,0:T(8,128)(2,1)} %get-tuple-element.23), channel_id=1, source_target_pairs={{0,4},{4,8},{8,12},{1,5},{5,9},{9,13},{2,6},{6,10},{10,14},{3,7},{... | collective-permute-start | bytes 1572872 | tf_op jit(solution)/shard_map/ppermute | solution.py:17
  27.1 11.2 %copy-start.2 = (f32[256,1024]{1,0:T(8,128)S(1)}, f32[256,1024]{1,0:T(8,128)}, u32[]{:S(2)}) copy-start(f32[256,1024]{1,0:T(8,128)} %get-tuple-element.40) | copy-start | bytes 3145732
  27.1 11.2 %copy-start.8 = (f32[1,1024]{1,0:T(1,128)S(1)}, f32[1,1024]{1,0:T(1,128)}, u32[]{:S(2)}) copy-start(f32[1,1024]{1,0:T(1,128)} %get-tuple-element.39) | copy-start | bytes 12292
  38.3 4.5 %copy-start.1 = (bf16[256,1024]{1,0:T(8,128)(2,1)}, bf16[256,1024]{1,0:T(8,128)(2,1)S(1)}, u32[]{:S(2)}) copy-start(bf16[256,1024]{1,0:T(8,128)(2,1)S(1)} %collective-permute-done.3.refs_13_) | copy-start | bytes 1572868
  38.4 15.1 %collective-permute-start.4 = (bf16[256,1024]{1,0:T(8,128)(2,1)S(1)}, bf16[256,1024]{1,0:T(8,128)(2,1)S(1)}, u32[]{:S(2)}, u32[]{:S(2)}) collective-permute-start(bf16[256,1024]{1,0:T(8,128)(2,1)S(1)} %add_convert_fusion), channel_id=1, source_target_pairs={{0,4},{4,8},{8,12},{1,5},{5,9},{9,13},{2,6},{6,10},{10,14},{3,7},{... | collective-permute-start | bytes 1572872 | tf_op jit(solution)/shard_map/ppermute | solution.py:17
  53.5 0.8 %copy-start.3 = (bf16[256,1024]{1,0:T(8,128)(2,1)}, bf16[256,1024]{1,0:T(8,128)(2,1)S(1)}, u32[]{:S(2)}) copy-start(bf16[256,1024]{1,0:T(8,128)(2,1)S(1)} %collective-permute-done.4.ein_ref) | copy-start | bytes 1572868

commit v22 on v21

--- a/solution.py
+++ b/solution.py
@@ -128,21 +128,10 @@
     return jax.nn.silu(summed).astype(jnp.bfloat16)
 
 
-def state_kernel(head_width, x_ref, tail_ref, wconv_ref, bias_ref, own_ref, other_ref, ownx_ref,
+def state_block(head_width, x_ref, tail_ref, wconv_ref, bias_ref, own_ref, other_ref, ownx_ref,
                  otherx_ref, dt_ref, rate_ref, info_ref, state_ref, l_ref, dtt_ref,
                  decay_ref, total_ref, xc_ref, bo_ref, sent_ref, prefix_ref, ltile_ref,
                  prev_ref, bcprev_ref, small_ref):
-    blk = pl.program_id(0)
-
-    @pl.when(blk == 0)
-    def _():
-        state_ref[...] = jnp.zeros(state_ref.shape, jnp.float32)
-        total_ref[...] = jnp.ones(total_ref.shape, jnp.float32)
-        prev_ref[...] = tail_ref[:, : x_ref.shape[1]].astype(jnp.float32)
-        small_ref[...] = jnp.ones(small_ref.shape, jnp.float32)
-        bcprev_ref[0] = ownx_ref[:, 0:8, :]
-        bcprev_ref[1] = otherx_ref[:, 0:8, :]
-
     info = info_ref[...]
     raw = x_ref[...].astype(jnp.float32)
     xc = causal_conv(raw, prev_ref[...], wconv_ref[...].astype(jnp.float32), bias_ref[...], info)
@@ -207,9 +196,36 @@
     )
     state_ref[...] = new_state
 
+
+def state_kernel(head_width, per_step, x_ref, tail_ref, wconv_ref, bias_ref, own_ref, other_ref,
+                 ownx_ref, otherx_ref, dt_ref, rate_ref, info_ref, state_ref, l_ref, dtt_ref,
+                 decay_ref, total_ref, xc_ref, bo_ref, sent_ref, prefix_ref, ltile_ref,
+                 prev_ref, bcprev_ref, small_ref):
+    blk = pl.program_id(0)
+
+    @pl.when(blk == 0)
+    def _():
+        state_ref[...] = jnp.zeros(state_ref.shape, jnp.float32)
+        total_ref[...] = jnp.ones(total_ref.shape, jnp.float32)
+        prev_ref[...] = tail_ref[:, : x_ref.shape[1]].astype(jnp.float32)
+        small_ref[...] = jnp.ones(small_ref.shape, jnp.float32)
+        bcprev_ref[0] = ownx_ref[:, 0:8, :]
+        bcprev_ref[1] = otherx_ref[:, 0:8, :]
+
+    for sub in range(per_step):
+        rows = pl.ds(sub * BLOCK, BLOCK)
+        state_block(
+            head_width, x_ref.at[rows, :], tail_ref, wconv_ref, bias_ref, own_ref.at[:, rows, :],
+            other_ref.at[:, rows, :], ownx_ref, otherx_ref, dt_ref.at[:, rows], rate_ref,
+            info_ref.at[rows, :], state_ref, l_ref.at[rows, :], dtt_ref.at[rows, :],
+            decay_ref.at[pl.ds(sub, 1)], total_ref, xc_ref.at[rows, :], bo_ref.at[rows, :],
+            sent_ref, prefix_ref.at[pl.ds(sub, 1)], ltile_ref.at[:, rows, :], prev_ref,
+            bcprev_ref, small_ref,
+        )
+
     @pl.when(blk == pl.num_programs(0) - 1)
     def _():
-        sent_ref[...] = new_state.astype(jnp.bfloat16)
+        sent_ref[...] = state_ref[...].astype(jnp.bfloat16)
 
 
 def run_state(x, tails, wconv, bias_row, own_raw, other_raw, own_extra, other_extra,
@@ -221,22 +237,24 @@
     block_count = rows // BLOCK
     tiles = width // CORRECT_TILE
     tile_heads = head_count // tiles
-    row_block = lambda cols: pl.BlockSpec((BLOCK, cols), lambda b: (b, 0))
+    per_step = 2 if block_count % 2 == 0 else 1
+    step_rows = per_step * BLOCK
+    row_block = lambda cols: pl.BlockSpec((step_rows, cols), lambda b: (b, 0))
     whole = lambda shape: pl.BlockSpec(shape, lambda b: (0,) * len(shape))
     return pl.pallas_call(
-        functools.partial(state_kernel, width // head_count),
-        grid=(block_count,),
+        functools.partial(state_kernel, width // head_count, per_step),
+        grid=(block_count // per_step,),
         in_specs=[row_block(width), whole(tails.shape), whole((4, width)), whole((1, width)),
-                  pl.BlockSpec((2, BLOCK, half), lambda b: (0, b, 0)),
-                  pl.BlockSpec((2, BLOCK, half), lambda b: (0, b, 0)),
+                  pl.BlockSpec((2, step_rows, half), lambda b: (0, b, 0)),
+                  pl.BlockSpec((2, step_rows, half), lambda b: (0, b, 0)),
                   whole(own_extra.shape), whole(own_extra.shape),
-                  pl.BlockSpec((head_count, BLOCK), lambda b: (0, b)),
+                  pl.BlockSpec((head_count, step_rows), lambda b: (0, b)),
                   whole((1, head_count)), row_block(info.shape[1])],
         out_specs=[whole((n_size, width)), row_block(head_count), row_block(head_count),
-                   pl.BlockSpec((1, 1, width), lambda b: (b, 0, 0)), whole((1, width)),
+                   pl.BlockSpec((per_step, 1, width), lambda b: (b, 0, 0)), whole((1, width)),
                    row_block(width), row_block(n_size),
-                   whole((n_size, width)), pl.BlockSpec((1, 1, width), lambda b: (b, 0, 0)),
-                   pl.BlockSpec((tiles, BLOCK, tile_heads), lambda b: (0, b, 0))],
+                   whole((n_size, width)), pl.BlockSpec((per_step, 1, width), lambda b: (b, 0, 0)),
+                   pl.BlockSpec((tiles, step_rows, tile_heads), lambda b: (0, b, 0))],
         out_shape=[jax.ShapeDtypeStruct((n_size, width), jnp.float32),
                    jax.ShapeDtypeStruct((rows, head_count), jnp.float32),
                    jax.ShapeDtypeStruct((rows, head_count), jnp.float32),

time: 60.9 us -> 60.5 us (level)
  no operation moved by 1% of the time
where the time goes in v22:
time: 60.5 us; the launch traced here: 60.1 us
  Pallas kernels  35.5 us (59%)
  starting transfers between devices  13 us (21%)
  local copies, waits for them, and re-layouts  4.97 us (8%)
  other arithmetic  3.28 us (5%)
  waiting for transfers between devices  3.19 us (5%)
    pallas_call x2, Pallas kernels, run_partial(): pl.pallas_call(functools.partial(partial_kernel, width // head_count, fro...  18.7 us
    ppermute x3, starting transfers between devices, shifted(): lax.ppermute(value, axis, [(source, source + steps) for source in range(i...  12.3 us
    pallas_call x1, Pallas kernels, run_state(): pl.pallas_call(functools.partial(state_kernel, width // head_count, per_s...  10.8 us
    pallas_call x1, Pallas kernels, run_correct(): pl.pallas_call(functools.partial(correct_kernel, head_width), grid=(tiles...  6.04 us
    ppermute x3, waiting for transfers between devices, shifted(): lax.ppermute(value, axis, [(source, source + steps) for source in range(i...  3.18 us
    unnamed x20, local copies, waits for them, and re-layouts  1.65 us
  transfers between devices with their start and end apart: 5, of which 2 were waited for; matrix products, arithmetic and copies ran while one was open for 11% of the time, Pallas kernels for 31%

profile of v22, /device:TPU:0, one launch (start us, length us, event | category | flops | bytes accessed | tf_op | source)
XLA Modules:
  0.0 60.1 jit_solution(8043074503028011908)
XLA Ops:
  0.0 0.5 collective-permute-start.1
  0.5 0.7 %slice_bitcast_fusion.1 = bf16[8,256]{1,0:T(8,128)(2,1)S(1)} fusion(bf16[2,1024,128]{2,1,0:T(8,128)(2,1)} %refs_14_.1), kind=kLoop, calls=%fused_computation.12 | loop fusion | bytes 8192 | tf_op jit(solution)/shard_map/reshape | solution.py:476
  1.1 0.7 %slice.27 = bf16[8,1024]{1,0:T(8,128)(2,1)S(1)} slice(bf16[1024,1024]{1,0:T(8,128)(2,1)} %x_ref.1), slice={[1016:1024], [0:1024]} | slice | bytes 32768 | tf_op jit(solution)/shard_map/slice | solution.py:476
  1.9 4.5 %collective-permute-start = (bf16[8,1280]{1,0:T(8,128)(2,1)S(1)}, bf16[8,1280]{1,0:T(8,128)(2,1)S(1)}, u32[]{:S(2)}, u32[]{:S(2)}) collective-permute-start(bf16[8,1280]{1,0:T(8,128)(2,1)S(1)} %pad_maximum_fusion), channel_id=1, source_target_pairs={{0,4},{4,8},{8,12},{1,5},{5,9},{9,13},{2,6},{6,10},{10,14},{3,7},{... | collective-permute-start | bytes 61448 | tf_op jit(solution)/shard_map/ppermute | solution.py:17
  6.3 0.8 %reduce-window.9 = s32[3,1]{0,1:T(1,128)S(1)} reduce-window(s32[3,1]{0,1:T(1,128)} %bitcast.41, s32[]{:T(128)} %constant.25.clone.1), window={size=3x1 pad=2_0x0_0}, to_apply=%region_0.0 | reduce-window | flops 6 | bytes 28 | tf_op jit(solution)/shard_map/reduce-window.4
  7.2 0.7 %bitcast_subtract_fusion = s32[3]{0:T(128)S(1)} fusion(s32[3]{0:T(128)} %param.19, s32[3,1]{0,1:T(1,128)S(1)} %reduce-window.9), kind=kLoop, calls=%fused_computation.19 | loop fusion | flops 3 | bytes 36 | tf_op jit(solution)/shard_map/sub | solution.py:31
  7.8 0.1 convert_reduce_fusion
  7.9 0.1 slice_bitcast_fusion.2
  8.0 0.0 copy-start.6
  8.0 0.1 slice_reduce_fusion
  8.1 0.7 %convert_element_type.37 = f32[2,4,128]{2,1,0:T(4,128)S(1)} convert(bf16[2,4,128]{2,1,0:T(4,128)(2,1)} %param.14) | non-fusion elementwise | flops 1024 | bytes 6144 | tf_op jit(solution)/shard_map/convert_element_type | solution.py:482
  8.8 0.0 collective-permute-done.tail_ref
  8.8 0.0 copy-start.7
  8.8 0.7 %pad_maximum_fusion.1.ownx_ref.refs_4_ = f32[2,13,128]{2,1,0:T(8,128)S(1)} fusion(f32[2,1,128]{2,1,0:T(1,128)} %bitcast.39, f32[2,4,128]{2,1,0:T(4,128)S(1)} %convert_element_type.37, f32[2,8,128]{2,1,0:T(8,128)S(1)} %convert_bitcast_fusion), kind=kLoop, calls=%fused_computation.3 | loop fusion | flops 6656 | bytes 26624 | tf_op jit(solution)/shard_map/concatenate | solution.py:480
  9.5 0.0 copy-start.4
  9.5 0.2 collective-permute-start.2
  9.8 0.1 fusion.2
  9.8 0.1 stack.39
  9.9 0.0 copy-start.9
  9.9 1.0 %copy.24.info_ref.refs_9_ = f32[1024,8]{1,0:T(8,128)} copy(f32[1024,8]{0,1:T(8,128)S(1)} %stack.39) | data formatting | bytes 65536 | tf_op jit(solution)/shard_map/stack | solution.py:496
  10.9 0.0 collective-permute-done.2.otherx_ref.refs_5_
  10.9 0.0 copy-start.5
  10.9 0.0 collective-permute-done.1.other_ref.refs_3_.refs_15_
  10.9 0.0 copy-start
  10.9 0.0 copy-done.7
  11.0 0.0 copy-done.4
  11.0 0.6 copy-done.5
  11.5 0.2 copy-done
  11.8 10.8 %shard_map.100 = (f32[256,1024]{1,0:T(8,128)}, f32[1024,16]{1,0:T(8,128)}, f32[1024,16]{1,0:T(8,128)}, f32[8,1,1024]{2,1,0:T(1,128)}, f32[1,1024]{1,0:T(1,128)},...) custom-call(bf16[1024,1024]{1,0:T(8,128)(2,1)} %x_ref.1, ...), custom_call_target="tpu_custom_call" | custom-call | tf_op jit(solution)/shard_map/pallas_call | solution.py:244
  22.5 0.0 copy-done.6
  22.5 3.5 %collective-permute-start.3 = (bf16[256,1024]{1,0:T(8,128)(2,1)}, bf16[256,1024]{1,0:T(8,128)(2,1)S(1)}, u32[]{:S(2)}, u32[]{:S(2)}) collective-permute-start(bf16[256,1024]{1,0:T(8,128)(2,1)} %get-tuple-element.23), channel_id=1, source_target_pairs={{0,4},{4,8},{8,12},{1,5},{5,9},{9,13},{2,6},{6,10},{10,14},{3,7},{... | collective-permute-start | bytes 1572872 | tf_op jit(solution)/shard_map/ppermute | solution.py:17
  26.1 0.0 copy-done.9
  26.1 0.1 broadcast_in_dim.9
  26.1 0.7 %reshape_reshape.3.refs_11_ = f32[1,1024]{1,0:T(1,128)} reshape(f32[16,64]{1,0:T(8,128)S(1)} %broadcast_in_dim.9) | data formatting | bytes 8192 | tf_op jit(solution)/shard_map/reshape;reshape | solution.py:489
  26.8 0.0 copy-start.2
  26.8 0.0 copy-start.8
  26.8 9.0 %shard_map.101 = (f32[512,1024]{1,0:T(8,128)}, bf16[512,256]{1,0:T(8,128)(2,1)}, f32[256,1024]{1,0:T(8,128)}) custom-call(bf16[1024,1024]{1,0:T(8,128)(2,1)} %get-tuple-element.24.refs_0_, bf16[1024,256]{1,0:T(8,128)(2,1)} %get-tuple-element.25.refs_1_, bf16[2,1024,128]{2,1,0:T(8,128)(2,1)} %refs_14_.1, bf16[2,1024,128]{2,1,0:T(8,128)(2,1)} %copy-done, ...), custom_call_target="tpu_custom_call" | custom-call | tf_op jit(solution)/shard_map/pallas_call | solution.py:374
  35.8 2.2 %collective-permute-done.3.refs_13_ = bf16[256,1024]{1,0:T(8,128)(2,1)S(1)} collective-permute-done((bf16[256,1024]{1,0:T(8,128)(2,1)}, bf16[256,1024]{1,0:T(8,128)(2,1)S(1)}, u32[]{:S(2)}, u32[]{:S(2)}) %collective-permute-start.3) | collective-permute-done | bytes 524320 | tf_op jit(solution)/shard_map/ppermute | solution.py:17
  37.9 0.0 copy-start.1
  37.9 0.0 copy-done.2
  38.0 0.0 copy-done.8
  38.0 0.2 add_convert_fusion
  38.1 4.3 %collective-permute-start.4 = (bf16[256,1024]{1,0:T(8,128)(2,1)S(1)}, bf16[256,1024]{1,0:T(8,128)(2,1)S(1)}, u32[]{:S(2)}, u32[]{:S(2)}) collective-permute-start(bf16[256,1024]{1,0:T(8,128)(2,1)S(1)} %add_convert_fusion), channel_id=1, source_target_pairs={{0,4},{4,8},{8,12},{1,5},{5,9},{9,13},{2,6},{6,10},{10,14},{3,7},{... | collective-permute-start | bytes 1572872 | tf_op jit(solution)/shard_map/ppermute | solution.py:17
  42.4 0.0 copy-done.1
  42.4 9.7 %shard_map.102 = (f32[512,1024]{1,0:T(8,128)}, bf16[512,256]{1,0:T(8,128)(2,1)}) custom-call(bf16[1024,1024]{1,0:T(8,128)(2,1)} %get-tuple-element.24.refs_0_, bf16[1024,256]{1,0:T(8,128)(2,1)} %get-tuple-element.25.refs_1_, bf16[2,1024,128]{2,1,0:T(8,128)(2,1)} %refs_14_.1, bf16[2,1024,128]{2,1,0:T(8,128)(2,1)} %copy-done, f32[2,13,128]{2,1,0:T(8,128)} %copy-done.4, ...), custom_call_target="tpu_custom_call" | custom-call | tf_op jit(solution)/shard_map/pallas_call | solution.py:374
  52.2 1.0 %collective-permute-done.4.ein_ref = bf16[256,1024]{1,0:T(8,128)(2,1)S(1)} collective-permute-done((bf16[256,1024]{1,0:T(8,128)(2,1)S(1)}, bf16[256,1024]{1,0:T(8,128)(2,1)S(1)}, u32[]{:S(2)}, u32[]{:S(2)}) %collective-permute-start.4) | collective-permute-done | bytes 524320 | tf_op jit(solution)/shard_map/ppermute | solution.py:17
  53.2 0.8 %copy-done.3 = bf16[256,1024]{1,0:T(8,128)(2,1)} copy-done((bf16[256,1024]{1,0:T(8,128)(2,1)}, bf16[256,1024]{1,0:T(8,128)(2,1)S(1)}, u32[]{:S(2)}) %copy-start.3) | copy-done | bytes 524312
  54.0 6.0 %shard_map.103 = bf16[1024,1024]{1,0:T(8,128)(2,1)} custom-call(f32[512,1024]{1,0:T(8,128)} %get-tuple-element.32.y_ref, f32[512,1024]{1,0:T(8,128)} %get-tuple-element.35.z_ref, bf16[512,256]{1,0:T(8,128)(2,1)} %get-tuple-element.36.c_ref, bf16[512,256]{1,0:T(8,128)(2,1)} %get-tuple-element.37.d_ref, f32[2,1024,8]{2,1,0:T(8,128)} %get-tuple-element.38.g_ref, ...), custom_call_target="tpu_custom_call" | custom-call | tf_op jit(solution)/shard_map/pallas_call | solution.py:403
  (7 shorter events, 0.0 us)
Async XLA Ops:
  0.0 10.9 %collective-permute-start.1 = (bf16[2,1024,128]{2,1,0:T(8,128)(2,1)}, bf16[2,1024,128]{2,1,0:T(8,128)(2,1)S(1)}, u32[]{:S(2)}, u32[]{:S(2)}) collective-permute-start(bf16[2,1024,128]{2,1,0:T(8,128)(2,1)} %refs_14_.1), channel_id=1, source_target_pairs={{0,1},{1,0},{2,3},{3,2},{4,5},{5,4},{6,7},{7,6},{8,9},{9,8},{10,11... | collective-permute-start | bytes 1572872 | tf_op jit(solution)/shard_map/ppermute | solution.py:27
  1.9 7.0 %collective-permute-start = (bf16[8,1280]{1,0:T(8,128)(2,1)S(1)}, bf16[8,1280]{1,0:T(8,128)(2,1)S(1)}, u32[]{:S(2)}, u32[]{:S(2)}) collective-permute-start(bf16[8,1280]{1,0:T(8,128)(2,1)S(1)} %pad_maximum_fusion), channel_id=1, source_target_pairs={{0,4},{4,8},{8,12},{1,5},{5,9},{9,13},{2,6},{6,10},{10,14},{3,7},{... | collective-permute-start | bytes 61448 | tf_op jit(solution)/shard_map/ppermute | solution.py:17
  8.0 14.5 %copy-start.6 = (f32[1024]{0:T(1024)}, f32[1024]{0:T(1024)S(1)}, u32[]{:S(2)}) copy-start(f32[1024]{0:T(1024)S(1)} %get-tuple-element.46) | copy-start | bytes 12292
  8.8 2.1 %copy-start.7 = (bf16[8,1280]{1,0:T(8,128)(2,1)}, bf16[8,1280]{1,0:T(8,128)(2,1)S(1)}, u32[]{:S(2)}) copy-start(bf16[8,1280]{1,0:T(8,128)(2,1)S(1)} %collective-permute-done.tail_ref) | copy-start | bytes 61444
  9.5 1.4 %copy-start.4 = (f32[2,13,128]{2,1,0:T(8,128)}, f32[2,13,128]{2,1,0:T(8,128)S(1)}, u32[]{:S(2)}) copy-start(f32[2,13,128]{2,1,0:T(8,128)S(1)} %pad_maximum_fusion.1.ownx_ref.refs_4_) | copy-start | bytes 39940
  9.5 1.4 %collective-permute-start.2 = (f32[2,13,128]{2,1,0:T(8,128)S(1)}, f32[2,13,128]{2,1,0:T(8,128)S(1)}, u32[]{:S(2)}, u32[]{:S(2)}) collective-permute-start(f32[2,13,128]{2,1,0:T(8,128)S(1)} %pad_maximum_fusion.1.ownx_ref.refs_4_), channel_id=1, source_target_pairs={{0,1},{1,0},{2,3},{3,2},{4,5},{5,4},{6,7},{7,6},{8,9},{9,8},{10,11... | collective-permute-start | bytes 39944 | tf_op jit(solution)/shard_map/ppermute | solution.py:27
  9.9 16.2 %copy-start.9 = (f32[16]{0:T(128)S(1)}, f32[16]{0:T(128)}, u32[]{:S(2)}) copy-start(f32[16]{0:T(128)} %param.18) | copy-start | bytes 196
  10.9 0.6 copy-start.5
  10.9 0.8 %copy-start = (bf16[2,1024,128]{2,1,0:T(8,128)(2,1)}, bf16[2,1024,128]{2,1,0:T(8,128)(2,1)S(1)}, u32[]{:S(2)}) copy-start(bf16[2,1024,128]{2,1,0:T(8,128)(2,1)S(1)} %collective-permute-done.1.other_ref.refs_3_.refs_15_) | copy-start | bytes 1572868
  22.5 15.4 %collective-permute-start.3 = (bf16[256,1024]{1,0:T(8,128)(2,1)}, bf16[256,1024]{1,0:T(8,128)(2,1)S(1)}, u32[]{:S(2)}, u32[]{:S(2)}) collective-permute-start(bf16[256,1024]{1,0:T(8,128)(2,1)} %get-tuple-element.23), channel_id=1, source_target_pairs={{0,4},{4,8},{8,12},{1,5},{5,9},{9,13},{2,6},{6,10},{10,14},{3,7},{... | collective-permute-start | bytes 1572872 | tf_op jit(solution)/shard_map/ppermute | solution.py:17
  26.8 11.2 %copy-start.2 = (f32[256,1024]{1,0:T(8,128)S(1)}, f32[256,1024]{1,0:T(8,128)}, u32[]{:S(2)}) copy-start(f32[256,1024]{1,0:T(8,128)} %get-tuple-element.40) | copy-start | bytes 3145732
  26.8 11.2 %copy-start.8 = (f32[1,1024]{1,0:T(1,128)S(1)}, f32[1,1024]{1,0:T(1,128)}, u32[]{:S(2)}) copy-start(f32[1,1024]{1,0:T(1,128)} %get-tuple-element.39) | copy-start | bytes 12292
  37.9 4.5 %copy-start.1 = (bf16[256,1024]{1,0:T(8,128)(2,1)}, bf16[256,1024]{1,0:T(8,128)(2,1)S(1)}, u32[]{:S(2)}) copy-start(bf16[256,1024]{1,0:T(8,128)(2,1)S(1)} %collective-permute-done.3.refs_13_) | copy-start | bytes 1572868
  38.1 15.1 %collective-permute-start.4 = (bf16[256,1024]{1,0:T(8,128)(2,1)S(1)}, bf16[256,1024]{1,0:T(8,128)(2,1)S(1)}, u32[]{:S(2)}, u32[]{:S(2)}) collective-permute-start(bf16[256,1024]{1,0:T(8,128)(2,1)S(1)} %add_convert_fusion), channel_id=1, source_target_pairs={{0,4},{4,8},{8,12},{1,5},{5,9},{9,13},{2,6},{6,10},{10,14},{3,7},{... | collective-permute-start | bytes 1572872 | tf_op jit(solution)/shard_map/ppermute | solution.py:17
  53.2 0.8 %copy-start.3 = (bf16[256,1024]{1,0:T(8,128)(2,1)}, bf16[256,1024]{1,0:T(8,128)(2,1)S(1)}, u32[]{:S(2)}) copy-start(bf16[256,1024]{1,0:T(8,128)(2,1)S(1)} %collective-permute-done.4.ein_ref) | copy-start | bytes 1572868

commit v23 on v22

--- a/solution.py
+++ b/solution.py
@@ -237,7 +237,7 @@
     block_count = rows // BLOCK
     tiles = width // CORRECT_TILE
     tile_heads = head_count // tiles
-    per_step = 2 if block_count % 2 == 0 else 1
+    per_step = 4 if block_count % 4 == 0 else 1
     step_rows = per_step * BLOCK
     row_block = lambda cols: pl.BlockSpec((step_rows, cols), lambda b: (b, 0))
     whole = lambda shape: pl.BlockSpec(shape, lambda b: (0,) * len(shape))

time: 60.5 us -> 61.3 us (1.013)
  Pallas kernels: 35.5 us -> 36.4 us
    pallas_call x1, Pallas kernels: 10.8 us -> 11.6 us  [run_state(): pl.pallas_call(functools.partial(state_kernel, width // head_count, per_s...]
where the time goes in v23:
time: 61.3 us; the launch traced here: 60.9 us
  Pallas kernels  36.4 us (59%)
  starting transfers between devices  13 us (21%)
  local copies, waits for them, and re-layouts  4.97 us (8%)
  other arithmetic  3.28 us (5%)
  waiting for transfers between devices  3.2 us (5%)
    pallas_call x2, Pallas kernels, run_partial(): pl.pallas_call(functools.partial(partial_kernel, width // head_count, fro...  18.7 us
    ppermute x3, starting transfers between devices, shifted(): lax.ppermute(value, axis, [(source, source + steps) for source in range(i...  12.3 us
    pallas_call x1, Pallas kernels, run_state(): pl.pallas_call(functools.partial(state_kernel, width // head_count, per_s...  11.6 us
    pallas_call x1, Pallas kernels, run_correct(): pl.pallas_call(functools.partial(correct_kernel, head_width), grid=(tiles...  6.04 us
    ppermute x3, waiting for transfers between devices, shifted(): lax.ppermute(value, axis, [(source, source + steps) for source in range(i...  3.19 us
    unnamed x20, local copies, waits for them, and re-layouts  1.65 us
  transfers between devices with their start and end apart: 5, of which 2 were waited for; matrix products, arithmetic and copies ran while one was open for 11% of the time, Pallas kernels for 31%

profile of v23, /device:TPU:0, one launch (start us, length us, event | category | flops | bytes accessed | tf_op | source)
XLA Modules:
  0.0 60.9 jit_solution(16738816412833272540)
XLA Ops:
  0.0 0.5 collective-permute-start.1
  0.5 0.7 %slice_bitcast_fusion.1 = bf16[8,256]{1,0:T(8,128)(2,1)S(1)} fusion(bf16[2,1024,128]{2,1,0:T(8,128)(2,1)} %refs_14_.1), kind=kLoop, calls=%fused_computation.12 | loop fusion | bytes 8192 | tf_op jit(solution)/shard_map/reshape | solution.py:476
  1.1 0.7 %slice.27 = bf16[8,1024]{1,0:T(8,128)(2,1)S(1)} slice(bf16[1024,1024]{1,0:T(8,128)(2,1)} %x_ref.1), slice={[1016:1024], [0:1024]} | slice | bytes 32768 | tf_op jit(solution)/shard_map/slice | solution.py:476
  1.9 4.5 %collective-permute-start = (bf16[8,1280]{1,0:T(8,128)(2,1)S(1)}, bf16[8,1280]{1,0:T(8,128)(2,1)S(1)}, u32[]{:S(2)}, u32[]{:S(2)}) collective-permute-start(bf16[8,1280]{1,0:T(8,128)(2,1)S(1)} %pad_maximum_fusion), channel_id=1, source_target_pairs={{0,4},{4,8},{8,12},{1,5},{5,9},{9,13},{2,6},{6,10},{10,14},{3,7},{... | collective-permute-start | bytes 61448 | tf_op jit(solution)/shard_map/ppermute | solution.py:17
  6.3 0.8 %reduce-window.9 = s32[3,1]{0,1:T(1,128)S(1)} reduce-window(s32[3,1]{0,1:T(1,128)} %bitcast.41, s32[]{:T(128)} %constant.25.clone.1), window={size=3x1 pad=2_0x0_0}, to_apply=%region_0.0 | reduce-window | flops 6 | bytes 28 | tf_op jit(solution)/shard_map/reduce-window.4
  7.2 0.7 %bitcast_subtract_fusion = s32[3]{0:T(128)S(1)} fusion(s32[3]{0:T(128)} %param.19, s32[3,1]{0,1:T(1,128)S(1)} %reduce-window.9), kind=kLoop, calls=%fused_computation.19 | loop fusion | flops 3 | bytes 36 | tf_op jit(solution)/shard_map/sub | solution.py:31
  7.8 0.1 convert_reduce_fusion
  7.9 0.1 slice_bitcast_fusion.2
  8.0 0.0 copy-start.6
  8.0 0.1 slice_reduce_fusion
  8.1 0.7 %convert_element_type.37 = f32[2,4,128]{2,1,0:T(4,128)S(1)} convert(bf16[2,4,128]{2,1,0:T(4,128)(2,1)} %param.14) | non-fusion elementwise | flops 1024 | bytes 6144 | tf_op jit(solution)/shard_map/convert_element_type | solution.py:482
  8.8 0.0 collective-permute-done.tail_ref
  8.8 0.0 copy-start.7
  8.8 0.7 %pad_maximum_fusion.1.ownx_ref.refs_4_ = f32[2,13,128]{2,1,0:T(8,128)S(1)} fusion(f32[2,1,128]{2,1,0:T(1,128)} %bitcast.39, f32[2,4,128]{2,1,0:T(4,128)S(1)} %convert_element_type.37, f32[2,8,128]{2,1,0:T(8,128)S(1)} %convert_bitcast_fusion), kind=kLoop, calls=%fused_computation.3 | loop fusion | flops 6656 | bytes 26624 | tf_op jit(solution)/shard_map/concatenate | solution.py:480
  9.5 0.0 copy-start.4
  9.5 0.2 collective-permute-start.2
  9.8 0.1 fusion.2
  9.8 0.1 stack.39
  9.9 0.0 copy-start.9
  9.9 1.0 %copy.24.info_ref.refs_9_ = f32[1024,8]{1,0:T(8,128)} copy(f32[1024,8]{0,1:T(8,128)S(1)} %stack.39) | data formatting | bytes 65536 | tf_op jit(solution)/shard_map/stack | solution.py:496
  10.9 0.0 collective-permute-done.2.otherx_ref.refs_5_
  10.9 0.0 copy-start.5
  10.9 0.0 collective-permute-done.1.other_ref.refs_3_.refs_15_
  10.9 0.0 copy-start
  10.9 0.0 copy-done.7
  11.0 0.0 copy-done.4
  11.0 0.6 copy-done.5
  11.5 0.2 copy-done
  11.8 11.6 %shard_map.100 = (f32[256,1024]{1,0:T(8,128)}, f32[1024,16]{1,0:T(8,128)}, f32[1024,16]{1,0:T(8,128)}, f32[8,1,1024]{2,1,0:T(1,128)}, f32[1,1024]{1,0:T(1,128)},...) custom-call(bf16[1024,1024]{1,0:T(8,128)(2,1)} %x_ref.1, ...), custom_call_target="tpu_custom_call" | custom-call | tf_op jit(solution)/shard_map/pallas_call | solution.py:244
  23.4 0.0 copy-done.6
  23.4 3.5 %collective-permute-start.3 = (bf16[256,1024]{1,0:T(8,128)(2,1)}, bf16[256,1024]{1,0:T(8,128)(2,1)S(1)}, u32[]{:S(2)}, u32[]{:S(2)}) collective-permute-start(bf16[256,1024]{1,0:T(8,128)(2,1)} %get-tuple-element.23), channel_id=1, source_target_pairs={{0,4},{4,8},{8,12},{1,5},{5,9},{9,13},{2,6},{6,10},{10,14},{3,7},{... | collective-permute-start | bytes 1572872 | tf_op jit(solution)/shard_map/ppermute | solution.py:17
  26.9 0.0 copy-done.9
  26.9 0.1 broadcast_in_dim.9
  27.0 0.7 %reshape_reshape.3.refs_11_ = f32[1,1024]{1,0:T(1,128)} reshape(f32[16,64]{1,0:T(8,128)S(1)} %broadcast_in_dim.9) | data formatting | bytes 8192 | tf_op jit(solution)/shard_map/reshape;reshape | solution.py:489
  27.6 0.0 copy-start.2
  27.6 0.0 copy-start.8
  27.6 9.0 %shard_map.101 = (f32[512,1024]{1,0:T(8,128)}, bf16[512,256]{1,0:T(8,128)(2,1)}, f32[256,1024]{1,0:T(8,128)}) custom-call(bf16[1024,1024]{1,0:T(8,128)(2,1)} %get-tuple-element.24.refs_0_, bf16[1024,256]{1,0:T(8,128)(2,1)} %get-tuple-element.25.refs_1_, bf16[2,1024,128]{2,1,0:T(8,128)(2,1)} %refs_14_.1, bf16[2,1024,128]{2,1,0:T(8,128)(2,1)} %copy-done, ...), custom_call_target="tpu_custom_call" | custom-call | tf_op jit(solution)/shard_map/pallas_call | solution.py:374
  36.6 2.2 %collective-permute-done.3.refs_13_ = bf16[256,1024]{1,0:T(8,128)(2,1)S(1)} collective-permute-done((bf16[256,1024]{1,0:T(8,128)(2,1)}, bf16[256,1024]{1,0:T(8,128)(2,1)S(1)}, u32[]{:S(2)}, u32[]{:S(2)}) %collective-permute-start.3) | collective-permute-done | bytes 524320 | tf_op jit(solution)/shard_map/ppermute | solution.py:17
  38.8 0.0 copy-start.1
  38.8 0.0 copy-done.2
  38.8 0.0 copy-done.8
  38.8 0.2 add_convert_fusion
  39.0 4.3 %collective-permute-start.4 = (bf16[256,1024]{1,0:T(8,128)(2,1)S(1)}, bf16[256,1024]{1,0:T(8,128)(2,1)S(1)}, u32[]{:S(2)}, u32[]{:S(2)}) collective-permute-start(bf16[256,1024]{1,0:T(8,128)(2,1)S(1)} %add_convert_fusion), channel_id=1, source_target_pairs={{0,4},{4,8},{8,12},{1,5},{5,9},{9,13},{2,6},{6,10},{10,14},{3,7},{... | collective-permute-start | bytes 1572872 | tf_op jit(solution)/shard_map/ppermute | solution.py:17
  43.3 0.0 copy-done.1
  43.3 9.7 %shard_map.102 = (f32[512,1024]{1,0:T(8,128)}, bf16[512,256]{1,0:T(8,128)(2,1)}) custom-call(bf16[1024,1024]{1,0:T(8,128)(2,1)} %get-tuple-element.24.refs_0_, bf16[1024,256]{1,0:T(8,128)(2,1)} %get-tuple-element.25.refs_1_, bf16[2,1024,128]{2,1,0:T(8,128)(2,1)} %refs_14_.1, bf16[2,1024,128]{2,1,0:T(8,128)(2,1)} %copy-done, f32[2,13,128]{2,1,0:T(8,128)} %copy-done.4, ...), custom_call_target="tpu_custom_call" | custom-call | tf_op jit(solution)/shard_map/pallas_call | solution.py:374
  53.0 1.0 %collective-permute-done.4.ein_ref = bf16[256,1024]{1,0:T(8,128)(2,1)S(1)} collective-permute-done((bf16[256,1024]{1,0:T(8,128)(2,1)S(1)}, bf16[256,1024]{1,0:T(8,128)(2,1)S(1)}, u32[]{:S(2)}, u32[]{:S(2)}) %collective-permute-start.4) | collective-permute-done | bytes 524320 | tf_op jit(solution)/shard_map/ppermute | solution.py:17
  54.1 0.8 %copy-done.3 = bf16[256,1024]{1,0:T(8,128)(2,1)} copy-done((bf16[256,1024]{1,0:T(8,128)(2,1)}, bf16[256,1024]{1,0:T(8,128)(2,1)S(1)}, u32[]{:S(2)}) %copy-start.3) | copy-done | bytes 524312
  54.9 6.0 %shard_map.103 = bf16[1024,1024]{1,0:T(8,128)(2,1)} custom-call(f32[512,1024]{1,0:T(8,128)} %get-tuple-element.32.y_ref, f32[512,1024]{1,0:T(8,128)} %get-tuple-element.35.z_ref, bf16[512,256]{1,0:T(8,128)(2,1)} %get-tuple-element.36.c_ref, bf16[512,256]{1,0:T(8,128)(2,1)} %get-tuple-element.37.d_ref, f32[2,1024,8]{2,1,0:T(8,128)} %get-tuple-element.38.g_ref, ...), custom_call_target="tpu_custom_call" | custom-call | tf_op jit(solution)/shard_map/pallas_call | solution.py:403
  (7 shorter events, 0.0 us)
Async XLA Ops:
  0.0 10.9 %collective-permute-start.1 = (bf16[2,1024,128]{2,1,0:T(8,128)(2,1)}, bf16[2,1024,128]{2,1,0:T(8,128)(2,1)S(1)}, u32[]{:S(2)}, u32[]{:S(2)}) collective-permute-start(bf16[2,1024,128]{2,1,0:T(8,128)(2,1)} %refs_14_.1), channel_id=1, source_target_pairs={{0,1},{1,0},{2,3},{3,2},{4,5},{5,4},{6,7},{7,6},{8,9},{9,8},{10,11... | collective-permute-start | bytes 1572872 | tf_op jit(solution)/shard_map/ppermute | solution.py:27
  1.9 7.0 %collective-permute-start = (bf16[8,1280]{1,0:T(8,128)(2,1)S(1)}, bf16[8,1280]{1,0:T(8,128)(2,1)S(1)}, u32[]{:S(2)}, u32[]{:S(2)}) collective-permute-start(bf16[8,1280]{1,0:T(8,128)(2,1)S(1)} %pad_maximum_fusion), channel_id=1, source_target_pairs={{0,4},{4,8},{8,12},{1,5},{5,9},{9,13},{2,6},{6,10},{10,14},{3,7},{... | collective-permute-start | bytes 61448 | tf_op jit(solution)/shard_map/ppermute | solution.py:17
  8.0 15.4 %copy-start.6 = (f32[1024]{0:T(1024)}, f32[1024]{0:T(1024)S(1)}, u32[]{:S(2)}) copy-start(f32[1024]{0:T(1024)S(1)} %get-tuple-element.46) | copy-start | bytes 12292
  8.8 2.1 %copy-start.7 = (bf16[8,1280]{1,0:T(8,128)(2,1)}, bf16[8,1280]{1,0:T(8,128)(2,1)S(1)}, u32[]{:S(2)}) copy-start(bf16[8,1280]{1,0:T(8,128)(2,1)S(1)} %collective-permute-done.tail_ref) | copy-start | bytes 61444
  9.5 1.4 %copy-start.4 = (f32[2,13,128]{2,1,0:T(8,128)}, f32[2,13,128]{2,1,0:T(8,128)S(1)}, u32[]{:S(2)}) copy-start(f32[2,13,128]{2,1,0:T(8,128)S(1)} %pad_maximum_fusion.1.ownx_ref.refs_4_) | copy-start | bytes 39940
  9.5 1.4 %collective-permute-start.2 = (f32[2,13,128]{2,1,0:T(8,128)S(1)}, f32[2,13,128]{2,1,0:T(8,128)S(1)}, u32[]{:S(2)}, u32[]{:S(2)}) collective-permute-start(f32[2,13,128]{2,1,0:T(8,128)S(1)} %pad_maximum_fusion.1.ownx_ref.refs_4_), channel_id=1, source_target_pairs={{0,1},{1,0},{2,3},{3,2},{4,5},{5,4},{6,7},{7,6},{8,9},{9,8},{10,11... | collective-permute-start | bytes 39944 | tf_op jit(solution)/shard_map/ppermute | solution.py:27
  9.9 17.0 %copy-start.9 = (f32[16]{0:T(128)S(1)}, f32[16]{0:T(128)}, u32[]{:S(2)}) copy-start(f32[16]{0:T(128)} %param.18) | copy-start | bytes 196
  10.9 0.6 copy-start.5
  10.9 0.8 %copy-start = (bf16[2,1024,128]{2,1,0:T(8,128)(2,1)}, bf16[2,1024,128]{2,1,0:T(8,128)(2,1)S(1)}, u32[]{:S(2)}) copy-start(bf16[2,1024,128]{2,1,0:T(8,128)(2,1)S(1)} %collective-permute-done.1.other_ref.refs_3_.refs_15_) | copy-start | bytes 1572868
  23.4 15.4 %collective-permute-start.3 = (bf16[256,1024]{1,0:T(8,128)(2,1)}, bf16[256,1024]{1,0:T(8,128)(2,1)S(1)}, u32[]{:S(2)}, u32[]{:S(2)}) collective-permute-start(bf16[256,1024]{1,0:T(8,128)(2,1)} %get-tuple-element.23), channel_id=1, source_target_pairs={{0,4},{4,8},{8,12},{1,5},{5,9},{9,13},{2,6},{6,10},{10,14},{3,7},{... | collective-permute-start | bytes 1572872 | tf_op jit(solution)/shard_map/ppermute | solution.py:17
  27.6 11.2 %copy-start.2 = (f32[256,1024]{1,0:T(8,128)S(1)}, f32[256,1024]{1,0:T(8,128)}, u32[]{:S(2)}) copy-start(f32[256,1024]{1,0:T(8,128)} %get-tuple-element.40) | copy-start | bytes 3145732
  27.6 11.2 %copy-start.8 = (f32[1,1024]{1,0:T(1,128)S(1)}, f32[1,1024]{1,0:T(1,128)}, u32[]{:S(2)}) copy-start(f32[1,1024]{1,0:T(1,128)} %get-tuple-element.39) | copy-start | bytes 12292
  38.8 4.5 %copy-start.1 = (bf16[256,1024]{1,0:T(8,128)(2,1)}, bf16[256,1024]{1,0:T(8,128)(2,1)S(1)}, u32[]{:S(2)}) copy-start(bf16[256,1024]{1,0:T(8,128)(2,1)S(1)} %collective-permute-done.3.refs_13_) | copy-start | bytes 1572868
  39.0 15.1 %collective-permute-start.4 = (bf16[256,1024]{1,0:T(8,128)(2,1)S(1)}, bf16[256,1024]{1,0:T(8,128)(2,1)S(1)}, u32[]{:S(2)}, u32[]{:S(2)}) collective-permute-start(bf16[256,1024]{1,0:T(8,128)(2,1)S(1)} %add_convert_fusion), channel_id=1, source_target_pairs={{0,4},{4,8},{8,12},{1,5},{5,9},{9,13},{2,6},{6,10},{10,14},{3,7},{... | collective-permute-start | bytes 1572872 | tf_op jit(solution)/shard_map/ppermute | solution.py:17
  54.1 0.8 %copy-start.3 = (bf16[256,1024]{1,0:T(8,128)(2,1)}, bf16[256,1024]{1,0:T(8,128)(2,1)S(1)}, u32[]{:S(2)}) copy-start(bf16[256,1024]{1,0:T(8,128)(2,1)S(1)} %collective-permute-done.4.ein_ref) | copy-start | bytes 1572868

commit v24 on v22

--- a/solution.py
+++ b/solution.py
@@ -8,7 +8,7 @@
 from jax.sharding import PartitionSpec as P
 
 BLOCK = 128
-CORRECT_TILE = 512
+CORRECT_TILE = 1024
 
 
 def shifted(value, axis, steps):

time: 60.5 us -> 60.5 us (level)
  no operation moved by 1% of the time
where the time goes in v24:
time: 60.5 us; the launch traced here: 60.1 us
  Pallas kernels  35.6 us (59%)
  starting transfers between devices  13 us (21%)
  local copies, waits for them, and re-layouts  4.96 us (8%)
  other arithmetic  3.28 us (5%)
  waiting for transfers between devices  3.17 us (5%)
    pallas_call x2, Pallas kernels, run_partial(): pl.pallas_call(functools.partial(partial_kernel, width // head_count, fro...  18.7 us
    ppermute x3, starting transfers between devices, shifted(): lax.ppermute(value, axis, [(source, source + steps) for source in range(i...  12.3 us
    pallas_call x1, Pallas kernels, run_state(): pl.pallas_call(functools.partial(state_kernel, width // head_count, per_s...  10.5 us
    pallas_call x1, Pallas kernels, run_correct(): pl.pallas_call(functools.partial(correct_kernel, head_width), grid=(tiles...  6.37 us
    ppermute x3, waiting for transfers between devices, shifted(): lax.ppermute(value, axis, [(source, source + steps) for source in range(i...  3.16 us
    unnamed x20, local copies, waits for them, and re-layouts  1.63 us
  transfers between devices with their start and end apart: 5, of which 2 were waited for; matrix products, arithmetic and copies ran while one was open for 11% of the time, Pallas kernels for 31%

profile of v24, /device:TPU:0, one launch (start us, length us, event | category | flops | bytes accessed | tf_op | source)
XLA Modules:
  0.0 60.1 jit_solution(2047901192284514434)
XLA Ops:
  0.0 0.5 collective-permute-start.1
  0.5 0.7 %slice_bitcast_fusion.1 = bf16[8,256]{1,0:T(8,128)(2,1)S(1)} fusion(bf16[2,1024,128]{2,1,0:T(8,128)(2,1)} %refs_14_.1), kind=kLoop, calls=%fused_computation.12 | loop fusion | bytes 8192 | tf_op jit(solution)/shard_map/reshape | solution.py:476
  1.1 0.7 %slice.27 = bf16[8,1024]{1,0:T(8,128)(2,1)S(1)} slice(bf16[1024,1024]{1,0:T(8,128)(2,1)} %x_ref.1), slice={[1016:1024], [0:1024]} | slice | bytes 32768 | tf_op jit(solution)/shard_map/slice | solution.py:476
  1.9 4.5 %collective-permute-start = (bf16[8,1280]{1,0:T(8,128)(2,1)S(1)}, bf16[8,1280]{1,0:T(8,128)(2,1)S(1)}, u32[]{:S(2)}, u32[]{:S(2)}) collective-permute-start(bf16[8,1280]{1,0:T(8,128)(2,1)S(1)} %pad_maximum_fusion), channel_id=1, source_target_pairs={{0,4},{4,8},{8,12},{1,5},{5,9},{9,13},{2,6},{6,10},{10,14},{3,7},{... | collective-permute-start | bytes 61448 | tf_op jit(solution)/shard_map/ppermute | solution.py:17
  6.3 0.8 %reduce-window.9 = s32[3,1]{0,1:T(1,128)S(1)} reduce-window(s32[3,1]{0,1:T(1,128)} %bitcast.41, s32[]{:T(128)} %constant.25.clone.1), window={size=3x1 pad=2_0x0_0}, to_apply=%region_0.0 | reduce-window | flops 6 | bytes 28 | tf_op jit(solution)/shard_map/reduce-window.4
  7.2 0.7 %bitcast_subtract_fusion = s32[3]{0:T(128)S(1)} fusion(s32[3]{0:T(128)} %param.19, s32[3,1]{0,1:T(1,128)S(1)} %reduce-window.9), kind=kLoop, calls=%fused_computation.19 | loop fusion | flops 3 | bytes 36 | tf_op jit(solution)/shard_map/sub | solution.py:31
  7.8 0.1 convert_reduce_fusion
  7.9 0.1 slice_bitcast_fusion.2
  8.0 0.0 copy-start.6
  8.0 0.1 slice_reduce_fusion
  8.1 0.7 %convert_element_type.37 = f32[2,4,128]{2,1,0:T(4,128)S(1)} convert(bf16[2,4,128]{2,1,0:T(4,128)(2,1)} %param.14) | non-fusion elementwise | flops 1024 | bytes 6144 | tf_op jit(solution)/shard_map/convert_element_type | solution.py:482
  8.8 0.0 collective-permute-done.tail_ref
  8.8 0.0 copy-start.7
  8.8 0.7 %pad_maximum_fusion.1.ownx_ref.refs_4_ = f32[2,13,128]{2,1,0:T(8,128)S(1)} fusion(f32[2,1,128]{2,1,0:T(1,128)} %bitcast.39, f32[2,4,128]{2,1,0:T(4,128)S(1)} %convert_element_type.37, f32[2,8,128]{2,1,0:T(8,128)S(1)} %convert_bitcast_fusion), kind=kLoop, calls=%fused_computation.3 | loop fusion | flops 6656 | bytes 26624 | tf_op jit(solution)/shard_map/concatenate | solution.py:480
  9.5 0.0 copy-start.4
  9.5 0.2 collective-permute-start.2
  9.8 0.1 fusion.2
  9.8 0.1 stack.39
  9.9 0.0 copy-start.9
  9.9 1.0 %copy.24.info_ref.refs_9_ = f32[1024,8]{1,0:T(8,128)} copy(f32[1024,8]{0,1:T(8,128)S(1)} %stack.39) | data formatting | bytes 65536 | tf_op jit(solution)/shard_map/stack | solution.py:496
  10.9 0.0 collective-permute-done.2.otherx_ref.refs_5_
  10.9 0.0 copy-start.5
  10.9 0.0 collective-permute-done.1.other_ref.refs_3_.refs_15_
  10.9 0.0 copy-start
  10.9 0.0 copy-done.7
  10.9 0.0 copy-done.4
  10.9 0.6 copy-done.5
  11.5 0.2 copy-done
  11.8 10.5 %shard_map.100 = (f32[256,1024]{1,0:T(8,128)}, f32[1024,16]{1,0:T(8,128)}, f32[1024,16]{1,0:T(8,128)}, f32[8,1,1024]{2,1,0:T(1,128)}, f32[1,1024]{1,0:T(1,128)},...) custom-call(bf16[1024,1024]{1,0:T(8,128)(2,1)} %x_ref.1, ...), custom_call_target="tpu_custom_call" | custom-call | tf_op jit(solution)/shard_map/pallas_call | solution.py:244
  22.3 0.0 copy-done.6
  22.3 3.5 %collective-permute-start.3 = (bf16[256,1024]{1,0:T(8,128)(2,1)}, bf16[256,1024]{1,0:T(8,128)(2,1)S(1)}, u32[]{:S(2)}, u32[]{:S(2)}) collective-permute-start(bf16[256,1024]{1,0:T(8,128)(2,1)} %get-tuple-element.23), channel_id=1, source_target_pairs={{0,4},{4,8},{8,12},{1,5},{5,9},{9,13},{2,6},{6,10},{10,14},{3,7},{... | collective-permute-start | bytes 1572872 | tf_op jit(solution)/shard_map/ppermute | solution.py:17
  25.8 0.0 copy-done.9
  25.8 0.1 broadcast_in_dim.9
  25.9 0.7 %reshape_reshape.3.refs_11_ = f32[1,1024]{1,0:T(1,128)} reshape(f32[16,64]{1,0:T(8,128)S(1)} %broadcast_in_dim.9) | data formatting | bytes 8192 | tf_op jit(solution)/shard_map/reshape;reshape | solution.py:489
  26.6 0.0 copy-start.2
  26.6 0.0 copy-start.8
  26.6 9.0 %shard_map.101 = (f32[512,1024]{1,0:T(8,128)}, bf16[512,256]{1,0:T(8,128)(2,1)}, f32[256,1024]{1,0:T(8,128)}) custom-call(bf16[1024,1024]{1,0:T(8,128)(2,1)} %get-tuple-element.24.refs_0_, bf16[1024,256]{1,0:T(8,128)(2,1)} %get-tuple-element.25.refs_1_, bf16[2,1024,128]{2,1,0:T(8,128)(2,1)} %refs_14_.1, bf16[2,1024,128]{2,1,0:T(8,128)(2,1)} %copy-done, ...), custom_call_target="tpu_custom_call" | custom-call | tf_op jit(solution)/shard_map/pallas_call | solution.py:374
  35.5 2.2 %collective-permute-done.3.refs_13_ = bf16[256,1024]{1,0:T(8,128)(2,1)S(1)} collective-permute-done((bf16[256,1024]{1,0:T(8,128)(2,1)}, bf16[256,1024]{1,0:T(8,128)(2,1)S(1)}, u32[]{:S(2)}, u32[]{:S(2)}) %collective-permute-start.3) | collective-permute-done | bytes 524320 | tf_op jit(solution)/shard_map/ppermute | solution.py:17
  37.7 0.0 copy-start.1
  37.7 0.0 copy-done.2
  37.7 0.0 copy-done.8
  37.7 0.2 add_convert_fusion
  37.9 4.3 %collective-permute-start.4 = (bf16[256,1024]{1,0:T(8,128)(2,1)S(1)}, bf16[256,1024]{1,0:T(8,128)(2,1)S(1)}, u32[]{:S(2)}, u32[]{:S(2)}) collective-permute-start(bf16[256,1024]{1,0:T(8,128)(2,1)S(1)} %add_convert_fusion), channel_id=1, source_target_pairs={{0,4},{4,8},{8,12},{1,5},{5,9},{9,13},{2,6},{6,10},{10,14},{3,7},{... | collective-permute-start | bytes 1572872 | tf_op jit(solution)/shard_map/ppermute | solution.py:17
  42.2 0.0 copy-done.1
  42.2 9.8 %shard_map.102 = (f32[512,1024]{1,0:T(8,128)}, bf16[512,256]{1,0:T(8,128)(2,1)}) custom-call(bf16[1024,1024]{1,0:T(8,128)(2,1)} %get-tuple-element.24.refs_0_, bf16[1024,256]{1,0:T(8,128)(2,1)} %get-tuple-element.25.refs_1_, bf16[2,1024,128]{2,1,0:T(8,128)(2,1)} %refs_14_.1, bf16[2,1024,128]{2,1,0:T(8,128)(2,1)} %copy-done, f32[2,13,128]{2,1,0:T(8,128)} %copy-done.4, ...), custom_call_target="tpu_custom_call" | custom-call | tf_op jit(solution)/shard_map/pallas_call | solution.py:374
  52.0 1.0 %collective-permute-done.4.ein_ref = bf16[256,1024]{1,0:T(8,128)(2,1)S(1)} collective-permute-done((bf16[256,1024]{1,0:T(8,128)(2,1)S(1)}, bf16[256,1024]{1,0:T(8,128)(2,1)S(1)}, u32[]{:S(2)}, u32[]{:S(2)}) %collective-permute-start.4) | collective-permute-done | bytes 524320 | tf_op jit(solution)/shard_map/ppermute | solution.py:17
  53.0 0.8 %copy-done.3 = bf16[256,1024]{1,0:T(8,128)(2,1)} copy-done((bf16[256,1024]{1,0:T(8,128)(2,1)}, bf16[256,1024]{1,0:T(8,128)(2,1)S(1)}, u32[]{:S(2)}) %copy-start.3) | copy-done | bytes 524312
  53.8 6.4 %shard_map.103 = bf16[1024,1024]{1,0:T(8,128)(2,1)} custom-call(f32[512,1024]{1,0:T(8,128)} %get-tuple-element.32.y_ref, f32[512,1024]{1,0:T(8,128)} %get-tuple-element.35.z_ref, bf16[512,256]{1,0:T(8,128)(2,1)} %get-tuple-element.36.c_ref, bf16[512,256]{1,0:T(8,128)(2,1)} %get-tuple-element.37.d_ref, f32[1,1024,16]{2,1,0:T(8,128)} %get-tuple-element.38.g_ref, ...), custom_call_target="tpu_custom_call" | custom-call | tf_op jit(solution)/shard_map/pallas_call | solution.py:403
  (7 shorter events, 0.0 us)
Async XLA Ops:
  0.0 10.9 %collective-permute-start.1 = (bf16[2,1024,128]{2,1,0:T(8,128)(2,1)}, bf16[2,1024,128]{2,1,0:T(8,128)(2,1)S(1)}, u32[]{:S(2)}, u32[]{:S(2)}) collective-permute-start(bf16[2,1024,128]{2,1,0:T(8,128)(2,1)} %refs_14_.1), channel_id=1, source_target_pairs={{0,1},{1,0},{2,3},{3,2},{4,5},{5,4},{6,7},{7,6},{8,9},{9,8},{10,11... | collective-permute-start | bytes 1572872 | tf_op jit(solution)/shard_map/ppermute | solution.py:27
  1.9 7.0 %collective-permute-start = (bf16[8,1280]{1,0:T(8,128)(2,1)S(1)}, bf16[8,1280]{1,0:T(8,128)(2,1)S(1)}, u32[]{:S(2)}, u32[]{:S(2)}) collective-permute-start(bf16[8,1280]{1,0:T(8,128)(2,1)S(1)} %pad_maximum_fusion), channel_id=1, source_target_pairs={{0,4},{4,8},{8,12},{1,5},{5,9},{9,13},{2,6},{6,10},{10,14},{3,7},{... | collective-permute-start | bytes 61448 | tf_op jit(solution)/shard_map/ppermute | solution.py:17
  8.0 14.3 %copy-start.6 = (f32[1024]{0:T(1024)}, f32[1024]{0:T(1024)S(1)}, u32[]{:S(2)}) copy-start(f32[1024]{0:T(1024)S(1)} %get-tuple-element.46) | copy-start | bytes 12292
  8.8 2.1 %copy-start.7 = (bf16[8,1280]{1,0:T(8,128)(2,1)}, bf16[8,1280]{1,0:T(8,128)(2,1)S(1)}, u32[]{:S(2)}) copy-start(bf16[8,1280]{1,0:T(8,128)(2,1)S(1)} %collective-permute-done.tail_ref) | copy-start | bytes 61444
  9.5 1.4 %copy-start.4 = (f32[2,13,128]{2,1,0:T(8,128)}, f32[2,13,128]{2,1,0:T(8,128)S(1)}, u32[]{:S(2)}) copy-start(f32[2,13,128]{2,1,0:T(8,128)S(1)} %pad_maximum_fusion.1.ownx_ref.refs_4_) | copy-start | bytes 39940
  9.5 1.4 %collective-permute-start.2 = (f32[2,13,128]{2,1,0:T(8,128)S(1)}, f32[2,13,128]{2,1,0:T(8,128)S(1)}, u32[]{:S(2)}, u32[]{:S(2)}) collective-permute-start(f32[2,13,128]{2,1,0:T(8,128)S(1)} %pad_maximum_fusion.1.ownx_ref.refs_4_), channel_id=1, source_target_pairs={{0,1},{1,0},{2,3},{3,2},{4,5},{5,4},{6,7},{7,6},{8,9},{9,8},{10,11... | collective-permute-start | bytes 39944 | tf_op jit(solution)/shard_map/ppermute | solution.py:27
  9.9 15.9 %copy-start.9 = (f32[16]{0:T(128)S(1)}, f32[16]{0:T(128)}, u32[]{:S(2)}) copy-start(f32[16]{0:T(128)} %param.18) | copy-start | bytes 196
  10.9 0.6 copy-start.5
  10.9 0.8 %copy-start = (bf16[2,1024,128]{2,1,0:T(8,128)(2,1)}, bf16[2,1024,128]{2,1,0:T(8,128)(2,1)S(1)}, u32[]{:S(2)}) copy-start(bf16[2,1024,128]{2,1,0:T(8,128)(2,1)S(1)} %collective-permute-done.1.other_ref.refs_3_.refs_15_) | copy-start | bytes 1572868
  22.3 15.4 %collective-permute-start.3 = (bf16[256,1024]{1,0:T(8,128)(2,1)}, bf16[256,1024]{1,0:T(8,128)(2,1)S(1)}, u32[]{:S(2)}, u32[]{:S(2)}) collective-permute-start(bf16[256,1024]{1,0:T(8,128)(2,1)} %get-tuple-element.23), channel_id=1, source_target_pairs={{0,4},{4,8},{8,12},{1,5},{5,9},{9,13},{2,6},{6,10},{10,14},{3,7},{... | collective-permute-start | bytes 1572872 | tf_op jit(solution)/shard_map/ppermute | solution.py:17
  26.6 11.1 %copy-start.2 = (f32[256,1024]{1,0:T(8,128)S(1)}, f32[256,1024]{1,0:T(8,128)}, u32[]{:S(2)}) copy-start(f32[256,1024]{1,0:T(8,128)} %get-tuple-element.40) | copy-start | bytes 3145732
  26.6 11.1 %copy-start.8 = (f32[1,1024]{1,0:T(1,128)S(1)}, f32[1,1024]{1,0:T(1,128)}, u32[]{:S(2)}) copy-start(f32[1,1024]{1,0:T(1,128)} %get-tuple-element.39) | copy-start | bytes 12292
  37.7 4.5 %copy-start.1 = (bf16[256,1024]{1,0:T(8,128)(2,1)}, bf16[256,1024]{1,0:T(8,128)(2,1)S(1)}, u32[]{:S(2)}) copy-start(bf16[256,1024]{1,0:T(8,128)(2,1)S(1)} %collective-permute-done.3.refs_13_) | copy-start | bytes 1572868
  37.9 15.1 %collective-permute-start.4 = (bf16[256,1024]{1,0:T(8,128)(2,1)S(1)}, bf16[256,1024]{1,0:T(8,128)(2,1)S(1)}, u32[]{:S(2)}, u32[]{:S(2)}) collective-permute-start(bf16[256,1024]{1,0:T(8,128)(2,1)S(1)} %add_convert_fusion), channel_id=1, source_target_pairs={{0,4},{4,8},{8,12},{1,5},{5,9},{9,13},{2,6},{6,10},{10,14},{3,7},{... | collective-permute-start | bytes 1572872 | tf_op jit(solution)/shard_map/ppermute | solution.py:17
  53.0 0.8 %copy-start.3 = (bf16[256,1024]{1,0:T(8,128)(2,1)}, bf16[256,1024]{1,0:T(8,128)(2,1)S(1)}, u32[]{:S(2)}) copy-start(bf16[256,1024]{1,0:T(8,128)(2,1)S(1)} %collective-permute-done.4.ein_ref) | copy-start | bytes 1572868
